TPU v7x, 512 devices: a whole 4x8x8 slice. The times are simulated.
512 devices in a mesh: req: 64 (over z, x, core), voc: 8 (over y).
Axes of the slice: x: 4, y: 8, z: 8, core: 2. Of those that a mesh axis runs over, the one named last changes fastest.
Arguments:
- hidden: bfloat16 [65536, 1600], P(('req', 'voc')), may hold values from -60 to 60
- norm_gain: float32 [1600], replicated, may hold values from 0.25 to 1.75
- unembed: bfloat16 [16384, 1600], P(('req', 'voc')), may hold values from -2 to 2
- targets: int32 [65536], P(('req', 'voc')), may hold values from 0 to 16383
- live: int32 [65536], P(('req', 'voc')), may hold values from 0 to 1, as said below
Outputs:
- logprob: float32 [65536], P(('req', 'voc'))
- entropy: float32 [65536], P(('req', 'voc'))
Inputs may be any that keep to these rules, and one draw needn't show every extreme that they name: Within each aligned block of 1024 slots (one owner's) the live slots form a prefix of 128 to 1024 slots, and in every draw at least one block is wholly live.
All inputs are finite; a program needn't handle non-finite values.
Results may differ from a plain program's by a relative error of at most 0.0067.
Values may be sent and summed in bfloat16 or wider, within the bound.
No kernel may reach another device: no remote copies, remote signals or barrier semaphores. Data moves between devices by JAX's collectives and lax.ppermute only.
A program may use at most 64 MiB of HBM per device.

v0:
```python
import jax
import jax.numpy as jnp
from jax import lax
from jax.sharding import PartitionSpec as P


def merged_2(value, axis, join):
    pieces = jax.tree.map(lambda part: lax.all_gather(part, axis), value)
    head = jax.tree.map(lambda part: part[0], pieces)
    tail = jax.tree.map(lambda part: part[1:], pieces)
    so_far, _ = lax.scan(lambda so_far, piece: (join(so_far, piece), None), head, tail)
    return so_far


def combine_stats(first, second):
    top = jnp.maximum(first[0], second[0])
    scale_one = jnp.exp(first[0] - top)
    scale_two = jnp.exp(second[0] - top)
    total = first[1] * scale_one + second[1] * scale_two
    spread = scale_one * (first[2] + (first[0] - top) * first[1]) + scale_two * (
        second[2] + (second[0] - top) * second[1]
    )
    return (top, total, spread, first[3] + second[3])


def on_device(hidden, norm_gain, unembed, targets, live):
    rows, wanted = (
        lax.all_gather(hidden, "voc", axis=0, tiled=True),
        lax.all_gather(targets, "voc", axis=0, tiled=True),
    )
    wide = rows.astype(jnp.float32)
    normed = (
        wide * lax.rsqrt(jnp.mean(wide * wide, axis=1, keepdims=True) + 1e-06) * norm_gain
    ).astype(jnp.bfloat16)
    groups = lax.axis_size("voc")
    column = lax.axis_index("voc")
    width = unembed.shape[0]
    count = normed.shape[0]
    zeros = jnp.zeros((count,), jnp.float32)
    start_carry = (jnp.full((count,), -1e30, jnp.float32), zeros, zeros, zeros)
    whole = lax.all_gather(unembed, "req", axis=0, tiled=True)
    stats = start_carry
    step = min(512, whole.shape[0])
    for first in range(0, whole.shape[0], step):
        piece = whole[first : first + step]
        logits = lax.dot_general(
            normed, piece, (((1,), (1,)), ((), ())), preferred_element_type=jnp.float32
        )
        local = first + jnp.arange(piece.shape[0], dtype=jnp.int32)
        vocab_ids = local // width * (groups * width) + column * width + local % width
        chosen = jnp.sum(jnp.where(vocab_ids[None, :] == wanted[:, None], logits, 0.0), axis=1)
        fold_top = jnp.max(logits, axis=1)
        shifted = logits - fold_top[:, None]
        weights = jnp.exp(shifted)
        newer = (fold_top, jnp.sum(weights, axis=1), jnp.sum(weights * shifted, axis=1), chosen)
        stats = combine_stats(stats, newer)
    mine = count // groups
    merged = merged_2(stats, "voc", combine_stats)
    top = lax.dynamic_slice_in_dim(merged[0], column * mine, mine)
    total = lax.dynamic_slice_in_dim(merged[1], column * mine, mine)
    spread = lax.dynamic_slice_in_dim(merged[2], column * mine, mine)
    picked = lax.dynamic_slice_in_dim(merged[3], column * mine, mine)
    mask = live.astype(jnp.float32)
    logprob = (picked - top - jnp.log(total)) * mask
    entropy = (jnp.log(total) - spread / total) * mask
    return (logprob, entropy)


def solution(mesh):
    return jax.shard_map(
        on_device,
        mesh=mesh,
        in_specs=(
            P(("req", "voc"), None),
            P(),
            P(("req", "voc"), None),
            P(("req", "voc")),
            P(("req", "voc")),
        ),
        out_specs=(P(("req", "voc")), P(("req", "voc"))),
        check_vma=False,
    )
```

profile of v0, /device:TPU:16, one launch (start us, length us, event | category | flops | bytes accessed | tf_op | source)
XLA Modules:
  0.0 284.1 jit_solution(10954525450019727820)
XLA Ops:
  7.2 0.0 copy-start.3
  7.2 0.0 all-gather.8.cloned.1.call-start
  7.2 0.7 all-gather.8.cloned.1.call-update
  7.9 0.0 all-gather.10.cloned.1.call-start
  8.0 0.7 all-gather.10.cloned.1.call-update
  8.7 16.5 %all-gather.4 = s32[8,1,128]{2,1,0:T(1,128)S(1)} all-gather(s32[1,1,128]{2,1,0:T(1,128)} %bitcast.74), channel_id=1, replica_groups=mesh['req'=64,'voc'=8] {'voc'}, dimensions={0}, use_global_device_ids=true | all-gather | bytes 4608 | tf_op jit(solution)/shard_map/all_gather | solution.py:29
  25.1 46.9 %all-gather.8.cloned.1.call-done = bf16[1024,1600]{0,1:T(8,128)(2,1)} async-done(((bf16[128,1600]{0,1:T(8,128)(2,1)}), bf16[1024,1600]{0,1:T(8,128)(2,1)}) %all-gather.8.cloned.1.call-update) | async-done | bytes 3276816 | tf_op jit(solution)/shard_map/all_gather | solution.py:28
  72.1 0.0 copy-start
  72.1 2.8 fusion
  74.9 87.4 %all-gather.10.cloned.1.call-done = bf16[2048,1600]{1,0:T(8,128)(2,1)} async-done(((bf16[32,1600]{1,0:T(8,128)(2,1)}), bf16[2048,1600]{1,0:T(8,128)(2,1)}) %all-gather.10.cloned.1.call-update) | async-done | bytes 6553616 | tf_op jit(solution)/shard_map/all_gather | solution.py:41
  162.3 0.0 copy-done.3
  162.3 0.0 copy-done
  162.3 0.0 copy-start.2
  162.3 3.8 %fusion.44 = (f32[1024]{0:T(1024)S(1)}, f32[1024,512]{0,1:T(8,128)S(1)}) fusion(bf16[1024,1600]{0,1:T(8,128)(2,1)S(1)} %copy-done, f32[1600]{0:T(1024)S(1)} %copy-done.3, f32[1024]{0:T(1024)S(1)} %add_rsqrt_fusion, bf16[2048,1600]{1,0:T(8,128)(2,1)} %all-gather.10.cloned.1.call-done), kind=kOutput, calls=%fused_computation.103 | convolution fusion | flops 1684798464 | bytes 7092480 | tf_op jit(solution)/shard_map/dot_general | solution.py:46
  166.2 0.0 copy-done.2
  166.2 2.2 fusion.45
  168.4 2.2 fusion.46
  170.7 2.2 fusion.47
  172.9 0.0 copy-start.1
  173.0 3.9 %fusion.3 = (f32[1024]{0:T(1024)S(1)}, f32[1024]{0:T(1024)S(1)}, f32[1024]{0:T(1024)S(1)}, f32[1024]{0:T(1024)S(1)}, f32[1024]{0:T(1024)S(1)}, /*index=5*/f32[10...) fusion(f32[1024,512]{0,1:T(8,128)S(1)} %get-tuple-element.108, ...), kind=kLoop, calls=%fused_computation.19 | loop fusion | flops 14667776 | bytes 8466432 | tf_op jit(solution)/shard_map/reduce_sum | solution.py:55
  176.9 25.4 %all-gather = f32[8192]{0:T(1024)S(1)} all-gather(f32[1024]{0:T(1024)S(1)} %add_add_fusion), channel_id=2, replica_groups=mesh['req'=64,'voc'=8] {'voc'}, dimensions={0}, use_global_device_ids=true | all-gather | bytes 36864 | tf_op jit(solution)/shard_map/all_gather | solution.py:8
  202.3 0.1 add_bitcast_fusion
  202.4 24.5 %all-gather.2 = f32[8,1,1024]{2,1,0:T(1,128)S(1)} all-gather(f32[1,1,1024]{2,1,0:T(1,128)S(1)} %get-tuple-element.94), channel_id=1, replica_groups=mesh['req'=64,'voc'=8] {'voc'}, dimensions={0}, use_global_device_ids=true | all-gather | bytes 36864 | tf_op jit(solution)/shard_map/all_gather | solution.py:8
  226.9 24.5 %all-gather.1 = f32[8,1,1024]{2,1,0:T(1,128)S(1)} all-gather(f32[1,1,1024]{2,1,0:T(1,128)S(1)} %get-tuple-element.95), channel_id=1, replica_groups=mesh['req'=64,'voc'=8] {'voc'}, dimensions={0}, use_global_device_ids=true | all-gather | bytes 36864 | tf_op jit(solution)/shard_map/all_gather | solution.py:8
  251.3 24.5 %all-gather.3 = f32[8,1,1024]{2,1,0:T(1,128)S(1)} all-gather(f32[1,1,1024]{2,1,0:T(1,128)S(1)} %get-tuple-element.88), channel_id=1, replica_groups=mesh['req'=64,'voc'=8] {'voc'}, dimensions={0}, use_global_device_ids=true | all-gather | bytes 36864 | tf_op jit(solution)/shard_map/all_gather | solution.py:8
  275.8 0.8 while.16
  276.7 0.0 copy-done.1
  276.7 0.6 subtract_multiply_fusion
  (59 shorter events, 0.5 us)
Async XLA Ops:
  7.2 155.2 %copy-start.3 = (f32[1600]{0:T(1024)S(1)}, f32[1600]{0:T(1024)}, u32[]{:S(2)}) copy-start(f32[1600]{0:T(1024)} %param.8) | copy-start | bytes 19204
  7.2 64.9 %all-gather.8.cloned.1.call-start = ((), (), s32[]{:S(2)}) async-start(), calls=%async_computation | async-start | bytes 3686400 | tf_op jit(solution)/shard_map/all_gather | solution.py:28
  7.9 154.4 %all-gather.10.cloned.1.call-start = ((), (), s32[]{:S(2)}) async-start(), calls=%async_computation.1 | async-start | bytes 6922240 | tf_op jit(solution)/shard_map/all_gather | solution.py:41
  72.1 90.2 %copy-start = (bf16[1024,1600]{0,1:T(8,128)(2,1)S(1)}, bf16[1024,1600]{0,1:T(8,128)(2,1)}, u32[]{:S(2)}) copy-start(bf16[1024,1600]{0,1:T(8,128)(2,1)} %all-gather.8.cloned.1.call-done) | copy-start | bytes 9830404
  162.3 3.8 %copy-start.2 = (bf16[2048,1600]{1,0:T(8,128)(2,1)S(1)}, bf16[2048,1600]{1,0:T(8,128)(2,1)}, u32[]{:S(2)}) copy-start(bf16[2048,1600]{1,0:T(8,128)(2,1)} %all-gather.10.cloned.1.call-done) | copy-start | bytes 19660804
  172.9 103.7 %copy-start.1 = (s32[128]{0:T(128)S(1)}, s32[128]{0:T(128)}, u32[]{:S(2)}) copy-start(s32[128]{0:T(128)} %param.11) | copy-start | bytes 1540
Sparse Core Ops, SparseCore 0:
  10.0 62.0 all-gather.7
  75.4 86.8 all-gather.9
where the time goes:
time: 284 us
  waiting for transfers between devices  136 us (48%)
  blocking collectives  115 us (40%)
  between operations  14.2 us (5%)
  matrix products  10.6 us (4%)
  other arithmetic  7.67 us (3%)
    all_gather x4, blocking collectives, merged_2(): pieces = jax.tree.map(lambda part: lax.all_gather(part, axis), value)  98.8 us
    all_gather x1, waiting for transfers between devices, on_device(): whole = lax.all_gather(unembed, 'req', axis=0, tiled=True)  87.4 us
    all_gather x1, waiting for transfers between devices, on_device(): lax.all_gather(hidden, 'voc', axis=0, tiled=True)  46.9 us
    all_gather x1, blocking collectives, on_device(): lax.all_gather(targets, 'voc', axis=0, tiled=True)  16.5 us
    dot_general x4, matrix products, on_device(): lax.dot_general(normed, piece, (((1,), (1,)), ((), ())), preferred_elemen...  10.6 us
  transfers between devices with their start and end apart: 2, of which 2 were waited for; matrix products, arithmetic and copies ran while one was open for 1% of the time, Pallas kernels for 0%

commit v1 on v0

v1 whole, which is shorter than its diff:
```python
import jax
import jax.numpy as jnp
from jax import lax
from jax.sharding import Mesh, PartitionSpec as P

FLAT = ("z", "x", "c", "y")


def combine_stats(first, second):
    top = jnp.maximum(first[0], second[0])
    scale_one = jnp.exp(first[0] - top)
    scale_two = jnp.exp(second[0] - top)
    total = first[1] * scale_one + second[1] * scale_two
    spread = scale_one * (first[2] + (first[0] - top) * first[1]) + scale_two * (
        second[2] + (second[0] - top) * second[1]
    )
    return (top, total, spread, first[3] + second[3])


def shift(value, axis, size, step):
    return lax.ppermute(value, axis, [(i, (i + step) % size) for i in range(size)])


def chunk_stats(normed, piece, ids, wanted):
    logits = lax.dot_general(
        normed, piece, (((1,), (1,)), ((), ())), preferred_element_type=jnp.float32
    )
    chosen = jnp.sum(jnp.where(ids[None, :] == wanted[:, None], logits, 0.0), axis=1)
    fold_top = jnp.max(logits, axis=1)
    shifted = logits - fold_top[:, None]
    weights = jnp.exp(shifted)
    return (fold_top, jnp.sum(weights, axis=1), jnp.sum(weights * shifted, axis=1), chosen)


def on_device(hidden, norm_gain, unembed, targets, live):
    ny = lax.axis_size("y")
    nc = lax.axis_size("c")
    y = lax.axis_index("y")
    c = lax.axis_index("c")
    mine = hidden.shape[0]
    width = unembed.shape[0]

    wide = hidden.astype(jnp.float32)
    normed = (
        wide * lax.rsqrt(jnp.mean(wide * wide, axis=1, keepdims=True) + 1e-06) * norm_gain
    ).astype(jnp.bfloat16)

    blocks = [None] * ny
    blocks[0] = (normed, targets)
    fwd = ny // 2
    cur = (normed, targets)
    for d in range(1, fwd + 1):
        cur = shift(cur, "y", ny, 1)
        blocks[ny - d] = cur
    cur = (normed, targets)
    for d in range(1, ny - fwd):
        cur = shift(cur, "y", ny, -1)
        blocks[d] = cur
    rows = jnp.concatenate([b[0] for b in blocks], axis=0)
    wanted = jnp.concatenate([b[1] for b in blocks], axis=0)

    half = lax.all_gather(unembed, ("z", "x"), axis=0, tiled=True)
    other = shift(half, "c", nc, 1)

    def ids_of(core):
        local = jnp.arange(half.shape[0], dtype=jnp.int32)
        return ((local // width) * (nc * ny) + core * ny + y) * width + local % width

    count = rows.shape[0]
    zeros = jnp.zeros((count,), jnp.float32)
    stats = (jnp.full((count,), -1e30, jnp.float32), zeros, zeros, zeros)
    step = min(512, half.shape[0])
    for table, core in ((half, c), (other, (c + 1) % nc)):
        ids = ids_of(core)
        for first in range(0, table.shape[0], step):
            stats = combine_stats(
                stats,
                chunk_stats(rows, table[first : first + step], ids[first : first + step], wanted),
            )

    packed = jnp.stack(stats).reshape(4, ny, mine)
    merged = tuple(packed[:, 0])
    for d in range(1, ny):
        got = shift(packed[:, d], "y", ny, d)
        merged = combine_stats(merged, tuple(got))
    top, total, spread, picked = merged
    mask = live.astype(jnp.float32)
    logprob = (picked - top - jnp.log(total)) * mask
    entropy = (jnp.log(total) - spread / total) * mask
    return (logprob, entropy)


def solution(mesh):
    nz, nx, nc = 8, 4, 2
    ny = mesh.devices.shape[1]
    req = mesh.devices.shape[0]
    nz = req // (nx * nc)
    flat = Mesh(mesh.devices.reshape(nz, nx, nc, ny), FLAT)
    return jax.shard_map(
        on_device,
        mesh=flat,
        in_specs=(P(FLAT, None), P(), P(FLAT, None), P(FLAT), P(FLAT)),
        out_specs=(P(FLAT), P(FLAT)),
        check_vma=False,
    )
```

time: 284 us -> 204 us (0.72)
  the two profiles are of different devices: /device:TPU:16 before, /device:TPU:1 now
where the time goes in v1:
time: 204 us; the launch traced here: 200 us
  starting transfers between devices  78 us (38%)
  waiting for transfers between devices  74.2 us (36%)
  between operations  14.5 us (7%)
  local copies, waits for them, and re-layouts  13.7 us (7%)
  matrix products  10.6 us (5%)
  other arithmetic  8.53 us (4%)
    ppermute x22, starting transfers between devices, shift(): lax.ppermute(value, axis, [(i, (i + step) % size) for i in range(size)])  78 us
    all_gather x1, waiting for transfers between devices, on_device(): half = lax.all_gather(unembed, ('z', 'x'), axis=0, tiled=True)  54.6 us
    ppermute x22, waiting for transfers between devices, shift(): lax.ppermute(value, axis, [(i, (i + step) % size) for i in range(size)])  18.9 us
    dot_general x4, matrix products, chunk_stats(): lax.dot_general(normed, piece, (((1,), (1,)), ((), ())), preferred_elemen...  10.6 us
    unnamed x19, local copies, waits for them, and re-layouts  7.66 us
    all_gather x1, local copies, waits for them, and re-layouts, on_device(): half = lax.all_gather(unembed, ('z', 'x'), axis=0, tiled=True)  4.26 us
  transfers between devices with their start and end apart: 23, of which 6 were waited for; matrix products, arithmetic and copies ran while one was open for 12% of the time, Pallas kernels for 0%

profile of v1, /device:TPU:1, one launch (start us, length us, event | category | flops | bytes accessed | tf_op | source)
XLA Modules:
  0.0 199.6 jit_solution(11467726991118370099)
XLA Ops:
  7.2 0.0 all-gather.2.cloned.1.call-start
  7.2 0.7 all-gather.2.cloned.1.call-update
  7.9 1.2 fusion.12
  9.1 2.2 %constant_dynamic-update-slice_fusion.8 = (bf16[1024,1600]{0,1:T(8,128)(2,1)}, bf16[128,1600]{0,1:T(8,128)(2,1)}) fusion(f32[1600]{0:T(1024)} %param.6, f32[128]{0:T(128)S(1)} %add_rsqrt_fusion, bf16[128,1600]{0,1:T(8,128)(2,1)} %param.5), kind=kLoop, calls=%fused_computation.37 | loop fusion | flops 819199 | bytes 1235712
  11.4 5.9 %collective-permute-start.7 = (bf16[128,1600]{0,1:T(8,128)(2,1)}, bf16[128,1600]{0,1:T(8,128)(2,1)}, u32[]{:S(2)}, u32[]{:S(2)}) collective-permute-start(bf16[128,1600]{0,1:T(8,128)(2,1)} %get-tuple-element.18), channel_id=1, source_target_pairs={{0,7},{1,0},{2,1},{3,2},{4,3},{5,4},{6,5},{7,6},{8,15},{9,8},{10,9... | collective-permute-start | bytes 1228808 | tf_op jit(solution)/shard_map/ppermute | solution.py:21
  17.3 1.9 collective-permute-start.10
  19.2 4.6 %collective-permute-start = (s32[128]{0:T(128)}, s32[128]{0:T(128)S(1)}, u32[]{:S(2)}, u32[]{:S(2)}) collective-permute-start(s32[128]{0:T(128)} %param.8), channel_id=1, source_target_pairs={{0,7},{1,0},{2,1},{3,2},{4,3},{5,4},{6,5},{7,6},{8,15},{9,8},{10,9... | collective-permute-start | bytes 1544 | tf_op jit(solution)/shard_map/ppermute | solution.py:21
  23.8 1.9 collective-permute-start.3
  25.8 0.7 constant_dynamic-update-slice_fusion
  26.5 4.6 %collective-permute-start.1 = (s32[128]{0:T(128)S(1)}, s32[128]{0:T(128)S(1)}, u32[]{:S(2)}, u32[]{:S(2)}) collective-permute-start(s32[128]{0:T(128)S(1)} %collective-permute-done), channel_id=1, source_target_pairs={{0,7},{1,0},{2,1},{3,2},{4,3},{5,4},{6,5},{7,6},{8,15},{9,8},{10,9... | collective-permute-start | bytes 1544 | tf_op jit(solution)/shard_map/ppermute | solution.py:21
  31.1 1.9 collective-permute-start.4
  33.0 4.6 %collective-permute-start.2 = (s32[128]{0:T(128)S(1)}, s32[128]{0:T(128)S(1)}, u32[]{:S(2)}, u32[]{:S(2)}) collective-permute-start(s32[128]{0:T(128)S(1)} %collective-permute-done.1), channel_id=1, source_target_pairs={{0,7},{1,0},{2,1},{3,2},{4,3},{5,4},{6,5},{7,6},{8,15},{9,8},{10,9... | collective-permute-start | bytes 1544 | tf_op jit(solution)/shard_map/ppermute | solution.py:21
  37.6 1.9 collective-permute-start.5
  39.5 1.9 collective-permute-start.11
  41.5 1.6 collective-permute-done.5
  43.1 1.9 collective-permute-start.6
  45.0 54.6 %all-gather.2.cloned.1.call-done = bf16[1024,1600]{1,0:T(8,128)(2,1)} async-done(((bf16[32,1600]{1,0:T(8,128)(2,1)}), bf16[1024,1600]{1,0:T(8,128)(2,1)}) %all-gather.2.cloned.1.call-update) | async-done | bytes 3276816 | tf_op jit(solution)/shard_map/all_gather | solution.py:62
  99.6 4.3 %copy.9 = bf16[1024,1600]{0,1:T(8,128)(2,1)S(1)} copy(bf16[1024,1600]{1,0:T(8,128)(2,1)} %all-gather.2.cloned.1.call-done) | data formatting | bytes 6553600 | tf_op jit(solution)/shard_map/all_gather | solution.py:62
  103.9 6.4 %collective-permute-start.14 = (bf16[1024,1600]{0,1:T(8,128)(2,1)S(1)}, bf16[1024,1600]{0,1:T(8,128)(2,1)S(1)}, u32[]{:S(2)}, u32[]{:S(2)}) collective-permute-start(bf16[1024,1600]{0,1:T(8,128)(2,1)S(1)} %copy.9), channel_id=1, source_target_pairs={{0,8},{8,0},{1,9},{9,1},{2,10},{10,2},{3,11},{11,3},{4,12},{12,4},... | collective-permute-start | bytes 9830408 | tf_op jit(solution)/shard_map/ppermute | solution.py:21
  110.3 4.5 %collective-permute-start.8 = (bf16[128,1600]{0,1:T(8,128)(2,1)}, bf16[128,1600]{0,1:T(8,128)(2,1)S(1)}, u32[]{:S(2)}, u32[]{:S(2)}) collective-permute-start(bf16[128,1600]{0,1:T(8,128)(2,1)} %collective-permute-done.7), channel_id=1, source_target_pairs={{0,7},{1,0},{2,1},{3,2},{4,3},{5,4},{6,5},{7,6},{8,15},{9,8},{10,9... | collective-permute-start | bytes 1228808 | tf_op jit(solution)/shard_map/ppermute | solution.py:21
  114.8 1.9 collective-permute-start.12
  116.8 7.2 %collective-permute-done.8 = bf16[128,1600]{0,1:T(8,128)(2,1)S(1)} collective-permute-done((bf16[128,1600]{0,1:T(8,128)(2,1)}, bf16[128,1600]{0,1:T(8,128)(2,1)S(1)}, u32[]{:S(2)}, u32[]{:S(2)}) %collective-permute-start.8) | collective-permute-done | bytes 409632 | tf_op jit(solution)/shard_map/ppermute | solution.py:21
  124.0 5.2 %collective-permute-start.9 = (bf16[128,1600]{0,1:T(8,128)(2,1)S(1)}, bf16[128,1600]{0,1:T(8,128)(2,1)S(1)}, u32[]{:S(2)}, u32[]{:S(2)}) collective-permute-start(bf16[128,1600]{0,1:T(8,128)(2,1)S(1)} %collective-permute-done.8), channel_id=1, source_target_pairs={{0,7},{1,0},{2,1},{3,2},{4,3},{5,4},{6,5},{7,6},{8,15},{9,8},{10,9... | collective-permute-start | bytes 1228808 | tf_op jit(solution)/shard_map/ppermute | solution.py:21
  129.2 1.8 constant_dynamic-update-slice_fusion.7
  131.0 1.9 collective-permute-start.13
  133.0 0.8 constant_dynamic-update-slice_fusion.6
  133.8 3.4 %collective-permute-done.9 = bf16[128,1600]{0,1:T(8,128)(2,1)S(1)} collective-permute-done((bf16[128,1600]{0,1:T(8,128)(2,1)S(1)}, bf16[128,1600]{0,1:T(8,128)(2,1)S(1)}, u32[]{:S(2)}, u32[]{:S(2)}) %collective-permute-start.9) | collective-permute-done | bytes 409632 | tf_op jit(solution)/shard_map/ppermute | solution.py:21
  137.2 0.8 constant_dynamic-update-slice_fusion.5
  138.0 6.0 %collective-permute-done.13 = bf16[128,1600]{0,1:T(8,128)(2,1)S(1)} collective-permute-done((bf16[128,1600]{0,1:T(8,128)(2,1)S(1)}, bf16[128,1600]{0,1:T(8,128)(2,1)S(1)}, u32[]{:S(2)}, u32[]{:S(2)}) %collective-permute-start.13) | collective-permute-done | bytes 409632 | tf_op jit(solution)/shard_map/ppermute | solution.py:21
  144.0 0.8 constant_dynamic-update-slice_fusion.4
  144.8 0.8 constant_dynamic-update-slice_fusion.3
  145.6 1.8 constant_dynamic-update-slice_fusion.2
  147.5 1.8 constant_dynamic-update-slice_fusion.1
  149.3 4.2 %fusion.87 = (f32[1024]{0:T(1024)S(1)}, f32[1024,512]{0,1:T(8,128)S(1)}) fusion(bf16[1024,1600]{0,1:T(8,128)(2,1)} %constant_dynamic-update-slice_fusion.1, bf16[1024,1600]{1,0:T(8,128)(2,1)S(1)} %copy-done), kind=kOutput, calls=%fused_computation.198 | convolution fusion | flops 1678244864 | bytes 7081984 | tf_op jit(solution)/shard_map/dot_general | solution.py:25
  153.5 2.1 %fusion.90 = (f32[1024]{0:T(1024)S(1)}, f32[1024,512]{0,1:T(8,128)S(1)}) fusion(bf16[1024,1600]{0,1:T(8,128)(2,1)S(1)} %copy-done.1, bf16[1024,1600]{1,0:T(8,128)(2,1)S(1)} %copy-done), kind=kOutput, calls=%fused_computation.201 | convolution fusion | flops 1678244864 | bytes 7081984 | tf_op jit(solution)/shard_map/dot_general | solution.py:25
  155.6 2.1 %fusion.88 = (f32[1024]{0:T(1024)S(1)}, f32[1024,512]{0,1:T(8,128)S(1)}) fusion(bf16[1024,1600]{0,1:T(8,128)(2,1)S(1)} %copy-done.1, bf16[1024,1600]{0,1:T(8,128)(2,1)S(1)} %collective-permute-done.14), kind=kOutput, calls=%fused_computation.199 | convolution fusion | flops 1678244864 | bytes 7016448 | tf_op jit(solution)/shard_map/dot_general | solution.py:25
  157.7 2.2 %fusion.89 = (f32[1024]{0:T(1024)S(1)}, f32[1024,512]{0,1:T(8,128)S(1)}) fusion(bf16[1024,1600]{0,1:T(8,128)(2,1)S(1)} %copy-done.1, bf16[1024,1600]{0,1:T(8,128)(2,1)S(1)} %collective-permute-done.14), kind=kOutput, calls=%fused_computation.200 | convolution fusion | flops 1678244864 | bytes 7016448 | tf_op jit(solution)/shard_map/dot_general | solution.py:25
  159.9 3.9 %exponential_reduce_fusion.2 = (f32[1024]{0:T(1024)S(1)}, f32[1024]{0:T(1024)S(1)}, f32[1024]{0:T(1024)S(1)}, f32[1024]{0:T(1024)S(1)}, f32[1024]{0:T(1024)S(1)}...) fusion(f32[1024,512]{0,1:T(8,128)S(1)} %get-tuple-element.43, ...), kind=kLoop, calls=%fused_computation.5 | loop fusion | flops 14667776 | bytes 8466432 | tf_op jit(solution)/shard_map/reduce_sum | solution.py:32
  163.9 1.9 collective-permute-start.15
  165.8 4.8 %collective-permute-start.18 = (f32[4,128]{1,0:T(4,128)S(1)}, f32[4,128]{1,0:T(4,128)S(1)}, u32[]{:S(2)}, u32[]{:S(2)}) collective-permute-start(f32[4,128]{1,0:T(4,128)S(1)} %bitcast.593), channel_id=1, source_target_pairs={{0,4},{1,5},{2,6},{3,7},{4,0},{5,1},{6,2},{7,3},{8,12},{9,13},{10,... | collective-permute-start | bytes 6152 | tf_op jit(solution)/shard_map/ppermute | solution.py:21
  170.6 2.3 %collective-permute-start.19 = (f32[4,128]{1,0:T(4,128)S(1)}, f32[4,128]{1,0:T(4,128)S(1)}, u32[]{:S(2)}, u32[]{:S(2)}) collective-permute-start(f32[4,128]{1,0:T(4,128)S(1)} %bitcast.592), channel_id=1, source_target_pairs={{0,5},{1,6},{2,7},{3,0},{4,1},{5,2},{6,3},{7,4},{8,13},{9,14},{10,... | collective-permute-start | bytes 6152 | tf_op jit(solution)/shard_map/ppermute | solution.py:21
  173.0 6.6 %collective-permute-start.20 = (f32[4,128]{1,0:T(4,128)S(1)}, f32[4,128]{1,0:T(4,128)S(1)}, u32[]{:S(2)}, u32[]{:S(2)}) collective-permute-start(f32[4,128]{1,0:T(4,128)S(1)} %bitcast.591), channel_id=1, source_target_pairs={{0,6},{1,7},{2,0},{3,1},{4,2},{5,3},{6,4},{7,5},{8,14},{9,15},{10,... | collective-permute-start | bytes 6152 | tf_op jit(solution)/shard_map/ppermute | solution.py:21
  179.6 1.9 collective-permute-start.16
  181.6 3.6 %collective-permute-start.17 = (f32[4,128]{1,0:T(4,128)S(1)}, f32[4,128]{1,0:T(4,128)S(1)}, u32[]{:S(2)}, u32[]{:S(2)}) collective-permute-start(f32[4,128]{1,0:T(4,128)S(1)} %bitcast.596), channel_id=1, source_target_pairs={{0,3},{1,4},{2,5},{3,6},{4,7},{5,0},{6,1},{7,2},{8,11},{9,12},{10,... | collective-permute-start | bytes 6152 | tf_op jit(solution)/shard_map/ppermute | solution.py:21
  185.2 5.8 %collective-permute-start.21 = (f32[4,128]{1,0:T(4,128)S(1)}, f32[4,128]{1,0:T(4,128)S(1)}, u32[]{:S(2)}, u32[]{:S(2)}) collective-permute-start(f32[4,128]{1,0:T(4,128)S(1)} %bitcast.595), channel_id=1, source_target_pairs={{0,7},{1,0},{2,1},{3,2},{4,3},{5,4},{6,5},{7,6},{8,15},{9,8},{10,9... | collective-permute-start | bytes 6152 | tf_op jit(solution)/shard_map/ppermute | solution.py:21
  191.0 0.7 collective-permute-done.21
  191.7 0.5 subtract_multiply_fusion
  192.2 0.5 fusion.82
  (39 shorter events, 0.2 us)
Async XLA Ops:
  7.2 92.5 %all-gather.2.cloned.1.call-start = ((), (), s32[]{:S(2)}) async-start(), calls=%async_computation | async-start | bytes 3514368 | tf_op jit(solution)/shard_map/all_gather | solution.py:62
  11.4 98.9 %collective-permute-start.7 = (bf16[128,1600]{0,1:T(8,128)(2,1)}, bf16[128,1600]{0,1:T(8,128)(2,1)}, u32[]{:S(2)}, u32[]{:S(2)}) collective-permute-start(bf16[128,1600]{0,1:T(8,128)(2,1)} %get-tuple-element.18), channel_id=1, source_target_pairs={{0,7},{1,0},{2,1},{3,2},{4,3},{5,4},{6,5},{7,6},{8,15},{9,8},{10,9... | collective-permute-start | bytes 1228808 | tf_op jit(solution)/shard_map/ppermute | solution.py:21
  17.3 22.2 %collective-permute-start.10 = (bf16[128,1600]{0,1:T(8,128)(2,1)}, bf16[128,1600]{0,1:T(8,128)(2,1)}, u32[]{:S(2)}, u32[]{:S(2)}) collective-permute-start(bf16[128,1600]{0,1:T(8,128)(2,1)} %get-tuple-element.18), channel_id=1, source_target_pairs={{0,1},{1,2},{2,3},{3,4},{4,5},{5,6},{6,7},{7,0},{8,9},{9,10},{10,1... | collective-permute-start | bytes 1228808 | tf_op jit(solution)/shard_map/ppermute | solution.py:21
  19.2 7.3 %collective-permute-start = (s32[128]{0:T(128)}, s32[128]{0:T(128)S(1)}, u32[]{:S(2)}, u32[]{:S(2)}) collective-permute-start(s32[128]{0:T(128)} %param.8), channel_id=1, source_target_pairs={{0,7},{1,0},{2,1},{3,2},{4,3},{5,4},{6,5},{7,6},{8,15},{9,8},{10,9... | collective-permute-start | bytes 1544 | tf_op jit(solution)/shard_map/ppermute | solution.py:21
  23.8 7.2 %collective-permute-start.3 = (s32[128]{0:T(128)}, s32[128]{0:T(128)S(1)}, u32[]{:S(2)}, u32[]{:S(2)}) collective-permute-start(s32[128]{0:T(128)} %param.8), channel_id=1, source_target_pairs={{0,1},{1,2},{2,3},{3,4},{4,5},{5,6},{6,7},{7,0},{8,9},{9,10},{10,1... | collective-permute-start | bytes 1544 | tf_op jit(solution)/shard_map/ppermute | solution.py:21
  26.5 6.5 %collective-permute-start.1 = (s32[128]{0:T(128)S(1)}, s32[128]{0:T(128)S(1)}, u32[]{:S(2)}, u32[]{:S(2)}) collective-permute-start(s32[128]{0:T(128)S(1)} %collective-permute-done), channel_id=1, source_target_pairs={{0,7},{1,0},{2,1},{3,2},{4,3},{5,4},{6,5},{7,6},{8,15},{9,8},{10,9... | collective-permute-start | bytes 1544 | tf_op jit(solution)/shard_map/ppermute | solution.py:21
  31.1 6.5 %collective-permute-start.4 = (s32[128]{0:T(128)S(1)}, s32[128]{0:T(128)S(1)}, u32[]{:S(2)}, u32[]{:S(2)}) collective-permute-start(s32[128]{0:T(128)S(1)} %collective-permute-done.3), channel_id=1, source_target_pairs={{0,1},{1,2},{2,3},{3,4},{4,5},{5,6},{6,7},{7,0},{8,9},{9,10},{10,1... | collective-permute-start | bytes 1544 | tf_op jit(solution)/shard_map/ppermute | solution.py:21
  33.0 77.3 %collective-permute-start.2 = (s32[128]{0:T(128)S(1)}, s32[128]{0:T(128)S(1)}, u32[]{:S(2)}, u32[]{:S(2)}) collective-permute-start(s32[128]{0:T(128)S(1)} %collective-permute-done.1), channel_id=1, source_target_pairs={{0,7},{1,0},{2,1},{3,2},{4,3},{5,4},{6,5},{7,6},{8,15},{9,8},{10,9... | collective-permute-start | bytes 1544 | tf_op jit(solution)/shard_map/ppermute | solution.py:21
  37.6 5.5 %collective-permute-start.5 = (s32[128]{0:T(128)S(1)}, s32[128]{0:T(128)S(1)}, u32[]{:S(2)}, u32[]{:S(2)}) collective-permute-start(s32[128]{0:T(128)S(1)} %collective-permute-done.4), channel_id=1, source_target_pairs={{0,1},{1,2},{2,3},{3,4},{4,5},{5,6},{6,7},{7,0},{8,9},{9,10},{10,1... | collective-permute-start | bytes 1544 | tf_op jit(solution)/shard_map/ppermute | solution.py:21
  39.5 75.3 %collective-permute-start.11 = (bf16[128,1600]{0,1:T(8,128)(2,1)}, bf16[128,1600]{0,1:T(8,128)(2,1)}, u32[]{:S(2)}, u32[]{:S(2)}) collective-permute-start(bf16[128,1600]{0,1:T(8,128)(2,1)} %collective-permute-done.10), channel_id=1, source_target_pairs={{0,1},{1,2},{2,3},{3,4},{4,5},{5,6},{6,7},{7,0},{8,9},{9,10},{10,1... | collective-permute-start | bytes 1228808 | tf_op jit(solution)/shard_map/ppermute | solution.py:21
  43.1 71.7 %collective-permute-start.6 = (s32[128]{0:T(128)S(1)}, s32[128]{0:T(128)S(1)}, u32[]{:S(2)}, u32[]{:S(2)}) collective-permute-start(s32[128]{0:T(128)S(1)} %collective-permute-done.5), channel_id=1, source_target_pairs={{0,1},{1,2},{2,3},{3,4},{4,5},{5,6},{6,7},{7,0},{8,9},{9,10},{10,1... | collective-permute-start | bytes 1544 | tf_op jit(solution)/shard_map/ppermute | solution.py:21
  103.9 45.4 %copy-start = (bf16[1024,1600]{1,0:T(8,128)(2,1)S(1)}, bf16[1024,1600]{1,0:T(8,128)(2,1)}, u32[]{:S(2)}) copy-start(bf16[1024,1600]{1,0:T(8,128)(2,1)} %all-gather.2.cloned.1.call-done) | copy-start | bytes 9830404
  103.9 51.7 %collective-permute-start.14 = (bf16[1024,1600]{0,1:T(8,128)(2,1)S(1)}, bf16[1024,1600]{0,1:T(8,128)(2,1)S(1)}, u32[]{:S(2)}, u32[]{:S(2)}) collective-permute-start(bf16[1024,1600]{0,1:T(8,128)(2,1)S(1)} %copy.9), channel_id=1, source_target_pairs={{0,8},{8,0},{1,9},{9,1},{2,10},{10,2},{3,11},{11,3},{4,12},{12,4},... | collective-permute-start | bytes 9830408 | tf_op jit(solution)/shard_map/ppermute | solution.py:21
  110.3 13.6 %collective-permute-start.8 = (bf16[128,1600]{0,1:T(8,128)(2,1)}, bf16[128,1600]{0,1:T(8,128)(2,1)S(1)}, u32[]{:S(2)}, u32[]{:S(2)}) collective-permute-start(bf16[128,1600]{0,1:T(8,128)(2,1)} %collective-permute-done.7), channel_id=1, source_target_pairs={{0,7},{1,0},{2,1},{3,2},{4,3},{5,4},{6,5},{7,6},{8,15},{9,8},{10,9... | collective-permute-start | bytes 1228808 | tf_op jit(solution)/shard_map/ppermute | solution.py:21
  114.8 16.2 %collective-permute-start.12 = (bf16[128,1600]{0,1:T(8,128)(2,1)}, bf16[128,1600]{0,1:T(8,128)(2,1)S(1)}, u32[]{:S(2)}, u32[]{:S(2)}) collective-permute-start(bf16[128,1600]{0,1:T(8,128)(2,1)} %collective-permute-done.11), channel_id=1, source_target_pairs={{0,1},{1,2},{2,3},{3,4},{4,5},{5,6},{6,7},{7,0},{8,9},{9,10},{10,1... | collective-permute-start | bytes 1228808 | tf_op jit(solution)/shard_map/ppermute | solution.py:21
  124.0 13.2 %collective-permute-start.9 = (bf16[128,1600]{0,1:T(8,128)(2,1)S(1)}, bf16[128,1600]{0,1:T(8,128)(2,1)S(1)}, u32[]{:S(2)}, u32[]{:S(2)}) collective-permute-start(bf16[128,1600]{0,1:T(8,128)(2,1)S(1)} %collective-permute-done.8), channel_id=1, source_target_pairs={{0,7},{1,0},{2,1},{3,2},{4,3},{5,4},{6,5},{7,6},{8,15},{9,8},{10,9... | collective-permute-start | bytes 1228808 | tf_op jit(solution)/shard_map/ppermute | solution.py:21
  131.0 13.0 %collective-permute-start.13 = (bf16[128,1600]{0,1:T(8,128)(2,1)S(1)}, bf16[128,1600]{0,1:T(8,128)(2,1)S(1)}, u32[]{:S(2)}, u32[]{:S(2)}) collective-permute-start(bf16[128,1600]{0,1:T(8,128)(2,1)S(1)} %collective-permute-done.12), channel_id=1, source_target_pairs={{0,1},{1,2},{2,3},{3,4},{4,5},{5,6},{6,7},{7,0},{8,9},{9,10},{10,1... | collective-permute-start | bytes 1228808 | tf_op jit(solution)/shard_map/ppermute | solution.py:21
  149.3 4.2 %copy-start.1 = (bf16[1024,1600]{0,1:T(8,128)(2,1)S(1)}, bf16[1024,1600]{0,1:T(8,128)(2,1)}, u32[]{:S(2)}) copy-start(bf16[1024,1600]{0,1:T(8,128)(2,1)} %constant_dynamic-update-slice_fusion.1) | copy-start | bytes 9830404
  159.9 31.8 %copy-start.2 = (s32[128]{0:T(128)S(1)}, s32[128]{0:T(128)}, u32[]{:S(2)}) copy-start(s32[128]{0:T(128)} %param.9) | copy-start | bytes 1540
  163.9 17.7 %collective-permute-start.15 = (f32[4,128]{1,0:T(4,128)S(1)}, f32[4,128]{1,0:T(4,128)S(1)}, u32[]{:S(2)}, u32[]{:S(2)}) collective-permute-start(f32[4,128]{1,0:T(4,128)S(1)} %bitcast.594), channel_id=1, source_target_pairs={{0,1},{1,2},{2,3},{3,4},{4,5},{5,6},{6,7},{7,0},{8,9},{9,10},{10,1... | collective-permute-start | bytes 6152 | tf_op jit(solution)/shard_map/ppermute | solution.py:21
  165.8 19.3 %collective-permute-start.18 = (f32[4,128]{1,0:T(4,128)S(1)}, f32[4,128]{1,0:T(4,128)S(1)}, u32[]{:S(2)}, u32[]{:S(2)}) collective-permute-start(f32[4,128]{1,0:T(4,128)S(1)} %bitcast.593), channel_id=1, source_target_pairs={{0,4},{1,5},{2,6},{3,7},{4,0},{5,1},{6,2},{7,3},{8,12},{9,13},{10,... | collective-permute-start | bytes 6152 | tf_op jit(solution)/shard_map/ppermute | solution.py:21
  170.6 20.3 %collective-permute-start.19 = (f32[4,128]{1,0:T(4,128)S(1)}, f32[4,128]{1,0:T(4,128)S(1)}, u32[]{:S(2)}, u32[]{:S(2)}) collective-permute-start(f32[4,128]{1,0:T(4,128)S(1)} %bitcast.592), channel_id=1, source_target_pairs={{0,5},{1,6},{2,7},{3,0},{4,1},{5,2},{6,3},{7,4},{8,13},{9,14},{10,... | collective-permute-start | bytes 6152 | tf_op jit(solution)/shard_map/ppermute | solution.py:21
  173.0 18.0 %collective-permute-start.20 = (f32[4,128]{1,0:T(4,128)S(1)}, f32[4,128]{1,0:T(4,128)S(1)}, u32[]{:S(2)}, u32[]{:S(2)}) collective-permute-start(f32[4,128]{1,0:T(4,128)S(1)} %bitcast.591), channel_id=1, source_target_pairs={{0,6},{1,7},{2,0},{3,1},{4,2},{5,3},{6,4},{7,5},{8,14},{9,15},{10,... | collective-permute-start | bytes 6152 | tf_op jit(solution)/shard_map/ppermute | solution.py:21
  179.6 11.4 %collective-permute-start.16 = (f32[4,128]{1,0:T(4,128)S(1)}, f32[4,128]{1,0:T(4,128)S(1)}, u32[]{:S(2)}, u32[]{:S(2)}) collective-permute-start(f32[4,128]{1,0:T(4,128)S(1)} %bitcast.597), channel_id=1, source_target_pairs={{0,2},{1,3},{2,4},{3,5},{4,6},{5,7},{6,0},{7,1},{8,10},{9,11},{10,... | collective-permute-start | bytes 6152 | tf_op jit(solution)/shard_map/ppermute | solution.py:21
  181.6 9.4 %collective-permute-start.17 = (f32[4,128]{1,0:T(4,128)S(1)}, f32[4,128]{1,0:T(4,128)S(1)}, u32[]{:S(2)}, u32[]{:S(2)}) collective-permute-start(f32[4,128]{1,0:T(4,128)S(1)} %bitcast.596), channel_id=1, source_target_pairs={{0,3},{1,4},{2,5},{3,6},{4,7},{5,0},{6,1},{7,2},{8,11},{9,12},{10,... | collective-permute-start | bytes 6152 | tf_op jit(solution)/shard_map/ppermute | solution.py:21
  185.2 6.5 %collective-permute-start.21 = (f32[4,128]{1,0:T(4,128)S(1)}, f32[4,128]{1,0:T(4,128)S(1)}, u32[]{:S(2)}, u32[]{:S(2)}) collective-permute-start(f32[4,128]{1,0:T(4,128)S(1)} %bitcast.595), channel_id=1, source_target_pairs={{0,7},{1,0},{2,1},{3,2},{4,3},{5,4},{6,5},{7,6},{8,15},{9,8},{10,9... | collective-permute-start | bytes 6152 | tf_op jit(solution)/shard_map/ppermute | solution.py:21
Sparse Core Ops, SparseCore 0:
  11.2 88.4 all-gather.1

commit v2 on v1

--- a/solution.py
+++ b/solution.py
@@ -38,6 +38,7 @@
     y = lax.axis_index("y")
     c = lax.axis_index("c")
     mine = hidden.shape[0]
+    dim = hidden.shape[1]
     width = unembed.shape[0]
 
     wide = hidden.astype(jnp.float32)
@@ -45,45 +46,49 @@
         wide * lax.rsqrt(jnp.mean(wide * wide, axis=1, keepdims=True) + 1e-06) * norm_gain
     ).astype(jnp.bfloat16)
 
+    code = jnp.zeros((mine, 16), jnp.bfloat16)
+    code = code.at[:, 0].set((targets // 128).astype(jnp.bfloat16))
+    code = code.at[:, 1].set((targets % 128).astype(jnp.bfloat16))
+    block = jnp.concatenate([normed, code], axis=1)
+
     blocks = [None] * ny
-    blocks[0] = (normed, targets)
+    blocks[0] = block
     fwd = ny // 2
-    cur = (normed, targets)
+    cur = block
     for d in range(1, fwd + 1):
         cur = shift(cur, "y", ny, 1)
         blocks[ny - d] = cur
-    cur = (normed, targets)
+    cur = block
     for d in range(1, ny - fwd):
         cur = shift(cur, "y", ny, -1)
         blocks[d] = cur
-    rows = jnp.concatenate([b[0] for b in blocks], axis=0)
-    wanted = jnp.concatenate([b[1] for b in blocks], axis=0)
+    rows = jnp.concatenate([b[:, :dim] for b in blocks], axis=0)
+    wanted = jnp.concatenate(
+        [b[:, dim].astype(jnp.int32) * 128 + b[:, dim + 1].astype(jnp.int32) for b in blocks], axis=0
+    )
 
-    half = lax.all_gather(unembed, ("z", "x"), axis=0, tiled=True)
-    other = shift(half, "c", nc, 1)
-
-    def ids_of(core):
-        local = jnp.arange(half.shape[0], dtype=jnp.int32)
-        return ((local // width) * (nc * ny) + core * ny + y) * width + local % width
+    whole = lax.all_gather(unembed, ("z", "x", "c"), axis=0, tiled=True)
+    local = jnp.arange(whole.shape[0], dtype=jnp.int32)
+    ids = ((local // width) * ny + y) * width + local % width
 
     count = rows.shape[0]
     zeros = jnp.zeros((count,), jnp.float32)
     stats = (jnp.full((count,), -1e30, jnp.float32), zeros, zeros, zeros)
-    step = min(512, half.shape[0])
-    for table, core in ((half, c), (other, (c + 1) % nc)):
-        ids = ids_of(core)
-        for first in range(0, table.shape[0], step):
-            stats = combine_stats(
-                stats,
-                chunk_stats(rows, table[first : first + step], ids[first : first + step], wanted),
-            )
+    step = min(512, whole.shape[0])
+    for first in range(0, whole.shape[0], step):
+        stats = combine_stats(
+            stats,
+            chunk_stats(rows, whole[first : first + step], ids[first : first + step], wanted),
+        )
 
-    packed = jnp.stack(stats).reshape(4, ny, mine)
-    merged = tuple(packed[:, 0])
-    for d in range(1, ny):
-        got = shift(packed[:, d], "y", ny, d)
-        merged = combine_stats(merged, tuple(got))
-    top, total, spread, picked = merged
+    packed = jnp.roll(jnp.stack(stats).reshape(4, ny, mine), y, axis=1).reshape(4, ny * mine)
+    got = lax.all_to_all(packed, "y", 1, 1, tiled=True).reshape(4, ny, mine)
+    tops, totals, spreads, chosen = got[0], got[1], got[2], got[3]
+    top = jnp.max(tops, axis=0)
+    scale = jnp.exp(tops - top[None])
+    total = jnp.sum(totals * scale, axis=0)
+    spread = jnp.sum(scale * (spreads + (tops - top[None]) * totals), axis=0)
+    picked = jnp.sum(chosen, axis=0)
     mask = live.astype(jnp.float32)
     logprob = (picked - top - jnp.log(total)) * mask
     entropy = (jnp.log(total) - spread / total) * mask

time: 204 us -> 141 us (0.69); the launches traced: 200 us -> 140 us
  starting transfers between devices: 78 us -> 26.4 us
  waiting for transfers between devices: 74.2 us -> 58.4 us
  blocking collectives: 0 us -> 12.9 us
  local copies, waits for them, and re-layouts: 13.7 us -> 5.97 us
  other arithmetic: 8.53 us -> 11.3 us
    ppermute x22 -> x7, starting transfers between devices: 78 us -> 26.4 us  [shift(): lax.ppermute(value, axis, [(i, (i + step) % size) for i in range(size)])]
    all_gather x1, waiting for transfers between devices: 54.6 us -> 40.9 us  [on_device(): whole = lax.all_gather(unembed, ('z', 'x', 'c'), axis=0, tiled=True)]
    all_to_all x0 -> x1, blocking collectives: none -> 12.9 us  [on_device(): got = lax.all_to_all(packed, 'y', 1, 1, tiled=True).reshape(4, ny, mine)]
    all_gather x1 -> x0, local copies, waits for them, and re-layouts: 4.26 us -> none  [on_device(): half = lax.all_gather(unembed, ('z', 'x'), axis=0, tiled=True)]
    unnamed x19 -> x12, local copies, waits for them, and re-layouts: 7.66 us -> 5.05 us
    ppermute x22 -> x7, waiting for transfers between devices: 18.9 us -> 16.8 us  [shift(): lax.ppermute(value, axis, [(i, (i + step) % size) for i in range(size)])]
  transfers between devices with their start and end apart: 23 -> 8, of which waited for: 6 -> 6; matrix products, arithmetic and copies ran while one was open for 12% -> 9% of each run, Pallas kernels for 0% -> 0%
where the time goes in v2:
time: 141 us; the launch traced here: 140 us
  waiting for transfers between devices  58.4 us (41%)
  starting transfers between devices  26.4 us (19%)
  between operations  14.3 us (10%)
  blocking collectives  12.9 us (9%)
  other arithmetic  11.3 us (8%)
  matrix products  11 us (8%)
  local copies, waits for them, and re-layouts  5.97 us (4%)
    all_gather x1, waiting for transfers between devices, on_device(): whole = lax.all_gather(unembed, ('z', 'x', 'c'), axis=0, tiled=True)  40.9 us
    ppermute x7, starting transfers between devices, shift(): lax.ppermute(value, axis, [(i, (i + step) % size) for i in range(size)])  26.4 us
    ppermute x7, waiting for transfers between devices, shift(): lax.ppermute(value, axis, [(i, (i + step) % size) for i in range(size)])  16.8 us
    all_to_all x1, blocking collectives, on_device(): got = lax.all_to_all(packed, 'y', 1, 1, tiled=True).reshape(4, ny, mine)  12.9 us
    dot_general x4, matrix products, chunk_stats(): lax.dot_general(normed, piece, (((1,), (1,)), ((), ())), preferred_elemen...  11 us
    unnamed x12, local copies, waits for them, and re-layouts  5.05 us
    reduce_sum x1, other arithmetic, chunk_stats(): jnp.sum(weights * shifted, axis=1)  3.9 us
  transfers between devices with their start and end apart: 8, of which 6 were waited for; matrix products, arithmetic and copies ran while one was open for 9% of the time, Pallas kernels for 0%

profile of v2, /device:TPU:1, one launch (start us, length us, event | category | flops | bytes accessed | tf_op | source)
XLA Modules:
  0.0 140.3 jit_solution(5805174977988451406)
XLA Ops:
  7.2 0.0 all-gather.2.cloned.1.call-start
  7.2 0.7 all-gather.2.cloned.1.call-update
  7.9 0.6 compare_reduce_fusion.1
  8.5 0.6 compare_reduce_fusion
  9.2 2.0 %broadcast_select_fusion = (bf16[128]{0:T(256)(128)(2,1)S(1)}, bf16[128,1]{0,1:T(2,128)(2,1)S(1)}) fusion(pred[]{:T(512)} %compare_reduce_fusion, s32[128]{0:T(128)} %param.12, pred[]{:T(512)} %compare_reduce_fusion.1), kind=kLoop, calls=%fused_computation.128 | loop fusion | flops 2944 | bytes 1026 | tf_op jit(solution)/shard_map/slice | solution.py:67
  11.2 1.2 fusion.12
  12.4 2.1 %constant_dynamic-update-slice_fusion = (bf16[1024,1600]{0,1:T(8,128)(2,1)}, bf16[128,1600]{0,1:T(8,128)(2,1)S(1)}) fusion(f32[1600]{0:T(1024)} %param.10, f32[128]{0:T(128)S(1)} %add_rsqrt_fusion, bf16[128,1600]{0,1:T(8,128)(2,1)} %param.9), kind=kLoop, calls=%fused_computation.45 | loop fusion | flops 819199 | bytes 1235712
  14.6 4.0 %collective-permute-start.3 = (bf16[128,1616]{0,1:T(8,128)(2,1)S(1)}, bf16[128,1616]{0,1:T(8,128)(2,1)S(1)}, u32[]{:S(2)}, u32[]{:S(2)}) collective-permute-start(bf16[128,1616]{0,1:T(8,128)(2,1)S(1)} %pad_maximum_fusion), channel_id=1, source_target_pairs={{0,1},{1,2},{2,3},{3,4},{4,5},{5,6},{6,7},{7,0},{8,9},{9,10},{10,1... | collective-permute-start | bytes 1241096 | tf_op jit(solution)/shard_map/ppermute | solution.py:21
  18.6 3.8 %collective-permute-start = (bf16[128,1616]{0,1:T(8,128)(2,1)S(1)}, bf16[128,1616]{0,1:T(8,128)(2,1)S(1)}, u32[]{:S(2)}, u32[]{:S(2)}) collective-permute-start(bf16[128,1616]{0,1:T(8,128)(2,1)S(1)} %pad_maximum_fusion), channel_id=1, source_target_pairs={{0,7},{1,0},{2,1},{3,2},{4,3},{5,4},{6,5},{7,6},{8,15},{9,8},{10,9... | collective-permute-start | bytes 1241096 | tf_op jit(solution)/shard_map/ppermute | solution.py:21
  22.5 3.4 %collective-permute-done.3 = bf16[128,1616]{0,1:T(8,128)(2,1)S(1)} collective-permute-done((bf16[128,1616]{0,1:T(8,128)(2,1)S(1)}, bf16[128,1616]{0,1:T(8,128)(2,1)S(1)}, u32[]{:S(2)}, u32[]{:S(2)}) %collective-permute-start.3) | collective-permute-done | bytes 413728 | tf_op jit(solution)/shard_map/ppermute | solution.py:21
  25.9 4.1 %collective-permute-start.4 = (bf16[128,1616]{0,1:T(8,128)(2,1)S(1)}, bf16[128,1616]{0,1:T(8,128)(2,1)S(1)}, u32[]{:S(2)}, u32[]{:S(2)}) collective-permute-start(bf16[128,1616]{0,1:T(8,128)(2,1)S(1)} %collective-permute-done.3), channel_id=1, source_target_pairs={{0,1},{1,2},{2,3},{3,4},{4,5},{5,6},{6,7},{7,0},{8,9},{9,10},{10,1... | collective-permute-start | bytes 1241096 | tf_op jit(solution)/shard_map/ppermute | solution.py:21
  30.0 0.0 collective-permute-done
  30.0 4.7 %collective-permute-start.1 = (bf16[128,1616]{0,1:T(8,128)(2,1)S(1)}, bf16[128,1616]{0,1:T(8,128)(2,1)S(1)}, u32[]{:S(2)}, u32[]{:S(2)}) collective-permute-start(bf16[128,1616]{0,1:T(8,128)(2,1)S(1)} %collective-permute-done), channel_id=1, source_target_pairs={{0,7},{1,0},{2,1},{3,2},{4,3},{5,4},{6,5},{7,6},{8,15},{9,8},{10,9... | collective-permute-start | bytes 1241096 | tf_op jit(solution)/shard_map/ppermute | solution.py:21
  34.8 0.8 slice_dynamic-update-slice_fusion.6
  35.6 2.9 %collective-permute-done.4 = bf16[128,1616]{0,1:T(8,128)(2,1)S(1)} collective-permute-done((bf16[128,1616]{0,1:T(8,128)(2,1)S(1)}, bf16[128,1616]{0,1:T(8,128)(2,1)S(1)}, u32[]{:S(2)}, u32[]{:S(2)}) %collective-permute-start.4) | collective-permute-done | bytes 413728 | tf_op jit(solution)/shard_map/ppermute | solution.py:21
  38.5 2.9 %collective-permute-start.5 = (bf16[128,1616]{0,1:T(8,128)(2,1)S(1)}, bf16[128,1616]{0,1:T(8,128)(2,1)S(1)}, u32[]{:S(2)}, u32[]{:S(2)}) collective-permute-start(bf16[128,1616]{0,1:T(8,128)(2,1)S(1)} %collective-permute-done.4), channel_id=1, source_target_pairs={{0,1},{1,2},{2,3},{3,4},{4,5},{5,6},{6,7},{7,0},{8,9},{9,10},{10,1... | collective-permute-start | bytes 1241096 | tf_op jit(solution)/shard_map/ppermute | solution.py:21
  41.4 0.0 collective-permute-done.1
  41.4 4.7 %collective-permute-start.2 = (bf16[128,1616]{0,1:T(8,128)(2,1)S(1)}, bf16[128,1616]{0,1:T(8,128)(2,1)S(1)}, u32[]{:S(2)}, u32[]{:S(2)}) collective-permute-start(bf16[128,1616]{0,1:T(8,128)(2,1)S(1)} %collective-permute-done.1), channel_id=1, source_target_pairs={{0,7},{1,0},{2,1},{3,2},{4,3},{5,4},{6,5},{7,6},{8,15},{9,8},{10,9... | collective-permute-start | bytes 1241096 | tf_op jit(solution)/shard_map/ppermute | solution.py:21
  46.1 0.9 slice_dynamic-update-slice_fusion.5
  47.0 2.9 %collective-permute-done.5 = bf16[128,1616]{0,1:T(8,128)(2,1)S(1)} collective-permute-done((bf16[128,1616]{0,1:T(8,128)(2,1)S(1)}, bf16[128,1616]{0,1:T(8,128)(2,1)S(1)}, u32[]{:S(2)}, u32[]{:S(2)}) %collective-permute-start.5) | collective-permute-done | bytes 413728 | tf_op jit(solution)/shard_map/ppermute | solution.py:21
  50.0 2.1 %collective-permute-start.6 = (bf16[128,1616]{0,1:T(8,128)(2,1)S(1)}, bf16[128,1616]{0,1:T(8,128)(2,1)S(1)}, u32[]{:S(2)}, u32[]{:S(2)}) collective-permute-start(bf16[128,1616]{0,1:T(8,128)(2,1)S(1)} %collective-permute-done.5), channel_id=1, source_target_pairs={{0,1},{1,2},{2,3},{3,4},{4,5},{5,6},{6,7},{7,0},{8,9},{9,10},{10,1... | collective-permute-start | bytes 1241096 | tf_op jit(solution)/shard_map/ppermute | solution.py:21
  52.1 2.0 %collective-permute-done.2 = bf16[128,1616]{0,1:T(8,128)(2,1)S(1)} collective-permute-done((bf16[128,1616]{0,1:T(8,128)(2,1)S(1)}, bf16[128,1616]{0,1:T(8,128)(2,1)S(1)}, u32[]{:S(2)}, u32[]{:S(2)}) %collective-permute-start.2) | collective-permute-done | bytes 413728 | tf_op jit(solution)/shard_map/ppermute | solution.py:21
  54.1 0.8 slice_dynamic-update-slice_fusion.4
  54.9 5.5 %collective-permute-done.6 = bf16[128,1616]{0,1:T(8,128)(2,1)S(1)} collective-permute-done((bf16[128,1616]{0,1:T(8,128)(2,1)S(1)}, bf16[128,1616]{0,1:T(8,128)(2,1)S(1)}, u32[]{:S(2)}, u32[]{:S(2)}) %collective-permute-start.6) | collective-permute-done | bytes 413728 | tf_op jit(solution)/shard_map/ppermute | solution.py:21
  60.5 0.8 slice_dynamic-update-slice_fusion.3
  61.4 0.9 slice_dynamic-update-slice_fusion.2
  62.2 0.8 slice_dynamic-update-slice_fusion.1
  63.1 0.9 slice_dynamic-update-slice_fusion
  63.9 0.0 copy-start
  63.9 40.9 %all-gather.2.cloned.1.call-done = bf16[2048,1600]{1,0:T(8,128)(2,1)} async-done(((bf16[32,1600]{1,0:T(8,128)(2,1)}), bf16[2048,1600]{1,0:T(8,128)(2,1)}) %all-gather.2.cloned.1.call-update) | async-done | bytes 6553616 | tf_op jit(solution)/shard_map/all_gather | solution.py:70
  104.8 0.0 copy-start.2
  104.8 4.7 %fusion.82 = (f32[1024]{0:T(1024)S(1)}, f32[1024,512]{0,1:T(8,128)S(1)}) fusion(bf16[1024,1600]{0,1:T(8,128)(2,1)} %slice_dynamic-update-slice_fusion, bf16[2048,1600]{1,0:T(8,128)(2,1)} %all-gather.2.cloned.1.call-done), kind=kOutput, calls=%fused_computation.177 | convolution fusion | flops 1678244864 | bytes 7081984 | tf_op jit(solution)/shard_map/dot_general | solution.py:25
  109.5 0.0 copy-done
  109.5 0.0 copy-done.2
  109.5 2.1 %fusion.83 = (f32[1024]{0:T(1024)S(1)}, f32[1024,512]{0,1:T(8,128)S(1)}) fusion(bf16[1024,1600]{0,1:T(8,128)(2,1)S(1)} %copy-done, bf16[2048,1600]{1,0:T(8,128)(2,1)S(1)} %copy-done.2), kind=kOutput, calls=%fused_computation.178 | convolution fusion | flops 1678244864 | bytes 7081984 | tf_op jit(solution)/shard_map/dot_general | solution.py:25
  111.7 2.1 %fusion.84 = (f32[1024]{0:T(1024)S(1)}, f32[1024,512]{0,1:T(8,128)S(1)}) fusion(bf16[1024,1600]{0,1:T(8,128)(2,1)S(1)} %copy-done, bf16[2048,1600]{1,0:T(8,128)(2,1)S(1)} %copy-done.2), kind=kOutput, calls=%fused_computation.179 | convolution fusion | flops 1678244864 | bytes 7081984 | tf_op jit(solution)/shard_map/dot_general | solution.py:25
  113.8 2.1 %fusion.85 = (f32[1024]{0:T(1024)S(1)}, f32[1024,512]{0,1:T(8,128)S(1)}) fusion(bf16[1024,1600]{0,1:T(8,128)(2,1)S(1)} %copy-done, bf16[2048,1600]{1,0:T(8,128)(2,1)S(1)} %copy-done.2), kind=kOutput, calls=%fused_computation.180 | convolution fusion | flops 1678244864 | bytes 7081984 | tf_op jit(solution)/shard_map/dot_general | solution.py:25
  115.9 0.0 copy-start.1
  115.9 3.9 %fusion = (f32[1024]{0:T(1024)S(1)}, f32[1024]{0:T(1024)S(1)}, f32[1024]{0:T(1024)S(1)}, f32[1024]{0:T(1024)S(1)}, f32[1024]{0:T(1024)S(1)}, /*index=5*/f32[1024...) fusion(f32[1024,512]{0,1:T(8,128)S(1)} %get-tuple-element.67, ...), kind=kLoop, calls=%fused_computation.8 | loop fusion | flops 14667776 | bytes 8466432 | tf_op jit(solution)/shard_map/reduce_sum | solution.py:32
  119.9 12.9 %all_to_all.6 = f32[4,8,128]{2,0,1:T(4,128)S(1)} all-to-all(f32[4,8,128]{2,0,1:T(4,128)S(1)} %copy.9), channel_id=1, replica_groups=mesh['z'=8,'x'=4,'c'=2,'y'=8] {'y'}, dimensions={1} | all-to-all | bytes 32768 | tf_op jit(solution)/shard_map/all_to_all | solution.py:85
  132.9 0.0 copy-done.1
  132.9 0.5 subtract_multiply_fusion
  (22 shorter events, 0.3 us)
Async XLA Ops:
  7.2 97.7 %all-gather.2.cloned.1.call-start = ((), (), s32[]{:S(2)}) async-start(), calls=%async_computation.1 | async-start | bytes 6922240 | tf_op jit(solution)/shard_map/all_gather | solution.py:70
  14.6 11.3 %collective-permute-start.3 = (bf16[128,1616]{0,1:T(8,128)(2,1)S(1)}, bf16[128,1616]{0,1:T(8,128)(2,1)S(1)}, u32[]{:S(2)}, u32[]{:S(2)}) collective-permute-start(bf16[128,1616]{0,1:T(8,128)(2,1)S(1)} %pad_maximum_fusion), channel_id=1, source_target_pairs={{0,1},{1,2},{2,3},{3,4},{4,5},{5,6},{6,7},{7,0},{8,9},{9,10},{10,1... | collective-permute-start | bytes 1241096 | tf_op jit(solution)/shard_map/ppermute | solution.py:21
  18.6 11.4 %collective-permute-start = (bf16[128,1616]{0,1:T(8,128)(2,1)S(1)}, bf16[128,1616]{0,1:T(8,128)(2,1)S(1)}, u32[]{:S(2)}, u32[]{:S(2)}) collective-permute-start(bf16[128,1616]{0,1:T(8,128)(2,1)S(1)} %pad_maximum_fusion), channel_id=1, source_target_pairs={{0,7},{1,0},{2,1},{3,2},{4,3},{5,4},{6,5},{7,6},{8,15},{9,8},{10,9... | collective-permute-start | bytes 1241096 | tf_op jit(solution)/shard_map/ppermute | solution.py:21
  25.9 12.6 %collective-permute-start.4 = (bf16[128,1616]{0,1:T(8,128)(2,1)S(1)}, bf16[128,1616]{0,1:T(8,128)(2,1)S(1)}, u32[]{:S(2)}, u32[]{:S(2)}) collective-permute-start(bf16[128,1616]{0,1:T(8,128)(2,1)S(1)} %collective-permute-done.3), channel_id=1, source_target_pairs={{0,1},{1,2},{2,3},{3,4},{4,5},{5,6},{6,7},{7,0},{8,9},{9,10},{10,1... | collective-permute-start | bytes 1241096 | tf_op jit(solution)/shard_map/ppermute | solution.py:21
  30.0 11.4 %collective-permute-start.1 = (bf16[128,1616]{0,1:T(8,128)(2,1)S(1)}, bf16[128,1616]{0,1:T(8,128)(2,1)S(1)}, u32[]{:S(2)}, u32[]{:S(2)}) collective-permute-start(bf16[128,1616]{0,1:T(8,128)(2,1)S(1)} %collective-permute-done), channel_id=1, source_target_pairs={{0,7},{1,0},{2,1},{3,2},{4,3},{5,4},{6,5},{7,6},{8,15},{9,8},{10,9... | collective-permute-start | bytes 1241096 | tf_op jit(solution)/shard_map/ppermute | solution.py:21
  38.5 11.5 %collective-permute-start.5 = (bf16[128,1616]{0,1:T(8,128)(2,1)S(1)}, bf16[128,1616]{0,1:T(8,128)(2,1)S(1)}, u32[]{:S(2)}, u32[]{:S(2)}) collective-permute-start(bf16[128,1616]{0,1:T(8,128)(2,1)S(1)} %collective-permute-done.4), channel_id=1, source_target_pairs={{0,1},{1,2},{2,3},{3,4},{4,5},{5,6},{6,7},{7,0},{8,9},{9,10},{10,1... | collective-permute-start | bytes 1241096 | tf_op jit(solution)/shard_map/ppermute | solution.py:21
  41.4 12.7 %collective-permute-start.2 = (bf16[128,1616]{0,1:T(8,128)(2,1)S(1)}, bf16[128,1616]{0,1:T(8,128)(2,1)S(1)}, u32[]{:S(2)}, u32[]{:S(2)}) collective-permute-start(bf16[128,1616]{0,1:T(8,128)(2,1)S(1)} %collective-permute-done.1), channel_id=1, source_target_pairs={{0,7},{1,0},{2,1},{3,2},{4,3},{5,4},{6,5},{7,6},{8,15},{9,8},{10,9... | collective-permute-start | bytes 1241096 | tf_op jit(solution)/shard_map/ppermute | solution.py:21
  50.0 10.5 %collective-permute-start.6 = (bf16[128,1616]{0,1:T(8,128)(2,1)S(1)}, bf16[128,1616]{0,1:T(8,128)(2,1)S(1)}, u32[]{:S(2)}, u32[]{:S(2)}) collective-permute-start(bf16[128,1616]{0,1:T(8,128)(2,1)S(1)} %collective-permute-done.5), channel_id=1, source_target_pairs={{0,1},{1,2},{2,3},{3,4},{4,5},{5,6},{6,7},{7,0},{8,9},{9,10},{10,1... | collective-permute-start | bytes 1241096 | tf_op jit(solution)/shard_map/ppermute | solution.py:21
  63.9 45.6 %copy-start = (bf16[1024,1600]{0,1:T(8,128)(2,1)S(1)}, bf16[1024,1600]{0,1:T(8,128)(2,1)}, u32[]{:S(2)}) copy-start(bf16[1024,1600]{0,1:T(8,128)(2,1)} %slice_dynamic-update-slice_fusion) | copy-start | bytes 9830404
  104.8 4.7 %copy-start.2 = (bf16[2048,1600]{1,0:T(8,128)(2,1)S(1)}, bf16[2048,1600]{1,0:T(8,128)(2,1)}, u32[]{:S(2)}) copy-start(bf16[2048,1600]{1,0:T(8,128)(2,1)} %all-gather.2.cloned.1.call-done) | copy-start | bytes 19660804
  115.9 17.0 %copy-start.1 = (s32[128]{0:T(128)S(1)}, s32[128]{0:T(128)}, u32[]{:S(2)}) copy-start(s32[128]{0:T(128)} %param.13) | copy-start | bytes 1540
Sparse Core Ops, SparseCore 0:
  11.3 93.4 all-gather.1

commit v3 on v2

--- a/solution.py
+++ b/solution.py
@@ -71,18 +71,29 @@
     local = jnp.arange(whole.shape[0], dtype=jnp.int32)
     ids = ((local // width) * ny + y) * width + local % width
 
-    count = rows.shape[0]
-    zeros = jnp.zeros((count,), jnp.float32)
-    stats = (jnp.full((count,), -1e30, jnp.float32), zeros, zeros, zeros)
+    parts = 2
+    part = mine // parts
     step = min(512, whole.shape[0])
-    for first in range(0, whole.shape[0], step):
-        stats = combine_stats(
-            stats,
-            chunk_stats(rows, whole[first : first + step], ids[first : first + step], wanted),
-        )
-
-    packed = jnp.roll(jnp.stack(stats).reshape(4, ny, mine), y, axis=1).reshape(4, ny * mine)
-    got = lax.all_to_all(packed, "y", 1, 1, tiled=True).reshape(4, ny, mine)
+    rows3 = rows.reshape(ny, mine, dim)
+    wanted3 = wanted.reshape(ny, mine)
+    results = []
+    for h in range(parts):
+        sub = rows3[:, h * part : (h + 1) * part].reshape(ny * part, dim)
+        if results:
+            results[-1], sub = lax.optimization_barrier((results[-1], sub))
+        sub_wanted = wanted3[:, h * part : (h + 1) * part].reshape(ny * part)
+        count = sub.shape[0]
+        zeros = jnp.zeros((count,), jnp.float32)
+        stats = (jnp.full((count,), -1e30, jnp.float32), zeros, zeros, zeros)
+        for first in range(0, whole.shape[0], step):
+            stats = combine_stats(
+                stats,
+                chunk_stats(sub, whole[first : first + step], ids[first : first + step], sub_wanted),
+            )
+        packed = jnp.roll(jnp.stack(stats).reshape(4, ny, part), y, axis=1).reshape(4, ny * part)
+        results.append(packed)
+    results = [lax.all_to_all(p, "y", 1, 1, tiled=True).reshape(4, ny, part) for p in results]
+    got = jnp.concatenate(results, axis=2)
     tops, totals, spreads, chosen = got[0], got[1], got[2], got[3]
     top = jnp.max(tops, axis=0)
     scale = jnp.exp(tops - top[None])

time: 141 us -> 171 us (1.21)
  matrix products: 11 us -> 27.5 us
  blocking collectives: 12.9 us -> 0 us
  starting transfers between devices: 26.4 us -> 38 us
  local copies, waits for them, and re-layouts: 5.97 us -> 16.9 us
  other arithmetic: 11.3 us -> 17.7 us
  waiting for transfers between devices: 58.4 us -> 55.6 us
    dot_general x4 -> x8, matrix products: 11 us -> 27.5 us  [chunk_stats(): lax.dot_general(normed, piece, (((1,), (1,)), ((), ())), preferred_elemen...]
    all_to_all x0 -> x2, starting transfers between devices: none -> 13.1 us  [on_device(): lax.all_to_all(p, 'y', 1, 1, tiled=True).reshape(4, ny, part)]
    all_to_all x1 -> x0, blocking collectives: 12.9 us -> none  [on_device(): got = lax.all_to_all(packed, 'y', 1, 1, tiled=True).reshape(4, ny, mine)]
    all_gather x1, waiting for transfers between devices: 40.9 us -> 28.4 us  [on_device(): whole = lax.all_gather(unembed, ('z', 'x', 'c'), axis=0, tiled=True)]
    all_to_all x0 -> x2, waiting for transfers between devices: none -> 5.31 us  [on_device(): lax.all_to_all(p, 'y', 1, 1, tiled=True).reshape(4, ny, part)]
    reshape x0 -> x2, local copies, waits for them, and re-layouts: none -> 4.42 us  [the longest x1 4.35 us: on_device(): rows3 = rows.reshape(ny, mine, dim)]
    ppermute x7, waiting for transfers between devices: 16.8 us -> 21.2 us  [shift(): lax.ppermute(value, axis, [(i, (i + step) % size) for i in range(size)])]
    unnamed x9, other arithmetic: 2.2 us -> 4.45 us
  transfers between devices with their start and end apart: 8 -> 10, of which waited for: 6 -> 6; matrix products, arithmetic and copies ran while one was open for 9% -> 25% of each run, Pallas kernels for 0% -> 0%
where the time goes in v3:
time: 171 us; the launch traced here: 170 us
  waiting for transfers between devices  55.6 us (33%)
  starting transfers between devices  38 us (22%)
  matrix products  27.5 us (16%)
  other arithmetic  17.7 us (10%)
  local copies, waits for them, and re-layouts  16.9 us (10%)
  between operations  14.3 us (8%)
    all_gather x1, waiting for transfers between devices, on_device(): whole = lax.all_gather(unembed, ('z', 'x', 'c'), axis=0, tiled=True)  28.4 us
    dot_general x8, matrix products, chunk_stats(): lax.dot_general(normed, piece, (((1,), (1,)), ((), ())), preferred_elemen...  27.5 us
    ppermute x7, starting transfers between devices, shift(): lax.ppermute(value, axis, [(i, (i + step) % size) for i in range(size)])  24.9 us
    ppermute x7, waiting for transfers between devices, shift(): lax.ppermute(value, axis, [(i, (i + step) % size) for i in range(size)])  21.2 us
    all_to_all x2, starting transfers between devices, on_device(): lax.all_to_all(p, 'y', 1, 1, tiled=True).reshape(4, ny, part)  13.1 us
    unnamed x24, local copies, waits for them, and re-layouts  6.65 us
    reduce_sum x2, other arithmetic, chunk_stats(): jnp.sum(weights * shifted, axis=1)  5.86 us
    all_to_all x2, waiting for transfers between devices, on_device(): lax.all_to_all(p, 'y', 1, 1, tiled=True).reshape(4, ny, part)  5.31 us
  transfers between devices with their start and end apart: 10, of which 6 were waited for; matrix products, arithmetic and copies ran while one was open for 25% of the time, Pallas kernels for 0%

profile of v3, /device:TPU:1, one launch (start us, length us, event | category | flops | bytes accessed | tf_op | source)
XLA Modules:
  0.0 169.9 jit_solution(6652861233476621255)
XLA Ops:
  7.2 0.7 all-gather.2.cloned.1.call-update
  7.9 0.6 compare_reduce_fusion
  8.5 0.6 compare_reduce_fusion.1
  9.2 2.0 %broadcast_select_fusion = (bf16[128]{0:T(256)(128)(2,1)S(1)}, bf16[128,1]{0,1:T(2,128)(2,1)S(1)}) fusion(pred[]{:T(512)} %compare_reduce_fusion, s32[128]{0:T(128)} %param.14, pred[]{:T(512)} %compare_reduce_fusion.1), kind=kLoop, calls=%fused_computation.161 | loop fusion | flops 2944 | bytes 1026 | tf_op jit(solution)/shard_map/slice | solution.py:67
  11.2 1.2 fusion.24
  12.4 2.1 %constant_dynamic-update-slice_fusion = (bf16[1024,1600]{0,1:T(8,128)(2,1)}, bf16[128,1600]{0,1:T(8,128)(2,1)S(1)}) fusion(f32[1600]{0:T(1024)} %param.12, f32[128]{0:T(128)S(1)} %add_rsqrt_fusion, bf16[128,1600]{0,1:T(8,128)(2,1)} %param.11), kind=kLoop, calls=%fused_computation.77 | loop fusion | flops 819199 | bytes 1235712
  14.6 5.9 %collective-permute-start = (bf16[128,1616]{0,1:T(8,128)(2,1)S(1)}, bf16[128,1616]{0,1:T(8,128)(2,1)S(1)}, u32[]{:S(2)}, u32[]{:S(2)}) collective-permute-start(bf16[128,1616]{0,1:T(8,128)(2,1)S(1)} %pad_maximum_fusion), channel_id=1, source_target_pairs={{0,7},{1,0},{2,1},{3,2},{4,3},{5,4},{6,5},{7,6},{8,15},{9,8},{10,9... | collective-permute-start | bytes 1241096 | tf_op jit(solution)/shard_map/ppermute | solution.py:21
  20.5 1.9 %collective-permute-start.3 = (bf16[128,1616]{0,1:T(8,128)(2,1)S(1)}, bf16[128,1616]{0,1:T(8,128)(2,1)S(1)}, u32[]{:S(2)}, u32[]{:S(2)}) collective-permute-start(bf16[128,1616]{0,1:T(8,128)(2,1)S(1)} %pad_maximum_fusion), channel_id=1, source_target_pairs={{0,1},{1,2},{2,3},{3,4},{4,5},{5,6},{6,7},{7,0},{8,9},{9,10},{10,1... | collective-permute-start | bytes 1241096 | tf_op jit(solution)/shard_map/ppermute | solution.py:21
  22.5 4.2 %collective-permute-done = bf16[128,1616]{0,1:T(8,128)(2,1)S(1)} collective-permute-done((bf16[128,1616]{0,1:T(8,128)(2,1)S(1)}, bf16[128,1616]{0,1:T(8,128)(2,1)S(1)}, u32[]{:S(2)}, u32[]{:S(2)}) %collective-permute-start) | collective-permute-done | bytes 413728 | tf_op jit(solution)/shard_map/ppermute | solution.py:21
  26.7 5.3 %collective-permute-start.1 = (bf16[128,1616]{0,1:T(8,128)(2,1)S(1)}, bf16[128,1616]{0,1:T(8,128)(2,1)S(1)}, u32[]{:S(2)}, u32[]{:S(2)}) collective-permute-start(bf16[128,1616]{0,1:T(8,128)(2,1)S(1)} %collective-permute-done), channel_id=1, source_target_pairs={{0,7},{1,0},{2,1},{3,2},{4,3},{5,4},{6,5},{7,6},{8,15},{9,8},{10,9... | collective-permute-start | bytes 1241096 | tf_op jit(solution)/shard_map/ppermute | solution.py:21
  32.1 1.9 %collective-permute-start.4 = (bf16[128,1616]{0,1:T(8,128)(2,1)S(1)}, bf16[128,1616]{0,1:T(8,128)(2,1)S(1)}, u32[]{:S(2)}, u32[]{:S(2)}) collective-permute-start(bf16[128,1616]{0,1:T(8,128)(2,1)S(1)} %collective-permute-done.3), channel_id=1, source_target_pairs={{0,1},{1,2},{2,3},{3,4},{4,5},{5,6},{6,7},{7,0},{8,9},{9,10},{10,1... | collective-permute-start | bytes 1241096 | tf_op jit(solution)/shard_map/ppermute | solution.py:21
  34.0 0.8 slice_dynamic-update-slice_fusion.6
  34.8 2.5 %collective-permute-done.1 = bf16[128,1616]{0,1:T(8,128)(2,1)S(1)} collective-permute-done((bf16[128,1616]{0,1:T(8,128)(2,1)S(1)}, bf16[128,1616]{0,1:T(8,128)(2,1)S(1)}, u32[]{:S(2)}, u32[]{:S(2)}) %collective-permute-start.1) | collective-permute-done | bytes 413728 | tf_op jit(solution)/shard_map/ppermute | solution.py:21
  37.4 5.7 %collective-permute-start.2 = (bf16[128,1616]{0,1:T(8,128)(2,1)S(1)}, bf16[128,1616]{0,1:T(8,128)(2,1)S(1)}, u32[]{:S(2)}, u32[]{:S(2)}) collective-permute-start(bf16[128,1616]{0,1:T(8,128)(2,1)S(1)} %collective-permute-done.1), channel_id=1, source_target_pairs={{0,7},{1,0},{2,1},{3,2},{4,3},{5,4},{6,5},{7,6},{8,15},{9,8},{10,9... | collective-permute-start | bytes 1241096 | tf_op jit(solution)/shard_map/ppermute | solution.py:21
  43.1 1.9 %collective-permute-start.5 = (bf16[128,1616]{0,1:T(8,128)(2,1)S(1)}, bf16[128,1616]{0,1:T(8,128)(2,1)S(1)}, u32[]{:S(2)}, u32[]{:S(2)}) collective-permute-start(bf16[128,1616]{0,1:T(8,128)(2,1)S(1)} %collective-permute-done.4), channel_id=1, source_target_pairs={{0,1},{1,2},{2,3},{3,4},{4,5},{5,6},{6,7},{7,0},{8,9},{9,10},{10,1... | collective-permute-start | bytes 1241096 | tf_op jit(solution)/shard_map/ppermute | solution.py:21
  45.0 0.9 slice_dynamic-update-slice_fusion.5
  45.9 7.5 %collective-permute-done.5 = bf16[128,1616]{0,1:T(8,128)(2,1)S(1)} collective-permute-done((bf16[128,1616]{0,1:T(8,128)(2,1)S(1)}, bf16[128,1616]{0,1:T(8,128)(2,1)S(1)}, u32[]{:S(2)}, u32[]{:S(2)}) %collective-permute-start.5) | collective-permute-done | bytes 413728 | tf_op jit(solution)/shard_map/ppermute | solution.py:21
  53.4 2.2 %collective-permute-start.6 = (bf16[128,1616]{0,1:T(8,128)(2,1)S(1)}, bf16[128,1616]{0,1:T(8,128)(2,1)S(1)}, u32[]{:S(2)}, u32[]{:S(2)}) collective-permute-start(bf16[128,1616]{0,1:T(8,128)(2,1)S(1)} %collective-permute-done.5), channel_id=1, source_target_pairs={{0,1},{1,2},{2,3},{3,4},{4,5},{5,6},{6,7},{7,0},{8,9},{9,10},{10,1... | collective-permute-start | bytes 1241096 | tf_op jit(solution)/shard_map/ppermute | solution.py:21
  55.7 0.8 slice_dynamic-update-slice_fusion.4
  56.5 6.9 %collective-permute-done.6 = bf16[128,1616]{0,1:T(8,128)(2,1)S(1)} collective-permute-done((bf16[128,1616]{0,1:T(8,128)(2,1)S(1)}, bf16[128,1616]{0,1:T(8,128)(2,1)S(1)}, u32[]{:S(2)}, u32[]{:S(2)}) %collective-permute-start.6) | collective-permute-done | bytes 413728 | tf_op jit(solution)/shard_map/ppermute | solution.py:21
  63.4 0.9 slice_dynamic-update-slice_fusion.3
  64.3 0.9 slice_dynamic-update-slice_fusion.2
  65.1 0.8 slice_dynamic-update-slice_fusion.1
  66.0 0.9 slice_dynamic-update-slice_fusion
  66.8 4.3 %copy.25 = bf16[1024,1600]{1,0:T(8,128)(2,1)S(1)} copy(bf16[1024,1600]{0,1:T(8,128)(2,1)} %slice_dynamic-update-slice_fusion) | data formatting | bytes 6553600 | tf_op jit(solution)/shard_map/reshape | solution.py:77
  71.2 0.8 constant_dynamic-update-slice_fusion.5
  72.0 0.8 constant_dynamic-update-slice_fusion.4
  72.7 0.8 constant_dynamic-update-slice_fusion.3
  73.5 0.7 constant_dynamic-update-slice_fusion.2
  74.4 2.0 %fusion.89 = (bf16[8,64,1600]{2,1,0:T(8,128)(2,1)}, bf16[8,64,1600]{2,1,0:T(8,128)(2,1)}) fusion(bf16[8,128,1600]{2,1,0:T(8,128)(2,1)S(1)} %bitcast.64), kind=kLoop, calls=%fused_computation.208 | loop fusion | bytes 6553600 | tf_op jit(solution)/shard_map/slice | solution.py:81
  76.5 28.4 %all-gather.2.cloned.1.call-done = bf16[2048,1600]{1,0:T(8,128)(2,1)} async-done(((bf16[32,1600]{1,0:T(8,128)(2,1)}), bf16[2048,1600]{1,0:T(8,128)(2,1)}) %all-gather.2.cloned.1.call-update) | async-done | bytes 6553616 | tf_op jit(solution)/shard_map/all_gather | solution.py:70
  104.9 3.2 %fusion.92 = (f32[512]{0:T(512)S(1)}, f32[512,512]{0,1:T(8,128)S(1)}) fusion(bf16[512,1600]{1,0:T(8,128)(2,1)} %bitcast.69, bf16[2048,1600]{1,0:T(8,128)(2,1)} %all-gather.2.cloned.1.call-done), kind=kOutput, calls=%fused_computation.211 | convolution fusion | flops 839122432 | bytes 4458496 | tf_op jit(solution)/shard_map/dot_general | solution.py:25
  108.2 3.6 %fusion.95 = (f32[512]{0:T(512)S(1)}, f32[512,512]{0,1:T(8,128)}) fusion(bf16[512,1600]{1,0:T(8,128)(2,1)S(1)} %bitcast.70, bf16[2048,1600]{1,0:T(8,128)(2,1)} %all-gather.2.cloned.1.call-done), kind=kOutput, calls=%fused_computation.214 | convolution fusion | flops 839122432 | bytes 4392960 | tf_op jit(solution)/shard_map/dot_general | solution.py:25
  111.9 3.6 %fusion.94 = (f32[512]{0:T(512)S(1)}, f32[512,512]{0,1:T(8,128)}) fusion(bf16[512,1600]{1,0:T(8,128)(2,1)S(1)} %bitcast.71, bf16[2048,1600]{1,0:T(8,128)(2,1)} %all-gather.2.cloned.1.call-done), kind=kOutput, calls=%fused_computation.213 | convolution fusion | flops 839122432 | bytes 4392960 | tf_op jit(solution)/shard_map/dot_general | solution.py:25
  115.5 3.6 %fusion.93 = (f32[512]{0:T(512)S(1)}, f32[512,512]{0,1:T(8,128)}) fusion(bf16[512,1600]{1,0:T(8,128)(2,1)S(1)} %bitcast.72, bf16[2048,1600]{1,0:T(8,128)(2,1)} %all-gather.2.cloned.1.call-done), kind=kOutput, calls=%fused_computation.212 | convolution fusion | flops 839122432 | bytes 4392960 | tf_op jit(solution)/shard_map/dot_general | solution.py:25
  119.2 3.0 %fusion.16 = (f32[512]{0:T(512)S(1)}, f32[512]{0:T(512)S(1)}, f32[512]{0:T(512)S(1)}, f32[512]{0:T(512)S(1)}, f32[512]{0:T(512)S(1)}, /*index=5*/f32[512]{0:T(51...) fusion(f32[512,512]{0,1:T(8,128)S(1)} %get-tuple-element.100, ...), kind=kLoop, calls=%fused_computation.32 | loop fusion | flops 7333888 | bytes 4237312 | tf_op jit(solution)/shard_map/reduce_sum | solution.py:32
  123.1 0.7 reshape.1029
  123.8 6.4 %all-to-all-start = ((f32[8,1,256]{2,1,0:T(1,128)}), f32[8,1,256]{2,1,0:T(1,128)S(1)}, u32[]{:S(2)}, u32[]{:S(2)}) async-start(f32[8,1,256]{2,1,0:T(1,128)} %reshape.1029), calls=%async_computation | async-start | bytes 16384 | tf_op jit(solution)/shard_map/all_to_all | solution.py:95
  130.3 2.6 %fusion.96 = (f32[512]{0:T(512)S(1)}, f32[512,512]{0,1:T(8,128)S(1)}) fusion(bf16[512,1600]{1,0:T(8,128)(2,1)S(1)} %bitcast.65, bf16[2048,1600]{1,0:T(8,128)(2,1)} %all-gather.2.cloned.1.call-done), kind=kOutput, calls=%fused_computation.215 | convolution fusion | flops 839122432 | bytes 4392960 | tf_op jit(solution)/shard_map/dot_general | solution.py:25
  132.9 3.6 %fusion.99 = (f32[512]{0:T(512)S(1)}, f32[512,512]{0,1:T(8,128)}) fusion(bf16[512,1600]{1,0:T(8,128)(2,1)S(1)} %bitcast.66, bf16[2048,1600]{1,0:T(8,128)(2,1)} %all-gather.2.cloned.1.call-done), kind=kOutput, calls=%fused_computation.218 | convolution fusion | flops 839122432 | bytes 4392960 | tf_op jit(solution)/shard_map/dot_general | solution.py:25
  136.7 3.7 %fusion.98 = (f32[512]{0:T(512)S(1)}, f32[512,512]{0,1:T(8,128)}) fusion(bf16[512,1600]{1,0:T(8,128)(2,1)S(1)} %bitcast.67, bf16[2048,1600]{1,0:T(8,128)(2,1)} %all-gather.2.cloned.1.call-done), kind=kOutput, calls=%fused_computation.217 | convolution fusion | flops 839122432 | bytes 4392960 | tf_op jit(solution)/shard_map/dot_general | solution.py:25
  140.4 3.6 %fusion.97 = (f32[512]{0:T(512)S(1)}, f32[512,512]{0,1:T(8,128)}) fusion(bf16[512,1600]{1,0:T(8,128)(2,1)S(1)} %bitcast.68, bf16[2048,1600]{1,0:T(8,128)(2,1)} %all-gather.2.cloned.1.call-done), kind=kOutput, calls=%fused_computation.216 | convolution fusion | flops 839122432 | bytes 4392960 | tf_op jit(solution)/shard_map/dot_general | solution.py:25
  144.1 2.9 %fusion.20 = (f32[512]{0:T(512)S(1)}, f32[512]{0:T(512)S(1)}, f32[512]{0:T(512)S(1)}, f32[512]{0:T(512)S(1)}, f32[512]{0:T(512)S(1)}, /*index=5*/f32[512]{0:T(51...) fusion(f32[512,512]{0,1:T(8,128)S(1)} %get-tuple-element.108, ...), kind=kLoop, calls=%fused_computation.36 | loop fusion | flops 7333888 | bytes 4237312 | tf_op jit(solution)/shard_map/reduce_sum | solution.py:32
  147.7 0.7 reshape.1027
  148.4 6.7 %all-to-all-start.1 = ((f32[8,1,256]{2,1,0:T(1,128)}), f32[8,1,256]{2,1,0:T(1,128)S(1)}, u32[]{:S(2)}, u32[]{:S(2)}) async-start(f32[8,1,256]{2,1,0:T(1,128)} %reshape.1027), calls=%async_computation.1 | async-start | bytes 16384 | tf_op jit(solution)/shard_map/all_to_all | solution.py:95
  155.5 0.7 reduce.18
  156.3 5.3 %all-to-all-done.1 = f32[8,1,256]{2,1,0:T(1,128)S(1)} async-done(((f32[8,1,256]{2,1,0:T(1,128)}), f32[8,1,256]{2,1,0:T(1,128)S(1)}, u32[]{:S(2)}, u32[]{:S(2)}) %all-to-all-start.1) | async-done | bytes 8224 | tf_op jit(solution)/shard_map/all_to_all | solution.py:95
  161.6 0.7 reduce.19
  (76 shorter events, 4.1 us)
Async XLA Ops:
  7.2 97.7 %all-gather.2.cloned.1.call-start = ((), (), s32[]{:S(2)}) async-start(), calls=%async_computation.2 | async-start | bytes 6922240 | tf_op jit(solution)/shard_map/all_gather | solution.py:70
  14.6 12.2 %collective-permute-start = (bf16[128,1616]{0,1:T(8,128)(2,1)S(1)}, bf16[128,1616]{0,1:T(8,128)(2,1)S(1)}, u32[]{:S(2)}, u32[]{:S(2)}) collective-permute-start(bf16[128,1616]{0,1:T(8,128)(2,1)S(1)} %pad_maximum_fusion), channel_id=1, source_target_pairs={{0,7},{1,0},{2,1},{3,2},{4,3},{5,4},{6,5},{7,6},{8,15},{9,8},{10,9... | collective-permute-start | bytes 1241096 | tf_op jit(solution)/shard_map/ppermute | solution.py:21
  20.5 11.5 %collective-permute-start.3 = (bf16[128,1616]{0,1:T(8,128)(2,1)S(1)}, bf16[128,1616]{0,1:T(8,128)(2,1)S(1)}, u32[]{:S(2)}, u32[]{:S(2)}) collective-permute-start(bf16[128,1616]{0,1:T(8,128)(2,1)S(1)} %pad_maximum_fusion), channel_id=1, source_target_pairs={{0,1},{1,2},{2,3},{3,4},{4,5},{5,6},{6,7},{7,0},{8,9},{9,10},{10,1... | collective-permute-start | bytes 1241096 | tf_op jit(solution)/shard_map/ppermute | solution.py:21
  26.7 10.6 %collective-permute-start.1 = (bf16[128,1616]{0,1:T(8,128)(2,1)S(1)}, bf16[128,1616]{0,1:T(8,128)(2,1)S(1)}, u32[]{:S(2)}, u32[]{:S(2)}) collective-permute-start(bf16[128,1616]{0,1:T(8,128)(2,1)S(1)} %collective-permute-done), channel_id=1, source_target_pairs={{0,7},{1,0},{2,1},{3,2},{4,3},{5,4},{6,5},{7,6},{8,15},{9,8},{10,9... | collective-permute-start | bytes 1241096 | tf_op jit(solution)/shard_map/ppermute | solution.py:21
  32.1 33.9 %copy-start.2 = (bf16[128,1616]{0,1:T(8,128)(2,1)}, bf16[128,1616]{0,1:T(8,128)(2,1)S(1)}, u32[]{:S(2)}) copy-start(bf16[128,1616]{0,1:T(8,128)(2,1)S(1)} %collective-permute-done.3) | copy-start | bytes 1241092
  32.1 11.0 %collective-permute-start.4 = (bf16[128,1616]{0,1:T(8,128)(2,1)S(1)}, bf16[128,1616]{0,1:T(8,128)(2,1)S(1)}, u32[]{:S(2)}, u32[]{:S(2)}) collective-permute-start(bf16[128,1616]{0,1:T(8,128)(2,1)S(1)} %collective-permute-done.3), channel_id=1, source_target_pairs={{0,1},{1,2},{2,3},{3,4},{4,5},{5,6},{6,7},{7,0},{8,9},{9,10},{10,1... | collective-permute-start | bytes 1241096 | tf_op jit(solution)/shard_map/ppermute | solution.py:21
  37.4 18.3 %collective-permute-start.2 = (bf16[128,1616]{0,1:T(8,128)(2,1)S(1)}, bf16[128,1616]{0,1:T(8,128)(2,1)S(1)}, u32[]{:S(2)}, u32[]{:S(2)}) collective-permute-start(bf16[128,1616]{0,1:T(8,128)(2,1)S(1)} %collective-permute-done.1), channel_id=1, source_target_pairs={{0,7},{1,0},{2,1},{3,2},{4,3},{5,4},{6,5},{7,6},{8,15},{9,8},{10,9... | collective-permute-start | bytes 1241096 | tf_op jit(solution)/shard_map/ppermute | solution.py:21
  43.1 22.9 %copy-start.3 = (bf16[128,1616]{0,1:T(8,128)(2,1)}, bf16[128,1616]{0,1:T(8,128)(2,1)S(1)}, u32[]{:S(2)}) copy-start(bf16[128,1616]{0,1:T(8,128)(2,1)S(1)} %collective-permute-done.4) | copy-start | bytes 1241092
  43.1 10.3 %collective-permute-start.5 = (bf16[128,1616]{0,1:T(8,128)(2,1)S(1)}, bf16[128,1616]{0,1:T(8,128)(2,1)S(1)}, u32[]{:S(2)}, u32[]{:S(2)}) collective-permute-start(bf16[128,1616]{0,1:T(8,128)(2,1)S(1)} %collective-permute-done.4), channel_id=1, source_target_pairs={{0,1},{1,2},{2,3},{3,4},{4,5},{5,6},{6,7},{7,0},{8,9},{9,10},{10,1... | collective-permute-start | bytes 1241096 | tf_op jit(solution)/shard_map/ppermute | solution.py:21
  53.4 12.6 %copy-start.4 = (bf16[128,1616]{0,1:T(8,128)(2,1)}, bf16[128,1616]{0,1:T(8,128)(2,1)S(1)}, u32[]{:S(2)}) copy-start(bf16[128,1616]{0,1:T(8,128)(2,1)S(1)} %collective-permute-done.5) | copy-start | bytes 1241092
  53.4 9.9 %collective-permute-start.6 = (bf16[128,1616]{0,1:T(8,128)(2,1)S(1)}, bf16[128,1616]{0,1:T(8,128)(2,1)S(1)}, u32[]{:S(2)}, u32[]{:S(2)}) collective-permute-start(bf16[128,1616]{0,1:T(8,128)(2,1)S(1)} %collective-permute-done.5), channel_id=1, source_target_pairs={{0,1},{1,2},{2,3},{3,4},{4,5},{5,6},{6,7},{7,0},{8,9},{9,10},{10,1... | collective-permute-start | bytes 1241096 | tf_op jit(solution)/shard_map/ppermute | solution.py:21
  63.4 2.6 %copy-start.5 = (bf16[128,1616]{0,1:T(8,128)(2,1)}, bf16[128,1616]{0,1:T(8,128)(2,1)S(1)}, u32[]{:S(2)}) copy-start(bf16[128,1616]{0,1:T(8,128)(2,1)S(1)} %collective-permute-done.6) | copy-start | bytes 1241092
  104.9 3.3 %copy-start.1 = (bf16[8,64,1600]{2,1,0:T(8,128)(2,1)S(1)}, bf16[8,64,1600]{2,1,0:T(8,128)(2,1)}, u32[]{:S(2)}) copy-start(bf16[8,64,1600]{2,1,0:T(8,128)(2,1)} %get-tuple-element.60) | copy-start | bytes 4915204
  119.2 11.0 %copy-start = (bf16[8,64,1600]{2,1,0:T(8,128)(2,1)S(1)}, bf16[8,64,1600]{2,1,0:T(8,128)(2,1)}, u32[]{:S(2)}) copy-start(bf16[8,64,1600]{2,1,0:T(8,128)(2,1)} %get-tuple-element.59) | copy-start | bytes 4915204
  123.8 24.6 %all-to-all-start = ((f32[8,1,256]{2,1,0:T(1,128)}), f32[8,1,256]{2,1,0:T(1,128)S(1)}, u32[]{:S(2)}, u32[]{:S(2)}) async-start(f32[8,1,256]{2,1,0:T(1,128)} %reshape.1029), calls=%async_computation | async-start | bytes 16384 | tf_op jit(solution)/shard_map/all_to_all | solution.py:95
  144.1 18.5 %copy-start.6 = (s32[128]{0:T(128)S(1)}, s32[128]{0:T(128)}, u32[]{:S(2)}) copy-start(s32[128]{0:T(128)} %param.15) | copy-start | bytes 1540
  148.4 13.2 %all-to-all-start.1 = ((f32[8,1,256]{2,1,0:T(1,128)}), f32[8,1,256]{2,1,0:T(1,128)S(1)}, u32[]{:S(2)}, u32[]{:S(2)}) async-start(f32[8,1,256]{2,1,0:T(1,128)} %reshape.1027), calls=%async_computation.1 | async-start | bytes 16384 | tf_op jit(solution)/shard_map/all_to_all | solution.py:95
Sparse Core Ops, SparseCore 0:
  11.3 93.4 all-gather.1

commit v4 on v2

--- a/solution.py
+++ b/solution.py
@@ -1,6 +1,7 @@
 import jax
 import jax.numpy as jnp
 from jax import lax
+from jax.experimental import pallas as pl
 from jax.sharding import Mesh, PartitionSpec as P
 
 FLAT = ("z", "x", "c", "y")
@@ -30,6 +31,62 @@
     shifted = logits - fold_top[:, None]
     weights = jnp.exp(shifted)
     return (fold_top, jnp.sum(weights, axis=1), jnp.sum(weights * shifted, axis=1), chosen)
+
+
+def stats_kernel(rows_ref, vocab_ref, wanted_ref, ids_ref, top_ref, total_ref, spread_ref, chosen_ref):
+    j = pl.program_id(0)
+
+    @pl.when(j == 0)
+    def _():
+        top_ref[...] = jnp.full(top_ref.shape, -1e30, jnp.float32)
+        total_ref[...] = jnp.zeros(total_ref.shape, jnp.float32)
+        spread_ref[...] = jnp.zeros(spread_ref.shape, jnp.float32)
+        chosen_ref[...] = jnp.zeros(chosen_ref.shape, jnp.float32)
+
+    logits = lax.dot_general(
+        rows_ref[...], vocab_ref[...], (((1,), (1,)), ((), ())), preferred_element_type=jnp.float32
+    )
+    hit = ids_ref[...] == wanted_ref[...]
+    chosen_ref[...] += jnp.sum(jnp.where(hit, logits, 0.0), axis=1, keepdims=True)
+    fold = jnp.max(logits, axis=1, keepdims=True)
+    shifted = logits - fold
+    weights = jnp.exp(shifted)
+    new_total = jnp.sum(weights, axis=1, keepdims=True)
+    new_spread = jnp.sum(weights * shifted, axis=1, keepdims=True)
+    old_top = top_ref[...]
+    top = jnp.maximum(old_top, fold)
+    scale_one = jnp.exp(old_top - top)
+    scale_two = jnp.exp(fold - top)
+    old_total = total_ref[...]
+    total_ref[...] = old_total * scale_one + new_total * scale_two
+    spread_ref[...] = scale_one * (spread_ref[...] + (old_top - top) * old_total) + scale_two * (
+        new_spread + (fold - top) * new_total
+    )
+    top_ref[...] = top
+
+
+def row_stats(rows, vocab, wanted, ids, tile=256):
+    count, dim = rows.shape
+    width = vocab.shape[0]
+    col = pl.BlockSpec((count, 1), lambda j: (0, 0))
+    outs = pl.pallas_call(
+        stats_kernel,
+        grid=(width // tile,),
+        in_specs=[
+            pl.BlockSpec((count, dim), lambda j: (0, 0)),
+            pl.BlockSpec((tile, dim), lambda j: (j, 0)),
+            col,
+            pl.BlockSpec((1, tile), lambda j: (0, j)),
+        ],
+        out_specs=[col, col, col, col],
+        out_shape=[jax.ShapeDtypeStruct((count, 1), jnp.float32)] * 4,
+        cost_estimate=pl.CostEstimate(
+            flops=2 * count * width * dim,
+            transcendentals=count * width,
+            bytes_accessed=2 * (count + width) * dim,
+        ),
+    )(rows, vocab, wanted.reshape(count, 1), ids.reshape(1, width))
+    return tuple(o[:, 0] for o in outs)
 
 
 def on_device(hidden, norm_gain, unembed, targets, live):
@@ -71,15 +128,7 @@
     local = jnp.arange(whole.shape[0], dtype=jnp.int32)
     ids = ((local // width) * ny + y) * width + local % width
 
-    count = rows.shape[0]
-    zeros = jnp.zeros((count,), jnp.float32)
-    stats = (jnp.full((count,), -1e30, jnp.float32), zeros, zeros, zeros)
-    step = min(512, whole.shape[0])
-    for first in range(0, whole.shape[0], step):
-        stats = combine_stats(
-            stats,
-            chunk_stats(rows, whole[first : first + step], ids[first : first + step], wanted),
-        )
+    stats = row_stats(rows, whole, wanted, ids)
 
     packed = jnp.roll(jnp.stack(stats).reshape(4, ny, mine), y, axis=1).reshape(4, ny * mine)
     got = lax.all_to_all(packed, "y", 1, 1, tiled=True).reshape(4, ny, mine)

time: 141 us -> 147 us (1.043)
  Pallas kernels: 0 us -> 16.5 us
  matrix products: 11 us -> 0 us
  local copies, waits for them, and re-layouts: 5.97 us -> 8.51 us
  waiting for transfers between devices: 58.4 us -> 56.6 us
  other arithmetic: 11.3 us -> 12.8 us
    pallas_call x0 -> x1, Pallas kernels: none -> 16.5 us  [row_stats(): pl.pallas_call(stats_kernel, grid=(width // tile,), in_specs=[pl.BlockSpe...]
    dot_general x4 -> x0, matrix products: 11 us -> none  [chunk_stats(): lax.dot_general(normed, piece, (((1,), (1,)), ((), ())), preferred_elemen...]
    pallas_call x0 -> x4, other arithmetic: none -> 4.99 us  [row_stats(): pl.pallas_call(stats_kernel, grid=(width // tile,), in_specs=[pl.BlockSpe...]
    all_gather x1, waiting for transfers between devices: 40.9 us -> 36.1 us  [on_device(): whole = lax.all_gather(unembed, ('z', 'x', 'c'), axis=0, tiled=True)]
    reduce_sum x1 -> x0, other arithmetic: 3.9 us -> none  [chunk_stats(): jnp.sum(weights * shifted, axis=1)]
    ppermute x7, waiting for transfers between devices: 16.8 us -> 19.8 us  [shift(): lax.ppermute(value, axis, [(i, (i + step) % size) for i in range(size)])]
    unnamed x12 -> x15, local copies, waits for them, and re-layouts: 5.05 us -> 6.19 us
  transfers between devices with their start and end apart: 8 -> 8, of which waited for: 6 -> 5; matrix products, arithmetic and copies ran while one was open for 9% -> 11% of each run, Pallas kernels for 0% -> 0%
where the time goes in v4:
time: 147 us
  waiting for transfers between devices  56.6 us (39%)
  starting transfers between devices  25.2 us (17%)
  Pallas kernels  16.5 us (11%)
  between operations  14.3 us (10%)
  blocking collectives  12.9 us (9%)
  other arithmetic  12.8 us (9%)
  local copies, waits for them, and re-layouts  8.51 us (6%)
    all_gather x1, waiting for transfers between devices, on_device(): whole = lax.all_gather(unembed, ('z', 'x', 'c'), axis=0, tiled=True)  36.1 us
    ppermute x7, starting transfers between devices, shift(): lax.ppermute(value, axis, [(i, (i + step) % size) for i in range(size)])  25.2 us
    ppermute x7, waiting for transfers between devices, shift(): lax.ppermute(value, axis, [(i, (i + step) % size) for i in range(size)])  19.8 us
    pallas_call x1, Pallas kernels, row_stats(): pl.pallas_call(stats_kernel, grid=(width // tile,), in_specs=[pl.BlockSpe...  16.5 us
    all_to_all x1, blocking collectives, on_device(): got = lax.all_to_all(packed, 'y', 1, 1, tiled=True).reshape(4, ny, mine)  12.9 us
    unnamed x15, local copies, waits for them, and re-layouts  6.19 us
    pallas_call x4, other arithmetic, row_stats(): pl.pallas_call(stats_kernel, grid=(width // tile,), in_specs=[pl.BlockSpe...  4.99 us
  transfers between devices with their start and end apart: 8, of which 5 were waited for; matrix products, arithmetic and copies ran while one was open for 11% of the time, Pallas kernels for 0%

profile of v4, /device:TPU:1, one launch (start us, length us, event | category | flops | bytes accessed | tf_op | source)
XLA Modules:
  0.0 146.8 jit_solution(6546150452747889521)
XLA Ops:
  7.2 0.0 all-gather.2.cloned.1.call-start
  7.2 0.7 all-gather.2.cloned.1.call-update
  7.9 0.6 compare_reduce_fusion
  8.5 0.6 compare_reduce_fusion.1
  9.2 2.0 %broadcast_select_fusion = (bf16[128]{0:T(256)(128)(2,1)S(1)}, bf16[128,1]{0,1:T(2,128)(2,1)S(1)}) fusion(pred[]{:T(512)} %compare_reduce_fusion, s32[128]{0:T(128)} %param.12, pred[]{:T(512)} %compare_reduce_fusion.1), kind=kLoop, calls=%fused_computation.64 | loop fusion | flops 2944 | bytes 1026 | tf_op jit(solution)/shard_map/slice | solution.py:124
  11.1 0.1 copy.16
  11.3 0.1 copy.15
  11.4 1.2 copy.14
  12.7 0.2 scatter.9
  12.9 0.2 fusion
  13.0 1.6 %constant_dynamic-update-slice_fusion = (bf16[1024,1600]{1,0:T(8,128)(2,1)}, bf16[128,1600]{1,0:T(8,128)(2,1)S(1)}) fusion(f32[1600]{0:T(1024)} %param.10, f32[128]{0:T(128)S(1)} %add_rsqrt_fusion, bf16[128,1600]{1,0:T(8,128)(2,1)S(1)} %copy.14), kind=kLoop, calls=%fused_computation.31 | loop fusion | flops 819199 | bytes 1252096
  14.7 0.1 pad_maximum_fusion
  14.8 5.9 %collective-permute-start = (bf16[128,1616]{1,0:T(8,128)(2,1)S(1)}, bf16[128,1616]{1,0:T(8,128)(2,1)S(1)}, u32[]{:S(2)}, u32[]{:S(2)}) collective-permute-start(bf16[128,1616]{1,0:T(8,128)(2,1)S(1)} %pad_maximum_fusion), channel_id=1, source_target_pairs={{0,7},{1,0},{2,1},{3,2},{4,3},{5,4},{6,5},{7,6},{8,15},{9,8},{10,9... | collective-permute-start | bytes 1241096 | tf_op jit(solution)/shard_map/ppermute | solution.py:22
  20.7 1.9 %collective-permute-start.3 = (bf16[128,1616]{1,0:T(8,128)(2,1)S(1)}, bf16[128,1616]{1,0:T(8,128)(2,1)S(1)}, u32[]{:S(2)}, u32[]{:S(2)}) collective-permute-start(bf16[128,1616]{1,0:T(8,128)(2,1)S(1)} %pad_maximum_fusion), channel_id=1, source_target_pairs={{0,1},{1,2},{2,3},{3,4},{4,5},{5,6},{6,7},{7,0},{8,9},{9,10},{10,1... | collective-permute-start | bytes 1241096 | tf_op jit(solution)/shard_map/ppermute | solution.py:22
  22.7 0.1 multiply_reduce_fusion
  22.8 0.6 fusion.10.ids_ref
  23.4 3.8 %collective-permute-done = bf16[128,1616]{1,0:T(8,128)(2,1)S(1)} collective-permute-done((bf16[128,1616]{1,0:T(8,128)(2,1)S(1)}, bf16[128,1616]{1,0:T(8,128)(2,1)S(1)}, u32[]{:S(2)}, u32[]{:S(2)}) %collective-permute-start) | collective-permute-done | bytes 413728 | tf_op jit(solution)/shard_map/ppermute | solution.py:22
  27.2 5.3 %collective-permute-start.1 = (bf16[128,1616]{1,0:T(8,128)(2,1)S(1)}, bf16[128,1616]{1,0:T(8,128)(2,1)S(1)}, u32[]{:S(2)}, u32[]{:S(2)}) collective-permute-start(bf16[128,1616]{1,0:T(8,128)(2,1)S(1)} %collective-permute-done), channel_id=1, source_target_pairs={{0,7},{1,0},{2,1},{3,2},{4,3},{5,4},{6,5},{7,6},{8,15},{9,8},{10,9... | collective-permute-start | bytes 1241096 | tf_op jit(solution)/shard_map/ppermute | solution.py:22
  32.5 1.9 %collective-permute-start.4 = (bf16[128,1616]{1,0:T(8,128)(2,1)S(1)}, bf16[128,1616]{1,0:T(8,128)(2,1)S(1)}, u32[]{:S(2)}, u32[]{:S(2)}) collective-permute-start(bf16[128,1616]{1,0:T(8,128)(2,1)S(1)} %collective-permute-done.3), channel_id=1, source_target_pairs={{0,1},{1,2},{2,3},{3,4},{4,5},{5,6},{6,7},{7,0},{8,9},{9,10},{10,1... | collective-permute-start | bytes 1241096 | tf_op jit(solution)/shard_map/ppermute | solution.py:22
  34.5 0.2 add_reduce_fusion.6
  34.6 0.2 add_reduce_fusion
  34.8 0.8 slice_dynamic-update-slice_fusion.6
  35.6 2.4 %collective-permute-done.1 = bf16[128,1616]{1,0:T(8,128)(2,1)S(1)} collective-permute-done((bf16[128,1616]{1,0:T(8,128)(2,1)S(1)}, bf16[128,1616]{1,0:T(8,128)(2,1)S(1)}, u32[]{:S(2)}, u32[]{:S(2)}) %collective-permute-start.1) | collective-permute-done | bytes 413728 | tf_op jit(solution)/shard_map/ppermute | solution.py:22
  38.1 5.7 %collective-permute-start.2 = (bf16[128,1616]{1,0:T(8,128)(2,1)S(1)}, bf16[128,1616]{1,0:T(8,128)(2,1)S(1)}, u32[]{:S(2)}, u32[]{:S(2)}) collective-permute-start(bf16[128,1616]{1,0:T(8,128)(2,1)S(1)} %collective-permute-done.1), channel_id=1, source_target_pairs={{0,7},{1,0},{2,1},{3,2},{4,3},{5,4},{6,5},{7,6},{8,15},{9,8},{10,9... | collective-permute-start | bytes 1241096 | tf_op jit(solution)/shard_map/ppermute | solution.py:22
  43.8 1.9 %collective-permute-start.5 = (bf16[128,1616]{1,0:T(8,128)(2,1)S(1)}, bf16[128,1616]{1,0:T(8,128)(2,1)S(1)}, u32[]{:S(2)}, u32[]{:S(2)}) collective-permute-start(bf16[128,1616]{1,0:T(8,128)(2,1)S(1)} %collective-permute-done.4), channel_id=1, source_target_pairs={{0,1},{1,2},{2,3},{3,4},{4,5},{5,6},{6,7},{7,0},{8,9},{9,10},{10,1... | collective-permute-start | bytes 1241096 | tf_op jit(solution)/shard_map/ppermute | solution.py:22
  45.7 0.2 add_reduce_fusion.5
  45.9 0.2 add_reduce_fusion.1
  46.1 0.8 slice_dynamic-update-slice_fusion.5
  46.9 7.0 %collective-permute-done.5 = bf16[128,1616]{1,0:T(8,128)(2,1)S(1)} collective-permute-done((bf16[128,1616]{1,0:T(8,128)(2,1)S(1)}, bf16[128,1616]{1,0:T(8,128)(2,1)S(1)}, u32[]{:S(2)}, u32[]{:S(2)}) %collective-permute-start.5) | collective-permute-done | bytes 413728 | tf_op jit(solution)/shard_map/ppermute | solution.py:22
  53.9 2.5 %collective-permute-start.6 = (bf16[128,1616]{1,0:T(8,128)(2,1)S(1)}, bf16[128,1616]{1,0:T(8,128)(2,1)S(1)}, u32[]{:S(2)}, u32[]{:S(2)}) collective-permute-start(bf16[128,1616]{1,0:T(8,128)(2,1)S(1)} %collective-permute-done.5), channel_id=1, source_target_pairs={{0,1},{1,2},{2,3},{3,4},{4,5},{5,6},{6,7},{7,0},{8,9},{9,10},{10,1... | collective-permute-start | bytes 1241096 | tf_op jit(solution)/shard_map/ppermute | solution.py:22
  56.4 0.2 add_reduce_fusion.4
  56.6 0.2 add_reduce_fusion.2
  56.8 0.8 slice_dynamic-update-slice_fusion.4
  57.6 6.5 %collective-permute-done.6 = bf16[128,1616]{1,0:T(8,128)(2,1)S(1)} collective-permute-done((bf16[128,1616]{1,0:T(8,128)(2,1)S(1)}, bf16[128,1616]{1,0:T(8,128)(2,1)S(1)}, u32[]{:S(2)}, u32[]{:S(2)}) %collective-permute-start.6) | collective-permute-done | bytes 413728 | tf_op jit(solution)/shard_map/ppermute | solution.py:22
  64.2 0.2 add_reduce_fusion.3
  64.4 1.0 copy.17.wanted_ref
  65.5 0.8 slice_dynamic-update-slice_fusion.3
  66.3 0.8 slice_dynamic-update-slice_fusion.2
  67.1 0.8 slice_dynamic-update-slice_fusion.1
  67.9 0.8 slice_dynamic-update-slice_fusion.rows_ref
  68.7 36.1 %all-gather.2.cloned.1.call-done.vocab_ref = bf16[2048,1600]{1,0:T(8,128)(2,1)} async-done(((bf16[32,1600]{1,0:T(8,128)(2,1)}), bf16[2048,1600]{1,0:T(8,128)(2,1)}) %all-gather.2.cloned.1.call-update) | async-done | bytes 6553616 | tf_op jit(solution)/shard_map/all_gather | solution.py:127
  104.9 16.5 %shard_map.68 = (f32[1024,1]{1,0:T(8,128)}, f32[1024,1]{1,0:T(8,128)}, f32[1024,1]{1,0:T(8,128)}, f32[1024,1]{1,0:T(8,128)}) custom-call(bf16[1024,1600]{1,0:T(8,128)(2,1)} %slice_dynamic-update-slice_fusion.rows_ref, bf16[2048,1600]{1,0:T(8,128)(2,1)} %all-gather.2.cloned.1.call-done.vocab_ref, s32[1024,1]{1,0:T(8,128)} %copy.17.wanted_ref, ...), custom_call_target="tpu_custom_call" | custom-call | flops 6710886400 | bytes 9830400 | tf_op jit(solution)/shard_map/pallas_call | solution.py:72
  121.4 1.2 reduce.24
  122.6 1.2 reduce.25
  123.9 1.2 reduce.26
  125.1 1.2 reduce.27
  126.4 12.9 %all_to_all.6 = f32[4,8,128]{2,0,1:T(4,128)S(1)} all-to-all(f32[4,8,128]{2,0,1:T(4,128)S(1)} %copy.18), channel_id=1, replica_groups=mesh['z'=8,'x'=4,'c'=2,'y'=8] {'y'}, dimensions={1} | all-to-all | bytes 32768 | tf_op jit(solution)/shard_map/all_to_all | solution.py:134
  139.4 0.5 subtract_multiply_fusion
  (21 shorter events, 0.2 us)
Async XLA Ops:
  7.2 97.7 %all-gather.2.cloned.1.call-start = ((), (), s32[]{:S(2)}) async-start(), calls=%async_computation.1 | async-start | bytes 6922240 | tf_op jit(solution)/shard_map/all_gather | solution.py:127
  14.8 12.4 %collective-permute-start = (bf16[128,1616]{1,0:T(8,128)(2,1)S(1)}, bf16[128,1616]{1,0:T(8,128)(2,1)S(1)}, u32[]{:S(2)}, u32[]{:S(2)}) collective-permute-start(bf16[128,1616]{1,0:T(8,128)(2,1)S(1)} %pad_maximum_fusion), channel_id=1, source_target_pairs={{0,7},{1,0},{2,1},{3,2},{4,3},{5,4},{6,5},{7,6},{8,15},{9,8},{10,9... | collective-permute-start | bytes 1241096 | tf_op jit(solution)/shard_map/ppermute | solution.py:22
  20.7 11.8 %collective-permute-start.3 = (bf16[128,1616]{1,0:T(8,128)(2,1)S(1)}, bf16[128,1616]{1,0:T(8,128)(2,1)S(1)}, u32[]{:S(2)}, u32[]{:S(2)}) collective-permute-start(bf16[128,1616]{1,0:T(8,128)(2,1)S(1)} %pad_maximum_fusion), channel_id=1, source_target_pairs={{0,1},{1,2},{2,3},{3,4},{4,5},{5,6},{6,7},{7,0},{8,9},{9,10},{10,1... | collective-permute-start | bytes 1241096 | tf_op jit(solution)/shard_map/ppermute | solution.py:22
  27.2 10.9 %collective-permute-start.1 = (bf16[128,1616]{1,0:T(8,128)(2,1)S(1)}, bf16[128,1616]{1,0:T(8,128)(2,1)S(1)}, u32[]{:S(2)}, u32[]{:S(2)}) collective-permute-start(bf16[128,1616]{1,0:T(8,128)(2,1)S(1)} %collective-permute-done), channel_id=1, source_target_pairs={{0,7},{1,0},{2,1},{3,2},{4,3},{5,4},{6,5},{7,6},{8,15},{9,8},{10,9... | collective-permute-start | bytes 1241096 | tf_op jit(solution)/shard_map/ppermute | solution.py:22
  32.5 11.3 %collective-permute-start.4 = (bf16[128,1616]{1,0:T(8,128)(2,1)S(1)}, bf16[128,1616]{1,0:T(8,128)(2,1)S(1)}, u32[]{:S(2)}, u32[]{:S(2)}) collective-permute-start(bf16[128,1616]{1,0:T(8,128)(2,1)S(1)} %collective-permute-done.3), channel_id=1, source_target_pairs={{0,1},{1,2},{2,3},{3,4},{4,5},{5,6},{6,7},{7,0},{8,9},{9,10},{10,1... | collective-permute-start | bytes 1241096 | tf_op jit(solution)/shard_map/ppermute | solution.py:22
  38.1 18.3 %collective-permute-start.2 = (bf16[128,1616]{1,0:T(8,128)(2,1)S(1)}, bf16[128,1616]{1,0:T(8,128)(2,1)S(1)}, u32[]{:S(2)}, u32[]{:S(2)}) collective-permute-start(bf16[128,1616]{1,0:T(8,128)(2,1)S(1)} %collective-permute-done.1), channel_id=1, source_target_pairs={{0,7},{1,0},{2,1},{3,2},{4,3},{5,4},{6,5},{7,6},{8,15},{9,8},{10,9... | collective-permute-start | bytes 1241096 | tf_op jit(solution)/shard_map/ppermute | solution.py:22
  43.8 10.1 %collective-permute-start.5 = (bf16[128,1616]{1,0:T(8,128)(2,1)S(1)}, bf16[128,1616]{1,0:T(8,128)(2,1)S(1)}, u32[]{:S(2)}, u32[]{:S(2)}) collective-permute-start(bf16[128,1616]{1,0:T(8,128)(2,1)S(1)} %collective-permute-done.4), channel_id=1, source_target_pairs={{0,1},{1,2},{2,3},{3,4},{4,5},{5,6},{6,7},{7,0},{8,9},{9,10},{10,1... | collective-permute-start | bytes 1241096 | tf_op jit(solution)/shard_map/ppermute | solution.py:22
  53.9 10.3 %collective-permute-start.6 = (bf16[128,1616]{1,0:T(8,128)(2,1)S(1)}, bf16[128,1616]{1,0:T(8,128)(2,1)S(1)}, u32[]{:S(2)}, u32[]{:S(2)}) collective-permute-start(bf16[128,1616]{1,0:T(8,128)(2,1)S(1)} %collective-permute-done.5), channel_id=1, source_target_pairs={{0,1},{1,2},{2,3},{3,4},{4,5},{5,6},{6,7},{7,0},{8,9},{9,10},{10,1... | collective-permute-start | bytes 1241096 | tf_op jit(solution)/shard_map/ppermute | solution.py:22
  68.7 70.7 %copy-start = (s32[128]{0:T(128)S(1)}, s32[128]{0:T(128)}, u32[]{:S(2)}) copy-start(s32[128]{0:T(128)} %param.13) | copy-start | bytes 1540
Sparse Core Ops, SparseCore 0:
  11.3 93.4 all-gather.1

commit v5 on v4

--- a/solution.py
+++ b/solution.py
@@ -44,15 +44,15 @@
         chosen_ref[...] = jnp.zeros(chosen_ref.shape, jnp.float32)
 
     logits = lax.dot_general(
-        rows_ref[...], vocab_ref[...], (((1,), (1,)), ((), ())), preferred_element_type=jnp.float32
+        vocab_ref[...], rows_ref[...], (((1,), (1,)), ((), ())), preferred_element_type=jnp.float32
     )
     hit = ids_ref[...] == wanted_ref[...]
-    chosen_ref[...] += jnp.sum(jnp.where(hit, logits, 0.0), axis=1, keepdims=True)
-    fold = jnp.max(logits, axis=1, keepdims=True)
+    chosen_ref[...] += jnp.sum(jnp.where(hit, logits, 0.0), axis=0, keepdims=True)
+    fold = jnp.max(logits, axis=0, keepdims=True)
     shifted = logits - fold
     weights = jnp.exp(shifted)
-    new_total = jnp.sum(weights, axis=1, keepdims=True)
-    new_spread = jnp.sum(weights * shifted, axis=1, keepdims=True)
+    new_total = jnp.sum(weights, axis=0, keepdims=True)
+    new_spread = jnp.sum(weights * shifted, axis=0, keepdims=True)
     old_top = top_ref[...]
     top = jnp.maximum(old_top, fold)
     scale_one = jnp.exp(old_top - top)
@@ -68,25 +68,25 @@
 def row_stats(rows, vocab, wanted, ids, tile=256):
     count, dim = rows.shape
     width = vocab.shape[0]
-    col = pl.BlockSpec((count, 1), lambda j: (0, 0))
+    line = pl.BlockSpec((1, count), lambda j: (0, 0))
     outs = pl.pallas_call(
         stats_kernel,
         grid=(width // tile,),
         in_specs=[
             pl.BlockSpec((count, dim), lambda j: (0, 0)),
             pl.BlockSpec((tile, dim), lambda j: (j, 0)),
-            col,
-            pl.BlockSpec((1, tile), lambda j: (0, j)),
+            line,
+            pl.BlockSpec((tile, 1), lambda j: (j, 0)),
         ],
-        out_specs=[col, col, col, col],
-        out_shape=[jax.ShapeDtypeStruct((count, 1), jnp.float32)] * 4,
+        out_specs=[line, line, line, line],
+        out_shape=[jax.ShapeDtypeStruct((1, count), jnp.float32)] * 4,
         cost_estimate=pl.CostEstimate(
             flops=2 * count * width * dim,
             transcendentals=count * width,
             bytes_accessed=2 * (count + width) * dim,
         ),
-    )(rows, vocab, wanted.reshape(count, 1), ids.reshape(1, width))
-    return tuple(o[:, 0] for o in outs)
+    )(rows, vocab, wanted.reshape(1, count), ids.reshape(width, 1))
+    return tuple(o.reshape(count) for o in outs)
 
 
 def on_device(hidden, norm_gain, unembed, targets, live):

time: 147 us -> 140 us (0.952)
  other arithmetic: 12.8 us -> 9.1 us
  Pallas kernels: 16.5 us -> 13.9 us
    pallas_call x4 -> x0, other arithmetic: 4.99 us -> none  [row_stats(): pl.pallas_call(stats_kernel, grid=(width // tile,), in_specs=[pl.BlockSpe...]
    pallas_call x1, Pallas kernels: 16.5 us -> 13.9 us  [row_stats(): pl.pallas_call(stats_kernel, grid=(width // tile,), in_specs=[pl.BlockSpe...]
    unnamed x15 -> x17, local copies, waits for them, and re-layouts: 6.19 us -> 6.19 us
where the time goes in v5:
time: 140 us
  waiting for transfers between devices  57 us (41%)
  starting transfers between devices  25.2 us (18%)
  between operations  14.3 us (10%)
  Pallas kernels  13.9 us (10%)
  blocking collectives  12.9 us (9%)
  other arithmetic  9.1 us (6%)
  local copies, waits for them, and re-layouts  7.46 us (5%)
    all_gather x1, waiting for transfers between devices, on_device(): whole = lax.all_gather(unembed, ('z', 'x', 'c'), axis=0, tiled=True)  37.2 us
    ppermute x7, starting transfers between devices, shift(): lax.ppermute(value, axis, [(i, (i + step) % size) for i in range(size)])  25.2 us
    ppermute x7, waiting for transfers between devices, shift(): lax.ppermute(value, axis, [(i, (i + step) % size) for i in range(size)])  19.2 us
    pallas_call x1, Pallas kernels, row_stats(): pl.pallas_call(stats_kernel, grid=(width // tile,), in_specs=[pl.BlockSpe...  13.9 us
    all_to_all x1, blocking collectives, on_device(): got = lax.all_to_all(packed, 'y', 1, 1, tiled=True).reshape(4, ny, mine)  12.9 us
    unnamed x17, local copies, waits for them, and re-layouts  6.19 us
  transfers between devices with their start and end apart: 8, of which 5 were waited for; matrix products, arithmetic and copies ran while one was open for 11% of the time, Pallas kernels for 0%

profile of v5, /device:TPU:1, one launch (start us, length us, event | category | flops | bytes accessed | tf_op | source)
XLA Modules:
  0.0 139.9 jit_solution(8701798262131942979)
XLA Ops:
  7.2 0.0 all-gather.2.cloned.1.call-start
  7.2 0.7 all-gather.2.cloned.1.call-update
  7.9 0.6 compare_reduce_fusion
  8.5 0.6 compare_reduce_fusion.1
  9.2 2.0 %broadcast_select_fusion = (bf16[128]{0:T(256)(128)(2,1)S(1)}, bf16[128,1]{0,1:T(2,128)(2,1)S(1)}) fusion(pred[]{:T(512)} %compare_reduce_fusion, s32[128]{0:T(128)} %param.12, pred[]{:T(512)} %compare_reduce_fusion.1), kind=kLoop, calls=%fused_computation.59 | loop fusion | flops 2944 | bytes 1026 | tf_op jit(solution)/shard_map/slice | solution.py:124
  11.1 0.1 copy.22
  11.3 0.1 copy.21
  11.4 1.2 copy.20
  12.7 0.2 scatter.9
  12.9 0.2 fusion.11
  13.0 1.6 %constant_dynamic-update-slice_fusion = (bf16[1024,1600]{1,0:T(8,128)(2,1)}, bf16[128,1600]{1,0:T(8,128)(2,1)S(1)}) fusion(f32[1600]{0:T(1024)} %param.10, f32[128]{0:T(128)S(1)} %add_rsqrt_fusion, bf16[128,1600]{1,0:T(8,128)(2,1)S(1)} %copy.20), kind=kLoop, calls=%fused_computation.38 | loop fusion | flops 819199 | bytes 1252096
  14.7 0.1 pad_maximum_fusion
  14.8 5.9 %collective-permute-start = (bf16[128,1616]{1,0:T(8,128)(2,1)S(1)}, bf16[128,1616]{1,0:T(8,128)(2,1)S(1)}, u32[]{:S(2)}, u32[]{:S(2)}) collective-permute-start(bf16[128,1616]{1,0:T(8,128)(2,1)S(1)} %pad_maximum_fusion), channel_id=1, source_target_pairs={{0,7},{1,0},{2,1},{3,2},{4,3},{5,4},{6,5},{7,6},{8,15},{9,8},{10,9... | collective-permute-start | bytes 1241096 | tf_op jit(solution)/shard_map/ppermute | solution.py:22
  20.7 1.9 %collective-permute-start.3 = (bf16[128,1616]{1,0:T(8,128)(2,1)S(1)}, bf16[128,1616]{1,0:T(8,128)(2,1)S(1)}, u32[]{:S(2)}, u32[]{:S(2)}) collective-permute-start(bf16[128,1616]{1,0:T(8,128)(2,1)S(1)} %pad_maximum_fusion), channel_id=1, source_target_pairs={{0,1},{1,2},{2,3},{3,4},{4,5},{5,6},{6,7},{7,0},{8,9},{9,10},{10,1... | collective-permute-start | bytes 1241096 | tf_op jit(solution)/shard_map/ppermute | solution.py:22
  22.7 0.1 multiply_reduce_fusion
  22.8 1.2 fusion.9.ids_ref
  24.0 3.2 %collective-permute-done = bf16[128,1616]{1,0:T(8,128)(2,1)S(1)} collective-permute-done((bf16[128,1616]{1,0:T(8,128)(2,1)S(1)}, bf16[128,1616]{1,0:T(8,128)(2,1)S(1)}, u32[]{:S(2)}, u32[]{:S(2)}) %collective-permute-start) | collective-permute-done | bytes 413728 | tf_op jit(solution)/shard_map/ppermute | solution.py:22
  27.2 5.3 %collective-permute-start.1 = (bf16[128,1616]{1,0:T(8,128)(2,1)S(1)}, bf16[128,1616]{1,0:T(8,128)(2,1)S(1)}, u32[]{:S(2)}, u32[]{:S(2)}) collective-permute-start(bf16[128,1616]{1,0:T(8,128)(2,1)S(1)} %collective-permute-done), channel_id=1, source_target_pairs={{0,7},{1,0},{2,1},{3,2},{4,3},{5,4},{6,5},{7,6},{8,15},{9,8},{10,9... | collective-permute-start | bytes 1241096 | tf_op jit(solution)/shard_map/ppermute | solution.py:22
  32.5 0.0 collective-permute-done.3
  32.5 1.9 %collective-permute-start.4 = (bf16[128,1616]{1,0:T(8,128)(2,1)S(1)}, bf16[128,1616]{1,0:T(8,128)(2,1)S(1)}, u32[]{:S(2)}, u32[]{:S(2)}) collective-permute-start(bf16[128,1616]{1,0:T(8,128)(2,1)S(1)} %collective-permute-done.3), channel_id=1, source_target_pairs={{0,1},{1,2},{2,3},{3,4},{4,5},{5,6},{6,7},{7,0},{8,9},{9,10},{10,1... | collective-permute-start | bytes 1241096 | tf_op jit(solution)/shard_map/ppermute | solution.py:22
  34.5 0.2 add_reduce_fusion.6
  34.6 0.2 add_reduce_fusion
  34.8 0.8 slice_dynamic-update-slice_fusion.6
  35.6 2.4 %collective-permute-done.1 = bf16[128,1616]{1,0:T(8,128)(2,1)S(1)} collective-permute-done((bf16[128,1616]{1,0:T(8,128)(2,1)S(1)}, bf16[128,1616]{1,0:T(8,128)(2,1)S(1)}, u32[]{:S(2)}, u32[]{:S(2)}) %collective-permute-start.1) | collective-permute-done | bytes 413728 | tf_op jit(solution)/shard_map/ppermute | solution.py:22
  38.1 5.7 %collective-permute-start.2 = (bf16[128,1616]{1,0:T(8,128)(2,1)S(1)}, bf16[128,1616]{1,0:T(8,128)(2,1)S(1)}, u32[]{:S(2)}, u32[]{:S(2)}) collective-permute-start(bf16[128,1616]{1,0:T(8,128)(2,1)S(1)} %collective-permute-done.1), channel_id=1, source_target_pairs={{0,7},{1,0},{2,1},{3,2},{4,3},{5,4},{6,5},{7,6},{8,15},{9,8},{10,9... | collective-permute-start | bytes 1241096 | tf_op jit(solution)/shard_map/ppermute | solution.py:22
  43.8 0.0 collective-permute-done.4
  43.8 1.9 %collective-permute-start.5 = (bf16[128,1616]{1,0:T(8,128)(2,1)S(1)}, bf16[128,1616]{1,0:T(8,128)(2,1)S(1)}, u32[]{:S(2)}, u32[]{:S(2)}) collective-permute-start(bf16[128,1616]{1,0:T(8,128)(2,1)S(1)} %collective-permute-done.4), channel_id=1, source_target_pairs={{0,1},{1,2},{2,3},{3,4},{4,5},{5,6},{6,7},{7,0},{8,9},{9,10},{10,1... | collective-permute-start | bytes 1241096 | tf_op jit(solution)/shard_map/ppermute | solution.py:22
  45.7 0.2 add_reduce_fusion.5
  45.9 0.2 add_reduce_fusion.1
  46.1 0.8 slice_dynamic-update-slice_fusion.5
  46.9 7.0 %collective-permute-done.5 = bf16[128,1616]{1,0:T(8,128)(2,1)S(1)} collective-permute-done((bf16[128,1616]{1,0:T(8,128)(2,1)S(1)}, bf16[128,1616]{1,0:T(8,128)(2,1)S(1)}, u32[]{:S(2)}, u32[]{:S(2)}) %collective-permute-start.5) | collective-permute-done | bytes 413728 | tf_op jit(solution)/shard_map/ppermute | solution.py:22
  53.9 2.5 %collective-permute-start.6 = (bf16[128,1616]{1,0:T(8,128)(2,1)S(1)}, bf16[128,1616]{1,0:T(8,128)(2,1)S(1)}, u32[]{:S(2)}, u32[]{:S(2)}) collective-permute-start(bf16[128,1616]{1,0:T(8,128)(2,1)S(1)} %collective-permute-done.5), channel_id=1, source_target_pairs={{0,1},{1,2},{2,3},{3,4},{4,5},{5,6},{6,7},{7,0},{8,9},{9,10},{10,1... | collective-permute-start | bytes 1241096 | tf_op jit(solution)/shard_map/ppermute | solution.py:22
  56.4 0.0 collective-permute-done.2
  56.4 0.2 add_reduce_fusion.4
  56.6 0.2 add_reduce_fusion.2
  56.8 0.8 slice_dynamic-update-slice_fusion.4
  57.6 6.5 %collective-permute-done.6 = bf16[128,1616]{1,0:T(8,128)(2,1)S(1)} collective-permute-done((bf16[128,1616]{1,0:T(8,128)(2,1)S(1)}, bf16[128,1616]{1,0:T(8,128)(2,1)S(1)}, u32[]{:S(2)}, u32[]{:S(2)}) %collective-permute-start.6) | collective-permute-done | bytes 413728 | tf_op jit(solution)/shard_map/ppermute | solution.py:22
  64.2 0.2 add_reduce_fusion.3
  64.4 0.8 slice_dynamic-update-slice_fusion.3
  65.3 0.8 slice_dynamic-update-slice_fusion.2
  66.1 0.8 slice_dynamic-update-slice_fusion.1
  66.9 0.8 slice_dynamic-update-slice_fusion.rows_ref
  67.7 37.2 %all-gather.2.cloned.1.call-done.vocab_ref = bf16[2048,1600]{1,0:T(8,128)(2,1)} async-done(((bf16[32,1600]{1,0:T(8,128)(2,1)}), bf16[2048,1600]{1,0:T(8,128)(2,1)}) %all-gather.2.cloned.1.call-update) | async-done | bytes 6553616 | tf_op jit(solution)/shard_map/all_gather | solution.py:127
  104.9 13.9 %shard_map.68 = (f32[1,1024]{1,0:T(1,128)}, f32[1,1024]{1,0:T(1,128)}, f32[1,1024]{1,0:T(1,128)}, f32[1,1024]{1,0:T(1,128)}) custom-call(bf16[1024,1600]{1,0:T(8,128)(2,1)} %slice_dynamic-update-slice_fusion.rows_ref, bf16[2048,1600]{1,0:T(8,128)(2,1)} %all-gather.2.cloned.1.call-done.vocab_ref, s32[1,1024]{1,0:T(1,128)} %bitcast.18, s32[2048,1]{1,0:T(8,128)} %fusion.9.ids_ref), custom_call_target="tpu_custom_call" | custom-call | flops 6710886400 | bytes 9830400 | tf_op jit(solution)/shard_map/pallas_call | solution.py:72
  118.8 0.7 maximum_bitcast_fusion
  119.5 12.9 %all_to_all.6 = f32[4,8,128]{2,0,1:T(4,128)S(1)} all-to-all(f32[4,8,128]{2,0,1:T(4,128)S(1)} %fusion.14), channel_id=1, replica_groups=mesh['z'=8,'x'=4,'c'=2,'y'=8] {'y'}, dimensions={1} | all-to-all | bytes 32768 | tf_op jit(solution)/shard_map/all_to_all | solution.py:134
  132.5 0.0 copy-done
  132.5 0.5 subtract_multiply_fusion
  (18 shorter events, 0.2 us)
Async XLA Ops:
  7.2 97.7 %all-gather.2.cloned.1.call-start = ((), (), s32[]{:S(2)}) async-start(), calls=%async_computation.1 | async-start | bytes 6922240 | tf_op jit(solution)/shard_map/all_gather | solution.py:127
  14.8 12.4 %collective-permute-start = (bf16[128,1616]{1,0:T(8,128)(2,1)S(1)}, bf16[128,1616]{1,0:T(8,128)(2,1)S(1)}, u32[]{:S(2)}, u32[]{:S(2)}) collective-permute-start(bf16[128,1616]{1,0:T(8,128)(2,1)S(1)} %pad_maximum_fusion), channel_id=1, source_target_pairs={{0,7},{1,0},{2,1},{3,2},{4,3},{5,4},{6,5},{7,6},{8,15},{9,8},{10,9... | collective-permute-start | bytes 1241096 | tf_op jit(solution)/shard_map/ppermute | solution.py:22
  20.7 11.8 %collective-permute-start.3 = (bf16[128,1616]{1,0:T(8,128)(2,1)S(1)}, bf16[128,1616]{1,0:T(8,128)(2,1)S(1)}, u32[]{:S(2)}, u32[]{:S(2)}) collective-permute-start(bf16[128,1616]{1,0:T(8,128)(2,1)S(1)} %pad_maximum_fusion), channel_id=1, source_target_pairs={{0,1},{1,2},{2,3},{3,4},{4,5},{5,6},{6,7},{7,0},{8,9},{9,10},{10,1... | collective-permute-start | bytes 1241096 | tf_op jit(solution)/shard_map/ppermute | solution.py:22
  27.2 10.9 %collective-permute-start.1 = (bf16[128,1616]{1,0:T(8,128)(2,1)S(1)}, bf16[128,1616]{1,0:T(8,128)(2,1)S(1)}, u32[]{:S(2)}, u32[]{:S(2)}) collective-permute-start(bf16[128,1616]{1,0:T(8,128)(2,1)S(1)} %collective-permute-done), channel_id=1, source_target_pairs={{0,7},{1,0},{2,1},{3,2},{4,3},{5,4},{6,5},{7,6},{8,15},{9,8},{10,9... | collective-permute-start | bytes 1241096 | tf_op jit(solution)/shard_map/ppermute | solution.py:22
  32.5 11.3 %collective-permute-start.4 = (bf16[128,1616]{1,0:T(8,128)(2,1)S(1)}, bf16[128,1616]{1,0:T(8,128)(2,1)S(1)}, u32[]{:S(2)}, u32[]{:S(2)}) collective-permute-start(bf16[128,1616]{1,0:T(8,128)(2,1)S(1)} %collective-permute-done.3), channel_id=1, source_target_pairs={{0,1},{1,2},{2,3},{3,4},{4,5},{5,6},{6,7},{7,0},{8,9},{9,10},{10,1... | collective-permute-start | bytes 1241096 | tf_op jit(solution)/shard_map/ppermute | solution.py:22
  38.1 18.3 %collective-permute-start.2 = (bf16[128,1616]{1,0:T(8,128)(2,1)S(1)}, bf16[128,1616]{1,0:T(8,128)(2,1)S(1)}, u32[]{:S(2)}, u32[]{:S(2)}) collective-permute-start(bf16[128,1616]{1,0:T(8,128)(2,1)S(1)} %collective-permute-done.1), channel_id=1, source_target_pairs={{0,7},{1,0},{2,1},{3,2},{4,3},{5,4},{6,5},{7,6},{8,15},{9,8},{10,9... | collective-permute-start | bytes 1241096 | tf_op jit(solution)/shard_map/ppermute | solution.py:22
  43.8 10.1 %collective-permute-start.5 = (bf16[128,1616]{1,0:T(8,128)(2,1)S(1)}, bf16[128,1616]{1,0:T(8,128)(2,1)S(1)}, u32[]{:S(2)}, u32[]{:S(2)}) collective-permute-start(bf16[128,1616]{1,0:T(8,128)(2,1)S(1)} %collective-permute-done.4), channel_id=1, source_target_pairs={{0,1},{1,2},{2,3},{3,4},{4,5},{5,6},{6,7},{7,0},{8,9},{9,10},{10,1... | collective-permute-start | bytes 1241096 | tf_op jit(solution)/shard_map/ppermute | solution.py:22
  53.9 10.3 %collective-permute-start.6 = (bf16[128,1616]{1,0:T(8,128)(2,1)S(1)}, bf16[128,1616]{1,0:T(8,128)(2,1)S(1)}, u32[]{:S(2)}, u32[]{:S(2)}) collective-permute-start(bf16[128,1616]{1,0:T(8,128)(2,1)S(1)} %collective-permute-done.5), channel_id=1, source_target_pairs={{0,1},{1,2},{2,3},{3,4},{4,5},{5,6},{6,7},{7,0},{8,9},{9,10},{10,1... | collective-permute-start | bytes 1241096 | tf_op jit(solution)/shard_map/ppermute | solution.py:22
  64.4 40.4 %copy-start.1 = (s32[1024]{0:T(1024)}, s32[1024]{0:T(1024)S(1)}, u32[]{:S(2)}) copy-start(s32[1024]{0:T(1024)S(1)} %constant_dynamic-update-slice_fusion.2) | copy-start | bytes 12292
  104.9 27.6 %copy-start = (s32[128]{0:T(128)S(1)}, s32[128]{0:T(128)}, u32[]{:S(2)}) copy-start(s32[128]{0:T(128)} %param.13) | copy-start | bytes 1540
Sparse Core Ops, SparseCore 0:
  11.3 93.4 all-gather.1

commit v6 on v5

--- a/solution.py
+++ b/solution.py
@@ -124,9 +124,24 @@
         [b[:, dim].astype(jnp.int32) * 128 + b[:, dim + 1].astype(jnp.int32) for b in blocks], axis=0
     )
 
-    whole = lax.all_gather(unembed, ("z", "x", "c"), axis=0, tiled=True)
+    nx = lax.axis_size("x")
+    x = lax.axis_index("x")
+    near = [None] * nx
+    near[0] = unembed
+    cur = unembed
+    for d in range(1, nx // 2 + 1):
+        cur = shift(cur, "x", nx, 1)
+        near[nx - d] = cur
+    cur = unembed
+    for d in range(1, nx - nx // 2):
+        cur = shift(cur, "x", nx, -1)
+        near[d] = cur
+    whole = lax.all_gather(jnp.concatenate(near, axis=0), ("z", "c"), axis=0, tiled=True)
     local = jnp.arange(whole.shape[0], dtype=jnp.int32)
-    ids = ((local // width) * ny + y) * width + local % width
+    group, place = local // (nx * width), local % (nx * width)
+    far_z, far_c = group // nc, group % nc
+    far_x = (x + place // width) % nx
+    ids = (((far_z * nx + far_x) * nc + far_c) * ny + y) * width + place % width
 
     stats = row_stats(rows, whole, wanted, ids)
 

time: 140 us -> 132 us (0.943)
  the two profiles are of different devices: /device:TPU:1 before, /device:TPU:8 now
where the time goes in v6:
time: 132 us; the launch traced here: 131 us
  waiting for transfers between devices  37.3 us (28%)
  starting transfers between devices  34.8 us (26%)
  between operations  14.3 us (11%)
  Pallas kernels  13.9 us (11%)
  blocking collectives  11.9 us (9%)
  other arithmetic  11.5 us (9%)
  local copies, waits for them, and re-layouts  7.47 us (6%)
    ppermute x10, waiting for transfers between devices, shift(): lax.ppermute(value, axis, [(i, (i + step) % size) for i in range(size)])  37.3 us
    ppermute x10, starting transfers between devices, shift(): lax.ppermute(value, axis, [(i, (i + step) % size) for i in range(size)])  34.8 us
    pallas_call x1, Pallas kernels, row_stats(): pl.pallas_call(stats_kernel, grid=(width // tile,), in_specs=[pl.BlockSpe...  13.9 us
    all_to_all x1, blocking collectives, on_device(): got = lax.all_to_all(packed, 'y', 1, 1, tiled=True).reshape(4, ny, mine)  11.9 us
    unnamed x17, local copies, waits for them, and re-layouts  6.2 us
  transfers between devices with their start and end apart: 11, of which 6 were waited for; matrix products, arithmetic and copies ran while one was open for 12% of the time, Pallas kernels for 0%

profile of v6, /device:TPU:8, one launch (start us, length us, event | category | flops | bytes accessed | tf_op | source)
XLA Modules:
  0.0 131.2 jit_solution(4857416602523512316)
XLA Ops:
  7.2 0.0 all-gather.2.cloned.1.call-start
  7.2 3.4 %collective-permute-start.8 = (bf16[32,1600]{1,0:T(8,128)(2,1)}, bf16[32,1600]{1,0:T(8,128)(2,1)S(1)}, u32[]{:S(2)}, u32[]{:S(2)}) collective-permute-start(bf16[32,1600]{1,0:T(8,128)(2,1)} %param.11), channel_id=1, source_target_pairs={{0,16},{16,32},{32,48},{48,0},{1,17},{17,33},{33,49},{49,1},{2,18}... | collective-permute-start | bytes 307208 | tf_op jit(solution)/shard_map/ppermute | solution.py:22
  10.6 3.7 %collective-permute-start.7 = (bf16[32,1600]{1,0:T(8,128)(2,1)}, bf16[32,1600]{1,0:T(8,128)(2,1)S(1)}, u32[]{:S(2)}, u32[]{:S(2)}) collective-permute-start(bf16[32,1600]{1,0:T(8,128)(2,1)} %param.11), channel_id=1, source_target_pairs={{0,48},{16,0},{32,16},{48,32},{1,49},{17,1},{33,17},{49,33},{2,50}... | collective-permute-start | bytes 307208 | tf_op jit(solution)/shard_map/ppermute | solution.py:22
  14.3 1.0 collective-permute-done.8
  15.2 2.2 %collective-permute-start.9 = (bf16[32,1600]{1,0:T(8,128)(2,1)S(1)}, bf16[32,1600]{1,0:T(8,128)(2,1)S(1)}, u32[]{:S(2)}, u32[]{:S(2)}) collective-permute-start(bf16[32,1600]{1,0:T(8,128)(2,1)S(1)} %collective-permute-done.8), channel_id=1, source_target_pairs={{0,16},{16,32},{32,48},{48,0},{1,17},{17,33},{33,49},{49,1},{2,18}... | collective-permute-start | bytes 307208 | tf_op jit(solution)/shard_map/ppermute | solution.py:22
  17.4 5.6 %collective-permute-done.9 = bf16[32,1600]{1,0:T(8,128)(2,1)S(1)} collective-permute-done((bf16[32,1600]{1,0:T(8,128)(2,1)S(1)}, bf16[32,1600]{1,0:T(8,128)(2,1)S(1)}, u32[]{:S(2)}, u32[]{:S(2)}) %collective-permute-start.9) | collective-permute-done | bytes 102432 | tf_op jit(solution)/shard_map/ppermute | solution.py:22
  23.0 1.7 %pad_maximum_fusion.1 = bf16[128,1600]{1,0:T(8,128)(2,1)} fusion(bf16[32,1600]{1,0:T(8,128)(2,1)S(1)} %collective-permute-done.8, bf16[32,1600]{1,0:T(8,128)(2,1)S(1)} %collective-permute-done.9, bf16[32,1600]{1,0:T(8,128)(2,1)S(1)} %collective-permute-done.7, bf16[32,1600]{1,0:T(8,128)(2,1)} %param.11), kind=kLoop, calls=%fused_computation.58 | loop fusion | flops 1638400 | bytes 819200 | tf_op jit(solution)/shard_map/concatenate | solution.py:139
  24.7 0.6 compare_reduce_fusion
  25.4 0.6 compare_reduce_fusion.1
  26.0 2.0 %broadcast_select_fusion = (bf16[128]{0:T(256)(128)(2,1)S(1)}, bf16[128,1]{0,1:T(2,128)(2,1)S(1)}) fusion(pred[]{:T(512)} %compare_reduce_fusion, s32[128]{0:T(128)} %param.12, pred[]{:T(512)} %compare_reduce_fusion.1), kind=kLoop, calls=%fused_computation.90 | loop fusion | flops 2944 | bytes 1026 | tf_op jit(solution)/shard_map/slice | solution.py:124
  28.0 0.1 copy.15
  28.1 0.1 copy.14
  28.2 1.2 copy.13
  29.5 0.2 scatter.9
  29.7 0.2 fusion.28
  29.9 1.6 %constant_dynamic-update-slice_fusion = (bf16[1024,1600]{1,0:T(8,128)(2,1)}, bf16[128,1600]{1,0:T(8,128)(2,1)S(1)}) fusion(f32[1600]{0:T(1024)} %param.10, f32[128]{0:T(128)S(1)} %add_rsqrt_fusion, bf16[128,1600]{1,0:T(8,128)(2,1)S(1)} %copy.13), kind=kLoop, calls=%fused_computation.69 | loop fusion | flops 819199 | bytes 1252096
  31.5 0.1 pad_maximum_fusion
  31.6 8.8 %collective-permute-start = (bf16[128,1616]{1,0:T(8,128)(2,1)S(1)}, bf16[128,1616]{1,0:T(8,128)(2,1)S(1)}, u32[]{:S(2)}, u32[]{:S(2)}) collective-permute-start(bf16[128,1616]{1,0:T(8,128)(2,1)S(1)} %pad_maximum_fusion), channel_id=1, source_target_pairs={{0,7},{1,0},{2,1},{3,2},{4,3},{5,4},{6,5},{7,6},{8,15},{9,8},{10,9... | collective-permute-start | bytes 1241096 | tf_op jit(solution)/shard_map/ppermute | solution.py:22
  40.4 1.9 %collective-permute-start.3 = (bf16[128,1616]{1,0:T(8,128)(2,1)S(1)}, bf16[128,1616]{1,0:T(8,128)(2,1)S(1)}, u32[]{:S(2)}, u32[]{:S(2)}) collective-permute-start(bf16[128,1616]{1,0:T(8,128)(2,1)S(1)} %pad_maximum_fusion), channel_id=1, source_target_pairs={{0,1},{1,2},{2,3},{3,4},{4,5},{5,6},{6,7},{7,0},{8,9},{9,10},{10,1... | collective-permute-start | bytes 1241096 | tf_op jit(solution)/shard_map/ppermute | solution.py:22
  42.4 0.1 multiply_reduce_fusion
  42.5 1.9 %fusion.13.ids_ref = s32[2048,1]{1,0:T(8,128)} fusion(s32[]{:T(128)S(6)} %axis_index.25, s32[]{:T(128)S(6)} %axis_index.23), kind=kLoop, calls=%fused_computation.32 | loop fusion | flops 143360 | bytes 8200 | tf_op jit(solution)/shard_map/add | solution.py:144
  44.4 6.0 %collective-permute-done = bf16[128,1616]{1,0:T(8,128)(2,1)S(1)} collective-permute-done((bf16[128,1616]{1,0:T(8,128)(2,1)S(1)}, bf16[128,1616]{1,0:T(8,128)(2,1)S(1)}, u32[]{:S(2)}, u32[]{:S(2)}) %collective-permute-start) | collective-permute-done | bytes 413728 | tf_op jit(solution)/shard_map/ppermute | solution.py:22
  50.4 4.4 %collective-permute-start.1 = (bf16[128,1616]{1,0:T(8,128)(2,1)S(1)}, bf16[128,1616]{1,0:T(8,128)(2,1)S(1)}, u32[]{:S(2)}, u32[]{:S(2)}) collective-permute-start(bf16[128,1616]{1,0:T(8,128)(2,1)S(1)} %collective-permute-done), channel_id=1, source_target_pairs={{0,7},{1,0},{2,1},{3,2},{4,3},{5,4},{6,5},{7,6},{8,15},{9,8},{10,9... | collective-permute-start | bytes 1241096 | tf_op jit(solution)/shard_map/ppermute | solution.py:22
  54.8 1.9 %collective-permute-start.4 = (bf16[128,1616]{1,0:T(8,128)(2,1)S(1)}, bf16[128,1616]{1,0:T(8,128)(2,1)S(1)}, u32[]{:S(2)}, u32[]{:S(2)}) collective-permute-start(bf16[128,1616]{1,0:T(8,128)(2,1)S(1)} %collective-permute-done.3), channel_id=1, source_target_pairs={{0,1},{1,2},{2,3},{3,4},{4,5},{5,6},{6,7},{7,0},{8,9},{9,10},{10,1... | collective-permute-start | bytes 1241096 | tf_op jit(solution)/shard_map/ppermute | solution.py:22
  56.7 0.2 add_reduce_fusion.6
  56.9 0.2 add_reduce_fusion
  57.1 0.8 slice_dynamic-update-slice_fusion.6
  57.9 6.6 %collective-permute-done.1 = bf16[128,1616]{1,0:T(8,128)(2,1)S(1)} collective-permute-done((bf16[128,1616]{1,0:T(8,128)(2,1)S(1)}, bf16[128,1616]{1,0:T(8,128)(2,1)S(1)}, u32[]{:S(2)}, u32[]{:S(2)}) %collective-permute-start.1) | collective-permute-done | bytes 413728 | tf_op jit(solution)/shard_map/ppermute | solution.py:22
  64.4 4.4 %collective-permute-start.2 = (bf16[128,1616]{1,0:T(8,128)(2,1)S(1)}, bf16[128,1616]{1,0:T(8,128)(2,1)S(1)}, u32[]{:S(2)}, u32[]{:S(2)}) collective-permute-start(bf16[128,1616]{1,0:T(8,128)(2,1)S(1)} %collective-permute-done.1), channel_id=1, source_target_pairs={{0,7},{1,0},{2,1},{3,2},{4,3},{5,4},{6,5},{7,6},{8,15},{9,8},{10,9... | collective-permute-start | bytes 1241096 | tf_op jit(solution)/shard_map/ppermute | solution.py:22
  68.8 2.2 %collective-permute-start.5 = (bf16[128,1616]{1,0:T(8,128)(2,1)S(1)}, bf16[128,1616]{1,0:T(8,128)(2,1)S(1)}, u32[]{:S(2)}, u32[]{:S(2)}) collective-permute-start(bf16[128,1616]{1,0:T(8,128)(2,1)S(1)} %collective-permute-done.4), channel_id=1, source_target_pairs={{0,1},{1,2},{2,3},{3,4},{4,5},{5,6},{6,7},{7,0},{8,9},{9,10},{10,1... | collective-permute-start | bytes 1241096 | tf_op jit(solution)/shard_map/ppermute | solution.py:22
  71.0 0.2 add_reduce_fusion.5
  71.2 0.2 add_reduce_fusion.1
  71.4 0.8 slice_dynamic-update-slice_fusion.5
  72.2 10.4 %collective-permute-done.5 = bf16[128,1616]{1,0:T(8,128)(2,1)S(1)} collective-permute-done((bf16[128,1616]{1,0:T(8,128)(2,1)S(1)}, bf16[128,1616]{1,0:T(8,128)(2,1)S(1)}, u32[]{:S(2)}, u32[]{:S(2)}) %collective-permute-start.5) | collective-permute-done | bytes 413728 | tf_op jit(solution)/shard_map/ppermute | solution.py:22
  82.7 2.0 %collective-permute-start.6 = (bf16[128,1616]{1,0:T(8,128)(2,1)S(1)}, bf16[128,1616]{1,0:T(8,128)(2,1)S(1)}, u32[]{:S(2)}, u32[]{:S(2)}) collective-permute-start(bf16[128,1616]{1,0:T(8,128)(2,1)S(1)} %collective-permute-done.5), channel_id=1, source_target_pairs={{0,1},{1,2},{2,3},{3,4},{4,5},{5,6},{6,7},{7,0},{8,9},{9,10},{10,1... | collective-permute-start | bytes 1241096 | tf_op jit(solution)/shard_map/ppermute | solution.py:22
  84.6 0.2 add_reduce_fusion.4
  84.8 0.2 add_reduce_fusion.2
  85.0 0.8 slice_dynamic-update-slice_fusion.4
  85.9 7.7 %collective-permute-done.6 = bf16[128,1616]{1,0:T(8,128)(2,1)S(1)} collective-permute-done((bf16[128,1616]{1,0:T(8,128)(2,1)S(1)}, bf16[128,1616]{1,0:T(8,128)(2,1)S(1)}, u32[]{:S(2)}, u32[]{:S(2)}) %collective-permute-start.6) | collective-permute-done | bytes 413728 | tf_op jit(solution)/shard_map/ppermute | solution.py:22
  93.6 0.2 add_reduce_fusion.3
  93.9 0.8 slice_dynamic-update-slice_fusion.3
  94.7 0.8 slice_dynamic-update-slice_fusion.2
  95.5 0.8 slice_dynamic-update-slice_fusion.1
  96.3 0.8 slice_dynamic-update-slice_fusion.rows_ref
  97.1 13.9 %shard_map.68 = (f32[1,1024]{1,0:T(1,128)}, f32[1,1024]{1,0:T(1,128)}, f32[1,1024]{1,0:T(1,128)}, f32[1,1024]{1,0:T(1,128)}) custom-call(bf16[1024,1600]{1,0:T(8,128)(2,1)} %slice_dynamic-update-slice_fusion.rows_ref, bf16[2048,1600]{1,0:T(8,128)(2,1)} %all-gather.2.cloned.1.call-done.vocab_ref, s32[1,1024]{1,0:T(1,128)} %bitcast.18, s32[2048,1]{1,0:T(8,128)} %fusion.13.ids_ref), custom_call_target="tpu_custom_call" | custom-call | flops 6710886400 | bytes 9830400 | tf_op jit(solution)/shard_map/pallas_call | solution.py:72
  111.1 0.7 maximum_bitcast_fusion
  111.8 11.9 %all_to_all.6 = f32[4,8,128]{2,0,1:T(4,128)S(1)} all-to-all(f32[4,8,128]{2,0,1:T(4,128)S(1)} %fusion.31), channel_id=1, replica_groups=mesh['z'=8,'x'=4,'c'=2,'y'=8] {'y'}, dimensions={1} | all-to-all | bytes 32768 | tf_op jit(solution)/shard_map/all_to_all | solution.py:149
  123.8 0.5 subtract_multiply_fusion
  (25 shorter events, 0.2 us)
Async XLA Ops:
  7.2 90.0 %all-gather.2.cloned.1.call-start = ((), (), s32[]{:S(2)}) async-start(), calls=%async_computation.1 | async-start | bytes 7241728 | tf_op jit(solution)/shard_map/all_gather | solution.py:139
  7.2 8.0 %collective-permute-start.8 = (bf16[32,1600]{1,0:T(8,128)(2,1)}, bf16[32,1600]{1,0:T(8,128)(2,1)S(1)}, u32[]{:S(2)}, u32[]{:S(2)}) collective-permute-start(bf16[32,1600]{1,0:T(8,128)(2,1)} %param.11), channel_id=1, source_target_pairs={{0,16},{16,32},{32,48},{48,0},{1,17},{17,33},{33,49},{49,1},{2,18}... | collective-permute-start | bytes 307208 | tf_op jit(solution)/shard_map/ppermute | solution.py:22
  10.6 6.8 %collective-permute-start.7 = (bf16[32,1600]{1,0:T(8,128)(2,1)}, bf16[32,1600]{1,0:T(8,128)(2,1)S(1)}, u32[]{:S(2)}, u32[]{:S(2)}) collective-permute-start(bf16[32,1600]{1,0:T(8,128)(2,1)} %param.11), channel_id=1, source_target_pairs={{0,48},{16,0},{32,16},{48,32},{1,49},{17,1},{33,17},{49,33},{2,50}... | collective-permute-start | bytes 307208 | tf_op jit(solution)/shard_map/ppermute | solution.py:22
  15.2 7.8 %collective-permute-start.9 = (bf16[32,1600]{1,0:T(8,128)(2,1)S(1)}, bf16[32,1600]{1,0:T(8,128)(2,1)S(1)}, u32[]{:S(2)}, u32[]{:S(2)}) collective-permute-start(bf16[32,1600]{1,0:T(8,128)(2,1)S(1)} %collective-permute-done.8), channel_id=1, source_target_pairs={{0,16},{16,32},{32,48},{48,0},{1,17},{17,33},{33,49},{49,1},{2,18}... | collective-permute-start | bytes 307208 | tf_op jit(solution)/shard_map/ppermute | solution.py:22
  31.6 18.8 %collective-permute-start = (bf16[128,1616]{1,0:T(8,128)(2,1)S(1)}, bf16[128,1616]{1,0:T(8,128)(2,1)S(1)}, u32[]{:S(2)}, u32[]{:S(2)}) collective-permute-start(bf16[128,1616]{1,0:T(8,128)(2,1)S(1)} %pad_maximum_fusion), channel_id=1, source_target_pairs={{0,7},{1,0},{2,1},{3,2},{4,3},{5,4},{6,5},{7,6},{8,15},{9,8},{10,9... | collective-permute-start | bytes 1241096 | tf_op jit(solution)/shard_map/ppermute | solution.py:22
  40.4 14.3 %collective-permute-start.3 = (bf16[128,1616]{1,0:T(8,128)(2,1)S(1)}, bf16[128,1616]{1,0:T(8,128)(2,1)S(1)}, u32[]{:S(2)}, u32[]{:S(2)}) collective-permute-start(bf16[128,1616]{1,0:T(8,128)(2,1)S(1)} %pad_maximum_fusion), channel_id=1, source_target_pairs={{0,1},{1,2},{2,3},{3,4},{4,5},{5,6},{6,7},{7,0},{8,9},{9,10},{10,1... | collective-permute-start | bytes 1241096 | tf_op jit(solution)/shard_map/ppermute | solution.py:22
  50.4 14.1 %collective-permute-start.1 = (bf16[128,1616]{1,0:T(8,128)(2,1)S(1)}, bf16[128,1616]{1,0:T(8,128)(2,1)S(1)}, u32[]{:S(2)}, u32[]{:S(2)}) collective-permute-start(bf16[128,1616]{1,0:T(8,128)(2,1)S(1)} %collective-permute-done), channel_id=1, source_target_pairs={{0,7},{1,0},{2,1},{3,2},{4,3},{5,4},{6,5},{7,6},{8,15},{9,8},{10,9... | collective-permute-start | bytes 1241096 | tf_op jit(solution)/shard_map/ppermute | solution.py:22
  54.8 14.1 %collective-permute-start.4 = (bf16[128,1616]{1,0:T(8,128)(2,1)S(1)}, bf16[128,1616]{1,0:T(8,128)(2,1)S(1)}, u32[]{:S(2)}, u32[]{:S(2)}) collective-permute-start(bf16[128,1616]{1,0:T(8,128)(2,1)S(1)} %collective-permute-done.3), channel_id=1, source_target_pairs={{0,1},{1,2},{2,3},{3,4},{4,5},{5,6},{6,7},{7,0},{8,9},{9,10},{10,1... | collective-permute-start | bytes 1241096 | tf_op jit(solution)/shard_map/ppermute | solution.py:22
  64.4 20.2 %collective-permute-start.2 = (bf16[128,1616]{1,0:T(8,128)(2,1)S(1)}, bf16[128,1616]{1,0:T(8,128)(2,1)S(1)}, u32[]{:S(2)}, u32[]{:S(2)}) collective-permute-start(bf16[128,1616]{1,0:T(8,128)(2,1)S(1)} %collective-permute-done.1), channel_id=1, source_target_pairs={{0,7},{1,0},{2,1},{3,2},{4,3},{5,4},{6,5},{7,6},{8,15},{9,8},{10,9... | collective-permute-start | bytes 1241096 | tf_op jit(solution)/shard_map/ppermute | solution.py:22
  68.8 13.8 %collective-permute-start.5 = (bf16[128,1616]{1,0:T(8,128)(2,1)S(1)}, bf16[128,1616]{1,0:T(8,128)(2,1)S(1)}, u32[]{:S(2)}, u32[]{:S(2)}) collective-permute-start(bf16[128,1616]{1,0:T(8,128)(2,1)S(1)} %collective-permute-done.4), channel_id=1, source_target_pairs={{0,1},{1,2},{2,3},{3,4},{4,5},{5,6},{6,7},{7,0},{8,9},{9,10},{10,1... | collective-permute-start | bytes 1241096 | tf_op jit(solution)/shard_map/ppermute | solution.py:22
  82.7 10.9 %collective-permute-start.6 = (bf16[128,1616]{1,0:T(8,128)(2,1)S(1)}, bf16[128,1616]{1,0:T(8,128)(2,1)S(1)}, u32[]{:S(2)}, u32[]{:S(2)}) collective-permute-start(bf16[128,1616]{1,0:T(8,128)(2,1)S(1)} %collective-permute-done.5), channel_id=1, source_target_pairs={{0,1},{1,2},{2,3},{3,4},{4,5},{5,6},{6,7},{7,0},{8,9},{9,10},{10,1... | collective-permute-start | bytes 1241096 | tf_op jit(solution)/shard_map/ppermute | solution.py:22
  93.8 3.3 %copy-start.1 = (s32[1024]{0:T(1024)}, s32[1024]{0:T(1024)S(1)}, u32[]{:S(2)}) copy-start(s32[1024]{0:T(1024)S(1)} %constant_dynamic-update-slice_fusion.2) | copy-start | bytes 12292
  97.1 26.7 %copy-start = (s32[128]{0:T(128)S(1)}, s32[128]{0:T(128)}, u32[]{:S(2)}) copy-start(s32[128]{0:T(128)} %param.13) | copy-start | bytes 1540
Sparse Core Ops, SparseCore 0:
  24.9 54.0 all-gather.1

commit v7 on v5

--- a/solution.py
+++ b/solution.py
@@ -108,25 +108,40 @@
     code = code.at[:, 1].set((targets % 128).astype(jnp.bfloat16))
     block = jnp.concatenate([normed, code], axis=1)
 
-    blocks = [None] * ny
-    blocks[0] = block
-    fwd = ny // 2
-    cur = block
-    for d in range(1, fwd + 1):
-        cur = shift(cur, "y", ny, 1)
-        blocks[ny - d] = cur
-    cur = block
-    for d in range(1, ny - fwd):
-        cur = shift(cur, "y", ny, -1)
-        blocks[d] = cur
+    nx = lax.axis_size("x")
+    x = lax.axis_index("x")
+    block, unembed = lax.optimization_barrier((block, unembed))
+
+    rings = {"y": (ny, block), "x": (nx, unembed)}
+    got = {name: {0: start} for name, (size, start) in rings.items()}
+    fronts = {name: {1: start, -1: start} for name, (size, start) in rings.items()}
+    for step in range(1, ny // 2 + 1):
+        moved = []
+        for name, (size, start) in rings.items():
+            for sign in (1, -1):
+                reach = size // 2 if sign == 1 else size - 1 - size // 2
+                if step <= reach:
+                    fronts[name][sign] = shift(fronts[name][sign], name, size, sign)
+                    got[name][(-sign * step) % size] = fronts[name][sign]
+                    moved.append((name, sign))
+        if step <= nx // 2:
+            values = lax.optimization_barrier(tuple(fronts[n][s] for n, s in moved))
+            for (n, s), v in zip(moved, values):
+                fronts[n][s] = v
+                got[n][(-s * step) % rings[n][0]] = v
+    blocks = [got["y"][d] for d in range(ny)]
+    near = [got["x"][d] for d in range(nx)]
     rows = jnp.concatenate([b[:, :dim] for b in blocks], axis=0)
     wanted = jnp.concatenate(
         [b[:, dim].astype(jnp.int32) * 128 + b[:, dim + 1].astype(jnp.int32) for b in blocks], axis=0
     )
 
-    whole = lax.all_gather(unembed, ("z", "x", "c"), axis=0, tiled=True)
+    whole = lax.all_gather(jnp.concatenate(near, axis=0), ("z", "c"), axis=0, tiled=True)
     local = jnp.arange(whole.shape[0], dtype=jnp.int32)
-    ids = ((local // width) * ny + y) * width + local % width
+    group, place = local // (nx * width), local % (nx * width)
+    far_z, far_c = group // nc, group % nc
+    far_x = (x + place // width) % nx
+    ids = (((far_z * nx + far_x) * nc + far_c) * ny + y) * width + place % width
 
     stats = row_stats(rows, whole, wanted, ids)
 

time: 140 us -> 142 us (1.014)
  starting transfers between devices: 25.2 us -> 35.7 us
  waiting for transfers between devices: 57 us -> 47.2 us
    ppermute x7 -> x10, starting transfers between devices: 25.2 us -> 35.6 us  [shift(): lax.ppermute(value, axis, [(i, (i + step) % size) for i in range(size)])]
    all_gather x1, waiting for transfers between devices: 37.2 us -> 27.2 us  [on_device(): lax.all_gather(jnp.concatenate(near, axis=0), ('z', 'c'), axis=0, tiled=T...]
    another operation x2 -> x3, other arithmetic: 1.28 us -> 3.25 us
    slice x1 -> x0, other arithmetic: 1.96 us -> none  [on_device(): b[:, dim + 1].astype(jnp.int32)]
    unnamed x3 -> x1, other arithmetic: 1.65 us -> 0.01 us
    ppermute x7 -> x10, waiting for transfers between devices: 19.2 us -> 19.9 us  [shift(): lax.ppermute(value, axis, [(i, (i + step) % size) for i in range(size)])]
    unnamed x17 -> x22, local copies, waits for them, and re-layouts: 6.19 us -> 6.45 us
  transfers between devices with their start and end apart: 8 -> 11, of which waited for: 5 -> 6; matrix products, arithmetic and copies ran while one was open for 11% -> 5% of each run, Pallas kernels for 0% -> 0%
where the time goes in v7:
time: 142 us; the launch traced here: 141 us
  waiting for transfers between devices  47.2 us (33%)
  starting transfers between devices  35.7 us (25%)
  between operations  14.3 us (10%)
  Pallas kernels  13.9 us (10%)
  blocking collectives  12.9 us (9%)
  other arithmetic  9.56 us (7%)
  local copies, waits for them, and re-layouts  7.72 us (5%)
    ppermute x10, starting transfers between devices, shift(): lax.ppermute(value, axis, [(i, (i + step) % size) for i in range(size)])  35.6 us
    all_gather x1, waiting for transfers between devices, on_device(): lax.all_gather(jnp.concatenate(near, axis=0), ('z', 'c'), axis=0, tiled=T...  27.2 us
    ppermute x10, waiting for transfers between devices, shift(): lax.ppermute(value, axis, [(i, (i + step) % size) for i in range(size)])  19.9 us
    pallas_call x1, Pallas kernels, row_stats(): pl.pallas_call(stats_kernel, grid=(width // tile,), in_specs=[pl.BlockSpe...  13.9 us
    all_to_all x1, blocking collectives, on_device(): got = lax.all_to_all(packed, 'y', 1, 1, tiled=True).reshape(4, ny, mine)  12.9 us
    unnamed x22, local copies, waits for them, and re-layouts  6.45 us
    another operation x3, other arithmetic  3.25 us
  transfers between devices with their start and end apart: 11, of which 6 were waited for; matrix products, arithmetic and copies ran while one was open for 5% of the time, Pallas kernels for 0%

profile of v7, /device:TPU:1, one launch (start us, length us, event | category | flops | bytes accessed | tf_op | source)
XLA Modules:
  0.0 141.2 jit_solution(6877108180128145120)
XLA Ops:
  7.2 0.0 copy-start
  7.2 0.0 all-gather.2.cloned.1.call-start
  7.2 0.6 compare_reduce_fusion
  7.9 0.6 compare_reduce_fusion.1
  8.5 1.2 copy.13
  9.7 0.2 fusion.28
  9.9 2.0 %fusion.33 = (bf16[128,1]{0,1:T(2,128)(2,1)S(1)}, bf16[128,1]{0,1:T(2,128)(2,1)S(1)}) fusion(pred[]{:T(512)} %compare_reduce_fusion, s32[128]{0:T(128)} %param.12, pred[]{:T(512)} %compare_reduce_fusion.1), kind=kLoop, calls=%fused_computation.93 | loop fusion | flops 2944 | bytes 1026 | tf_op jit(solution)/shard_map/reshape.177
  11.9 0.1 copy.14
  12.0 0.1 copy.15
  12.2 0.9 fusion.30
  13.1 0.2 scatter.9
  13.2 0.1 pad_maximum_fusion
  13.3 4.0 %collective-permute-start = (bf16[128,1616]{1,0:T(8,128)(2,1)S(1)}, bf16[128,1616]{1,0:T(8,128)(2,1)S(1)}, u32[]{:S(2)}, u32[]{:S(2)}) collective-permute-start(bf16[128,1616]{1,0:T(8,128)(2,1)S(1)} %pad_maximum_fusion), channel_id=1, source_target_pairs={{0,1},{1,2},{2,3},{3,4},{4,5},{5,6},{6,7},{7,0},{8,9},{9,10},{10,1... | collective-permute-start | bytes 1241096 | tf_op jit(solution)/shard_map/ppermute | solution.py:22
  17.4 3.8 %collective-permute-start.1 = (bf16[128,1616]{1,0:T(8,128)(2,1)S(1)}, bf16[128,1616]{1,0:T(8,128)(2,1)S(1)}, u32[]{:S(2)}, u32[]{:S(2)}) collective-permute-start(bf16[128,1616]{1,0:T(8,128)(2,1)S(1)} %pad_maximum_fusion), channel_id=1, source_target_pairs={{0,7},{1,0},{2,1},{3,2},{4,3},{5,4},{6,5},{7,6},{8,15},{9,8},{10,9... | collective-permute-start | bytes 1241096 | tf_op jit(solution)/shard_map/ppermute | solution.py:22
  21.2 3.1 %collective-permute-start.2 = (bf16[32,1600]{1,0:T(8,128)(2,1)}, bf16[32,1600]{1,0:T(8,128)(2,1)S(1)}, u32[]{:S(2)}, u32[]{:S(2)}) collective-permute-start(bf16[32,1600]{1,0:T(8,128)(2,1)} %param.11), channel_id=1, source_target_pairs={{0,16},{16,32},{32,48},{48,0},{1,17},{17,33},{33,49},{49,1},{2,18}... | collective-permute-start | bytes 307208 | tf_op jit(solution)/shard_map/ppermute | solution.py:22
  24.3 3.4 %collective-permute-start.3 = (bf16[32,1600]{1,0:T(8,128)(2,1)}, bf16[32,1600]{1,0:T(8,128)(2,1)S(1)}, u32[]{:S(2)}, u32[]{:S(2)}) collective-permute-start(bf16[32,1600]{1,0:T(8,128)(2,1)} %param.11), channel_id=1, source_target_pairs={{0,48},{16,0},{32,16},{48,32},{1,49},{17,1},{33,17},{49,33},{2,50}... | collective-permute-start | bytes 307208 | tf_op jit(solution)/shard_map/ppermute | solution.py:22
  27.7 0.6 collective-permute-done.2
  28.4 1.9 %collective-permute-done.3 = bf16[32,1600]{1,0:T(8,128)(2,1)S(1)} collective-permute-done((bf16[32,1600]{1,0:T(8,128)(2,1)}, bf16[32,1600]{1,0:T(8,128)(2,1)S(1)}, u32[]{:S(2)}, u32[]{:S(2)}) %collective-permute-start.3) | collective-permute-done | bytes 102432 | tf_op jit(solution)/shard_map/ppermute | solution.py:22
  30.3 2.5 %collective-permute-start.4 = (bf16[128,1616]{1,0:T(8,128)(2,1)S(1)}, bf16[128,1616]{1,0:T(8,128)(2,1)S(1)}, u32[]{:S(2)}, u32[]{:S(2)}) collective-permute-start(bf16[128,1616]{1,0:T(8,128)(2,1)S(1)} %collective-permute-done), channel_id=1, source_target_pairs={{0,1},{1,2},{2,3},{3,4},{4,5},{5,6},{6,7},{7,0},{8,9},{9,10},{10,1... | collective-permute-start | bytes 1241096 | tf_op jit(solution)/shard_map/ppermute | solution.py:22
  32.8 3.9 %collective-permute-start.5 = (bf16[128,1616]{1,0:T(8,128)(2,1)S(1)}, bf16[128,1616]{1,0:T(8,128)(2,1)S(1)}, u32[]{:S(2)}, u32[]{:S(2)}) collective-permute-start(bf16[128,1616]{1,0:T(8,128)(2,1)S(1)} %collective-permute-done.1), channel_id=1, source_target_pairs={{0,7},{1,0},{2,1},{3,2},{4,3},{5,4},{6,5},{7,6},{8,15},{9,8},{10,9... | collective-permute-start | bytes 1241096 | tf_op jit(solution)/shard_map/ppermute | solution.py:22
  36.8 3.2 %collective-permute-start.6 = (bf16[32,1600]{1,0:T(8,128)(2,1)S(1)}, bf16[32,1600]{1,0:T(8,128)(2,1)S(1)}, u32[]{:S(2)}, u32[]{:S(2)}) collective-permute-start(bf16[32,1600]{1,0:T(8,128)(2,1)S(1)} %collective-permute-done.2), channel_id=1, source_target_pairs={{0,16},{16,32},{32,48},{48,0},{1,17},{17,33},{33,49},{49,1},{2,18}... | collective-permute-start | bytes 307208 | tf_op jit(solution)/shard_map/ppermute | solution.py:22
  40.1 3.7 %collective-permute-done.6 = bf16[32,1600]{1,0:T(8,128)(2,1)S(1)} collective-permute-done((bf16[32,1600]{1,0:T(8,128)(2,1)S(1)}, bf16[32,1600]{1,0:T(8,128)(2,1)S(1)}, u32[]{:S(2)}, u32[]{:S(2)}) %collective-permute-start.6) | collective-permute-done | bytes 102432 | tf_op jit(solution)/shard_map/ppermute | solution.py:22
  43.7 0.0 collective-permute-done.4
  43.8 0.8 pad_maximum_fusion.1
  44.6 1.8 %copy-done.1 = bf16[1024,1600]{1,0:T(8,128)(2,1)} copy-done((bf16[1024,1600]{1,0:T(8,128)(2,1)}, bf16[1024,1600]{1,0:T(8,128)(2,1)S(1)}, u32[]{:S(2)}) %copy-start.1) | copy-done | bytes 3276824
  46.4 0.0 all-gather.2.cloned.1.call-update
  46.4 0.2 add_reduce_fusion.7
  46.6 1.9 %fusion.13.ids_ref = s32[2048,1]{1,0:T(8,128)} fusion(s32[]{:T(128)S(6)} %axis_index.25, s32[]{:T(128)S(6)} %axis_index.23), kind=kLoop, calls=%fused_computation.32 | loop fusion | flops 143360 | bytes 8200 | tf_op jit(solution)/shard_map/add | solution.py:144
  48.5 3.1 %collective-permute-start.7 = (bf16[128,1616]{1,0:T(8,128)(2,1)S(1)}, bf16[128,1616]{1,0:T(8,128)(2,1)S(1)}, u32[]{:S(2)}, u32[]{:S(2)}) collective-permute-start(bf16[128,1616]{1,0:T(8,128)(2,1)S(1)} %collective-permute-done.5), channel_id=1, source_target_pairs={{0,7},{1,0},{2,1},{3,2},{4,3},{5,4},{6,5},{7,6},{8,15},{9,8},{10,9... | collective-permute-start | bytes 1241096 | tf_op jit(solution)/shard_map/ppermute | solution.py:22
  51.6 4.7 %collective-permute-start.8 = (bf16[128,1616]{1,0:T(8,128)(2,1)S(1)}, bf16[128,1616]{1,0:T(8,128)(2,1)S(1)}, u32[]{:S(2)}, u32[]{:S(2)}) collective-permute-start(bf16[128,1616]{1,0:T(8,128)(2,1)S(1)} %collective-permute-done.4), channel_id=1, source_target_pairs={{0,1},{1,2},{2,3},{3,4},{4,5},{5,6},{6,7},{7,0},{8,9},{9,10},{10,1... | collective-permute-start | bytes 1241096 | tf_op jit(solution)/shard_map/ppermute | solution.py:22
  56.3 0.2 add_reduce_fusion
  56.5 0.2 add_reduce_fusion.1
  56.7 5.0 %collective-permute-done.8 = bf16[128,1616]{1,0:T(8,128)(2,1)S(1)} collective-permute-done((bf16[128,1616]{1,0:T(8,128)(2,1)S(1)}, bf16[128,1616]{1,0:T(8,128)(2,1)S(1)}, u32[]{:S(2)}, u32[]{:S(2)}) %collective-permute-start.8) | collective-permute-done | bytes 413728 | tf_op jit(solution)/shard_map/ppermute | solution.py:22
  61.7 3.8 %collective-permute-start.9 = (bf16[128,1616]{1,0:T(8,128)(2,1)S(1)}, bf16[128,1616]{1,0:T(8,128)(2,1)S(1)}, u32[]{:S(2)}, u32[]{:S(2)}) collective-permute-start(bf16[128,1616]{1,0:T(8,128)(2,1)S(1)} %collective-permute-done.8), channel_id=1, source_target_pairs={{0,1},{1,2},{2,3},{3,4},{4,5},{5,6},{6,7},{7,0},{8,9},{9,10},{10,1... | collective-permute-start | bytes 1241096 | tf_op jit(solution)/shard_map/ppermute | solution.py:22
  65.5 0.2 add_reduce_fusion.4
  65.7 0.2 add_reduce_fusion.2
  65.9 0.8 slice_dynamic-update-slice_fusion.2
  66.7 8.8 %collective-permute-done.9 = bf16[128,1616]{1,0:T(8,128)(2,1)S(1)} collective-permute-done((bf16[128,1616]{1,0:T(8,128)(2,1)S(1)}, bf16[128,1616]{1,0:T(8,128)(2,1)S(1)}, u32[]{:S(2)}, u32[]{:S(2)}) %collective-permute-start.9) | collective-permute-done | bytes 413728 | tf_op jit(solution)/shard_map/ppermute | solution.py:22
  75.5 0.2 add_reduce_fusion.3
  75.7 0.8 slice_dynamic-update-slice_fusion.1
  76.6 0.8 slice_dynamic-update-slice_fusion
  77.4 0.8 slice_dynamic-update-slice_fusion.4
  78.2 0.8 slice_dynamic-update-slice_fusion.3.rows_ref
  79.0 27.2 %all-gather.2.cloned.1.call-done.vocab_ref = bf16[2048,1600]{1,0:T(8,128)(2,1)} async-done(((bf16[128,1600]{1,0:T(8,128)(2,1)}), bf16[2048,1600]{1,0:T(8,128)(2,1)}) %all-gather.2.cloned.1.call-update) | async-done | bytes 6553616 | tf_op jit(solution)/shard_map/all_gather | solution.py:139
  106.2 13.9 %shard_map.68 = (f32[1,1024]{1,0:T(1,128)}, f32[1,1024]{1,0:T(1,128)}, f32[1,1024]{1,0:T(1,128)}, f32[1,1024]{1,0:T(1,128)}) custom-call(bf16[1024,1600]{1,0:T(8,128)(2,1)} %slice_dynamic-update-slice_fusion.3.rows_ref, bf16[2048,1600]{1,0:T(8,128)(2,1)} %all-gather.2.cloned.1.call-done.vocab_ref, s32[1,1024]{1,0:T(1,128)} %bitcast.18, s32[2048,1]{1,0:T(8,128)} %fusion.13.ids_ref), custom_call_target="tpu_custom_call" | custom-call | flops 6710886400 | bytes 9830400 | tf_op jit(solution)/shard_map/pallas_call | solution.py:72
  120.1 0.7 maximum_bitcast_fusion
  120.9 12.9 %all_to_all.6 = f32[4,8,128]{2,0,1:T(4,128)S(1)} all-to-all(f32[4,8,128]{2,0,1:T(4,128)S(1)} %fusion.31), channel_id=1, replica_groups=mesh['z'=8,'x'=4,'c'=2,'y'=8] {'y'}, dimensions={1} | all-to-all | bytes 32768 | tf_op jit(solution)/shard_map/all_to_all | solution.py:149
  133.8 0.5 subtract_multiply_fusion
  (27 shorter events, 0.3 us)
Async XLA Ops:
  7.2 36.6 %copy-start = (bf16[32,1600]{1,0:T(8,128)(2,1)S(1)}, bf16[32,1600]{1,0:T(8,128)(2,1)}, u32[]{:S(2)}) copy-start(bf16[32,1600]{1,0:T(8,128)(2,1)} %param.11) | copy-start | bytes 307204
  7.2 99.0 %all-gather.2.cloned.1.call-start = ((), (), s32[]{:S(2)}) async-start(), calls=%async_computation.1 | async-start | bytes 7241728 | tf_op jit(solution)/shard_map/all_gather | solution.py:139
  13.3 17.0 %collective-permute-start = (bf16[128,1616]{1,0:T(8,128)(2,1)S(1)}, bf16[128,1616]{1,0:T(8,128)(2,1)S(1)}, u32[]{:S(2)}, u32[]{:S(2)}) collective-permute-start(bf16[128,1616]{1,0:T(8,128)(2,1)S(1)} %pad_maximum_fusion), channel_id=1, source_target_pairs={{0,1},{1,2},{2,3},{3,4},{4,5},{5,6},{6,7},{7,0},{8,9},{9,10},{10,1... | collective-permute-start | bytes 1241096 | tf_op jit(solution)/shard_map/ppermute | solution.py:22
  17.4 12.9 %collective-permute-start.1 = (bf16[128,1616]{1,0:T(8,128)(2,1)S(1)}, bf16[128,1616]{1,0:T(8,128)(2,1)S(1)}, u32[]{:S(2)}, u32[]{:S(2)}) collective-permute-start(bf16[128,1616]{1,0:T(8,128)(2,1)S(1)} %pad_maximum_fusion), channel_id=1, source_target_pairs={{0,7},{1,0},{2,1},{3,2},{4,3},{5,4},{6,5},{7,6},{8,15},{9,8},{10,9... | collective-permute-start | bytes 1241096 | tf_op jit(solution)/shard_map/ppermute | solution.py:22
  21.2 7.2 %collective-permute-start.2 = (bf16[32,1600]{1,0:T(8,128)(2,1)}, bf16[32,1600]{1,0:T(8,128)(2,1)S(1)}, u32[]{:S(2)}, u32[]{:S(2)}) collective-permute-start(bf16[32,1600]{1,0:T(8,128)(2,1)} %param.11), channel_id=1, source_target_pairs={{0,16},{16,32},{32,48},{48,0},{1,17},{17,33},{33,49},{49,1},{2,18}... | collective-permute-start | bytes 307208 | tf_op jit(solution)/shard_map/ppermute | solution.py:22
  24.3 6.0 %collective-permute-start.3 = (bf16[32,1600]{1,0:T(8,128)(2,1)}, bf16[32,1600]{1,0:T(8,128)(2,1)S(1)}, u32[]{:S(2)}, u32[]{:S(2)}) collective-permute-start(bf16[32,1600]{1,0:T(8,128)(2,1)} %param.11), channel_id=1, source_target_pairs={{0,48},{16,0},{32,16},{48,32},{1,49},{17,1},{33,17},{49,33},{2,50}... | collective-permute-start | bytes 307208 | tf_op jit(solution)/shard_map/ppermute | solution.py:22
  30.3 13.5 %collective-permute-start.4 = (bf16[128,1616]{1,0:T(8,128)(2,1)S(1)}, bf16[128,1616]{1,0:T(8,128)(2,1)S(1)}, u32[]{:S(2)}, u32[]{:S(2)}) collective-permute-start(bf16[128,1616]{1,0:T(8,128)(2,1)S(1)} %collective-permute-done), channel_id=1, source_target_pairs={{0,1},{1,2},{2,3},{3,4},{4,5},{5,6},{6,7},{7,0},{8,9},{9,10},{10,1... | collective-permute-start | bytes 1241096 | tf_op jit(solution)/shard_map/ppermute | solution.py:22
  32.8 10.9 %collective-permute-start.5 = (bf16[128,1616]{1,0:T(8,128)(2,1)S(1)}, bf16[128,1616]{1,0:T(8,128)(2,1)S(1)}, u32[]{:S(2)}, u32[]{:S(2)}) collective-permute-start(bf16[128,1616]{1,0:T(8,128)(2,1)S(1)} %collective-permute-done.1), channel_id=1, source_target_pairs={{0,7},{1,0},{2,1},{3,2},{4,3},{5,4},{6,5},{7,6},{8,15},{9,8},{10,9... | collective-permute-start | bytes 1241096 | tf_op jit(solution)/shard_map/ppermute | solution.py:22
  36.8 7.0 %collective-permute-start.6 = (bf16[32,1600]{1,0:T(8,128)(2,1)S(1)}, bf16[32,1600]{1,0:T(8,128)(2,1)S(1)}, u32[]{:S(2)}, u32[]{:S(2)}) collective-permute-start(bf16[32,1600]{1,0:T(8,128)(2,1)S(1)} %collective-permute-done.2), channel_id=1, source_target_pairs={{0,16},{16,32},{32,48},{48,0},{1,17},{17,33},{33,49},{49,1},{2,18}... | collective-permute-start | bytes 307208 | tf_op jit(solution)/shard_map/ppermute | solution.py:22
  44.6 1.8 %copy-start.1 = (bf16[1024,1600]{1,0:T(8,128)(2,1)}, bf16[1024,1600]{1,0:T(8,128)(2,1)S(1)}, u32[]{:S(2)}) copy-start(bf16[1024,1600]{1,0:T(8,128)(2,1)S(1)} %get-tuple-element.65) | copy-start | bytes 9830404
  48.5 17.0 %collective-permute-start.7 = (bf16[128,1616]{1,0:T(8,128)(2,1)S(1)}, bf16[128,1616]{1,0:T(8,128)(2,1)S(1)}, u32[]{:S(2)}, u32[]{:S(2)}) collective-permute-start(bf16[128,1616]{1,0:T(8,128)(2,1)S(1)} %collective-permute-done.5), channel_id=1, source_target_pairs={{0,7},{1,0},{2,1},{3,2},{4,3},{5,4},{6,5},{7,6},{8,15},{9,8},{10,9... | collective-permute-start | bytes 1241096 | tf_op jit(solution)/shard_map/ppermute | solution.py:22
  51.6 10.1 %collective-permute-start.8 = (bf16[128,1616]{1,0:T(8,128)(2,1)S(1)}, bf16[128,1616]{1,0:T(8,128)(2,1)S(1)}, u32[]{:S(2)}, u32[]{:S(2)}) collective-permute-start(bf16[128,1616]{1,0:T(8,128)(2,1)S(1)} %collective-permute-done.4), channel_id=1, source_target_pairs={{0,1},{1,2},{2,3},{3,4},{4,5},{5,6},{6,7},{7,0},{8,9},{9,10},{10,1... | collective-permute-start | bytes 1241096 | tf_op jit(solution)/shard_map/ppermute | solution.py:22
  61.7 13.8 %collective-permute-start.9 = (bf16[128,1616]{1,0:T(8,128)(2,1)S(1)}, bf16[128,1616]{1,0:T(8,128)(2,1)S(1)}, u32[]{:S(2)}, u32[]{:S(2)}) collective-permute-start(bf16[128,1616]{1,0:T(8,128)(2,1)S(1)} %collective-permute-done.8), channel_id=1, source_target_pairs={{0,1},{1,2},{2,3},{3,4},{4,5},{5,6},{6,7},{7,0},{8,9},{9,10},{10,1... | collective-permute-start | bytes 1241096 | tf_op jit(solution)/shard_map/ppermute | solution.py:22
  75.7 30.5 %copy-start.3 = (s32[1024]{0:T(1024)}, s32[1024]{0:T(1024)S(1)}, u32[]{:S(2)}) copy-start(s32[1024]{0:T(1024)S(1)} %constant_dynamic-update-slice_fusion.1) | copy-start | bytes 12292
  106.2 27.6 %copy-start.2 = (s32[128]{0:T(128)S(1)}, s32[128]{0:T(128)}, u32[]{:S(2)}) copy-start(s32[128]{0:T(128)} %param.13) | copy-start | bytes 1540
Sparse Core Ops, SparseCore 0:
  46.5 59.6 all-gather.1

commit v8 on v7

--- a/solution.py
+++ b/solution.py
@@ -124,7 +124,7 @@
                     fronts[name][sign] = shift(fronts[name][sign], name, size, sign)
                     got[name][(-sign * step) % size] = fronts[name][sign]
                     moved.append((name, sign))
-        if step <= nx // 2:
+        if step == 1:
             values = lax.optimization_barrier(tuple(fronts[n][s] for n, s in moved))
             for (n, s), v in zip(moved, values):
                 fronts[n][s] = v

time: 142 us -> 133 us (0.937)
  waiting for transfers between devices: 47.2 us -> 38.7 us
  starting transfers between devices: 35.7 us -> 33.3 us
    all_gather x1, waiting for transfers between devices: 27.2 us -> 12.6 us  [on_device(): lax.all_gather(jnp.concatenate(near, axis=0), ('z', 'c'), axis=0, tiled=T...]
    ppermute x10, waiting for transfers between devices: 19.9 us -> 26 us  [shift(): lax.ppermute(value, axis, [(i, (i + step) % size) for i in range(size)])]
    ppermute x10, starting transfers between devices: 35.6 us -> 33.2 us  [shift(): lax.ppermute(value, axis, [(i, (i + step) % size) for i in range(size)])]
    unnamed x22 -> x19, local copies, waits for them, and re-layouts: 6.45 us -> 7 us
  transfers between devices with their start and end apart: 11 -> 11, of which waited for: 6 -> 7; matrix products, arithmetic and copies ran while one was open for 5% -> 7% of each run, Pallas kernels for 0% -> 0%
where the time goes in v8:
time: 133 us; the launch traced here: 132 us
  waiting for transfers between devices  38.7 us (29%)
  starting transfers between devices  33.3 us (25%)
  between operations  14.3 us (11%)
  Pallas kernels  13.9 us (10%)
  blocking collectives  12.9 us (10%)
  other arithmetic  10.6 us (8%)
  local copies, waits for them, and re-layouts  8.27 us (6%)
    ppermute x10, starting transfers between devices, shift(): lax.ppermute(value, axis, [(i, (i + step) % size) for i in range(size)])  33.2 us
    ppermute x10, waiting for transfers between devices, shift(): lax.ppermute(value, axis, [(i, (i + step) % size) for i in range(size)])  26 us
    pallas_call x1, Pallas kernels, row_stats(): pl.pallas_call(stats_kernel, grid=(width // tile,), in_specs=[pl.BlockSpe...  13.9 us
    all_to_all x1, blocking collectives, on_device(): got = lax.all_to_all(packed, 'y', 1, 1, tiled=True).reshape(4, ny, mine)  12.9 us
    all_gather x1, waiting for transfers between devices, on_device(): lax.all_gather(jnp.concatenate(near, axis=0), ('z', 'c'), axis=0, tiled=T...  12.6 us
    unnamed x19, local copies, waits for them, and re-layouts  7 us
    another operation x3, other arithmetic  3.25 us
  transfers between devices with their start and end apart: 11, of which 7 were waited for; matrix products, arithmetic and copies ran while one was open for 7% of the time, Pallas kernels for 0%

profile of v8, /device:TPU:1, one launch (start us, length us, event | category | flops | bytes accessed | tf_op | source)
XLA Modules:
  0.0 131.8 jit_solution(15859725385434971190)
XLA Ops:
  7.2 0.6 compare_reduce_fusion
  7.8 0.6 compare_reduce_fusion.1
  8.5 1.2 copy.13
  9.7 0.2 fusion.28
  9.9 2.0 %fusion.33 = (bf16[128,1]{0,1:T(2,128)(2,1)S(1)}, bf16[128,1]{0,1:T(2,128)(2,1)S(1)}) fusion(pred[]{:T(512)} %compare_reduce_fusion, s32[128]{0:T(128)} %param.12, pred[]{:T(512)} %compare_reduce_fusion.1), kind=kLoop, calls=%fused_computation.93 | loop fusion | flops 2944 | bytes 1026 | tf_op jit(solution)/shard_map/reshape.177
  11.9 0.1 copy.14
  12.0 0.1 copy.15
  12.2 0.9 fusion.30
  13.0 0.2 scatter.9
  13.2 0.1 pad_maximum_fusion
  13.3 4.0 %collective-permute-start = (bf16[128,1616]{1,0:T(8,128)(2,1)S(1)}, bf16[128,1616]{1,0:T(8,128)(2,1)S(1)}, u32[]{:S(2)}, u32[]{:S(2)}) collective-permute-start(bf16[128,1616]{1,0:T(8,128)(2,1)S(1)} %pad_maximum_fusion), channel_id=1, source_target_pairs={{0,1},{1,2},{2,3},{3,4},{4,5},{5,6},{6,7},{7,0},{8,9},{9,10},{10,1... | collective-permute-start | bytes 1241096 | tf_op jit(solution)/shard_map/ppermute | solution.py:22
  17.4 3.8 %collective-permute-start.1 = (bf16[128,1616]{1,0:T(8,128)(2,1)S(1)}, bf16[128,1616]{1,0:T(8,128)(2,1)S(1)}, u32[]{:S(2)}, u32[]{:S(2)}) collective-permute-start(bf16[128,1616]{1,0:T(8,128)(2,1)S(1)} %pad_maximum_fusion), channel_id=1, source_target_pairs={{0,7},{1,0},{2,1},{3,2},{4,3},{5,4},{6,5},{7,6},{8,15},{9,8},{10,9... | collective-permute-start | bytes 1241096 | tf_op jit(solution)/shard_map/ppermute | solution.py:22
  21.2 3.1 %collective-permute-start.2 = (bf16[32,1600]{1,0:T(8,128)(2,1)}, bf16[32,1600]{1,0:T(8,128)(2,1)S(1)}, u32[]{:S(2)}, u32[]{:S(2)}) collective-permute-start(bf16[32,1600]{1,0:T(8,128)(2,1)} %param.11), channel_id=1, source_target_pairs={{0,16},{16,32},{32,48},{48,0},{1,17},{17,33},{33,49},{49,1},{2,18}... | collective-permute-start | bytes 307208 | tf_op jit(solution)/shard_map/ppermute | solution.py:22
  24.3 3.4 %collective-permute-start.3 = (bf16[32,1600]{1,0:T(8,128)(2,1)}, bf16[32,1600]{1,0:T(8,128)(2,1)S(1)}, u32[]{:S(2)}, u32[]{:S(2)}) collective-permute-start(bf16[32,1600]{1,0:T(8,128)(2,1)} %param.11), channel_id=1, source_target_pairs={{0,48},{16,0},{32,16},{48,32},{1,49},{17,1},{33,17},{49,33},{2,50}... | collective-permute-start | bytes 307208 | tf_op jit(solution)/shard_map/ppermute | solution.py:22
  27.7 0.7 collective-permute-done.2
  28.3 1.9 %collective-permute-done.3 = bf16[32,1600]{1,0:T(8,128)(2,1)S(1)} collective-permute-done((bf16[32,1600]{1,0:T(8,128)(2,1)}, bf16[32,1600]{1,0:T(8,128)(2,1)S(1)}, u32[]{:S(2)}, u32[]{:S(2)}) %collective-permute-start.3) | collective-permute-done | bytes 102432 | tf_op jit(solution)/shard_map/ppermute | solution.py:22
  30.3 3.1 %collective-permute-start.9 = (bf16[32,1600]{1,0:T(8,128)(2,1)S(1)}, bf16[32,1600]{1,0:T(8,128)(2,1)S(1)}, u32[]{:S(2)}, u32[]{:S(2)}) collective-permute-start(bf16[32,1600]{1,0:T(8,128)(2,1)S(1)} %collective-permute-done.2), channel_id=1, source_target_pairs={{0,16},{16,32},{32,48},{48,0},{1,17},{17,33},{33,49},{49,1},{2,18}... | collective-permute-start | bytes 307208 | tf_op jit(solution)/shard_map/ppermute | solution.py:22
  33.4 3.5 %collective-permute-done.9 = bf16[32,1600]{1,0:T(8,128)(2,1)S(1)} collective-permute-done((bf16[32,1600]{1,0:T(8,128)(2,1)S(1)}, bf16[32,1600]{1,0:T(8,128)(2,1)S(1)}, u32[]{:S(2)}, u32[]{:S(2)}) %collective-permute-start.9) | collective-permute-done | bytes 102432 | tf_op jit(solution)/shard_map/ppermute | solution.py:22
  36.9 1.7 %pad_maximum_fusion.1 = bf16[128,1600]{1,0:T(8,128)(2,1)} fusion(bf16[32,1600]{1,0:T(8,128)(2,1)S(1)} %collective-permute-done.2, bf16[32,1600]{1,0:T(8,128)(2,1)S(1)} %collective-permute-done.9, bf16[32,1600]{1,0:T(8,128)(2,1)S(1)} %collective-permute-done.3, bf16[32,1600]{1,0:T(8,128)(2,1)} %param.11), kind=kLoop, calls=%fused_computation.56 | loop fusion | flops 1638400 | bytes 819200 | tf_op jit(solution)/shard_map/concatenate | solution.py:139
  38.7 0.2 add_reduce_fusion.7
  38.8 0.8 slice_dynamic-update-slice_fusion.7
  39.7 1.9 %fusion.13.ids_ref = s32[2048,1]{1,0:T(8,128)} fusion(s32[]{:T(128)S(6)} %axis_index.25, s32[]{:T(128)S(6)} %axis_index.23), kind=kLoop, calls=%fused_computation.32 | loop fusion | flops 143360 | bytes 8200 | tf_op jit(solution)/shard_map/add | solution.py:144
  41.6 4.5 %collective-permute-start.4 = (bf16[128,1616]{1,0:T(8,128)(2,1)S(1)}, bf16[128,1616]{1,0:T(8,128)(2,1)S(1)}, u32[]{:S(2)}, u32[]{:S(2)}) collective-permute-start(bf16[128,1616]{1,0:T(8,128)(2,1)S(1)} %collective-permute-done.1), channel_id=1, source_target_pairs={{0,7},{1,0},{2,1},{3,2},{4,3},{5,4},{6,5},{7,6},{8,15},{9,8},{10,9... | collective-permute-start | bytes 1241096 | tf_op jit(solution)/shard_map/ppermute | solution.py:22
  46.1 1.9 %collective-permute-start.6 = (bf16[128,1616]{1,0:T(8,128)(2,1)S(1)}, bf16[128,1616]{1,0:T(8,128)(2,1)S(1)}, u32[]{:S(2)}, u32[]{:S(2)}) collective-permute-start(bf16[128,1616]{1,0:T(8,128)(2,1)S(1)} %collective-permute-done), channel_id=1, source_target_pairs={{0,1},{1,2},{2,3},{3,4},{4,5},{5,6},{6,7},{7,0},{8,9},{9,10},{10,1... | collective-permute-start | bytes 1241096 | tf_op jit(solution)/shard_map/ppermute | solution.py:22
  48.0 0.2 add_reduce_fusion
  48.2 0.8 slice_dynamic-update-slice_fusion.6
  49.0 2.1 %collective-permute-done.4 = bf16[128,1616]{1,0:T(8,128)(2,1)S(1)} collective-permute-done((bf16[128,1616]{1,0:T(8,128)(2,1)S(1)}, bf16[128,1616]{1,0:T(8,128)(2,1)S(1)}, u32[]{:S(2)}, u32[]{:S(2)}) %collective-permute-start.4) | collective-permute-done | bytes 413728 | tf_op jit(solution)/shard_map/ppermute | solution.py:22
  51.1 5.0 %collective-permute-start.5 = (bf16[128,1616]{1,0:T(8,128)(2,1)S(1)}, bf16[128,1616]{1,0:T(8,128)(2,1)S(1)}, u32[]{:S(2)}, u32[]{:S(2)}) collective-permute-start(bf16[128,1616]{1,0:T(8,128)(2,1)S(1)} %collective-permute-done.4), channel_id=1, source_target_pairs={{0,7},{1,0},{2,1},{3,2},{4,3},{5,4},{6,5},{7,6},{8,15},{9,8},{10,9... | collective-permute-start | bytes 1241096 | tf_op jit(solution)/shard_map/ppermute | solution.py:22
  56.1 1.9 %collective-permute-start.7 = (bf16[128,1616]{1,0:T(8,128)(2,1)S(1)}, bf16[128,1616]{1,0:T(8,128)(2,1)S(1)}, u32[]{:S(2)}, u32[]{:S(2)}) collective-permute-start(bf16[128,1616]{1,0:T(8,128)(2,1)S(1)} %collective-permute-done.6), channel_id=1, source_target_pairs={{0,1},{1,2},{2,3},{3,4},{4,5},{5,6},{6,7},{7,0},{8,9},{9,10},{10,1... | collective-permute-start | bytes 1241096 | tf_op jit(solution)/shard_map/ppermute | solution.py:22
  58.1 0.2 add_reduce_fusion.5
  58.3 0.2 add_reduce_fusion.1
  58.4 0.8 slice_dynamic-update-slice_fusion.4
  59.3 7.8 %collective-permute-done.7 = bf16[128,1616]{1,0:T(8,128)(2,1)S(1)} collective-permute-done((bf16[128,1616]{1,0:T(8,128)(2,1)S(1)}, bf16[128,1616]{1,0:T(8,128)(2,1)S(1)}, u32[]{:S(2)}, u32[]{:S(2)}) %collective-permute-start.7) | collective-permute-done | bytes 413728 | tf_op jit(solution)/shard_map/ppermute | solution.py:22
  67.1 2.4 %collective-permute-start.8 = (bf16[128,1616]{1,0:T(8,128)(2,1)S(1)}, bf16[128,1616]{1,0:T(8,128)(2,1)S(1)}, u32[]{:S(2)}, u32[]{:S(2)}) collective-permute-start(bf16[128,1616]{1,0:T(8,128)(2,1)S(1)} %collective-permute-done.7), channel_id=1, source_target_pairs={{0,1},{1,2},{2,3},{3,4},{4,5},{5,6},{6,7},{7,0},{8,9},{9,10},{10,1... | collective-permute-start | bytes 1241096 | tf_op jit(solution)/shard_map/ppermute | solution.py:22
  69.5 0.2 add_reduce_fusion.4
  69.7 0.2 add_reduce_fusion.2
  69.9 0.8 slice_dynamic-update-slice_fusion.3
  70.7 9.9 %collective-permute-done.8 = bf16[128,1616]{1,0:T(8,128)(2,1)S(1)} collective-permute-done((bf16[128,1616]{1,0:T(8,128)(2,1)S(1)}, bf16[128,1616]{1,0:T(8,128)(2,1)S(1)}, u32[]{:S(2)}, u32[]{:S(2)}) %collective-permute-start.8) | collective-permute-done | bytes 413728 | tf_op jit(solution)/shard_map/ppermute | solution.py:22
  80.7 0.2 add_reduce_fusion.3
  80.9 0.8 slice_dynamic-update-slice_fusion.2
  81.8 0.8 slice_dynamic-update-slice_fusion.1
  82.6 0.8 slice_dynamic-update-slice_fusion
  83.4 0.8 slice_dynamic-update-slice_fusion.5.rows_ref
  84.2 12.6 %all-gather.2.cloned.1.call-done.vocab_ref = bf16[2048,1600]{1,0:T(8,128)(2,1)} async-done(((bf16[128,1600]{1,0:T(8,128)(2,1)}), bf16[2048,1600]{1,0:T(8,128)(2,1)}) %all-gather.2.cloned.1.call-update) | async-done | bytes 6553616 | tf_op jit(solution)/shard_map/all_gather | solution.py:139
  96.8 13.9 %shard_map.68 = (f32[1,1024]{1,0:T(1,128)}, f32[1,1024]{1,0:T(1,128)}, f32[1,1024]{1,0:T(1,128)}, f32[1,1024]{1,0:T(1,128)}) custom-call(bf16[1024,1600]{1,0:T(8,128)(2,1)} %slice_dynamic-update-slice_fusion.5.rows_ref, bf16[2048,1600]{1,0:T(8,128)(2,1)} %all-gather.2.cloned.1.call-done.vocab_ref, s32[1,1024]{1,0:T(1,128)} %bitcast.18, s32[2048,1]{1,0:T(8,128)} %fusion.13.ids_ref), custom_call_target="tpu_custom_call" | custom-call | flops 6710886400 | bytes 9830400 | tf_op jit(solution)/shard_map/pallas_call | solution.py:72
  110.8 0.7 maximum_bitcast_fusion
  111.5 12.9 %all_to_all.6 = f32[4,8,128]{2,0,1:T(4,128)S(1)} all-to-all(f32[4,8,128]{2,0,1:T(4,128)S(1)} %fusion.31), channel_id=1, replica_groups=mesh['z'=8,'x'=4,'c'=2,'y'=8] {'y'}, dimensions={1} | all-to-all | bytes 32768 | tf_op jit(solution)/shard_map/all_to_all | solution.py:149
  124.5 0.5 subtract_multiply_fusion
  (25 shorter events, 0.3 us)
Async XLA Ops:
  7.2 89.7 %all-gather.2.cloned.1.call-start = ((), (), s32[]{:S(2)}) async-start(), calls=%async_computation.1 | async-start | bytes 7241728 | tf_op jit(solution)/shard_map/all_gather | solution.py:139
  13.3 17.0 %collective-permute-start = (bf16[128,1616]{1,0:T(8,128)(2,1)S(1)}, bf16[128,1616]{1,0:T(8,128)(2,1)S(1)}, u32[]{:S(2)}, u32[]{:S(2)}) collective-permute-start(bf16[128,1616]{1,0:T(8,128)(2,1)S(1)} %pad_maximum_fusion), channel_id=1, source_target_pairs={{0,1},{1,2},{2,3},{3,4},{4,5},{5,6},{6,7},{7,0},{8,9},{9,10},{10,1... | collective-permute-start | bytes 1241096 | tf_op jit(solution)/shard_map/ppermute | solution.py:22
  17.4 12.9 %collective-permute-start.1 = (bf16[128,1616]{1,0:T(8,128)(2,1)S(1)}, bf16[128,1616]{1,0:T(8,128)(2,1)S(1)}, u32[]{:S(2)}, u32[]{:S(2)}) collective-permute-start(bf16[128,1616]{1,0:T(8,128)(2,1)S(1)} %pad_maximum_fusion), channel_id=1, source_target_pairs={{0,7},{1,0},{2,1},{3,2},{4,3},{5,4},{6,5},{7,6},{8,15},{9,8},{10,9... | collective-permute-start | bytes 1241096 | tf_op jit(solution)/shard_map/ppermute | solution.py:22
  21.2 7.2 %collective-permute-start.2 = (bf16[32,1600]{1,0:T(8,128)(2,1)}, bf16[32,1600]{1,0:T(8,128)(2,1)S(1)}, u32[]{:S(2)}, u32[]{:S(2)}) collective-permute-start(bf16[32,1600]{1,0:T(8,128)(2,1)} %param.11), channel_id=1, source_target_pairs={{0,16},{16,32},{32,48},{48,0},{1,17},{17,33},{33,49},{49,1},{2,18}... | collective-permute-start | bytes 307208 | tf_op jit(solution)/shard_map/ppermute | solution.py:22
  24.3 6.0 %collective-permute-start.3 = (bf16[32,1600]{1,0:T(8,128)(2,1)}, bf16[32,1600]{1,0:T(8,128)(2,1)S(1)}, u32[]{:S(2)}, u32[]{:S(2)}) collective-permute-start(bf16[32,1600]{1,0:T(8,128)(2,1)} %param.11), channel_id=1, source_target_pairs={{0,48},{16,0},{32,16},{48,32},{1,49},{17,1},{33,17},{49,33},{2,50}... | collective-permute-start | bytes 307208 | tf_op jit(solution)/shard_map/ppermute | solution.py:22
  30.3 6.7 %collective-permute-start.9 = (bf16[32,1600]{1,0:T(8,128)(2,1)S(1)}, bf16[32,1600]{1,0:T(8,128)(2,1)S(1)}, u32[]{:S(2)}, u32[]{:S(2)}) collective-permute-start(bf16[32,1600]{1,0:T(8,128)(2,1)S(1)} %collective-permute-done.2), channel_id=1, source_target_pairs={{0,16},{16,32},{32,48},{48,0},{1,17},{17,33},{33,49},{49,1},{2,18}... | collective-permute-start | bytes 307208 | tf_op jit(solution)/shard_map/ppermute | solution.py:22
  41.6 9.5 %collective-permute-start.4 = (bf16[128,1616]{1,0:T(8,128)(2,1)S(1)}, bf16[128,1616]{1,0:T(8,128)(2,1)S(1)}, u32[]{:S(2)}, u32[]{:S(2)}) collective-permute-start(bf16[128,1616]{1,0:T(8,128)(2,1)S(1)} %collective-permute-done.1), channel_id=1, source_target_pairs={{0,7},{1,0},{2,1},{3,2},{4,3},{5,4},{6,5},{7,6},{8,15},{9,8},{10,9... | collective-permute-start | bytes 1241096 | tf_op jit(solution)/shard_map/ppermute | solution.py:22
  46.1 10.1 %collective-permute-start.6 = (bf16[128,1616]{1,0:T(8,128)(2,1)S(1)}, bf16[128,1616]{1,0:T(8,128)(2,1)S(1)}, u32[]{:S(2)}, u32[]{:S(2)}) collective-permute-start(bf16[128,1616]{1,0:T(8,128)(2,1)S(1)} %collective-permute-done), channel_id=1, source_target_pairs={{0,1},{1,2},{2,3},{3,4},{4,5},{5,6},{6,7},{7,0},{8,9},{9,10},{10,1... | collective-permute-start | bytes 1241096 | tf_op jit(solution)/shard_map/ppermute | solution.py:22
  51.1 18.4 %collective-permute-start.5 = (bf16[128,1616]{1,0:T(8,128)(2,1)S(1)}, bf16[128,1616]{1,0:T(8,128)(2,1)S(1)}, u32[]{:S(2)}, u32[]{:S(2)}) collective-permute-start(bf16[128,1616]{1,0:T(8,128)(2,1)S(1)} %collective-permute-done.4), channel_id=1, source_target_pairs={{0,7},{1,0},{2,1},{3,2},{4,3},{5,4},{6,5},{7,6},{8,15},{9,8},{10,9... | collective-permute-start | bytes 1241096 | tf_op jit(solution)/shard_map/ppermute | solution.py:22
  56.1 10.9 %collective-permute-start.7 = (bf16[128,1616]{1,0:T(8,128)(2,1)S(1)}, bf16[128,1616]{1,0:T(8,128)(2,1)S(1)}, u32[]{:S(2)}, u32[]{:S(2)}) collective-permute-start(bf16[128,1616]{1,0:T(8,128)(2,1)S(1)} %collective-permute-done.6), channel_id=1, source_target_pairs={{0,1},{1,2},{2,3},{3,4},{4,5},{5,6},{6,7},{7,0},{8,9},{9,10},{10,1... | collective-permute-start | bytes 1241096 | tf_op jit(solution)/shard_map/ppermute | solution.py:22
  67.1 13.6 %collective-permute-start.8 = (bf16[128,1616]{1,0:T(8,128)(2,1)S(1)}, bf16[128,1616]{1,0:T(8,128)(2,1)S(1)}, u32[]{:S(2)}, u32[]{:S(2)}) collective-permute-start(bf16[128,1616]{1,0:T(8,128)(2,1)S(1)} %collective-permute-done.7), channel_id=1, source_target_pairs={{0,1},{1,2},{2,3},{3,4},{4,5},{5,6},{6,7},{7,0},{8,9},{9,10},{10,1... | collective-permute-start | bytes 1241096 | tf_op jit(solution)/shard_map/ppermute | solution.py:22
  80.9 15.9 %copy-start.1 = (s32[1024]{0:T(1024)}, s32[1024]{0:T(1024)S(1)}, u32[]{:S(2)}) copy-start(s32[1024]{0:T(1024)S(1)} %constant_dynamic-update-slice_fusion.1) | copy-start | bytes 12292
  96.8 27.6 %copy-start = (s32[128]{0:T(128)S(1)}, s32[128]{0:T(128)}, u32[]{:S(2)}) copy-start(s32[128]{0:T(128)} %param.13) | copy-start | bytes 1540
Sparse Core Ops, SparseCore 0:
  38.7 58.0 all-gather.1

commit v9 on v5

--- a/solution.py
+++ b/solution.py
@@ -108,25 +108,39 @@
     code = code.at[:, 1].set((targets % 128).astype(jnp.bfloat16))
     block = jnp.concatenate([normed, code], axis=1)
 
+    nx = lax.axis_size("x")
+    x = lax.axis_index("x")
+    near = [None] * nx
+    near[0] = unembed
+    fronts = {1: shift(unembed, "x", nx, 1), -1: shift(unembed, "x", nx, -1)}
+    block, fronts[1], fronts[-1] = lax.optimization_barrier((block, fronts[1], fronts[-1]))
+    for sign in (1, -1):
+        cur = fronts[sign]
+        reach = nx // 2 if sign == 1 else nx - 1 - nx // 2
+        for step in range(1, reach + 1):
+            if step > 1:
+                cur = shift(cur, "x", nx, sign)
+            near[(-sign * step) % nx] = cur
+
     blocks = [None] * ny
     blocks[0] = block
-    fwd = ny // 2
-    cur = block
-    for d in range(1, fwd + 1):
-        cur = shift(cur, "y", ny, 1)
-        blocks[ny - d] = cur
-    cur = block
-    for d in range(1, ny - fwd):
-        cur = shift(cur, "y", ny, -1)
-        blocks[d] = cur
+    for sign in (1, -1):
+        cur = block
+        reach = ny // 2 if sign == 1 else ny - 1 - ny // 2
+        for step in range(1, reach + 1):
+            cur = shift(cur, "y", ny, sign)
+            blocks[(-sign * step) % ny] = cur
     rows = jnp.concatenate([b[:, :dim] for b in blocks], axis=0)
     wanted = jnp.concatenate(
         [b[:, dim].astype(jnp.int32) * 128 + b[:, dim + 1].astype(jnp.int32) for b in blocks], axis=0
     )
 
-    whole = lax.all_gather(unembed, ("z", "x", "c"), axis=0, tiled=True)
+    whole = lax.all_gather(jnp.concatenate(near, axis=0), ("z", "c"), axis=0, tiled=True)
     local = jnp.arange(whole.shape[0], dtype=jnp.int32)
-    ids = ((local // width) * ny + y) * width + local % width
+    group, place = local // (nx * width), local % (nx * width)
+    far_z, far_c = group // nc, group % nc
+    far_x = (x + place // width) % nx
+    ids = (((far_z * nx + far_x) * nc + far_c) * ny + y) * width + place % width
 
     stats = row_stats(rows, whole, wanted, ids)
 

time: 140 us -> 124 us (0.89)
  the two profiles are of different devices: /device:TPU:1 before, /device:TPU:8 now
where the time goes in v9:
time: 124 us; the launch traced here: 123 us
  starting transfers between devices  33.4 us (27%)
  waiting for transfers between devices  32.9 us (27%)
  between operations  14.3 us (12%)
  Pallas kernels  13.9 us (11%)
  other arithmetic  10.8 us (9%)
  blocking collectives  9.87 us (8%)
  local copies, waits for them, and re-layouts  8.27 us (7%)
    ppermute x10, starting transfers between devices, shift(): lax.ppermute(value, axis, [(i, (i + step) % size) for i in range(size)])  33.4 us
    ppermute x10, waiting for transfers between devices, shift(): lax.ppermute(value, axis, [(i, (i + step) % size) for i in range(size)])  32.9 us
    pallas_call x1, Pallas kernels, row_stats(): pl.pallas_call(stats_kernel, grid=(width // tile,), in_specs=[pl.BlockSpe...  13.9 us
    all_to_all x1, blocking collectives, on_device(): got = lax.all_to_all(packed, 'y', 1, 1, tiled=True).reshape(4, ny, mine)  9.87 us
    unnamed x19, local copies, waits for them, and re-layouts  7 us
    another operation x3, other arithmetic  3.25 us
  transfers between devices with their start and end apart: 11, of which 5 were waited for; matrix products, arithmetic and copies ran while one was open for 13% of the time, Pallas kernels for 0%

profile of v9, /device:TPU:8, one launch (start us, length us, event | category | flops | bytes accessed | tf_op | source)
XLA Modules:
  0.0 123.5 jit_solution(16690217511147774331)
XLA Ops:
  7.2 0.0 all-gather.2.cloned.1.call-start
  7.2 3.4 %collective-permute-start = (bf16[32,1600]{1,0:T(8,128)(2,1)}, bf16[32,1600]{1,0:T(8,128)(2,1)S(1)}, u32[]{:S(2)}, u32[]{:S(2)}) collective-permute-start(bf16[32,1600]{1,0:T(8,128)(2,1)} %param.11), channel_id=1, source_target_pairs={{0,16},{16,32},{32,48},{48,0},{1,17},{17,33},{33,49},{49,1},{2,18}... | collective-permute-start | bytes 307208 | tf_op jit(solution)/shard_map/ppermute | solution.py:22
  10.6 3.7 %collective-permute-start.1 = (bf16[32,1600]{1,0:T(8,128)(2,1)}, bf16[32,1600]{1,0:T(8,128)(2,1)S(1)}, u32[]{:S(2)}, u32[]{:S(2)}) collective-permute-start(bf16[32,1600]{1,0:T(8,128)(2,1)} %param.11), channel_id=1, source_target_pairs={{0,48},{16,0},{32,16},{48,32},{1,49},{17,1},{33,17},{49,33},{2,50}... | collective-permute-start | bytes 307208 | tf_op jit(solution)/shard_map/ppermute | solution.py:22
  14.3 0.6 compare_reduce_fusion
  14.9 0.6 compare_reduce_fusion.1
  15.6 1.2 %copy.13 = bf16[128,1600]{1,0:T(8,128)(2,1)S(1)} copy(bf16[128,1600]{0,1:T(8,128)(2,1)} %param.9) | data formatting | bytes 819200 | tf_op args[0]
  16.8 0.2 fusion.28
  17.0 2.0 %fusion.33 = (bf16[128,1]{0,1:T(2,128)(2,1)S(1)}, bf16[128,1]{0,1:T(2,128)(2,1)S(1)}) fusion(pred[]{:T(512)} %compare_reduce_fusion, s32[128]{0:T(128)} %param.12, pred[]{:T(512)} %compare_reduce_fusion.1), kind=kLoop, calls=%fused_computation.93 | loop fusion | flops 2944 | bytes 1026 | tf_op jit(solution)/shard_map/reshape.177
  19.0 0.1 copy.14
  19.1 0.1 copy.15
  19.2 0.9 fusion.30
  20.1 0.2 scatter.9
  20.3 0.1 pad_maximum_fusion
  20.4 2.2 %collective-permute-start.9 = (bf16[32,1600]{1,0:T(8,128)(2,1)S(1)}, bf16[32,1600]{1,0:T(8,128)(2,1)S(1)}, u32[]{:S(2)}, u32[]{:S(2)}) collective-permute-start(bf16[32,1600]{1,0:T(8,128)(2,1)S(1)} %collective-permute-done), channel_id=1, source_target_pairs={{0,16},{16,32},{32,48},{48,0},{1,17},{17,33},{33,49},{49,1},{2,18}... | collective-permute-start | bytes 307208 | tf_op jit(solution)/shard_map/ppermute | solution.py:22
  22.6 5.6 %collective-permute-done.9 = bf16[32,1600]{1,0:T(8,128)(2,1)S(1)} collective-permute-done((bf16[32,1600]{1,0:T(8,128)(2,1)S(1)}, bf16[32,1600]{1,0:T(8,128)(2,1)S(1)}, u32[]{:S(2)}, u32[]{:S(2)}) %collective-permute-start.9) | collective-permute-done | bytes 102432 | tf_op jit(solution)/shard_map/ppermute | solution.py:22
  28.2 1.7 %pad_maximum_fusion.1 = bf16[128,1600]{1,0:T(8,128)(2,1)} fusion(bf16[32,1600]{1,0:T(8,128)(2,1)S(1)} %collective-permute-done, bf16[32,1600]{1,0:T(8,128)(2,1)S(1)} %collective-permute-done.9, bf16[32,1600]{1,0:T(8,128)(2,1)S(1)} %collective-permute-done.1, bf16[32,1600]{1,0:T(8,128)(2,1)} %param.11), kind=kLoop, calls=%fused_computation.58 | loop fusion | flops 1638400 | bytes 819200 | tf_op jit(solution)/shard_map/concatenate | solution.py:138
  30.0 1.9 %fusion.13.ids_ref = s32[2048,1]{1,0:T(8,128)} fusion(s32[]{:T(128)S(6)} %axis_index.25, s32[]{:T(128)S(6)} %axis_index.23), kind=kLoop, calls=%fused_computation.32 | loop fusion | flops 143360 | bytes 8200 | tf_op jit(solution)/shard_map/add | solution.py:143
  31.9 7.7 %collective-permute-start.2 = (bf16[128,1616]{1,0:T(8,128)(2,1)S(1)}, bf16[128,1616]{1,0:T(8,128)(2,1)S(1)}, u32[]{:S(2)}, u32[]{:S(2)}) collective-permute-start(bf16[128,1616]{1,0:T(8,128)(2,1)S(1)} %pad_maximum_fusion), channel_id=1, source_target_pairs={{0,7},{1,0},{2,1},{3,2},{4,3},{5,4},{6,5},{7,6},{8,15},{9,8},{10,9... | collective-permute-start | bytes 1241096 | tf_op jit(solution)/shard_map/ppermute | solution.py:22
  39.6 1.9 %collective-permute-start.5 = (bf16[128,1616]{1,0:T(8,128)(2,1)S(1)}, bf16[128,1616]{1,0:T(8,128)(2,1)S(1)}, u32[]{:S(2)}, u32[]{:S(2)}) collective-permute-start(bf16[128,1616]{1,0:T(8,128)(2,1)S(1)} %pad_maximum_fusion), channel_id=1, source_target_pairs={{0,1},{1,2},{2,3},{3,4},{4,5},{5,6},{6,7},{7,0},{8,9},{9,10},{10,1... | collective-permute-start | bytes 1241096 | tf_op jit(solution)/shard_map/ppermute | solution.py:22
  41.5 0.2 add_reduce_fusion.7
  41.7 0.8 slice_dynamic-update-slice_fusion.7
  42.5 4.8 %collective-permute-done.2 = bf16[128,1616]{1,0:T(8,128)(2,1)S(1)} collective-permute-done((bf16[128,1616]{1,0:T(8,128)(2,1)S(1)}, bf16[128,1616]{1,0:T(8,128)(2,1)S(1)}, u32[]{:S(2)}, u32[]{:S(2)}) %collective-permute-start.2) | collective-permute-done | bytes 413728 | tf_op jit(solution)/shard_map/ppermute | solution.py:22
  47.3 4.4 %collective-permute-start.3 = (bf16[128,1616]{1,0:T(8,128)(2,1)S(1)}, bf16[128,1616]{1,0:T(8,128)(2,1)S(1)}, u32[]{:S(2)}, u32[]{:S(2)}) collective-permute-start(bf16[128,1616]{1,0:T(8,128)(2,1)S(1)} %collective-permute-done.2), channel_id=1, source_target_pairs={{0,7},{1,0},{2,1},{3,2},{4,3},{5,4},{6,5},{7,6},{8,15},{9,8},{10,9... | collective-permute-start | bytes 1241096 | tf_op jit(solution)/shard_map/ppermute | solution.py:22
  51.7 1.9 %collective-permute-start.6 = (bf16[128,1616]{1,0:T(8,128)(2,1)S(1)}, bf16[128,1616]{1,0:T(8,128)(2,1)S(1)}, u32[]{:S(2)}, u32[]{:S(2)}) collective-permute-start(bf16[128,1616]{1,0:T(8,128)(2,1)S(1)} %collective-permute-done.5), channel_id=1, source_target_pairs={{0,1},{1,2},{2,3},{3,4},{4,5},{5,6},{6,7},{7,0},{8,9},{9,10},{10,1... | collective-permute-start | bytes 1241096 | tf_op jit(solution)/shard_map/ppermute | solution.py:22
  53.6 0.2 add_reduce_fusion.6
  53.8 0.2 add_reduce_fusion
  54.0 0.8 slice_dynamic-update-slice_fusion.6
  54.8 5.2 %collective-permute-done.3 = bf16[128,1616]{1,0:T(8,128)(2,1)S(1)} collective-permute-done((bf16[128,1616]{1,0:T(8,128)(2,1)S(1)}, bf16[128,1616]{1,0:T(8,128)(2,1)S(1)}, u32[]{:S(2)}, u32[]{:S(2)}) %collective-permute-start.3) | collective-permute-done | bytes 413728 | tf_op jit(solution)/shard_map/ppermute | solution.py:22
  60.0 4.4 %collective-permute-start.4 = (bf16[128,1616]{1,0:T(8,128)(2,1)S(1)}, bf16[128,1616]{1,0:T(8,128)(2,1)S(1)}, u32[]{:S(2)}, u32[]{:S(2)}) collective-permute-start(bf16[128,1616]{1,0:T(8,128)(2,1)S(1)} %collective-permute-done.3), channel_id=1, source_target_pairs={{0,7},{1,0},{2,1},{3,2},{4,3},{5,4},{6,5},{7,6},{8,15},{9,8},{10,9... | collective-permute-start | bytes 1241096 | tf_op jit(solution)/shard_map/ppermute | solution.py:22
  64.4 1.9 %collective-permute-start.7 = (bf16[128,1616]{1,0:T(8,128)(2,1)S(1)}, bf16[128,1616]{1,0:T(8,128)(2,1)S(1)}, u32[]{:S(2)}, u32[]{:S(2)}) collective-permute-start(bf16[128,1616]{1,0:T(8,128)(2,1)S(1)} %collective-permute-done.6), channel_id=1, source_target_pairs={{0,1},{1,2},{2,3},{3,4},{4,5},{5,6},{6,7},{7,0},{8,9},{9,10},{10,1... | collective-permute-start | bytes 1241096 | tf_op jit(solution)/shard_map/ppermute | solution.py:22
  66.4 0.2 add_reduce_fusion.5
  66.6 0.2 add_reduce_fusion.1
  66.7 0.8 slice_dynamic-update-slice_fusion.5
  67.5 10.4 %collective-permute-done.7 = bf16[128,1616]{1,0:T(8,128)(2,1)S(1)} collective-permute-done((bf16[128,1616]{1,0:T(8,128)(2,1)S(1)}, bf16[128,1616]{1,0:T(8,128)(2,1)S(1)}, u32[]{:S(2)}, u32[]{:S(2)}) %collective-permute-start.7) | collective-permute-done | bytes 413728 | tf_op jit(solution)/shard_map/ppermute | solution.py:22
  77.9 1.9 %collective-permute-start.8 = (bf16[128,1616]{1,0:T(8,128)(2,1)S(1)}, bf16[128,1616]{1,0:T(8,128)(2,1)S(1)}, u32[]{:S(2)}, u32[]{:S(2)}) collective-permute-start(bf16[128,1616]{1,0:T(8,128)(2,1)S(1)} %collective-permute-done.7), channel_id=1, source_target_pairs={{0,1},{1,2},{2,3},{3,4},{4,5},{5,6},{6,7},{7,0},{8,9},{9,10},{10,1... | collective-permute-start | bytes 1241096 | tf_op jit(solution)/shard_map/ppermute | solution.py:22
  79.9 0.2 add_reduce_fusion.4
  80.1 0.2 add_reduce_fusion.2
  80.3 0.8 slice_dynamic-update-slice_fusion.4
  81.1 6.9 %collective-permute-done.8 = bf16[128,1616]{1,0:T(8,128)(2,1)S(1)} collective-permute-done((bf16[128,1616]{1,0:T(8,128)(2,1)S(1)}, bf16[128,1616]{1,0:T(8,128)(2,1)S(1)}, u32[]{:S(2)}, u32[]{:S(2)}) %collective-permute-start.8) | collective-permute-done | bytes 413728 | tf_op jit(solution)/shard_map/ppermute | solution.py:22
  88.0 0.2 add_reduce_fusion.3
  88.2 0.8 slice_dynamic-update-slice_fusion.3
  89.0 0.8 slice_dynamic-update-slice_fusion.2
  89.9 0.8 slice_dynamic-update-slice_fusion.1
  90.7 0.8 slice_dynamic-update-slice_fusion.rows_ref
  91.5 13.9 %shard_map.68 = (f32[1,1024]{1,0:T(1,128)}, f32[1,1024]{1,0:T(1,128)}, f32[1,1024]{1,0:T(1,128)}, f32[1,1024]{1,0:T(1,128)}) custom-call(bf16[1024,1600]{1,0:T(8,128)(2,1)} %slice_dynamic-update-slice_fusion.rows_ref, bf16[2048,1600]{1,0:T(8,128)(2,1)} %all-gather.2.cloned.1.call-done.vocab_ref, s32[1,1024]{1,0:T(1,128)} %bitcast.18, s32[2048,1]{1,0:T(8,128)} %fusion.13.ids_ref), custom_call_target="tpu_custom_call" | custom-call | flops 6710886400 | bytes 9830400 | tf_op jit(solution)/shard_map/pallas_call | solution.py:72
  105.4 0.7 maximum_bitcast_fusion
  106.2 9.9 %all_to_all.6 = f32[4,8,128]{2,0,1:T(4,128)S(1)} all-to-all(f32[4,8,128]{2,0,1:T(4,128)S(1)} %fusion.31), channel_id=1, replica_groups=mesh['z'=8,'x'=4,'c'=2,'y'=8] {'y'}, dimensions={1} | all-to-all | bytes 32768 | tf_op jit(solution)/shard_map/all_to_all | solution.py:148
  116.1 0.5 subtract_multiply_fusion
  (26 shorter events, 0.2 us)
Async XLA Ops:
  7.2 84.3 %all-gather.2.cloned.1.call-start = ((), (), s32[]{:S(2)}) async-start(), calls=%async_computation.1 | async-start | bytes 7241728 | tf_op jit(solution)/shard_map/all_gather | solution.py:138
  7.2 13.2 %collective-permute-start = (bf16[32,1600]{1,0:T(8,128)(2,1)}, bf16[32,1600]{1,0:T(8,128)(2,1)S(1)}, u32[]{:S(2)}, u32[]{:S(2)}) collective-permute-start(bf16[32,1600]{1,0:T(8,128)(2,1)} %param.11), channel_id=1, source_target_pairs={{0,16},{16,32},{32,48},{48,0},{1,17},{17,33},{33,49},{49,1},{2,18}... | collective-permute-start | bytes 307208 | tf_op jit(solution)/shard_map/ppermute | solution.py:22
  10.6 9.8 %collective-permute-start.1 = (bf16[32,1600]{1,0:T(8,128)(2,1)}, bf16[32,1600]{1,0:T(8,128)(2,1)S(1)}, u32[]{:S(2)}, u32[]{:S(2)}) collective-permute-start(bf16[32,1600]{1,0:T(8,128)(2,1)} %param.11), channel_id=1, source_target_pairs={{0,48},{16,0},{32,16},{48,32},{1,49},{17,1},{33,17},{49,33},{2,50}... | collective-permute-start | bytes 307208 | tf_op jit(solution)/shard_map/ppermute | solution.py:22
  20.4 7.8 %collective-permute-start.9 = (bf16[32,1600]{1,0:T(8,128)(2,1)S(1)}, bf16[32,1600]{1,0:T(8,128)(2,1)S(1)}, u32[]{:S(2)}, u32[]{:S(2)}) collective-permute-start(bf16[32,1600]{1,0:T(8,128)(2,1)S(1)} %collective-permute-done), channel_id=1, source_target_pairs={{0,16},{16,32},{32,48},{48,0},{1,17},{17,33},{33,49},{49,1},{2,18}... | collective-permute-start | bytes 307208 | tf_op jit(solution)/shard_map/ppermute | solution.py:22
  31.9 15.4 %collective-permute-start.2 = (bf16[128,1616]{1,0:T(8,128)(2,1)S(1)}, bf16[128,1616]{1,0:T(8,128)(2,1)S(1)}, u32[]{:S(2)}, u32[]{:S(2)}) collective-permute-start(bf16[128,1616]{1,0:T(8,128)(2,1)S(1)} %pad_maximum_fusion), channel_id=1, source_target_pairs={{0,7},{1,0},{2,1},{3,2},{4,3},{5,4},{6,5},{7,6},{8,15},{9,8},{10,9... | collective-permute-start | bytes 1241096 | tf_op jit(solution)/shard_map/ppermute | solution.py:22
  39.6 12.1 %collective-permute-start.5 = (bf16[128,1616]{1,0:T(8,128)(2,1)S(1)}, bf16[128,1616]{1,0:T(8,128)(2,1)S(1)}, u32[]{:S(2)}, u32[]{:S(2)}) collective-permute-start(bf16[128,1616]{1,0:T(8,128)(2,1)S(1)} %pad_maximum_fusion), channel_id=1, source_target_pairs={{0,1},{1,2},{2,3},{3,4},{4,5},{5,6},{6,7},{7,0},{8,9},{9,10},{10,1... | collective-permute-start | bytes 1241096 | tf_op jit(solution)/shard_map/ppermute | solution.py:22
  47.3 12.8 %collective-permute-start.3 = (bf16[128,1616]{1,0:T(8,128)(2,1)S(1)}, bf16[128,1616]{1,0:T(8,128)(2,1)S(1)}, u32[]{:S(2)}, u32[]{:S(2)}) collective-permute-start(bf16[128,1616]{1,0:T(8,128)(2,1)S(1)} %collective-permute-done.2), channel_id=1, source_target_pairs={{0,7},{1,0},{2,1},{3,2},{4,3},{5,4},{6,5},{7,6},{8,15},{9,8},{10,9... | collective-permute-start | bytes 1241096 | tf_op jit(solution)/shard_map/ppermute | solution.py:22
  51.7 12.8 %collective-permute-start.6 = (bf16[128,1616]{1,0:T(8,128)(2,1)S(1)}, bf16[128,1616]{1,0:T(8,128)(2,1)S(1)}, u32[]{:S(2)}, u32[]{:S(2)}) collective-permute-start(bf16[128,1616]{1,0:T(8,128)(2,1)S(1)} %collective-permute-done.5), channel_id=1, source_target_pairs={{0,1},{1,2},{2,3},{3,4},{4,5},{5,6},{6,7},{7,0},{8,9},{9,10},{10,1... | collective-permute-start | bytes 1241096 | tf_op jit(solution)/shard_map/ppermute | solution.py:22
  60.0 19.8 %collective-permute-start.4 = (bf16[128,1616]{1,0:T(8,128)(2,1)S(1)}, bf16[128,1616]{1,0:T(8,128)(2,1)S(1)}, u32[]{:S(2)}, u32[]{:S(2)}) collective-permute-start(bf16[128,1616]{1,0:T(8,128)(2,1)S(1)} %collective-permute-done.3), channel_id=1, source_target_pairs={{0,7},{1,0},{2,1},{3,2},{4,3},{5,4},{6,5},{7,6},{8,15},{9,8},{10,9... | collective-permute-start | bytes 1241096 | tf_op jit(solution)/shard_map/ppermute | solution.py:22
  64.4 13.5 %collective-permute-start.7 = (bf16[128,1616]{1,0:T(8,128)(2,1)S(1)}, bf16[128,1616]{1,0:T(8,128)(2,1)S(1)}, u32[]{:S(2)}, u32[]{:S(2)}) collective-permute-start(bf16[128,1616]{1,0:T(8,128)(2,1)S(1)} %collective-permute-done.6), channel_id=1, source_target_pairs={{0,1},{1,2},{2,3},{3,4},{4,5},{5,6},{6,7},{7,0},{8,9},{9,10},{10,1... | collective-permute-start | bytes 1241096 | tf_op jit(solution)/shard_map/ppermute | solution.py:22
  77.9 10.0 %collective-permute-start.8 = (bf16[128,1616]{1,0:T(8,128)(2,1)S(1)}, bf16[128,1616]{1,0:T(8,128)(2,1)S(1)}, u32[]{:S(2)}, u32[]{:S(2)}) collective-permute-start(bf16[128,1616]{1,0:T(8,128)(2,1)S(1)} %collective-permute-done.7), channel_id=1, source_target_pairs={{0,1},{1,2},{2,3},{3,4},{4,5},{5,6},{6,7},{7,0},{8,9},{9,10},{10,1... | collective-permute-start | bytes 1241096 | tf_op jit(solution)/shard_map/ppermute | solution.py:22
  88.2 3.3 %copy-start.1 = (s32[1024]{0:T(1024)}, s32[1024]{0:T(1024)S(1)}, u32[]{:S(2)}) copy-start(s32[1024]{0:T(1024)S(1)} %constant_dynamic-update-slice_fusion.1) | copy-start | bytes 12292
  91.5 24.6 %copy-start = (s32[128]{0:T(128)S(1)}, s32[128]{0:T(128)}, u32[]{:S(2)}) copy-start(s32[128]{0:T(128)} %param.13) | copy-start | bytes 1540
Sparse Core Ops, SparseCore 0:
  30.0 54.0 all-gather.1

commit v10 on v9

--- a/solution.py
+++ b/solution.py
@@ -110,17 +110,9 @@
 
     nx = lax.axis_size("x")
     x = lax.axis_index("x")
-    near = [None] * nx
-    near[0] = unembed
-    fronts = {1: shift(unembed, "x", nx, 1), -1: shift(unembed, "x", nx, -1)}
-    block, fronts[1], fronts[-1] = lax.optimization_barrier((block, fronts[1], fronts[-1]))
-    for sign in (1, -1):
-        cur = fronts[sign]
-        reach = nx // 2 if sign == 1 else nx - 1 - nx // 2
-        for step in range(1, reach + 1):
-            if step > 1:
-                cur = shift(cur, "x", nx, sign)
-            near[(-sign * step) % nx] = cur
+    near = [unembed] + [shift(unembed, "x", nx, -d) for d in range(1, nx)]
+    block, *rest = lax.optimization_barrier((block, *near[1:]))
+    near[1:] = rest
 
     blocks = [None] * ny
     blocks[0] = block

time: 124 us -> 121 us (0.976)
  the two profiles are of different devices: /device:TPU:8 before, /device:TPU:450 now
where the time goes in v10:
time: 121 us; the launch traced here: 120 us
  starting transfers between devices  34.7 us (29%)
  waiting for transfers between devices  26.4 us (22%)
  between operations  14.3 us (12%)
  Pallas kernels  13.9 us (11%)
  blocking collectives  11.7 us (10%)
  other arithmetic  10.8 us (9%)
  local copies, waits for them, and re-layouts  8.27 us (7%)
    ppermute x10, starting transfers between devices, shift(): lax.ppermute(value, axis, [(i, (i + step) % size) for i in range(size)])  34.7 us
    ppermute x10, waiting for transfers between devices, shift(): lax.ppermute(value, axis, [(i, (i + step) % size) for i in range(size)])  26.4 us
    pallas_call x1, Pallas kernels, row_stats(): pl.pallas_call(stats_kernel, grid=(width // tile,), in_specs=[pl.BlockSpe...  13.9 us
    all_to_all x1, blocking collectives, on_device(): got = lax.all_to_all(packed, 'y', 1, 1, tiled=True).reshape(4, ny, mine)  11.7 us
    unnamed x19, local copies, waits for them, and re-layouts  7 us
    another operation x3, other arithmetic  3.25 us
  transfers between devices with their start and end apart: 11, of which 4 were waited for; matrix products, arithmetic and copies ran while one was open for 13% of the time, Pallas kernels for 0%

profile of v10, /device:TPU:450, one launch (start us, length us, event | category | flops | bytes accessed | tf_op | source)
XLA Modules:
  0.0 120.1 jit_solution(10061713637829114814)
XLA Ops:
  7.2 0.0 all-gather.2.cloned.1.call-start
  7.2 2.4 %collective-permute-start = (bf16[32,1600]{1,0:T(8,128)(2,1)}, bf16[32,1600]{1,0:T(8,128)(2,1)S(1)}, u32[]{:S(2)}, u32[]{:S(2)}) collective-permute-start(bf16[32,1600]{1,0:T(8,128)(2,1)} %param.11), channel_id=1, source_target_pairs={{0,48},{16,0},{32,16},{48,32},{1,49},{17,1},{33,17},{49,33},{2,50}... | collective-permute-start | bytes 307208 | tf_op jit(solution)/shard_map/ppermute | solution.py:22
  9.7 4.3 %collective-permute-start.1 = (bf16[32,1600]{1,0:T(8,128)(2,1)}, bf16[32,1600]{1,0:T(8,128)(2,1)S(1)}, u32[]{:S(2)}, u32[]{:S(2)}) collective-permute-start(bf16[32,1600]{1,0:T(8,128)(2,1)} %param.11), channel_id=1, source_target_pairs={{0,32},{16,48},{32,0},{48,16},{1,33},{17,49},{33,1},{49,17},{2,34}... | collective-permute-start | bytes 307208 | tf_op jit(solution)/shard_map/ppermute | solution.py:22
  14.0 3.7 %collective-permute-start.2 = (bf16[32,1600]{1,0:T(8,128)(2,1)}, bf16[32,1600]{1,0:T(8,128)(2,1)S(1)}, u32[]{:S(2)}, u32[]{:S(2)}) collective-permute-start(bf16[32,1600]{1,0:T(8,128)(2,1)} %param.11), channel_id=1, source_target_pairs={{0,16},{16,32},{32,48},{48,0},{1,17},{17,33},{33,49},{49,1},{2,18}... | collective-permute-start | bytes 307208 | tf_op jit(solution)/shard_map/ppermute | solution.py:22
  17.7 0.6 compare_reduce_fusion
  18.4 0.6 compare_reduce_fusion.1
  19.0 1.2 %copy.13 = bf16[128,1600]{1,0:T(8,128)(2,1)S(1)} copy(bf16[128,1600]{0,1:T(8,128)(2,1)} %param.9) | data formatting | bytes 819200 | tf_op args[0]
  20.2 0.2 fusion.28
  20.4 2.0 %fusion.33 = (bf16[128,1]{0,1:T(2,128)(2,1)S(1)}, bf16[128,1]{0,1:T(2,128)(2,1)S(1)}) fusion(pred[]{:T(512)} %compare_reduce_fusion, s32[128]{0:T(128)} %param.12, pred[]{:T(512)} %compare_reduce_fusion.1), kind=kLoop, calls=%fused_computation.93 | loop fusion | flops 2944 | bytes 1026 | tf_op jit(solution)/shard_map/reshape.177
  22.4 0.1 copy.14
  22.5 0.1 copy.15
  22.7 0.9 fusion.30
  23.6 0.2 scatter.9
  23.7 0.1 pad_maximum_fusion
  23.9 1.7 %pad_maximum_fusion.1 = bf16[128,1600]{1,0:T(8,128)(2,1)} fusion(bf16[32,1600]{1,0:T(8,128)(2,1)S(1)} %collective-permute-done.2, bf16[32,1600]{1,0:T(8,128)(2,1)S(1)} %collective-permute-done.1, bf16[32,1600]{1,0:T(8,128)(2,1)S(1)} %collective-permute-done, bf16[32,1600]{1,0:T(8,128)(2,1)} %param.11), kind=kLoop, calls=%fused_computation.58 | loop fusion | flops 1638400 | bytes 819200 | tf_op jit(solution)/shard_map/concatenate | solution.py:130
  25.5 0.0 all-gather.2.cloned.1.call-update
  25.6 1.9 %fusion.13.ids_ref = s32[2048,1]{1,0:T(8,128)} fusion(s32[]{:T(128)S(6)} %axis_index.25, s32[]{:T(128)S(6)} %axis_index.23), kind=kLoop, calls=%fused_computation.32 | loop fusion | flops 143360 | bytes 8200 | tf_op jit(solution)/shard_map/add | solution.py:135
  27.5 5.4 %collective-permute-start.3 = (bf16[128,1616]{1,0:T(8,128)(2,1)S(1)}, bf16[128,1616]{1,0:T(8,128)(2,1)S(1)}, u32[]{:S(2)}, u32[]{:S(2)}) collective-permute-start(bf16[128,1616]{1,0:T(8,128)(2,1)S(1)} %pad_maximum_fusion), channel_id=1, source_target_pairs={{0,7},{1,0},{2,1},{3,2},{4,3},{5,4},{6,5},{7,6},{8,15},{9,8},{10,9... | collective-permute-start | bytes 1241096 | tf_op jit(solution)/shard_map/ppermute | solution.py:22
  32.9 1.9 %collective-permute-start.6 = (bf16[128,1616]{1,0:T(8,128)(2,1)S(1)}, bf16[128,1616]{1,0:T(8,128)(2,1)S(1)}, u32[]{:S(2)}, u32[]{:S(2)}) collective-permute-start(bf16[128,1616]{1,0:T(8,128)(2,1)S(1)} %pad_maximum_fusion), channel_id=1, source_target_pairs={{0,1},{1,2},{2,3},{3,4},{4,5},{5,6},{6,7},{7,0},{8,9},{9,10},{10,1... | collective-permute-start | bytes 1241096 | tf_op jit(solution)/shard_map/ppermute | solution.py:22
  34.8 0.2 add_reduce_fusion.7
  35.0 0.8 slice_dynamic-update-slice_fusion.7
  35.8 5.3 %collective-permute-done.3 = bf16[128,1616]{1,0:T(8,128)(2,1)S(1)} collective-permute-done((bf16[128,1616]{1,0:T(8,128)(2,1)S(1)}, bf16[128,1616]{1,0:T(8,128)(2,1)S(1)}, u32[]{:S(2)}, u32[]{:S(2)}) %collective-permute-start.3) | collective-permute-done | bytes 413728 | tf_op jit(solution)/shard_map/ppermute | solution.py:22
  41.1 5.6 %collective-permute-start.4 = (bf16[128,1616]{1,0:T(8,128)(2,1)S(1)}, bf16[128,1616]{1,0:T(8,128)(2,1)S(1)}, u32[]{:S(2)}, u32[]{:S(2)}) collective-permute-start(bf16[128,1616]{1,0:T(8,128)(2,1)S(1)} %collective-permute-done.3), channel_id=1, source_target_pairs={{0,7},{1,0},{2,1},{3,2},{4,3},{5,4},{6,5},{7,6},{8,15},{9,8},{10,9... | collective-permute-start | bytes 1241096 | tf_op jit(solution)/shard_map/ppermute | solution.py:22
  46.7 1.9 %collective-permute-start.7 = (bf16[128,1616]{1,0:T(8,128)(2,1)S(1)}, bf16[128,1616]{1,0:T(8,128)(2,1)S(1)}, u32[]{:S(2)}, u32[]{:S(2)}) collective-permute-start(bf16[128,1616]{1,0:T(8,128)(2,1)S(1)} %collective-permute-done.6), channel_id=1, source_target_pairs={{0,1},{1,2},{2,3},{3,4},{4,5},{5,6},{6,7},{7,0},{8,9},{9,10},{10,1... | collective-permute-start | bytes 1241096 | tf_op jit(solution)/shard_map/ppermute | solution.py:22
  48.6 0.2 add_reduce_fusion.6
  48.8 0.2 add_reduce_fusion
  49.0 0.8 slice_dynamic-update-slice_fusion.6
  49.8 4.3 %collective-permute-done.4 = bf16[128,1616]{1,0:T(8,128)(2,1)S(1)} collective-permute-done((bf16[128,1616]{1,0:T(8,128)(2,1)S(1)}, bf16[128,1616]{1,0:T(8,128)(2,1)S(1)}, u32[]{:S(2)}, u32[]{:S(2)}) %collective-permute-start.4) | collective-permute-done | bytes 413728 | tf_op jit(solution)/shard_map/ppermute | solution.py:22
  54.1 5.6 %collective-permute-start.5 = (bf16[128,1616]{1,0:T(8,128)(2,1)S(1)}, bf16[128,1616]{1,0:T(8,128)(2,1)S(1)}, u32[]{:S(2)}, u32[]{:S(2)}) collective-permute-start(bf16[128,1616]{1,0:T(8,128)(2,1)S(1)} %collective-permute-done.4), channel_id=1, source_target_pairs={{0,7},{1,0},{2,1},{3,2},{4,3},{5,4},{6,5},{7,6},{8,15},{9,8},{10,9... | collective-permute-start | bytes 1241096 | tf_op jit(solution)/shard_map/ppermute | solution.py:22
  59.7 1.9 %collective-permute-start.8 = (bf16[128,1616]{1,0:T(8,128)(2,1)S(1)}, bf16[128,1616]{1,0:T(8,128)(2,1)S(1)}, u32[]{:S(2)}, u32[]{:S(2)}) collective-permute-start(bf16[128,1616]{1,0:T(8,128)(2,1)S(1)} %collective-permute-done.7), channel_id=1, source_target_pairs={{0,1},{1,2},{2,3},{3,4},{4,5},{5,6},{6,7},{7,0},{8,9},{9,10},{10,1... | collective-permute-start | bytes 1241096 | tf_op jit(solution)/shard_map/ppermute | solution.py:22
  61.6 0.2 add_reduce_fusion.5
  61.8 0.2 add_reduce_fusion.1
  62.0 0.8 slice_dynamic-update-slice_fusion.5
  62.8 8.8 %collective-permute-done.8 = bf16[128,1616]{1,0:T(8,128)(2,1)S(1)} collective-permute-done((bf16[128,1616]{1,0:T(8,128)(2,1)S(1)}, bf16[128,1616]{1,0:T(8,128)(2,1)S(1)}, u32[]{:S(2)}, u32[]{:S(2)}) %collective-permute-start.8) | collective-permute-done | bytes 413728 | tf_op jit(solution)/shard_map/ppermute | solution.py:22
  71.6 1.9 %collective-permute-start.9 = (bf16[128,1616]{1,0:T(8,128)(2,1)S(1)}, bf16[128,1616]{1,0:T(8,128)(2,1)S(1)}, u32[]{:S(2)}, u32[]{:S(2)}) collective-permute-start(bf16[128,1616]{1,0:T(8,128)(2,1)S(1)} %collective-permute-done.8), channel_id=1, source_target_pairs={{0,1},{1,2},{2,3},{3,4},{4,5},{5,6},{6,7},{7,0},{8,9},{9,10},{10,1... | collective-permute-start | bytes 1241096 | tf_op jit(solution)/shard_map/ppermute | solution.py:22
  73.5 0.2 add_reduce_fusion.4
  73.7 0.2 add_reduce_fusion.2
  73.9 0.8 slice_dynamic-update-slice_fusion.4
  74.7 8.1 %collective-permute-done.9 = bf16[128,1616]{1,0:T(8,128)(2,1)S(1)} collective-permute-done((bf16[128,1616]{1,0:T(8,128)(2,1)S(1)}, bf16[128,1616]{1,0:T(8,128)(2,1)S(1)}, u32[]{:S(2)}, u32[]{:S(2)}) %collective-permute-start.9) | collective-permute-done | bytes 413728 | tf_op jit(solution)/shard_map/ppermute | solution.py:22
  82.8 0.2 add_reduce_fusion.3
  83.1 0.8 slice_dynamic-update-slice_fusion.3
  83.9 0.8 slice_dynamic-update-slice_fusion.2
  84.7 0.8 slice_dynamic-update-slice_fusion.1
  85.5 0.8 slice_dynamic-update-slice_fusion.rows_ref
  86.3 13.9 %shard_map.68 = (f32[1,1024]{1,0:T(1,128)}, f32[1,1024]{1,0:T(1,128)}, f32[1,1024]{1,0:T(1,128)}, f32[1,1024]{1,0:T(1,128)}) custom-call(bf16[1024,1600]{1,0:T(8,128)(2,1)} %slice_dynamic-update-slice_fusion.rows_ref, bf16[2048,1600]{1,0:T(8,128)(2,1)} %all-gather.2.cloned.1.call-done.vocab_ref, s32[1,1024]{1,0:T(1,128)} %bitcast.18, s32[2048,1]{1,0:T(8,128)} %fusion.13.ids_ref), custom_call_target="tpu_custom_call" | custom-call | flops 6710886400 | bytes 9830400 | tf_op jit(solution)/shard_map/pallas_call | solution.py:72
  100.2 0.7 maximum_bitcast_fusion
  101.0 11.7 %all_to_all.6 = f32[4,8,128]{2,0,1:T(4,128)S(1)} all-to-all(f32[4,8,128]{2,0,1:T(4,128)S(1)} %fusion.31), channel_id=1, replica_groups=mesh['z'=8,'x'=4,'c'=2,'y'=8] {'y'}, dimensions={1} | all-to-all | bytes 32768 | tf_op jit(solution)/shard_map/all_to_all | solution.py:140
  112.7 0.5 subtract_multiply_fusion
  (26 shorter events, 0.2 us)
Async XLA Ops:
  7.2 79.2 %all-gather.2.cloned.1.call-start = ((), (), s32[]{:S(2)}) async-start(), calls=%async_computation.1 | async-start | bytes 7241728 | tf_op jit(solution)/shard_map/all_gather | solution.py:130
  7.2 16.6 %collective-permute-start = (bf16[32,1600]{1,0:T(8,128)(2,1)}, bf16[32,1600]{1,0:T(8,128)(2,1)S(1)}, u32[]{:S(2)}, u32[]{:S(2)}) collective-permute-start(bf16[32,1600]{1,0:T(8,128)(2,1)} %param.11), channel_id=1, source_target_pairs={{0,48},{16,0},{32,16},{48,32},{1,49},{17,1},{33,17},{49,33},{2,50}... | collective-permute-start | bytes 307208 | tf_op jit(solution)/shard_map/ppermute | solution.py:22
  9.7 14.2 %collective-permute-start.1 = (bf16[32,1600]{1,0:T(8,128)(2,1)}, bf16[32,1600]{1,0:T(8,128)(2,1)S(1)}, u32[]{:S(2)}, u32[]{:S(2)}) collective-permute-start(bf16[32,1600]{1,0:T(8,128)(2,1)} %param.11), channel_id=1, source_target_pairs={{0,32},{16,48},{32,0},{48,16},{1,33},{17,49},{33,1},{49,17},{2,34}... | collective-permute-start | bytes 307208 | tf_op jit(solution)/shard_map/ppermute | solution.py:22
  14.0 9.9 %collective-permute-start.2 = (bf16[32,1600]{1,0:T(8,128)(2,1)}, bf16[32,1600]{1,0:T(8,128)(2,1)S(1)}, u32[]{:S(2)}, u32[]{:S(2)}) collective-permute-start(bf16[32,1600]{1,0:T(8,128)(2,1)} %param.11), channel_id=1, source_target_pairs={{0,16},{16,32},{32,48},{48,0},{1,17},{17,33},{33,49},{49,1},{2,18}... | collective-permute-start | bytes 307208 | tf_op jit(solution)/shard_map/ppermute | solution.py:22
  27.5 13.6 %collective-permute-start.3 = (bf16[128,1616]{1,0:T(8,128)(2,1)S(1)}, bf16[128,1616]{1,0:T(8,128)(2,1)S(1)}, u32[]{:S(2)}, u32[]{:S(2)}) collective-permute-start(bf16[128,1616]{1,0:T(8,128)(2,1)S(1)} %pad_maximum_fusion), channel_id=1, source_target_pairs={{0,7},{1,0},{2,1},{3,2},{4,3},{5,4},{6,5},{7,6},{8,15},{9,8},{10,9... | collective-permute-start | bytes 1241096 | tf_op jit(solution)/shard_map/ppermute | solution.py:22
  32.9 13.8 %collective-permute-start.6 = (bf16[128,1616]{1,0:T(8,128)(2,1)S(1)}, bf16[128,1616]{1,0:T(8,128)(2,1)S(1)}, u32[]{:S(2)}, u32[]{:S(2)}) collective-permute-start(bf16[128,1616]{1,0:T(8,128)(2,1)S(1)} %pad_maximum_fusion), channel_id=1, source_target_pairs={{0,1},{1,2},{2,3},{3,4},{4,5},{5,6},{6,7},{7,0},{8,9},{9,10},{10,1... | collective-permute-start | bytes 1241096 | tf_op jit(solution)/shard_map/ppermute | solution.py:22
  41.1 13.0 %collective-permute-start.4 = (bf16[128,1616]{1,0:T(8,128)(2,1)S(1)}, bf16[128,1616]{1,0:T(8,128)(2,1)S(1)}, u32[]{:S(2)}, u32[]{:S(2)}) collective-permute-start(bf16[128,1616]{1,0:T(8,128)(2,1)S(1)} %collective-permute-done.3), channel_id=1, source_target_pairs={{0,7},{1,0},{2,1},{3,2},{4,3},{5,4},{6,5},{7,6},{8,15},{9,8},{10,9... | collective-permute-start | bytes 1241096 | tf_op jit(solution)/shard_map/ppermute | solution.py:22
  46.7 13.0 %collective-permute-start.7 = (bf16[128,1616]{1,0:T(8,128)(2,1)S(1)}, bf16[128,1616]{1,0:T(8,128)(2,1)S(1)}, u32[]{:S(2)}, u32[]{:S(2)}) collective-permute-start(bf16[128,1616]{1,0:T(8,128)(2,1)S(1)} %collective-permute-done.6), channel_id=1, source_target_pairs={{0,1},{1,2},{2,3},{3,4},{4,5},{5,6},{6,7},{7,0},{8,9},{9,10},{10,1... | collective-permute-start | bytes 1241096 | tf_op jit(solution)/shard_map/ppermute | solution.py:22
  54.1 19.4 %collective-permute-start.5 = (bf16[128,1616]{1,0:T(8,128)(2,1)S(1)}, bf16[128,1616]{1,0:T(8,128)(2,1)S(1)}, u32[]{:S(2)}, u32[]{:S(2)}) collective-permute-start(bf16[128,1616]{1,0:T(8,128)(2,1)S(1)} %collective-permute-done.4), channel_id=1, source_target_pairs={{0,7},{1,0},{2,1},{3,2},{4,3},{5,4},{6,5},{7,6},{8,15},{9,8},{10,9... | collective-permute-start | bytes 1241096 | tf_op jit(solution)/shard_map/ppermute | solution.py:22
  59.7 11.9 %collective-permute-start.8 = (bf16[128,1616]{1,0:T(8,128)(2,1)S(1)}, bf16[128,1616]{1,0:T(8,128)(2,1)S(1)}, u32[]{:S(2)}, u32[]{:S(2)}) collective-permute-start(bf16[128,1616]{1,0:T(8,128)(2,1)S(1)} %collective-permute-done.7), channel_id=1, source_target_pairs={{0,1},{1,2},{2,3},{3,4},{4,5},{5,6},{6,7},{7,0},{8,9},{9,10},{10,1... | collective-permute-start | bytes 1241096 | tf_op jit(solution)/shard_map/ppermute | solution.py:22
  71.6 11.2 %collective-permute-start.9 = (bf16[128,1616]{1,0:T(8,128)(2,1)S(1)}, bf16[128,1616]{1,0:T(8,128)(2,1)S(1)}, u32[]{:S(2)}, u32[]{:S(2)}) collective-permute-start(bf16[128,1616]{1,0:T(8,128)(2,1)S(1)} %collective-permute-done.8), channel_id=1, source_target_pairs={{0,1},{1,2},{2,3},{3,4},{4,5},{5,6},{6,7},{7,0},{8,9},{9,10},{10,1... | collective-permute-start | bytes 1241096 | tf_op jit(solution)/shard_map/ppermute | solution.py:22
  83.0 3.3 %copy-start.1 = (s32[1024]{0:T(1024)}, s32[1024]{0:T(1024)S(1)}, u32[]{:S(2)}) copy-start(s32[1024]{0:T(1024)S(1)} %constant_dynamic-update-slice_fusion.1) | copy-start | bytes 12292
  86.3 26.4 %copy-start = (s32[128]{0:T(128)S(1)}, s32[128]{0:T(128)}, u32[]{:S(2)}) copy-start(s32[128]{0:T(128)} %param.13) | copy-start | bytes 1540
Sparse Core Ops, SparseCore 0:
  25.7 47.8 all-gather.1

commit v11 on v10

--- a/solution.py
+++ b/solution.py
@@ -65,7 +65,7 @@
     top_ref[...] = top
 
 
-def row_stats(rows, vocab, wanted, ids, tile=256):
+def row_stats(rows, vocab, wanted, ids, tile=512):
     count, dim = rows.shape
     width = vocab.shape[0]
     line = pl.BlockSpec((1, count), lambda j: (0, 0))
@@ -110,9 +110,8 @@
 
     nx = lax.axis_size("x")
     x = lax.axis_index("x")
+    block, unembed = lax.optimization_barrier((block, unembed))
     near = [unembed] + [shift(unembed, "x", nx, -d) for d in range(1, nx)]
-    block, *rest = lax.optimization_barrier((block, *near[1:]))
-    near[1:] = rest
 
     blocks = [None] * ny
     blocks[0] = block

time: 121 us -> 122 us (level)
  the two profiles are of different devices: /device:TPU:450 before, /device:TPU:1 now
where the time goes in v11:
time: 122 us; the launch traced here: 121 us
  starting transfers between devices  34.2 us (28%)
  waiting for transfers between devices  27.6 us (23%)
  between operations  14.3 us (12%)
  Pallas kernels  13.3 us (11%)
  blocking collectives  12.9 us (11%)
  other arithmetic  10.8 us (9%)
  local copies, waits for them, and re-layouts  8.27 us (7%)
    ppermute x10, starting transfers between devices, shift(): lax.ppermute(value, axis, [(i, (i + step) % size) for i in range(size)])  34.2 us
    ppermute x10, waiting for transfers between devices, shift(): lax.ppermute(value, axis, [(i, (i + step) % size) for i in range(size)])  24.8 us
    pallas_call x1, Pallas kernels, row_stats(): pl.pallas_call(stats_kernel, grid=(width // tile,), in_specs=[pl.BlockSpe...  13.3 us
    all_to_all x1, blocking collectives, on_device(): got = lax.all_to_all(packed, 'y', 1, 1, tiled=True).reshape(4, ny, mine)  12.9 us
    unnamed x19, local copies, waits for them, and re-layouts  7 us
    another operation x3, other arithmetic  3.25 us
    all_gather x1, waiting for transfers between devices, on_device(): lax.all_gather(jnp.concatenate(near, axis=0), ('z', 'c'), axis=0, tiled=T...  2.72 us
  transfers between devices with their start and end apart: 11, of which 7 were waited for; matrix products, arithmetic and copies ran while one was open for 8% of the time, Pallas kernels for 0%

profile of v11, /device:TPU:1, one launch (start us, length us, event | category | flops | bytes accessed | tf_op | source)
XLA Modules:
  0.0 121.3 jit_solution(7106905447121729339)
XLA Ops:
  7.2 0.6 compare_reduce_fusion
  7.8 0.6 compare_reduce_fusion.1
  8.5 1.2 %copy.13 = bf16[128,1600]{1,0:T(8,128)(2,1)S(1)} copy(bf16[128,1600]{0,1:T(8,128)(2,1)} %param.9) | data formatting | bytes 819200 | tf_op args[0]
  9.7 0.2 fusion.28
  9.9 2.0 %fusion.33 = (bf16[128,1]{0,1:T(2,128)(2,1)S(1)}, bf16[128,1]{0,1:T(2,128)(2,1)S(1)}) fusion(pred[]{:T(512)} %compare_reduce_fusion, s32[128]{0:T(128)} %param.12, pred[]{:T(512)} %compare_reduce_fusion.1), kind=kLoop, calls=%fused_computation.93 | loop fusion | flops 2944 | bytes 1026 | tf_op jit(solution)/shard_map/reshape.177
  11.9 0.1 copy.14
  12.0 0.1 copy.15
  12.2 0.9 fusion.30
  13.0 0.2 scatter.9
  13.3 5.2 %collective-permute-start.7 = (bf16[32,1600]{1,0:T(8,128)(2,1)}, bf16[32,1600]{1,0:T(8,128)(2,1)S(1)}, u32[]{:S(2)}, u32[]{:S(2)}) collective-permute-start(bf16[32,1600]{1,0:T(8,128)(2,1)} %param.11), channel_id=1, source_target_pairs={{0,48},{16,0},{32,16},{48,32},{1,49},{17,1},{33,17},{49,33},{2,50}... | collective-permute-start | bytes 307208 | tf_op jit(solution)/shard_map/ppermute | solution.py:22
  18.5 2.4 %collective-permute-start.8 = (bf16[32,1600]{1,0:T(8,128)(2,1)}, bf16[32,1600]{1,0:T(8,128)(2,1)S(1)}, u32[]{:S(2)}, u32[]{:S(2)}) collective-permute-start(bf16[32,1600]{1,0:T(8,128)(2,1)} %param.11), channel_id=1, source_target_pairs={{0,32},{16,48},{32,0},{48,16},{1,33},{17,49},{33,1},{49,17},{2,34}... | collective-permute-start | bytes 307208 | tf_op jit(solution)/shard_map/ppermute | solution.py:22
  21.0 2.5 %collective-permute-start.9 = (bf16[32,1600]{1,0:T(8,128)(2,1)}, bf16[32,1600]{1,0:T(8,128)(2,1)S(1)}, u32[]{:S(2)}, u32[]{:S(2)}) collective-permute-start(bf16[32,1600]{1,0:T(8,128)(2,1)} %param.11), channel_id=1, source_target_pairs={{0,16},{16,32},{32,48},{48,0},{1,17},{17,33},{33,49},{49,1},{2,18}... | collective-permute-start | bytes 307208 | tf_op jit(solution)/shard_map/ppermute | solution.py:22
  23.5 2.2 %collective-permute-done.8 = bf16[32,1600]{1,0:T(8,128)(2,1)S(1)} collective-permute-done((bf16[32,1600]{1,0:T(8,128)(2,1)}, bf16[32,1600]{1,0:T(8,128)(2,1)S(1)}, u32[]{:S(2)}, u32[]{:S(2)}) %collective-permute-start.8) | collective-permute-done | bytes 102432 | tf_op jit(solution)/shard_map/ppermute | solution.py:22
  25.7 2.1 %collective-permute-done.9 = bf16[32,1600]{1,0:T(8,128)(2,1)S(1)} collective-permute-done((bf16[32,1600]{1,0:T(8,128)(2,1)}, bf16[32,1600]{1,0:T(8,128)(2,1)S(1)}, u32[]{:S(2)}, u32[]{:S(2)}) %collective-permute-start.9) | collective-permute-done | bytes 102432 | tf_op jit(solution)/shard_map/ppermute | solution.py:22
  27.9 1.7 %pad_maximum_fusion.1 = bf16[128,1600]{1,0:T(8,128)(2,1)} fusion(bf16[32,1600]{1,0:T(8,128)(2,1)S(1)} %collective-permute-done.9, bf16[32,1600]{1,0:T(8,128)(2,1)S(1)} %collective-permute-done.8, bf16[32,1600]{1,0:T(8,128)(2,1)S(1)} %collective-permute-done.7, bf16[32,1600]{1,0:T(8,128)(2,1)} %param.11), kind=kLoop, calls=%fused_computation.58 | loop fusion | flops 1638400 | bytes 819200 | tf_op jit(solution)/shard_map/concatenate | solution.py:129
  29.6 5.7 %collective-permute-start = (bf16[128,1616]{1,0:T(8,128)(2,1)S(1)}, bf16[128,1616]{1,0:T(8,128)(2,1)S(1)}, u32[]{:S(2)}, u32[]{:S(2)}) collective-permute-start(bf16[128,1616]{1,0:T(8,128)(2,1)S(1)} %pad_maximum_fusion), channel_id=1, source_target_pairs={{0,7},{1,0},{2,1},{3,2},{4,3},{5,4},{6,5},{7,6},{8,15},{9,8},{10,9... | collective-permute-start | bytes 1241096 | tf_op jit(solution)/shard_map/ppermute | solution.py:22
  35.2 1.9 %collective-permute-start.3 = (bf16[128,1616]{1,0:T(8,128)(2,1)S(1)}, bf16[128,1616]{1,0:T(8,128)(2,1)S(1)}, u32[]{:S(2)}, u32[]{:S(2)}) collective-permute-start(bf16[128,1616]{1,0:T(8,128)(2,1)S(1)} %pad_maximum_fusion), channel_id=1, source_target_pairs={{0,1},{1,2},{2,3},{3,4},{4,5},{5,6},{6,7},{7,0},{8,9},{9,10},{10,1... | collective-permute-start | bytes 1241096 | tf_op jit(solution)/shard_map/ppermute | solution.py:22
  37.2 0.2 add_reduce_fusion.7
  37.4 1.9 %fusion.13.ids_ref = s32[2048,1]{1,0:T(8,128)} fusion(s32[]{:T(128)S(6)} %axis_index.25, s32[]{:T(128)S(6)} %axis_index.23), kind=kLoop, calls=%fused_computation.32 | loop fusion | flops 143360 | bytes 8200 | tf_op jit(solution)/shard_map/add | solution.py:134
  39.3 0.8 slice_dynamic-update-slice_fusion.7
  40.1 2.4 %collective-permute-done = bf16[128,1616]{1,0:T(8,128)(2,1)S(1)} collective-permute-done((bf16[128,1616]{1,0:T(8,128)(2,1)S(1)}, bf16[128,1616]{1,0:T(8,128)(2,1)S(1)}, u32[]{:S(2)}, u32[]{:S(2)}) %collective-permute-start) | collective-permute-done | bytes 413728 | tf_op jit(solution)/shard_map/ppermute | solution.py:22
  42.5 5.3 %collective-permute-start.1 = (bf16[128,1616]{1,0:T(8,128)(2,1)S(1)}, bf16[128,1616]{1,0:T(8,128)(2,1)S(1)}, u32[]{:S(2)}, u32[]{:S(2)}) collective-permute-start(bf16[128,1616]{1,0:T(8,128)(2,1)S(1)} %collective-permute-done), channel_id=1, source_target_pairs={{0,7},{1,0},{2,1},{3,2},{4,3},{5,4},{6,5},{7,6},{8,15},{9,8},{10,9... | collective-permute-start | bytes 1241096 | tf_op jit(solution)/shard_map/ppermute | solution.py:22
  47.8 1.9 %collective-permute-start.4 = (bf16[128,1616]{1,0:T(8,128)(2,1)S(1)}, bf16[128,1616]{1,0:T(8,128)(2,1)S(1)}, u32[]{:S(2)}, u32[]{:S(2)}) collective-permute-start(bf16[128,1616]{1,0:T(8,128)(2,1)S(1)} %collective-permute-done.3), channel_id=1, source_target_pairs={{0,1},{1,2},{2,3},{3,4},{4,5},{5,6},{6,7},{7,0},{8,9},{9,10},{10,1... | collective-permute-start | bytes 1241096 | tf_op jit(solution)/shard_map/ppermute | solution.py:22
  49.7 0.2 add_reduce_fusion.6
  49.9 0.2 add_reduce_fusion
  50.1 0.8 slice_dynamic-update-slice_fusion.6
  50.9 3.2 %collective-permute-done.1 = bf16[128,1616]{1,0:T(8,128)(2,1)S(1)} collective-permute-done((bf16[128,1616]{1,0:T(8,128)(2,1)S(1)}, bf16[128,1616]{1,0:T(8,128)(2,1)S(1)}, u32[]{:S(2)}, u32[]{:S(2)}) %collective-permute-start.1) | collective-permute-done | bytes 413728 | tf_op jit(solution)/shard_map/ppermute | solution.py:22
  54.1 5.4 %collective-permute-start.2 = (bf16[128,1616]{1,0:T(8,128)(2,1)S(1)}, bf16[128,1616]{1,0:T(8,128)(2,1)S(1)}, u32[]{:S(2)}, u32[]{:S(2)}) collective-permute-start(bf16[128,1616]{1,0:T(8,128)(2,1)S(1)} %collective-permute-done.1), channel_id=1, source_target_pairs={{0,7},{1,0},{2,1},{3,2},{4,3},{5,4},{6,5},{7,6},{8,15},{9,8},{10,9... | collective-permute-start | bytes 1241096 | tf_op jit(solution)/shard_map/ppermute | solution.py:22
  59.6 1.9 %collective-permute-start.5 = (bf16[128,1616]{1,0:T(8,128)(2,1)S(1)}, bf16[128,1616]{1,0:T(8,128)(2,1)S(1)}, u32[]{:S(2)}, u32[]{:S(2)}) collective-permute-start(bf16[128,1616]{1,0:T(8,128)(2,1)S(1)} %collective-permute-done.4), channel_id=1, source_target_pairs={{0,1},{1,2},{2,3},{3,4},{4,5},{5,6},{6,7},{7,0},{8,9},{9,10},{10,1... | collective-permute-start | bytes 1241096 | tf_op jit(solution)/shard_map/ppermute | solution.py:22
  61.5 0.2 add_reduce_fusion.5
  61.7 0.2 add_reduce_fusion.1
  61.9 0.8 slice_dynamic-update-slice_fusion.5
  62.7 7.6 %collective-permute-done.5 = bf16[128,1616]{1,0:T(8,128)(2,1)S(1)} collective-permute-done((bf16[128,1616]{1,0:T(8,128)(2,1)S(1)}, bf16[128,1616]{1,0:T(8,128)(2,1)S(1)}, u32[]{:S(2)}, u32[]{:S(2)}) %collective-permute-start.5) | collective-permute-done | bytes 413728 | tf_op jit(solution)/shard_map/ppermute | solution.py:22
  70.2 1.9 %collective-permute-start.6 = (bf16[128,1616]{1,0:T(8,128)(2,1)S(1)}, bf16[128,1616]{1,0:T(8,128)(2,1)S(1)}, u32[]{:S(2)}, u32[]{:S(2)}) collective-permute-start(bf16[128,1616]{1,0:T(8,128)(2,1)S(1)} %collective-permute-done.5), channel_id=1, source_target_pairs={{0,1},{1,2},{2,3},{3,4},{4,5},{5,6},{6,7},{7,0},{8,9},{9,10},{10,1... | collective-permute-start | bytes 1241096 | tf_op jit(solution)/shard_map/ppermute | solution.py:22
  72.2 0.2 add_reduce_fusion.4
  72.3 0.2 add_reduce_fusion.2
  72.5 0.8 slice_dynamic-update-slice_fusion.4
  73.4 7.3 %collective-permute-done.6 = bf16[128,1616]{1,0:T(8,128)(2,1)S(1)} collective-permute-done((bf16[128,1616]{1,0:T(8,128)(2,1)S(1)}, bf16[128,1616]{1,0:T(8,128)(2,1)S(1)}, u32[]{:S(2)}, u32[]{:S(2)}) %collective-permute-start.6) | collective-permute-done | bytes 413728 | tf_op jit(solution)/shard_map/ppermute | solution.py:22
  80.7 0.2 add_reduce_fusion.3
  80.9 0.8 slice_dynamic-update-slice_fusion.3
  81.8 0.8 slice_dynamic-update-slice_fusion.2
  82.6 0.8 slice_dynamic-update-slice_fusion.1
  83.4 0.8 slice_dynamic-update-slice_fusion.rows_ref
  84.2 2.7 %all-gather.2.cloned.1.call-done.vocab_ref = bf16[2048,1600]{1,0:T(8,128)(2,1)} async-done(((bf16[128,1600]{1,0:T(8,128)(2,1)}), bf16[2048,1600]{1,0:T(8,128)(2,1)}) %all-gather.2.cloned.1.call-update) | async-done | bytes 6553616 | tf_op jit(solution)/shard_map/all_gather | solution.py:129
  86.9 13.3 %shard_map.68 = (f32[1,1024]{1,0:T(1,128)}, f32[1,1024]{1,0:T(1,128)}, f32[1,1024]{1,0:T(1,128)}, f32[1,1024]{1,0:T(1,128)}) custom-call(bf16[1024,1600]{1,0:T(8,128)(2,1)} %slice_dynamic-update-slice_fusion.rows_ref, bf16[2048,1600]{1,0:T(8,128)(2,1)} %all-gather.2.cloned.1.call-done.vocab_ref, s32[1,1024]{1,0:T(1,128)} %bitcast.18, s32[2048,1]{1,0:T(8,128)} %fusion.13.ids_ref), custom_call_target="tpu_custom_call" | custom-call | flops 6710886400 | bytes 9830400 | tf_op jit(solution)/shard_map/pallas_call | solution.py:72
  100.3 0.7 maximum_bitcast_fusion
  101.0 12.9 %all_to_all.6 = f32[4,8,128]{2,0,1:T(4,128)S(1)} all-to-all(f32[4,8,128]{2,0,1:T(4,128)S(1)} %fusion.31), channel_id=1, replica_groups=mesh['z'=8,'x'=4,'c'=2,'y'=8] {'y'}, dimensions={1} | all-to-all | bytes 32768 | tf_op jit(solution)/shard_map/all_to_all | solution.py:139
  114.0 0.5 subtract_multiply_fusion
  (26 shorter events, 0.3 us)
Async XLA Ops:
  7.2 79.8 %all-gather.2.cloned.1.call-start = ((), (), s32[]{:S(2)}) async-start(), calls=%async_computation.1 | async-start | bytes 7241728 | tf_op jit(solution)/shard_map/all_gather | solution.py:129
  13.3 10.2 %collective-permute-start.7 = (bf16[32,1600]{1,0:T(8,128)(2,1)}, bf16[32,1600]{1,0:T(8,128)(2,1)S(1)}, u32[]{:S(2)}, u32[]{:S(2)}) collective-permute-start(bf16[32,1600]{1,0:T(8,128)(2,1)} %param.11), channel_id=1, source_target_pairs={{0,48},{16,0},{32,16},{48,32},{1,49},{17,1},{33,17},{49,33},{2,50}... | collective-permute-start | bytes 307208 | tf_op jit(solution)/shard_map/ppermute | solution.py:22
  18.5 7.2 %collective-permute-start.8 = (bf16[32,1600]{1,0:T(8,128)(2,1)}, bf16[32,1600]{1,0:T(8,128)(2,1)S(1)}, u32[]{:S(2)}, u32[]{:S(2)}) collective-permute-start(bf16[32,1600]{1,0:T(8,128)(2,1)} %param.11), channel_id=1, source_target_pairs={{0,32},{16,48},{32,0},{48,16},{1,33},{17,49},{33,1},{49,17},{2,34}... | collective-permute-start | bytes 307208 | tf_op jit(solution)/shard_map/ppermute | solution.py:22
  21.0 6.9 %collective-permute-start.9 = (bf16[32,1600]{1,0:T(8,128)(2,1)}, bf16[32,1600]{1,0:T(8,128)(2,1)S(1)}, u32[]{:S(2)}, u32[]{:S(2)}) collective-permute-start(bf16[32,1600]{1,0:T(8,128)(2,1)} %param.11), channel_id=1, source_target_pairs={{0,16},{16,32},{32,48},{48,0},{1,17},{17,33},{33,49},{49,1},{2,18}... | collective-permute-start | bytes 307208 | tf_op jit(solution)/shard_map/ppermute | solution.py:22
  29.6 12.9 %collective-permute-start = (bf16[128,1616]{1,0:T(8,128)(2,1)S(1)}, bf16[128,1616]{1,0:T(8,128)(2,1)S(1)}, u32[]{:S(2)}, u32[]{:S(2)}) collective-permute-start(bf16[128,1616]{1,0:T(8,128)(2,1)S(1)} %pad_maximum_fusion), channel_id=1, source_target_pairs={{0,7},{1,0},{2,1},{3,2},{4,3},{5,4},{6,5},{7,6},{8,15},{9,8},{10,9... | collective-permute-start | bytes 1241096 | tf_op jit(solution)/shard_map/ppermute | solution.py:22
  35.2 12.6 %collective-permute-start.3 = (bf16[128,1616]{1,0:T(8,128)(2,1)S(1)}, bf16[128,1616]{1,0:T(8,128)(2,1)S(1)}, u32[]{:S(2)}, u32[]{:S(2)}) collective-permute-start(bf16[128,1616]{1,0:T(8,128)(2,1)S(1)} %pad_maximum_fusion), channel_id=1, source_target_pairs={{0,1},{1,2},{2,3},{3,4},{4,5},{5,6},{6,7},{7,0},{8,9},{9,10},{10,1... | collective-permute-start | bytes 1241096 | tf_op jit(solution)/shard_map/ppermute | solution.py:22
  42.5 11.6 %collective-permute-start.1 = (bf16[128,1616]{1,0:T(8,128)(2,1)S(1)}, bf16[128,1616]{1,0:T(8,128)(2,1)S(1)}, u32[]{:S(2)}, u32[]{:S(2)}) collective-permute-start(bf16[128,1616]{1,0:T(8,128)(2,1)S(1)} %collective-permute-done), channel_id=1, source_target_pairs={{0,7},{1,0},{2,1},{3,2},{4,3},{5,4},{6,5},{7,6},{8,15},{9,8},{10,9... | collective-permute-start | bytes 1241096 | tf_op jit(solution)/shard_map/ppermute | solution.py:22
  47.8 11.7 %collective-permute-start.4 = (bf16[128,1616]{1,0:T(8,128)(2,1)S(1)}, bf16[128,1616]{1,0:T(8,128)(2,1)S(1)}, u32[]{:S(2)}, u32[]{:S(2)}) collective-permute-start(bf16[128,1616]{1,0:T(8,128)(2,1)S(1)} %collective-permute-done.3), channel_id=1, source_target_pairs={{0,1},{1,2},{2,3},{3,4},{4,5},{5,6},{6,7},{7,0},{8,9},{9,10},{10,1... | collective-permute-start | bytes 1241096 | tf_op jit(solution)/shard_map/ppermute | solution.py:22
  54.1 18.0 %collective-permute-start.2 = (bf16[128,1616]{1,0:T(8,128)(2,1)S(1)}, bf16[128,1616]{1,0:T(8,128)(2,1)S(1)}, u32[]{:S(2)}, u32[]{:S(2)}) collective-permute-start(bf16[128,1616]{1,0:T(8,128)(2,1)S(1)} %collective-permute-done.1), channel_id=1, source_target_pairs={{0,7},{1,0},{2,1},{3,2},{4,3},{5,4},{6,5},{7,6},{8,15},{9,8},{10,9... | collective-permute-start | bytes 1241096 | tf_op jit(solution)/shard_map/ppermute | solution.py:22
  59.6 10.7 %collective-permute-start.5 = (bf16[128,1616]{1,0:T(8,128)(2,1)S(1)}, bf16[128,1616]{1,0:T(8,128)(2,1)S(1)}, u32[]{:S(2)}, u32[]{:S(2)}) collective-permute-start(bf16[128,1616]{1,0:T(8,128)(2,1)S(1)} %collective-permute-done.4), channel_id=1, source_target_pairs={{0,1},{1,2},{2,3},{3,4},{4,5},{5,6},{6,7},{7,0},{8,9},{9,10},{10,1... | collective-permute-start | bytes 1241096 | tf_op jit(solution)/shard_map/ppermute | solution.py:22
  70.2 10.5 %collective-permute-start.6 = (bf16[128,1616]{1,0:T(8,128)(2,1)S(1)}, bf16[128,1616]{1,0:T(8,128)(2,1)S(1)}, u32[]{:S(2)}, u32[]{:S(2)}) collective-permute-start(bf16[128,1616]{1,0:T(8,128)(2,1)S(1)} %collective-permute-done.5), channel_id=1, source_target_pairs={{0,1},{1,2},{2,3},{3,4},{4,5},{5,6},{6,7},{7,0},{8,9},{9,10},{10,1... | collective-permute-start | bytes 1241096 | tf_op jit(solution)/shard_map/ppermute | solution.py:22
  80.9 6.0 %copy-start.1 = (s32[1024]{0:T(1024)}, s32[1024]{0:T(1024)S(1)}, u32[]{:S(2)}) copy-start(s32[1024]{0:T(1024)S(1)} %constant_dynamic-update-slice_fusion.1) | copy-start | bytes 12292
  86.9 27.0 %copy-start = (s32[128]{0:T(128)S(1)}, s32[128]{0:T(128)}, u32[]{:S(2)}) copy-start(s32[128]{0:T(128)} %param.13) | copy-start | bytes 1540
Sparse Core Ops, SparseCore 0:
  29.7 57.2 all-gather.1

commit v12 on v10

--- a/solution.py
+++ b/solution.py
@@ -1,7 +1,10 @@
+import functools
+
 import jax
 import jax.numpy as jnp
 from jax import lax
 from jax.experimental import pallas as pl
+from jax.experimental.pallas import tpu as pltpu
 from jax.sharding import Mesh, PartitionSpec as P
 
 FLAT = ("z", "x", "c", "y")
@@ -33,8 +36,17 @@
     return (fold_top, jnp.sum(weights, axis=1), jnp.sum(weights * shifted, axis=1), chosen)
 
 
-def stats_kernel(rows_ref, vocab_ref, wanted_ref, ids_ref, top_ref, total_ref, spread_ref, chosen_ref):
+def stats_kernel(
+    sizes, where_ref, rows_ref, vocab_ref, wanted_ref, top_ref, total_ref, spread_ref, chosen_ref
+):
     j = pl.program_id(0)
+    nx, nc, ny, width = sizes
+    tile = vocab_ref.shape[0]
+    x, y = where_ref[0], where_ref[1]
+    local = j * tile + lax.broadcasted_iota(jnp.int32, (tile, 1), 0)
+    group, place = local // (nx * width), local % (nx * width)
+    far_x = (x + place // width) % nx
+    ids = ((((group // nc) * nx + far_x) * nc + group % nc) * ny + y) * width + place % width
 
     @pl.when(j == 0)
     def _():
@@ -46,7 +58,7 @@
     logits = lax.dot_general(
         vocab_ref[...], rows_ref[...], (((1,), (1,)), ((), ())), preferred_element_type=jnp.float32
     )
-    hit = ids_ref[...] == wanted_ref[...]
+    hit = ids == wanted_ref[...]
     chosen_ref[...] += jnp.sum(jnp.where(hit, logits, 0.0), axis=0, keepdims=True)
     fold = jnp.max(logits, axis=0, keepdims=True)
     shifted = logits - fold
@@ -65,18 +77,18 @@
     top_ref[...] = top
 
 
-def row_stats(rows, vocab, wanted, ids, tile=256):
+def row_stats(rows, vocab, wanted, where, sizes, tile=512):
     count, dim = rows.shape
     width = vocab.shape[0]
     line = pl.BlockSpec((1, count), lambda j: (0, 0))
     outs = pl.pallas_call(
-        stats_kernel,
+        functools.partial(stats_kernel, sizes),
         grid=(width // tile,),
         in_specs=[
+            pl.BlockSpec(memory_space=pltpu.SMEM),
             pl.BlockSpec((count, dim), lambda j: (0, 0)),
             pl.BlockSpec((tile, dim), lambda j: (j, 0)),
             line,
-            pl.BlockSpec((tile, 1), lambda j: (j, 0)),
         ],
         out_specs=[line, line, line, line],
         out_shape=[jax.ShapeDtypeStruct((1, count), jnp.float32)] * 4,
@@ -85,7 +97,7 @@
             transcendentals=count * width,
             bytes_accessed=2 * (count + width) * dim,
         ),
-    )(rows, vocab, wanted.reshape(1, count), ids.reshape(width, 1))
+    )(where, rows, vocab, wanted.reshape(1, count))
     return tuple(o.reshape(count) for o in outs)
 
 
@@ -128,13 +140,8 @@
     )
 
     whole = lax.all_gather(jnp.concatenate(near, axis=0), ("z", "c"), axis=0, tiled=True)
-    local = jnp.arange(whole.shape[0], dtype=jnp.int32)
-    group, place = local // (nx * width), local % (nx * width)
-    far_z, far_c = group // nc, group % nc
-    far_x = (x + place // width) % nx
-    ids = (((far_z * nx + far_x) * nc + far_c) * ny + y) * width + place % width
-
-    stats = row_stats(rows, whole, wanted, ids)
+    where = jnp.stack([x, y]).astype(jnp.int32)
+    stats = row_stats(rows, whole, wanted, where, (nx, nc, ny, width))
 
     packed = jnp.roll(jnp.stack(stats).reshape(4, ny, mine), y, axis=1).reshape(4, ny * mine)
     got = lax.all_to_all(packed, "y", 1, 1, tiled=True).reshape(4, ny, mine)

time: 121 us -> 122 us (level)
  the two profiles are of different devices: /device:TPU:450 before, /device:TPU:1 now
where the time goes in v12:
time: 122 us; the launch traced here: 121 us
  starting transfers between devices  33.7 us (28%)
  waiting for transfers between devices  25.1 us (21%)
  Pallas kernels  17.1 us (14%)
  between operations  14.3 us (12%)
  blocking collectives  12.9 us (11%)
  other arithmetic  9.48 us (8%)
  local copies, waits for them, and re-layouts  8.27 us (7%)
    ppermute x10, starting transfers between devices, shift(): lax.ppermute(value, axis, [(i, (i + step) % size) for i in range(size)])  33.6 us
    ppermute x10, waiting for transfers between devices, shift(): lax.ppermute(value, axis, [(i, (i + step) % size) for i in range(size)])  23.4 us
    pallas_call x1, Pallas kernels, row_stats(): pl.pallas_call(functools.partial(stats_kernel, sizes), grid=(width // til...  17.1 us
    all_to_all x1, blocking collectives, on_device(): got = lax.all_to_all(packed, 'y', 1, 1, tiled=True).reshape(4, ny, mine)  12.9 us
    unnamed x19, local copies, waits for them, and re-layouts  7 us
    another operation x3, other arithmetic  3.25 us
  transfers between devices with their start and end apart: 11, of which 5 were waited for; matrix products, arithmetic and copies ran while one was open for 12% of the time, Pallas kernels for 0%

profile of v12, /device:TPU:1, one launch (start us, length us, event | category | flops | bytes accessed | tf_op | source)
XLA Modules:
  0.0 120.8 jit_solution(3477118697874616329)
XLA Ops:
  7.2 0.0 all-gather.2.cloned.1.call-start
  7.2 5.2 %collective-permute-start = (bf16[32,1600]{1,0:T(8,128)(2,1)}, bf16[32,1600]{1,0:T(8,128)(2,1)S(1)}, u32[]{:S(2)}, u32[]{:S(2)}) collective-permute-start(bf16[32,1600]{1,0:T(8,128)(2,1)} %param.11), channel_id=1, source_target_pairs={{0,48},{16,0},{32,16},{48,32},{1,49},{17,1},{33,17},{49,33},{2,50}... | collective-permute-start | bytes 307208 | tf_op jit(solution)/shard_map/ppermute | solution.py:25
  12.4 2.4 %collective-permute-start.1 = (bf16[32,1600]{1,0:T(8,128)(2,1)}, bf16[32,1600]{1,0:T(8,128)(2,1)S(1)}, u32[]{:S(2)}, u32[]{:S(2)}) collective-permute-start(bf16[32,1600]{1,0:T(8,128)(2,1)} %param.11), channel_id=1, source_target_pairs={{0,32},{16,48},{32,0},{48,16},{1,33},{17,49},{33,1},{49,17},{2,34}... | collective-permute-start | bytes 307208 | tf_op jit(solution)/shard_map/ppermute | solution.py:25
  14.9 2.5 %collective-permute-start.2 = (bf16[32,1600]{1,0:T(8,128)(2,1)}, bf16[32,1600]{1,0:T(8,128)(2,1)S(1)}, u32[]{:S(2)}, u32[]{:S(2)}) collective-permute-start(bf16[32,1600]{1,0:T(8,128)(2,1)} %param.11), channel_id=1, source_target_pairs={{0,16},{16,32},{32,48},{48,0},{1,17},{17,33},{33,49},{49,1},{2,18}... | collective-permute-start | bytes 307208 | tf_op jit(solution)/shard_map/ppermute | solution.py:25
  17.4 0.6 compare_reduce_fusion
  18.0 0.6 compare_reduce_fusion.1
  18.7 1.2 %copy.13 = bf16[128,1600]{1,0:T(8,128)(2,1)S(1)} copy(bf16[128,1600]{0,1:T(8,128)(2,1)} %param.9) | data formatting | bytes 819200 | tf_op args[0]
  19.9 0.2 fusion
  20.1 2.0 %fusion.5 = (bf16[128,1]{0,1:T(2,128)(2,1)S(1)}, bf16[128,1]{0,1:T(2,128)(2,1)S(1)}) fusion(pred[]{:T(512)} %compare_reduce_fusion, s32[128]{0:T(128)} %param.12, pred[]{:T(512)} %compare_reduce_fusion.1), kind=kLoop, calls=%fused_computation.48 | loop fusion | flops 2944 | bytes 1026 | tf_op jit(solution)/shard_map/reshape.85
  22.1 0.1 copy.14
  22.2 0.1 copy.15
  22.3 0.9 fusion.2
  23.2 0.2 scatter.9
  23.4 0.1 pad_maximum_fusion
  23.5 1.7 %pad_maximum_fusion.1 = bf16[128,1600]{1,0:T(8,128)(2,1)} fusion(bf16[32,1600]{1,0:T(8,128)(2,1)S(1)} %collective-permute-done.2, bf16[32,1600]{1,0:T(8,128)(2,1)S(1)} %collective-permute-done.1, bf16[32,1600]{1,0:T(8,128)(2,1)S(1)} %collective-permute-done, bf16[32,1600]{1,0:T(8,128)(2,1)} %param.11), kind=kLoop, calls=%fused_computation.13 | loop fusion | flops 1638400 | bytes 819200 | tf_op jit(solution)/shard_map/concatenate | solution.py:142
  25.3 0.6 pad_add_fusion.where_ref
  25.9 5.1 %collective-permute-start.3 = (bf16[128,1616]{1,0:T(8,128)(2,1)S(1)}, bf16[128,1616]{1,0:T(8,128)(2,1)S(1)}, u32[]{:S(2)}, u32[]{:S(2)}) collective-permute-start(bf16[128,1616]{1,0:T(8,128)(2,1)S(1)} %pad_maximum_fusion), channel_id=1, source_target_pairs={{0,7},{1,0},{2,1},{3,2},{4,3},{5,4},{6,5},{7,6},{8,15},{9,8},{10,9... | collective-permute-start | bytes 1241096 | tf_op jit(solution)/shard_map/ppermute | solution.py:25
  31.0 1.9 %collective-permute-start.6 = (bf16[128,1616]{1,0:T(8,128)(2,1)S(1)}, bf16[128,1616]{1,0:T(8,128)(2,1)S(1)}, u32[]{:S(2)}, u32[]{:S(2)}) collective-permute-start(bf16[128,1616]{1,0:T(8,128)(2,1)S(1)} %pad_maximum_fusion), channel_id=1, source_target_pairs={{0,1},{1,2},{2,3},{3,4},{4,5},{5,6},{6,7},{7,0},{8,9},{9,10},{10,1... | collective-permute-start | bytes 1241096 | tf_op jit(solution)/shard_map/ppermute | solution.py:25
  32.9 0.2 add_reduce_fusion.7
  33.1 0.8 slice_dynamic-update-slice_fusion.7
  33.9 4.6 %collective-permute-done.3 = bf16[128,1616]{1,0:T(8,128)(2,1)S(1)} collective-permute-done((bf16[128,1616]{1,0:T(8,128)(2,1)S(1)}, bf16[128,1616]{1,0:T(8,128)(2,1)S(1)}, u32[]{:S(2)}, u32[]{:S(2)}) %collective-permute-start.3) | collective-permute-done | bytes 413728 | tf_op jit(solution)/shard_map/ppermute | solution.py:25
  38.5 5.3 %collective-permute-start.4 = (bf16[128,1616]{1,0:T(8,128)(2,1)S(1)}, bf16[128,1616]{1,0:T(8,128)(2,1)S(1)}, u32[]{:S(2)}, u32[]{:S(2)}) collective-permute-start(bf16[128,1616]{1,0:T(8,128)(2,1)S(1)} %collective-permute-done.3), channel_id=1, source_target_pairs={{0,7},{1,0},{2,1},{3,2},{4,3},{5,4},{6,5},{7,6},{8,15},{9,8},{10,9... | collective-permute-start | bytes 1241096 | tf_op jit(solution)/shard_map/ppermute | solution.py:25
  43.9 1.9 %collective-permute-start.7 = (bf16[128,1616]{1,0:T(8,128)(2,1)S(1)}, bf16[128,1616]{1,0:T(8,128)(2,1)S(1)}, u32[]{:S(2)}, u32[]{:S(2)}) collective-permute-start(bf16[128,1616]{1,0:T(8,128)(2,1)S(1)} %collective-permute-done.6), channel_id=1, source_target_pairs={{0,1},{1,2},{2,3},{3,4},{4,5},{5,6},{6,7},{7,0},{8,9},{9,10},{10,1... | collective-permute-start | bytes 1241096 | tf_op jit(solution)/shard_map/ppermute | solution.py:25
  45.8 0.2 add_reduce_fusion.6
  46.0 0.2 add_reduce_fusion
  46.2 0.8 slice_dynamic-update-slice_fusion.6
  47.0 3.5 %collective-permute-done.4 = bf16[128,1616]{1,0:T(8,128)(2,1)S(1)} collective-permute-done((bf16[128,1616]{1,0:T(8,128)(2,1)S(1)}, bf16[128,1616]{1,0:T(8,128)(2,1)S(1)}, u32[]{:S(2)}, u32[]{:S(2)}) %collective-permute-start.4) | collective-permute-done | bytes 413728 | tf_op jit(solution)/shard_map/ppermute | solution.py:25
  50.5 5.4 %collective-permute-start.5 = (bf16[128,1616]{1,0:T(8,128)(2,1)S(1)}, bf16[128,1616]{1,0:T(8,128)(2,1)S(1)}, u32[]{:S(2)}, u32[]{:S(2)}) collective-permute-start(bf16[128,1616]{1,0:T(8,128)(2,1)S(1)} %collective-permute-done.4), channel_id=1, source_target_pairs={{0,7},{1,0},{2,1},{3,2},{4,3},{5,4},{6,5},{7,6},{8,15},{9,8},{10,9... | collective-permute-start | bytes 1241096 | tf_op jit(solution)/shard_map/ppermute | solution.py:25
  55.9 1.9 %collective-permute-start.8 = (bf16[128,1616]{1,0:T(8,128)(2,1)S(1)}, bf16[128,1616]{1,0:T(8,128)(2,1)S(1)}, u32[]{:S(2)}, u32[]{:S(2)}) collective-permute-start(bf16[128,1616]{1,0:T(8,128)(2,1)S(1)} %collective-permute-done.7), channel_id=1, source_target_pairs={{0,1},{1,2},{2,3},{3,4},{4,5},{5,6},{6,7},{7,0},{8,9},{9,10},{10,1... | collective-permute-start | bytes 1241096 | tf_op jit(solution)/shard_map/ppermute | solution.py:25
  57.9 0.2 add_reduce_fusion.5
  58.1 0.2 add_reduce_fusion.1
  58.2 0.8 slice_dynamic-update-slice_fusion.5
  59.0 7.9 %collective-permute-done.8 = bf16[128,1616]{1,0:T(8,128)(2,1)S(1)} collective-permute-done((bf16[128,1616]{1,0:T(8,128)(2,1)S(1)}, bf16[128,1616]{1,0:T(8,128)(2,1)S(1)}, u32[]{:S(2)}, u32[]{:S(2)}) %collective-permute-start.8) | collective-permute-done | bytes 413728 | tf_op jit(solution)/shard_map/ppermute | solution.py:25
  66.9 1.9 %collective-permute-start.9 = (bf16[128,1616]{1,0:T(8,128)(2,1)S(1)}, bf16[128,1616]{1,0:T(8,128)(2,1)S(1)}, u32[]{:S(2)}, u32[]{:S(2)}) collective-permute-start(bf16[128,1616]{1,0:T(8,128)(2,1)S(1)} %collective-permute-done.8), channel_id=1, source_target_pairs={{0,1},{1,2},{2,3},{3,4},{4,5},{5,6},{6,7},{7,0},{8,9},{9,10},{10,1... | collective-permute-start | bytes 1241096 | tf_op jit(solution)/shard_map/ppermute | solution.py:25
  68.8 0.2 add_reduce_fusion.4
  69.0 0.2 add_reduce_fusion.2
  69.2 0.8 slice_dynamic-update-slice_fusion.4
  70.1 7.3 %collective-permute-done.9 = bf16[128,1616]{1,0:T(8,128)(2,1)S(1)} collective-permute-done((bf16[128,1616]{1,0:T(8,128)(2,1)S(1)}, bf16[128,1616]{1,0:T(8,128)(2,1)S(1)}, u32[]{:S(2)}, u32[]{:S(2)}) %collective-permute-start.9) | collective-permute-done | bytes 413728 | tf_op jit(solution)/shard_map/ppermute | solution.py:25
  77.4 0.2 add_reduce_fusion.3
  77.6 0.8 slice_dynamic-update-slice_fusion.3
  78.5 0.8 slice_dynamic-update-slice_fusion.2
  79.3 0.8 slice_dynamic-update-slice_fusion.1
  80.1 0.8 slice_dynamic-update-slice_fusion.rows_ref
  80.9 1.7 %all-gather.2.cloned.1.call-done.vocab_ref = bf16[2048,1600]{1,0:T(8,128)(2,1)} async-done(((bf16[128,1600]{1,0:T(8,128)(2,1)}), bf16[2048,1600]{1,0:T(8,128)(2,1)}) %all-gather.2.cloned.1.call-update) | async-done | bytes 6553616 | tf_op jit(solution)/shard_map/all_gather | solution.py:142
  82.6 17.1 %shard_map.68 = (f32[1,1024]{1,0:T(1,128)}, f32[1,1024]{1,0:T(1,128)}, f32[1,1024]{1,0:T(1,128)}, f32[1,1024]{1,0:T(1,128)}) custom-call(s32[2]{0:T(128)} %pad_add_fusion.where_ref, bf16[1024,1600]{1,0:T(8,128)(2,1)} %slice_dynamic-update-slice_fusion.rows_ref, bf16[2048,1600]{1,0:T(8,128)(2,1)} %all-gather.2.cloned.1.call-done.vocab_ref, s32[1,1024]{1,0:T(1,128)} %bitcast.20), custom_call_target="tpu_custom_call" | custom-call | flops 6710886400 | bytes 9830400 | tf_op jit(solution)/shard_map/pallas_call | solution.py:84
  99.7 0.7 maximum_bitcast_fusion
  100.4 12.9 %all_to_all.6 = f32[4,8,128]{2,0,1:T(4,128)S(1)} all-to-all(f32[4,8,128]{2,0,1:T(4,128)S(1)} %fusion.3), channel_id=1, replica_groups=mesh['z'=8,'x'=4,'c'=2,'y'=8] {'y'}, dimensions={1} | all-to-all | bytes 32768 | tf_op jit(solution)/shard_map/all_to_all | solution.py:147
  113.4 0.5 subtract_multiply_fusion
  (26 shorter events, 0.2 us)
Async XLA Ops:
  7.2 75.4 %all-gather.2.cloned.1.call-start = ((), (), s32[]{:S(2)}) async-start(), calls=%async_computation.1 | async-start | bytes 7241728 | tf_op jit(solution)/shard_map/all_gather | solution.py:142
  7.2 16.3 %collective-permute-start = (bf16[32,1600]{1,0:T(8,128)(2,1)}, bf16[32,1600]{1,0:T(8,128)(2,1)S(1)}, u32[]{:S(2)}, u32[]{:S(2)}) collective-permute-start(bf16[32,1600]{1,0:T(8,128)(2,1)} %param.11), channel_id=1, source_target_pairs={{0,48},{16,0},{32,16},{48,32},{1,49},{17,1},{33,17},{49,33},{2,50}... | collective-permute-start | bytes 307208 | tf_op jit(solution)/shard_map/ppermute | solution.py:25
  12.4 11.1 %collective-permute-start.1 = (bf16[32,1600]{1,0:T(8,128)(2,1)}, bf16[32,1600]{1,0:T(8,128)(2,1)S(1)}, u32[]{:S(2)}, u32[]{:S(2)}) collective-permute-start(bf16[32,1600]{1,0:T(8,128)(2,1)} %param.11), channel_id=1, source_target_pairs={{0,32},{16,48},{32,0},{48,16},{1,33},{17,49},{33,1},{49,17},{2,34}... | collective-permute-start | bytes 307208 | tf_op jit(solution)/shard_map/ppermute | solution.py:25
  14.9 8.7 %collective-permute-start.2 = (bf16[32,1600]{1,0:T(8,128)(2,1)}, bf16[32,1600]{1,0:T(8,128)(2,1)S(1)}, u32[]{:S(2)}, u32[]{:S(2)}) collective-permute-start(bf16[32,1600]{1,0:T(8,128)(2,1)} %param.11), channel_id=1, source_target_pairs={{0,16},{16,32},{32,48},{48,0},{1,17},{17,33},{33,49},{49,1},{2,18}... | collective-permute-start | bytes 307208 | tf_op jit(solution)/shard_map/ppermute | solution.py:25
  25.9 12.7 %collective-permute-start.3 = (bf16[128,1616]{1,0:T(8,128)(2,1)S(1)}, bf16[128,1616]{1,0:T(8,128)(2,1)S(1)}, u32[]{:S(2)}, u32[]{:S(2)}) collective-permute-start(bf16[128,1616]{1,0:T(8,128)(2,1)S(1)} %pad_maximum_fusion), channel_id=1, source_target_pairs={{0,7},{1,0},{2,1},{3,2},{4,3},{5,4},{6,5},{7,6},{8,15},{9,8},{10,9... | collective-permute-start | bytes 1241096 | tf_op jit(solution)/shard_map/ppermute | solution.py:25
  31.0 12.9 %collective-permute-start.6 = (bf16[128,1616]{1,0:T(8,128)(2,1)S(1)}, bf16[128,1616]{1,0:T(8,128)(2,1)S(1)}, u32[]{:S(2)}, u32[]{:S(2)}) collective-permute-start(bf16[128,1616]{1,0:T(8,128)(2,1)S(1)} %pad_maximum_fusion), channel_id=1, source_target_pairs={{0,1},{1,2},{2,3},{3,4},{4,5},{5,6},{6,7},{7,0},{8,9},{9,10},{10,1... | collective-permute-start | bytes 1241096 | tf_op jit(solution)/shard_map/ppermute | solution.py:25
  38.5 12.0 %collective-permute-start.4 = (bf16[128,1616]{1,0:T(8,128)(2,1)S(1)}, bf16[128,1616]{1,0:T(8,128)(2,1)S(1)}, u32[]{:S(2)}, u32[]{:S(2)}) collective-permute-start(bf16[128,1616]{1,0:T(8,128)(2,1)S(1)} %collective-permute-done.3), channel_id=1, source_target_pairs={{0,7},{1,0},{2,1},{3,2},{4,3},{5,4},{6,5},{7,6},{8,15},{9,8},{10,9... | collective-permute-start | bytes 1241096 | tf_op jit(solution)/shard_map/ppermute | solution.py:25
  43.9 12.1 %collective-permute-start.7 = (bf16[128,1616]{1,0:T(8,128)(2,1)S(1)}, bf16[128,1616]{1,0:T(8,128)(2,1)S(1)}, u32[]{:S(2)}, u32[]{:S(2)}) collective-permute-start(bf16[128,1616]{1,0:T(8,128)(2,1)S(1)} %collective-permute-done.6), channel_id=1, source_target_pairs={{0,1},{1,2},{2,3},{3,4},{4,5},{5,6},{6,7},{7,0},{8,9},{9,10},{10,1... | collective-permute-start | bytes 1241096 | tf_op jit(solution)/shard_map/ppermute | solution.py:25
  50.5 18.3 %collective-permute-start.5 = (bf16[128,1616]{1,0:T(8,128)(2,1)S(1)}, bf16[128,1616]{1,0:T(8,128)(2,1)S(1)}, u32[]{:S(2)}, u32[]{:S(2)}) collective-permute-start(bf16[128,1616]{1,0:T(8,128)(2,1)S(1)} %collective-permute-done.4), channel_id=1, source_target_pairs={{0,7},{1,0},{2,1},{3,2},{4,3},{5,4},{6,5},{7,6},{8,15},{9,8},{10,9... | collective-permute-start | bytes 1241096 | tf_op jit(solution)/shard_map/ppermute | solution.py:25
  55.9 11.0 %collective-permute-start.8 = (bf16[128,1616]{1,0:T(8,128)(2,1)S(1)}, bf16[128,1616]{1,0:T(8,128)(2,1)S(1)}, u32[]{:S(2)}, u32[]{:S(2)}) collective-permute-start(bf16[128,1616]{1,0:T(8,128)(2,1)S(1)} %collective-permute-done.7), channel_id=1, source_target_pairs={{0,1},{1,2},{2,3},{3,4},{4,5},{5,6},{6,7},{7,0},{8,9},{9,10},{10,1... | collective-permute-start | bytes 1241096 | tf_op jit(solution)/shard_map/ppermute | solution.py:25
  66.9 10.5 %collective-permute-start.9 = (bf16[128,1616]{1,0:T(8,128)(2,1)S(1)}, bf16[128,1616]{1,0:T(8,128)(2,1)S(1)}, u32[]{:S(2)}, u32[]{:S(2)}) collective-permute-start(bf16[128,1616]{1,0:T(8,128)(2,1)S(1)} %collective-permute-done.8), channel_id=1, source_target_pairs={{0,1},{1,2},{2,3},{3,4},{4,5},{5,6},{6,7},{7,0},{8,9},{9,10},{10,1... | collective-permute-start | bytes 1241096 | tf_op jit(solution)/shard_map/ppermute | solution.py:25
  77.6 5.0 %copy-start.1 = (s32[1024]{0:T(1024)}, s32[1024]{0:T(1024)S(1)}, u32[]{:S(2)}) copy-start(s32[1024]{0:T(1024)S(1)} %constant_dynamic-update-slice_fusion.1) | copy-start | bytes 12292
  82.6 30.8 %copy-start = (s32[128]{0:T(128)S(1)}, s32[128]{0:T(128)}, u32[]{:S(2)}) copy-start(s32[128]{0:T(128)} %param.13) | copy-start | bytes 1540
Sparse Core Ops, SparseCore 0:
  25.4 57.1 all-gather.1

commit v13 on v10

--- a/solution.py
+++ b/solution.py
@@ -33,8 +33,10 @@
     return (fold_top, jnp.sum(weights, axis=1), jnp.sum(weights * shifted, axis=1), chosen)
 
 
-def stats_kernel(rows_ref, vocab_ref, wanted_ref, ids_ref, top_ref, total_ref, spread_ref, chosen_ref):
+def stats_kernel(rows_ref, vocab_ref, spot_ref, top_ref, total_ref, spread_ref, chosen_ref):
     j = pl.program_id(0)
+    tile = vocab_ref.shape[0]
+    position = j * tile + lax.broadcasted_iota(jnp.int32, (tile, 1), 0)
 
     @pl.when(j == 0)
     def _():
@@ -46,7 +48,7 @@
     logits = lax.dot_general(
         vocab_ref[...], rows_ref[...], (((1,), (1,)), ((), ())), preferred_element_type=jnp.float32
     )
-    hit = ids_ref[...] == wanted_ref[...]
+    hit = position == spot_ref[...]
     chosen_ref[...] += jnp.sum(jnp.where(hit, logits, 0.0), axis=0, keepdims=True)
     fold = jnp.max(logits, axis=0, keepdims=True)
     shifted = logits - fold
@@ -65,7 +67,7 @@
     top_ref[...] = top
 
 
-def row_stats(rows, vocab, wanted, ids, tile=256):
+def row_stats(rows, vocab, spot, tile=512):
     count, dim = rows.shape
     width = vocab.shape[0]
     line = pl.BlockSpec((1, count), lambda j: (0, 0))
@@ -76,7 +78,6 @@
             pl.BlockSpec((count, dim), lambda j: (0, 0)),
             pl.BlockSpec((tile, dim), lambda j: (j, 0)),
             line,
-            pl.BlockSpec((tile, 1), lambda j: (j, 0)),
         ],
         out_specs=[line, line, line, line],
         out_shape=[jax.ShapeDtypeStruct((1, count), jnp.float32)] * 4,
@@ -85,7 +86,7 @@
             transcendentals=count * width,
             bytes_accessed=2 * (count + width) * dim,
         ),
-    )(rows, vocab, wanted.reshape(1, count), ids.reshape(width, 1))
+    )(rows, vocab, spot.reshape(1, count))
     return tuple(o.reshape(count) for o in outs)
 
 
@@ -128,13 +129,13 @@
     )
 
     whole = lax.all_gather(jnp.concatenate(near, axis=0), ("z", "c"), axis=0, tiled=True)
-    local = jnp.arange(whole.shape[0], dtype=jnp.int32)
-    group, place = local // (nx * width), local % (nx * width)
-    far_z, far_c = group // nc, group % nc
-    far_x = (x + place // width) % nx
-    ids = (((far_z * nx + far_x) * nc + far_c) * ny + y) * width + place % width
+    owner, entry = wanted // width, wanted % width
+    req, shard = owner // ny, owner % ny
+    far_c, far_x, far_z = req % nc, (req // nc) % nx, req // (nc * nx)
+    spot = ((far_z * nc + far_c) * nx + (far_x - x) % nx) * width + entry
+    spot = jnp.where(shard == y, spot, -1)
 
-    stats = row_stats(rows, whole, wanted, ids)
+    stats = row_stats(rows, whole, spot)
 
     packed = jnp.roll(jnp.stack(stats).reshape(4, ny, mine), y, axis=1).reshape(4, ny * mine)
     got = lax.all_to_all(packed, "y", 1, 1, tiled=True).reshape(4, ny, mine)

time: 121 us -> 119 us (0.983)
  the two profiles are of different devices: /device:TPU:450 before, /device:TPU:1 now
where the time goes in v13:
time: 119 us; the launch traced here: 117 us
  starting transfers between devices  33.7 us (28%)
  waiting for transfers between devices  24.9 us (21%)
  between operations  14.3 us (12%)
  Pallas kernels  13.4 us (11%)
  blocking collectives  12.9 us (11%)
  other arithmetic  9.63 us (8%)
  local copies, waits for them, and re-layouts  8.27 us (7%)
    ppermute x10, starting transfers between devices, shift(): lax.ppermute(value, axis, [(i, (i + step) % size) for i in range(size)])  33.7 us
    ppermute x10, waiting for transfers between devices, shift(): lax.ppermute(value, axis, [(i, (i + step) % size) for i in range(size)])  23.4 us
    pallas_call x1, Pallas kernels, row_stats(): pl.pallas_call(stats_kernel, grid=(width // tile,), in_specs=[pl.BlockSpe...  13.4 us
    all_to_all x1, blocking collectives, on_device(): got = lax.all_to_all(packed, 'y', 1, 1, tiled=True).reshape(4, ny, mine)  12.9 us
    unnamed x17, local copies, waits for them, and re-layouts  7 us
    another operation x3, other arithmetic  3.25 us
  transfers between devices with their start and end apart: 11, of which 5 were waited for; matrix products, arithmetic and copies ran while one was open for 13% of the time, Pallas kernels for 0%

profile of v13, /device:TPU:1, one launch (start us, length us, event | category | flops | bytes accessed | tf_op | source)
XLA Modules:
  0.0 117.1 jit_solution(3736268672923674362)
XLA Ops:
  7.2 0.0 all-gather.2.cloned.1.call-start
  7.2 5.2 %collective-permute-start = (bf16[32,1600]{1,0:T(8,128)(2,1)}, bf16[32,1600]{1,0:T(8,128)(2,1)S(1)}, u32[]{:S(2)}, u32[]{:S(2)}) collective-permute-start(bf16[32,1600]{1,0:T(8,128)(2,1)} %param.11), channel_id=1, source_target_pairs={{0,48},{16,0},{32,16},{48,32},{1,49},{17,1},{33,17},{49,33},{2,50}... | collective-permute-start | bytes 307208 | tf_op jit(solution)/shard_map/ppermute | solution.py:22
  12.4 2.4 %collective-permute-start.1 = (bf16[32,1600]{1,0:T(8,128)(2,1)}, bf16[32,1600]{1,0:T(8,128)(2,1)S(1)}, u32[]{:S(2)}, u32[]{:S(2)}) collective-permute-start(bf16[32,1600]{1,0:T(8,128)(2,1)} %param.11), channel_id=1, source_target_pairs={{0,32},{16,48},{32,0},{48,16},{1,33},{17,49},{33,1},{49,17},{2,34}... | collective-permute-start | bytes 307208 | tf_op jit(solution)/shard_map/ppermute | solution.py:22
  14.9 2.5 %collective-permute-start.2 = (bf16[32,1600]{1,0:T(8,128)(2,1)}, bf16[32,1600]{1,0:T(8,128)(2,1)S(1)}, u32[]{:S(2)}, u32[]{:S(2)}) collective-permute-start(bf16[32,1600]{1,0:T(8,128)(2,1)} %param.11), channel_id=1, source_target_pairs={{0,16},{16,32},{32,48},{48,0},{1,17},{17,33},{33,49},{49,1},{2,18}... | collective-permute-start | bytes 307208 | tf_op jit(solution)/shard_map/ppermute | solution.py:22
  17.4 0.6 compare_reduce_fusion
  18.0 0.6 compare_reduce_fusion.1
  18.7 1.2 %copy.13 = bf16[128,1600]{1,0:T(8,128)(2,1)S(1)} copy(bf16[128,1600]{0,1:T(8,128)(2,1)} %param.9) | data formatting | bytes 819200 | tf_op args[0]
  19.9 0.2 fusion
  20.1 2.0 %fusion.11 = (bf16[128,1]{0,1:T(2,128)(2,1)S(1)}, bf16[128,1]{0,1:T(2,128)(2,1)S(1)}) fusion(pred[]{:T(512)} %compare_reduce_fusion, s32[128]{0:T(128)} %param.12, pred[]{:T(512)} %compare_reduce_fusion.1), kind=kLoop, calls=%fused_computation.79 | loop fusion | flops 2944 | bytes 1026 | tf_op jit(solution)/shard_map/reshape.452
  22.1 0.1 copy.14
  22.2 0.1 copy.15
  22.3 0.9 fusion.2
  23.2 0.2 scatter.9
  23.4 0.1 pad_maximum_fusion
  23.5 1.7 %pad_maximum_fusion.1 = bf16[128,1600]{1,0:T(8,128)(2,1)} fusion(bf16[32,1600]{1,0:T(8,128)(2,1)S(1)} %collective-permute-done.2, bf16[32,1600]{1,0:T(8,128)(2,1)S(1)} %collective-permute-done.1, bf16[32,1600]{1,0:T(8,128)(2,1)S(1)} %collective-permute-done, bf16[32,1600]{1,0:T(8,128)(2,1)} %param.11), kind=kLoop, calls=%fused_computation.13 | loop fusion | flops 1638400 | bytes 819200 | tf_op jit(solution)/shard_map/concatenate | solution.py:131
  25.3 5.1 %collective-permute-start.3 = (bf16[128,1616]{1,0:T(8,128)(2,1)S(1)}, bf16[128,1616]{1,0:T(8,128)(2,1)S(1)}, u32[]{:S(2)}, u32[]{:S(2)}) collective-permute-start(bf16[128,1616]{1,0:T(8,128)(2,1)S(1)} %pad_maximum_fusion), channel_id=1, source_target_pairs={{0,7},{1,0},{2,1},{3,2},{4,3},{5,4},{6,5},{7,6},{8,15},{9,8},{10,9... | collective-permute-start | bytes 1241096 | tf_op jit(solution)/shard_map/ppermute | solution.py:22
  30.4 1.9 %collective-permute-start.6 = (bf16[128,1616]{1,0:T(8,128)(2,1)S(1)}, bf16[128,1616]{1,0:T(8,128)(2,1)S(1)}, u32[]{:S(2)}, u32[]{:S(2)}) collective-permute-start(bf16[128,1616]{1,0:T(8,128)(2,1)S(1)} %pad_maximum_fusion), channel_id=1, source_target_pairs={{0,1},{1,2},{2,3},{3,4},{4,5},{5,6},{6,7},{7,0},{8,9},{9,10},{10,1... | collective-permute-start | bytes 1241096 | tf_op jit(solution)/shard_map/ppermute | solution.py:22
  32.3 0.2 add_reduce_fusion.7
  32.5 0.8 slice_dynamic-update-slice_fusion.7
  33.3 4.6 %collective-permute-done.3 = bf16[128,1616]{1,0:T(8,128)(2,1)S(1)} collective-permute-done((bf16[128,1616]{1,0:T(8,128)(2,1)S(1)}, bf16[128,1616]{1,0:T(8,128)(2,1)S(1)}, u32[]{:S(2)}, u32[]{:S(2)}) %collective-permute-start.3) | collective-permute-done | bytes 413728 | tf_op jit(solution)/shard_map/ppermute | solution.py:22
  37.9 5.3 %collective-permute-start.4 = (bf16[128,1616]{1,0:T(8,128)(2,1)S(1)}, bf16[128,1616]{1,0:T(8,128)(2,1)S(1)}, u32[]{:S(2)}, u32[]{:S(2)}) collective-permute-start(bf16[128,1616]{1,0:T(8,128)(2,1)S(1)} %collective-permute-done.3), channel_id=1, source_target_pairs={{0,7},{1,0},{2,1},{3,2},{4,3},{5,4},{6,5},{7,6},{8,15},{9,8},{10,9... | collective-permute-start | bytes 1241096 | tf_op jit(solution)/shard_map/ppermute | solution.py:22
  43.3 1.9 %collective-permute-start.7 = (bf16[128,1616]{1,0:T(8,128)(2,1)S(1)}, bf16[128,1616]{1,0:T(8,128)(2,1)S(1)}, u32[]{:S(2)}, u32[]{:S(2)}) collective-permute-start(bf16[128,1616]{1,0:T(8,128)(2,1)S(1)} %collective-permute-done.6), channel_id=1, source_target_pairs={{0,1},{1,2},{2,3},{3,4},{4,5},{5,6},{6,7},{7,0},{8,9},{9,10},{10,1... | collective-permute-start | bytes 1241096 | tf_op jit(solution)/shard_map/ppermute | solution.py:22
  45.2 0.2 add_reduce_fusion.6
  45.4 0.2 add_reduce_fusion
  45.6 0.8 slice_dynamic-update-slice_fusion.6
  46.4 3.5 %collective-permute-done.4 = bf16[128,1616]{1,0:T(8,128)(2,1)S(1)} collective-permute-done((bf16[128,1616]{1,0:T(8,128)(2,1)S(1)}, bf16[128,1616]{1,0:T(8,128)(2,1)S(1)}, u32[]{:S(2)}, u32[]{:S(2)}) %collective-permute-start.4) | collective-permute-done | bytes 413728 | tf_op jit(solution)/shard_map/ppermute | solution.py:22
  49.9 5.4 %collective-permute-start.5 = (bf16[128,1616]{1,0:T(8,128)(2,1)S(1)}, bf16[128,1616]{1,0:T(8,128)(2,1)S(1)}, u32[]{:S(2)}, u32[]{:S(2)}) collective-permute-start(bf16[128,1616]{1,0:T(8,128)(2,1)S(1)} %collective-permute-done.4), channel_id=1, source_target_pairs={{0,7},{1,0},{2,1},{3,2},{4,3},{5,4},{6,5},{7,6},{8,15},{9,8},{10,9... | collective-permute-start | bytes 1241096 | tf_op jit(solution)/shard_map/ppermute | solution.py:22
  55.3 1.9 %collective-permute-start.8 = (bf16[128,1616]{1,0:T(8,128)(2,1)S(1)}, bf16[128,1616]{1,0:T(8,128)(2,1)S(1)}, u32[]{:S(2)}, u32[]{:S(2)}) collective-permute-start(bf16[128,1616]{1,0:T(8,128)(2,1)S(1)} %collective-permute-done.7), channel_id=1, source_target_pairs={{0,1},{1,2},{2,3},{3,4},{4,5},{5,6},{6,7},{7,0},{8,9},{9,10},{10,1... | collective-permute-start | bytes 1241096 | tf_op jit(solution)/shard_map/ppermute | solution.py:22
  57.3 0.8 slice_dynamic-update-slice_fusion.5
  58.1 0.2 add_reduce_fusion.5
  58.2 0.2 add_reduce_fusion.1
  58.4 7.9 %collective-permute-done.8 = bf16[128,1616]{1,0:T(8,128)(2,1)S(1)} collective-permute-done((bf16[128,1616]{1,0:T(8,128)(2,1)S(1)}, bf16[128,1616]{1,0:T(8,128)(2,1)S(1)}, u32[]{:S(2)}, u32[]{:S(2)}) %collective-permute-start.8) | collective-permute-done | bytes 413728 | tf_op jit(solution)/shard_map/ppermute | solution.py:22
  66.3 1.9 %collective-permute-start.9 = (bf16[128,1616]{1,0:T(8,128)(2,1)S(1)}, bf16[128,1616]{1,0:T(8,128)(2,1)S(1)}, u32[]{:S(2)}, u32[]{:S(2)}) collective-permute-start(bf16[128,1616]{1,0:T(8,128)(2,1)S(1)} %collective-permute-done.8), channel_id=1, source_target_pairs={{0,1},{1,2},{2,3},{3,4},{4,5},{5,6},{6,7},{7,0},{8,9},{9,10},{10,1... | collective-permute-start | bytes 1241096 | tf_op jit(solution)/shard_map/ppermute | solution.py:22
  68.2 0.2 add_reduce_fusion.2
  68.4 0.2 add_reduce_fusion.4
  68.6 0.8 slice_dynamic-update-slice_fusion.4
  69.5 7.3 %collective-permute-done.9 = bf16[128,1616]{1,0:T(8,128)(2,1)S(1)} collective-permute-done((bf16[128,1616]{1,0:T(8,128)(2,1)S(1)}, bf16[128,1616]{1,0:T(8,128)(2,1)S(1)}, u32[]{:S(2)}, u32[]{:S(2)}) %collective-permute-start.9) | collective-permute-done | bytes 413728 | tf_op jit(solution)/shard_map/ppermute | solution.py:22
  76.8 0.2 add_reduce_fusion.3
  77.0 0.7 compare_select_fusion.4.spot_ref
  77.8 0.8 slice_dynamic-update-slice_fusion.3
  78.6 0.8 slice_dynamic-update-slice_fusion.2
  79.4 0.8 slice_dynamic-update-slice_fusion.1
  80.2 0.8 slice_dynamic-update-slice_fusion.rows_ref
  81.0 1.6 %all-gather.2.cloned.1.call-done.vocab_ref = bf16[2048,1600]{1,0:T(8,128)(2,1)} async-done(((bf16[128,1600]{1,0:T(8,128)(2,1)}), bf16[2048,1600]{1,0:T(8,128)(2,1)}) %all-gather.2.cloned.1.call-update) | async-done | bytes 6553616 | tf_op jit(solution)/shard_map/all_gather | solution.py:131
  82.6 13.4 %shard_map.68 = (f32[1,1024]{1,0:T(1,128)}, f32[1,1024]{1,0:T(1,128)}, f32[1,1024]{1,0:T(1,128)}, f32[1,1024]{1,0:T(1,128)}) custom-call(bf16[1024,1600]{1,0:T(8,128)(2,1)} %slice_dynamic-update-slice_fusion.rows_ref, bf16[2048,1600]{1,0:T(8,128)(2,1)} %all-gather.2.cloned.1.call-done.vocab_ref, s32[1,1024]{1,0:T(1,128)} %compare_select_fusion.4.spot_ref), custom_call_target="tpu_custom_call" | custom-call | flops 6710886400 | bytes 9830400 | tf_op jit(solution)/shard_map/pallas_call | solution.py:74
  96.0 0.7 maximum_bitcast_fusion
  96.7 12.9 %all_to_all.6 = f32[4,8,128]{2,0,1:T(4,128)S(1)} all-to-all(f32[4,8,128]{2,0,1:T(4,128)S(1)} %fusion.3), channel_id=1, replica_groups=mesh['z'=8,'x'=4,'c'=2,'y'=8] {'y'}, dimensions={1} | all-to-all | bytes 32768 | tf_op jit(solution)/shard_map/all_to_all | solution.py:141
  109.7 0.5 subtract_multiply_fusion
  (23 shorter events, 0.2 us)
Async XLA Ops:
  7.2 75.4 %all-gather.2.cloned.1.call-start = ((), (), s32[]{:S(2)}) async-start(), calls=%async_computation.1 | async-start | bytes 7241728 | tf_op jit(solution)/shard_map/all_gather | solution.py:131
  7.2 16.3 %collective-permute-start = (bf16[32,1600]{1,0:T(8,128)(2,1)}, bf16[32,1600]{1,0:T(8,128)(2,1)S(1)}, u32[]{:S(2)}, u32[]{:S(2)}) collective-permute-start(bf16[32,1600]{1,0:T(8,128)(2,1)} %param.11), channel_id=1, source_target_pairs={{0,48},{16,0},{32,16},{48,32},{1,49},{17,1},{33,17},{49,33},{2,50}... | collective-permute-start | bytes 307208 | tf_op jit(solution)/shard_map/ppermute | solution.py:22
  12.4 11.1 %collective-permute-start.1 = (bf16[32,1600]{1,0:T(8,128)(2,1)}, bf16[32,1600]{1,0:T(8,128)(2,1)S(1)}, u32[]{:S(2)}, u32[]{:S(2)}) collective-permute-start(bf16[32,1600]{1,0:T(8,128)(2,1)} %param.11), channel_id=1, source_target_pairs={{0,32},{16,48},{32,0},{48,16},{1,33},{17,49},{33,1},{49,17},{2,34}... | collective-permute-start | bytes 307208 | tf_op jit(solution)/shard_map/ppermute | solution.py:22
  14.9 8.7 %collective-permute-start.2 = (bf16[32,1600]{1,0:T(8,128)(2,1)}, bf16[32,1600]{1,0:T(8,128)(2,1)S(1)}, u32[]{:S(2)}, u32[]{:S(2)}) collective-permute-start(bf16[32,1600]{1,0:T(8,128)(2,1)} %param.11), channel_id=1, source_target_pairs={{0,16},{16,32},{32,48},{48,0},{1,17},{17,33},{33,49},{49,1},{2,18}... | collective-permute-start | bytes 307208 | tf_op jit(solution)/shard_map/ppermute | solution.py:22
  25.3 12.7 %collective-permute-start.3 = (bf16[128,1616]{1,0:T(8,128)(2,1)S(1)}, bf16[128,1616]{1,0:T(8,128)(2,1)S(1)}, u32[]{:S(2)}, u32[]{:S(2)}) collective-permute-start(bf16[128,1616]{1,0:T(8,128)(2,1)S(1)} %pad_maximum_fusion), channel_id=1, source_target_pairs={{0,7},{1,0},{2,1},{3,2},{4,3},{5,4},{6,5},{7,6},{8,15},{9,8},{10,9... | collective-permute-start | bytes 1241096 | tf_op jit(solution)/shard_map/ppermute | solution.py:22
  30.4 12.9 %collective-permute-start.6 = (bf16[128,1616]{1,0:T(8,128)(2,1)S(1)}, bf16[128,1616]{1,0:T(8,128)(2,1)S(1)}, u32[]{:S(2)}, u32[]{:S(2)}) collective-permute-start(bf16[128,1616]{1,0:T(8,128)(2,1)S(1)} %pad_maximum_fusion), channel_id=1, source_target_pairs={{0,1},{1,2},{2,3},{3,4},{4,5},{5,6},{6,7},{7,0},{8,9},{9,10},{10,1... | collective-permute-start | bytes 1241096 | tf_op jit(solution)/shard_map/ppermute | solution.py:22
  37.9 12.0 %collective-permute-start.4 = (bf16[128,1616]{1,0:T(8,128)(2,1)S(1)}, bf16[128,1616]{1,0:T(8,128)(2,1)S(1)}, u32[]{:S(2)}, u32[]{:S(2)}) collective-permute-start(bf16[128,1616]{1,0:T(8,128)(2,1)S(1)} %collective-permute-done.3), channel_id=1, source_target_pairs={{0,7},{1,0},{2,1},{3,2},{4,3},{5,4},{6,5},{7,6},{8,15},{9,8},{10,9... | collective-permute-start | bytes 1241096 | tf_op jit(solution)/shard_map/ppermute | solution.py:22
  43.3 12.1 %collective-permute-start.7 = (bf16[128,1616]{1,0:T(8,128)(2,1)S(1)}, bf16[128,1616]{1,0:T(8,128)(2,1)S(1)}, u32[]{:S(2)}, u32[]{:S(2)}) collective-permute-start(bf16[128,1616]{1,0:T(8,128)(2,1)S(1)} %collective-permute-done.6), channel_id=1, source_target_pairs={{0,1},{1,2},{2,3},{3,4},{4,5},{5,6},{6,7},{7,0},{8,9},{9,10},{10,1... | collective-permute-start | bytes 1241096 | tf_op jit(solution)/shard_map/ppermute | solution.py:22
  49.9 18.5 %collective-permute-start.5 = (bf16[128,1616]{1,0:T(8,128)(2,1)S(1)}, bf16[128,1616]{1,0:T(8,128)(2,1)S(1)}, u32[]{:S(2)}, u32[]{:S(2)}) collective-permute-start(bf16[128,1616]{1,0:T(8,128)(2,1)S(1)} %collective-permute-done.4), channel_id=1, source_target_pairs={{0,7},{1,0},{2,1},{3,2},{4,3},{5,4},{6,5},{7,6},{8,15},{9,8},{10,9... | collective-permute-start | bytes 1241096 | tf_op jit(solution)/shard_map/ppermute | solution.py:22
  55.3 11.0 %collective-permute-start.8 = (bf16[128,1616]{1,0:T(8,128)(2,1)S(1)}, bf16[128,1616]{1,0:T(8,128)(2,1)S(1)}, u32[]{:S(2)}, u32[]{:S(2)}) collective-permute-start(bf16[128,1616]{1,0:T(8,128)(2,1)S(1)} %collective-permute-done.7), channel_id=1, source_target_pairs={{0,1},{1,2},{2,3},{3,4},{4,5},{5,6},{6,7},{7,0},{8,9},{9,10},{10,1... | collective-permute-start | bytes 1241096 | tf_op jit(solution)/shard_map/ppermute | solution.py:22
  66.3 10.5 %collective-permute-start.9 = (bf16[128,1616]{1,0:T(8,128)(2,1)S(1)}, bf16[128,1616]{1,0:T(8,128)(2,1)S(1)}, u32[]{:S(2)}, u32[]{:S(2)}) collective-permute-start(bf16[128,1616]{1,0:T(8,128)(2,1)S(1)} %collective-permute-done.8), channel_id=1, source_target_pairs={{0,1},{1,2},{2,3},{3,4},{4,5},{5,6},{6,7},{7,0},{8,9},{9,10},{10,1... | collective-permute-start | bytes 1241096 | tf_op jit(solution)/shard_map/ppermute | solution.py:22
  81.0 28.7 %copy-start = (s32[128]{0:T(128)S(1)}, s32[128]{0:T(128)}, u32[]{:S(2)}) copy-start(s32[128]{0:T(128)} %param.13) | copy-start | bytes 1540
Sparse Core Ops, SparseCore 0:
  25.4 57.1 all-gather.1

commit v14 on v13

--- a/solution.py
+++ b/solution.py
@@ -117,12 +117,19 @@
 
     blocks = [None] * ny
     blocks[0] = block
+    half = ny // 2
+    fronts = {}
     for sign in (1, -1):
         cur = block
-        reach = ny // 2 if sign == 1 else ny - 1 - ny // 2
-        for step in range(1, reach + 1):
+        for step in range(1, half):
             cur = shift(cur, "y", ny, sign)
             blocks[(-sign * step) % ny] = cur
+        fronts[sign] = cur
+    if ny % 2 == 0:
+        cut = mine // 2
+        first = shift(fronts[1][:cut], "y", ny, 1)
+        second = shift(fronts[-1][cut:], "y", ny, -1)
+        blocks[half] = jnp.concatenate([first, second], axis=0)
     rows = jnp.concatenate([b[:, :dim] for b in blocks], axis=0)
     wanted = jnp.concatenate(
         [b[:, dim].astype(jnp.int32) * 128 + b[:, dim + 1].astype(jnp.int32) for b in blocks], axis=0

time: 119 us -> 119 us (level)
  waiting for transfers between devices: 24.9 us -> 20.3 us
  starting transfers between devices: 33.7 us -> 38.3 us
    ppermute x10 -> x11, waiting for transfers between devices: 23.4 us -> 17.6 us  [shift(): lax.ppermute(value, axis, [(i, (i + step) % size) for i in range(size)])]
    ppermute x10 -> x11, starting transfers between devices: 33.7 us -> 38.2 us  [shift(): lax.ppermute(value, axis, [(i, (i + step) % size) for i in range(size)])]
    unnamed x17 -> x18, local copies, waits for them, and re-layouts: 7 us -> 7.02 us
  transfers between devices with their start and end apart: 11 -> 12, of which waited for: 5 -> 6; matrix products, arithmetic and copies ran while one was open for 13% -> 13% of each run, Pallas kernels for 0% -> 0%
where the time goes in v14:
time: 119 us; the launch traced here: 117 us
  starting transfers between devices  38.3 us (32%)
  waiting for transfers between devices  20.3 us (17%)
  between operations  14.3 us (12%)
  Pallas kernels  13.4 us (11%)
  blocking collectives  12.9 us (11%)
  other arithmetic  9.64 us (8%)
  local copies, waits for them, and re-layouts  8.35 us (7%)
    ppermute x11, starting transfers between devices, shift(): lax.ppermute(value, axis, [(i, (i + step) % size) for i in range(size)])  38.2 us
    ppermute x11, waiting for transfers between devices, shift(): lax.ppermute(value, axis, [(i, (i + step) % size) for i in range(size)])  17.6 us
    pallas_call x1, Pallas kernels, row_stats(): pl.pallas_call(stats_kernel, grid=(width // tile,), in_specs=[pl.BlockSpe...  13.4 us
    all_to_all x1, blocking collectives, on_device(): got = lax.all_to_all(packed, 'y', 1, 1, tiled=True).reshape(4, ny, mine)  12.9 us
    unnamed x18, local copies, waits for them, and re-layouts  7.02 us
    another operation x3, other arithmetic  3.25 us
    all_gather x1, waiting for transfers between devices, on_device(): lax.all_gather(jnp.concatenate(near, axis=0), ('z', 'c'), axis=0, tiled=T...  2.67 us
  transfers between devices with their start and end apart: 12, of which 6 were waited for; matrix products, arithmetic and copies ran while one was open for 13% of the time, Pallas kernels for 0%

profile of v14, /device:TPU:1, one launch (start us, length us, event | category | flops | bytes accessed | tf_op | source)
XLA Modules:
  0.0 117.1 jit_solution(9338717588383659779)
XLA Ops:
  7.2 5.2 %collective-permute-start = (bf16[32,1600]{1,0:T(8,128)(2,1)}, bf16[32,1600]{1,0:T(8,128)(2,1)S(1)}, u32[]{:S(2)}, u32[]{:S(2)}) collective-permute-start(bf16[32,1600]{1,0:T(8,128)(2,1)} %param.11), channel_id=1, source_target_pairs={{0,48},{16,0},{32,16},{48,32},{1,49},{17,1},{33,17},{49,33},{2,50}... | collective-permute-start | bytes 307208 | tf_op jit(solution)/shard_map/ppermute | solution.py:22
  12.4 2.4 %collective-permute-start.1 = (bf16[32,1600]{1,0:T(8,128)(2,1)}, bf16[32,1600]{1,0:T(8,128)(2,1)S(1)}, u32[]{:S(2)}, u32[]{:S(2)}) collective-permute-start(bf16[32,1600]{1,0:T(8,128)(2,1)} %param.11), channel_id=1, source_target_pairs={{0,32},{16,48},{32,0},{48,16},{1,33},{17,49},{33,1},{49,17},{2,34}... | collective-permute-start | bytes 307208 | tf_op jit(solution)/shard_map/ppermute | solution.py:22
  14.9 2.5 %collective-permute-start.2 = (bf16[32,1600]{1,0:T(8,128)(2,1)}, bf16[32,1600]{1,0:T(8,128)(2,1)S(1)}, u32[]{:S(2)}, u32[]{:S(2)}) collective-permute-start(bf16[32,1600]{1,0:T(8,128)(2,1)} %param.11), channel_id=1, source_target_pairs={{0,16},{16,32},{32,48},{48,0},{1,17},{17,33},{33,49},{49,1},{2,18}... | collective-permute-start | bytes 307208 | tf_op jit(solution)/shard_map/ppermute | solution.py:22
  17.4 0.6 compare_reduce_fusion
  18.0 0.6 compare_reduce_fusion.1
  18.7 1.2 %copy.13 = bf16[128,1600]{1,0:T(8,128)(2,1)S(1)} copy(bf16[128,1600]{0,1:T(8,128)(2,1)} %param.9) | data formatting | bytes 819200 | tf_op args[0]
  19.9 0.2 fusion
  20.1 2.0 %fusion.11 = (bf16[128,1]{0,1:T(2,128)(2,1)S(1)}, bf16[128,1]{0,1:T(2,128)(2,1)S(1)}) fusion(pred[]{:T(512)} %compare_reduce_fusion, s32[128]{0:T(128)} %param.12, pred[]{:T(512)} %compare_reduce_fusion.1), kind=kLoop, calls=%fused_computation.81 | loop fusion | flops 2944 | bytes 1026 | tf_op jit(solution)/shard_map/reshape.452
  22.1 0.1 copy.14
  22.2 0.1 copy.15
  22.3 0.9 fusion.2
  23.2 0.2 scatter.9
  23.5 1.7 %pad_maximum_fusion.1 = bf16[128,1600]{1,0:T(8,128)(2,1)} fusion(bf16[32,1600]{1,0:T(8,128)(2,1)S(1)} %collective-permute-done.2, bf16[32,1600]{1,0:T(8,128)(2,1)S(1)} %collective-permute-done.1, bf16[32,1600]{1,0:T(8,128)(2,1)S(1)} %collective-permute-done, bf16[32,1600]{1,0:T(8,128)(2,1)} %param.11), kind=kLoop, calls=%fused_computation.13 | loop fusion | flops 1638400 | bytes 819200 | tf_op jit(solution)/shard_map/concatenate | solution.py:138
  25.3 5.1 %collective-permute-start.3 = (bf16[128,1616]{1,0:T(8,128)(2,1)S(1)}, bf16[128,1616]{1,0:T(8,128)(2,1)S(1)}, u32[]{:S(2)}, u32[]{:S(2)}) collective-permute-start(bf16[128,1616]{1,0:T(8,128)(2,1)S(1)} %pad_maximum_fusion), channel_id=1, source_target_pairs={{0,7},{1,0},{2,1},{3,2},{4,3},{5,4},{6,5},{7,6},{8,15},{9,8},{10,9... | collective-permute-start | bytes 1241096 | tf_op jit(solution)/shard_map/ppermute | solution.py:22
  30.4 1.9 %collective-permute-start.6 = (bf16[128,1616]{1,0:T(8,128)(2,1)S(1)}, bf16[128,1616]{1,0:T(8,128)(2,1)S(1)}, u32[]{:S(2)}, u32[]{:S(2)}) collective-permute-start(bf16[128,1616]{1,0:T(8,128)(2,1)S(1)} %pad_maximum_fusion), channel_id=1, source_target_pairs={{0,1},{1,2},{2,3},{3,4},{4,5},{5,6},{6,7},{7,0},{8,9},{9,10},{10,1... | collective-permute-start | bytes 1241096 | tf_op jit(solution)/shard_map/ppermute | solution.py:22
  32.3 0.2 add_reduce_fusion.7
  32.5 0.8 slice_dynamic-update-slice_fusion.7
  33.3 4.6 %collective-permute-done.3 = bf16[128,1616]{1,0:T(8,128)(2,1)S(1)} collective-permute-done((bf16[128,1616]{1,0:T(8,128)(2,1)S(1)}, bf16[128,1616]{1,0:T(8,128)(2,1)S(1)}, u32[]{:S(2)}, u32[]{:S(2)}) %collective-permute-start.3) | collective-permute-done | bytes 413728 | tf_op jit(solution)/shard_map/ppermute | solution.py:22
  37.9 5.3 %collective-permute-start.4 = (bf16[128,1616]{1,0:T(8,128)(2,1)S(1)}, bf16[128,1616]{1,0:T(8,128)(2,1)S(1)}, u32[]{:S(2)}, u32[]{:S(2)}) collective-permute-start(bf16[128,1616]{1,0:T(8,128)(2,1)S(1)} %collective-permute-done.3), channel_id=1, source_target_pairs={{0,7},{1,0},{2,1},{3,2},{4,3},{5,4},{6,5},{7,6},{8,15},{9,8},{10,9... | collective-permute-start | bytes 1241096 | tf_op jit(solution)/shard_map/ppermute | solution.py:22
  43.3 1.9 %collective-permute-start.7 = (bf16[128,1616]{1,0:T(8,128)(2,1)S(1)}, bf16[128,1616]{1,0:T(8,128)(2,1)S(1)}, u32[]{:S(2)}, u32[]{:S(2)}) collective-permute-start(bf16[128,1616]{1,0:T(8,128)(2,1)S(1)} %collective-permute-done.6), channel_id=1, source_target_pairs={{0,1},{1,2},{2,3},{3,4},{4,5},{5,6},{6,7},{7,0},{8,9},{9,10},{10,1... | collective-permute-start | bytes 1241096 | tf_op jit(solution)/shard_map/ppermute | solution.py:22
  45.2 0.2 add_reduce_fusion.6
  45.4 0.2 add_reduce_fusion
  45.6 0.8 slice_dynamic-update-slice_fusion.6
  46.4 3.5 %collective-permute-done.4 = bf16[128,1616]{1,0:T(8,128)(2,1)S(1)} collective-permute-done((bf16[128,1616]{1,0:T(8,128)(2,1)S(1)}, bf16[128,1616]{1,0:T(8,128)(2,1)S(1)}, u32[]{:S(2)}, u32[]{:S(2)}) %collective-permute-start.4) | collective-permute-done | bytes 413728 | tf_op jit(solution)/shard_map/ppermute | solution.py:22
  49.9 5.4 %collective-permute-start.5 = (bf16[128,1616]{1,0:T(8,128)(2,1)S(1)}, bf16[128,1616]{1,0:T(8,128)(2,1)S(1)}, u32[]{:S(2)}, u32[]{:S(2)}) collective-permute-start(bf16[128,1616]{1,0:T(8,128)(2,1)S(1)} %collective-permute-done.4), channel_id=1, source_target_pairs={{0,7},{1,0},{2,1},{3,2},{4,3},{5,4},{6,5},{7,6},{8,15},{9,8},{10,9... | collective-permute-start | bytes 1241096 | tf_op jit(solution)/shard_map/ppermute | solution.py:22
  55.3 1.9 %collective-permute-start.8 = (bf16[128,1616]{1,0:T(8,128)(2,1)S(1)}, bf16[128,1616]{1,0:T(8,128)(2,1)S(1)}, u32[]{:S(2)}, u32[]{:S(2)}) collective-permute-start(bf16[128,1616]{1,0:T(8,128)(2,1)S(1)} %collective-permute-done.7), channel_id=1, source_target_pairs={{0,1},{1,2},{2,3},{3,4},{4,5},{5,6},{6,7},{7,0},{8,9},{9,10},{10,1... | collective-permute-start | bytes 1241096 | tf_op jit(solution)/shard_map/ppermute | solution.py:22
  57.3 0.2 add_reduce_fusion.5
  57.4 0.2 add_reduce_fusion.1
  57.7 0.8 slice_dynamic-update-slice_fusion.5
  58.5 7.9 %collective-permute-done.8 = bf16[128,1616]{1,0:T(8,128)(2,1)S(1)} collective-permute-done((bf16[128,1616]{1,0:T(8,128)(2,1)S(1)}, bf16[128,1616]{1,0:T(8,128)(2,1)S(1)}, u32[]{:S(2)}, u32[]{:S(2)}) %collective-permute-start.8) | collective-permute-done | bytes 413728 | tf_op jit(solution)/shard_map/ppermute | solution.py:22
  66.3 1.9 %collective-permute-start.9 = (bf16[64,1616]{1,0:T(8,128)(2,1)S(1)}, bf16[64,1616]{1,0:T(8,128)(2,1)S(1)}, u32[]{:S(2)}, u32[]{:S(2)}) collective-permute-start(bf16[64,1616]{1,0:T(8,128)(2,1)S(1)} %slice.160), channel_id=1, source_target_pairs={{0,1},{1,2},{2,3},{3,4},{4,5},{5,6},{6,7},{7,0},{8,9},{9,10},{10,1... | collective-permute-start | bytes 620552 | tf_op jit(solution)/shard_map/ppermute | solution.py:22
  68.3 4.6 %collective-permute-start.10 = (bf16[64,1616]{1,0:T(8,128)(2,1)S(1)}, bf16[64,1616]{1,0:T(8,128)(2,1)S(1)}, u32[]{:S(2)}, u32[]{:S(2)}) collective-permute-start(bf16[64,1616]{1,0:T(8,128)(2,1)S(1)} %slice.161), channel_id=1, source_target_pairs={{0,7},{1,0},{2,1},{3,2},{4,3},{5,4},{6,5},{7,6},{8,15},{9,8},{10,9... | collective-permute-start | bytes 620552 | tf_op jit(solution)/shard_map/ppermute | solution.py:22
  72.9 0.2 add_reduce_fusion.4
  73.1 0.2 add_reduce_fusion.2
  73.3 0.8 slice_dynamic-update-slice_fusion.4
  74.1 0.4 collective-permute-done.9
  74.6 1.1 collective-permute-done.10
  75.7 0.2 add_reduce_fusion.3
  75.9 0.7 compare_select_fusion.4.spot_ref
  76.6 0.8 slice_dynamic-update-slice_fusion.3
  77.5 0.8 slice_dynamic-update-slice_fusion.2
  78.3 0.8 slice_dynamic-update-slice_fusion.1
  79.1 0.8 slice_dynamic-update-slice_fusion.rows_ref
  79.9 2.7 %all-gather.2.cloned.1.call-done.vocab_ref = bf16[2048,1600]{1,0:T(8,128)(2,1)} async-done(((bf16[128,1600]{1,0:T(8,128)(2,1)}), bf16[2048,1600]{1,0:T(8,128)(2,1)}) %all-gather.2.cloned.1.call-update) | async-done | bytes 6553616 | tf_op jit(solution)/shard_map/all_gather | solution.py:138
  82.6 13.4 %shard_map.68 = (f32[1,1024]{1,0:T(1,128)}, f32[1,1024]{1,0:T(1,128)}, f32[1,1024]{1,0:T(1,128)}, f32[1,1024]{1,0:T(1,128)}) custom-call(bf16[1024,1600]{1,0:T(8,128)(2,1)} %slice_dynamic-update-slice_fusion.rows_ref, bf16[2048,1600]{1,0:T(8,128)(2,1)} %all-gather.2.cloned.1.call-done.vocab_ref, s32[1,1024]{1,0:T(1,128)} %compare_select_fusion.4.spot_ref), custom_call_target="tpu_custom_call" | custom-call | flops 6710886400 | bytes 9830400 | tf_op jit(solution)/shard_map/pallas_call | solution.py:74
  96.0 0.7 maximum_bitcast_fusion
  96.7 12.9 %all_to_all.6 = f32[4,8,128]{2,0,1:T(4,128)S(1)} all-to-all(f32[4,8,128]{2,0,1:T(4,128)S(1)} %fusion.3), channel_id=1, replica_groups=mesh['z'=8,'x'=4,'c'=2,'y'=8] {'y'}, dimensions={1} | all-to-all | bytes 32768 | tf_op jit(solution)/shard_map/all_to_all | solution.py:148
  109.7 0.5 subtract_multiply_fusion
  (29 shorter events, 0.4 us)
Async XLA Ops:
  7.2 75.4 %all-gather.2.cloned.1.call-start = ((), (), s32[]{:S(2)}) async-start(), calls=%async_computation.1 | async-start | bytes 7241728 | tf_op jit(solution)/shard_map/all_gather | solution.py:138
  7.2 16.3 %collective-permute-start = (bf16[32,1600]{1,0:T(8,128)(2,1)}, bf16[32,1600]{1,0:T(8,128)(2,1)S(1)}, u32[]{:S(2)}, u32[]{:S(2)}) collective-permute-start(bf16[32,1600]{1,0:T(8,128)(2,1)} %param.11), channel_id=1, source_target_pairs={{0,48},{16,0},{32,16},{48,32},{1,49},{17,1},{33,17},{49,33},{2,50}... | collective-permute-start | bytes 307208 | tf_op jit(solution)/shard_map/ppermute | solution.py:22
  12.4 11.1 %collective-permute-start.1 = (bf16[32,1600]{1,0:T(8,128)(2,1)}, bf16[32,1600]{1,0:T(8,128)(2,1)S(1)}, u32[]{:S(2)}, u32[]{:S(2)}) collective-permute-start(bf16[32,1600]{1,0:T(8,128)(2,1)} %param.11), channel_id=1, source_target_pairs={{0,32},{16,48},{32,0},{48,16},{1,33},{17,49},{33,1},{49,17},{2,34}... | collective-permute-start | bytes 307208 | tf_op jit(solution)/shard_map/ppermute | solution.py:22
  14.9 8.7 %collective-permute-start.2 = (bf16[32,1600]{1,0:T(8,128)(2,1)}, bf16[32,1600]{1,0:T(8,128)(2,1)S(1)}, u32[]{:S(2)}, u32[]{:S(2)}) collective-permute-start(bf16[32,1600]{1,0:T(8,128)(2,1)} %param.11), channel_id=1, source_target_pairs={{0,16},{16,32},{32,48},{48,0},{1,17},{17,33},{33,49},{49,1},{2,18}... | collective-permute-start | bytes 307208 | tf_op jit(solution)/shard_map/ppermute | solution.py:22
  25.3 12.7 %collective-permute-start.3 = (bf16[128,1616]{1,0:T(8,128)(2,1)S(1)}, bf16[128,1616]{1,0:T(8,128)(2,1)S(1)}, u32[]{:S(2)}, u32[]{:S(2)}) collective-permute-start(bf16[128,1616]{1,0:T(8,128)(2,1)S(1)} %pad_maximum_fusion), channel_id=1, source_target_pairs={{0,7},{1,0},{2,1},{3,2},{4,3},{5,4},{6,5},{7,6},{8,15},{9,8},{10,9... | collective-permute-start | bytes 1241096 | tf_op jit(solution)/shard_map/ppermute | solution.py:22
  30.4 12.9 %collective-permute-start.6 = (bf16[128,1616]{1,0:T(8,128)(2,1)S(1)}, bf16[128,1616]{1,0:T(8,128)(2,1)S(1)}, u32[]{:S(2)}, u32[]{:S(2)}) collective-permute-start(bf16[128,1616]{1,0:T(8,128)(2,1)S(1)} %pad_maximum_fusion), channel_id=1, source_target_pairs={{0,1},{1,2},{2,3},{3,4},{4,5},{5,6},{6,7},{7,0},{8,9},{9,10},{10,1... | collective-permute-start | bytes 1241096 | tf_op jit(solution)/shard_map/ppermute | solution.py:22
  37.9 12.0 %collective-permute-start.4 = (bf16[128,1616]{1,0:T(8,128)(2,1)S(1)}, bf16[128,1616]{1,0:T(8,128)(2,1)S(1)}, u32[]{:S(2)}, u32[]{:S(2)}) collective-permute-start(bf16[128,1616]{1,0:T(8,128)(2,1)S(1)} %collective-permute-done.3), channel_id=1, source_target_pairs={{0,7},{1,0},{2,1},{3,2},{4,3},{5,4},{6,5},{7,6},{8,15},{9,8},{10,9... | collective-permute-start | bytes 1241096 | tf_op jit(solution)/shard_map/ppermute | solution.py:22
  43.3 12.1 %collective-permute-start.7 = (bf16[128,1616]{1,0:T(8,128)(2,1)S(1)}, bf16[128,1616]{1,0:T(8,128)(2,1)S(1)}, u32[]{:S(2)}, u32[]{:S(2)}) collective-permute-start(bf16[128,1616]{1,0:T(8,128)(2,1)S(1)} %collective-permute-done.6), channel_id=1, source_target_pairs={{0,1},{1,2},{2,3},{3,4},{4,5},{5,6},{6,7},{7,0},{8,9},{9,10},{10,1... | collective-permute-start | bytes 1241096 | tf_op jit(solution)/shard_map/ppermute | solution.py:22
  49.9 18.4 %collective-permute-start.5 = (bf16[128,1616]{1,0:T(8,128)(2,1)S(1)}, bf16[128,1616]{1,0:T(8,128)(2,1)S(1)}, u32[]{:S(2)}, u32[]{:S(2)}) collective-permute-start(bf16[128,1616]{1,0:T(8,128)(2,1)S(1)} %collective-permute-done.4), channel_id=1, source_target_pairs={{0,7},{1,0},{2,1},{3,2},{4,3},{5,4},{6,5},{7,6},{8,15},{9,8},{10,9... | collective-permute-start | bytes 1241096 | tf_op jit(solution)/shard_map/ppermute | solution.py:22
  55.3 11.0 %collective-permute-start.8 = (bf16[128,1616]{1,0:T(8,128)(2,1)S(1)}, bf16[128,1616]{1,0:T(8,128)(2,1)S(1)}, u32[]{:S(2)}, u32[]{:S(2)}) collective-permute-start(bf16[128,1616]{1,0:T(8,128)(2,1)S(1)} %collective-permute-done.7), channel_id=1, source_target_pairs={{0,1},{1,2},{2,3},{3,4},{4,5},{5,6},{6,7},{7,0},{8,9},{9,10},{10,1... | collective-permute-start | bytes 1241096 | tf_op jit(solution)/shard_map/ppermute | solution.py:22
  66.3 8.2 %collective-permute-start.9 = (bf16[64,1616]{1,0:T(8,128)(2,1)S(1)}, bf16[64,1616]{1,0:T(8,128)(2,1)S(1)}, u32[]{:S(2)}, u32[]{:S(2)}) collective-permute-start(bf16[64,1616]{1,0:T(8,128)(2,1)S(1)} %slice.160), channel_id=1, source_target_pairs={{0,1},{1,2},{2,3},{3,4},{4,5},{5,6},{6,7},{7,0},{8,9},{9,10},{10,1... | collective-permute-start | bytes 620552 | tf_op jit(solution)/shard_map/ppermute | solution.py:22
  68.3 7.3 %collective-permute-start.10 = (bf16[64,1616]{1,0:T(8,128)(2,1)S(1)}, bf16[64,1616]{1,0:T(8,128)(2,1)S(1)}, u32[]{:S(2)}, u32[]{:S(2)}) collective-permute-start(bf16[64,1616]{1,0:T(8,128)(2,1)S(1)} %slice.161), channel_id=1, source_target_pairs={{0,7},{1,0},{2,1},{3,2},{4,3},{5,4},{6,5},{7,6},{8,15},{9,8},{10,9... | collective-permute-start | bytes 620552 | tf_op jit(solution)/shard_map/ppermute | solution.py:22
  79.9 29.8 %copy-start = (s32[128]{0:T(128)S(1)}, s32[128]{0:T(128)}, u32[]{:S(2)}) copy-start(s32[128]{0:T(128)} %param.13) | copy-start | bytes 1540
Sparse Core Ops, SparseCore 0:
  25.4 57.1 all-gather.1

commit v15 on v13

--- a/solution.py
+++ b/solution.py
@@ -1,7 +1,10 @@
+import functools
+
 import jax
 import jax.numpy as jnp
 from jax import lax
 from jax.experimental import pallas as pl
+from jax.experimental.pallas import tpu as pltpu
 from jax.sharding import Mesh, PartitionSpec as P
 
 FLAT = ("z", "x", "c", "y")
@@ -33,13 +36,18 @@
     return (fold_top, jnp.sum(weights, axis=1), jnp.sum(weights * shifted, axis=1), chosen)
 
 
-def stats_kernel(rows_ref, vocab_ref, spot_ref, top_ref, total_ref, spread_ref, chosen_ref):
+def stats_kernel(parts, dim, *refs):
+    block_refs = refs[:parts]
+    vocab_ref, spot_ref, top_ref, total_ref, spread_ref, chosen_ref, rows_ref = refs[parts:]
     j = pl.program_id(0)
     tile = vocab_ref.shape[0]
     position = j * tile + lax.broadcasted_iota(jnp.int32, (tile, 1), 0)
 
     @pl.when(j == 0)
     def _():
+        size = block_refs[0].shape[0]
+        for b, block_ref in enumerate(block_refs):
+            rows_ref[b * size : (b + 1) * size, :] = block_ref[:, :dim]
         top_ref[...] = jnp.full(top_ref.shape, -1e30, jnp.float32)
         total_ref[...] = jnp.zeros(total_ref.shape, jnp.float32)
         spread_ref[...] = jnp.zeros(spread_ref.shape, jnp.float32)
@@ -67,26 +75,25 @@
     top_ref[...] = top
 
 
-def row_stats(rows, vocab, spot, tile=512):
-    count, dim = rows.shape
+def row_stats(blocks, dim, vocab, spot, tile=512):
+    size = blocks[0].shape[0]
+    count = size * len(blocks)
     width = vocab.shape[0]
     line = pl.BlockSpec((1, count), lambda j: (0, 0))
+    whole_block = pl.BlockSpec(blocks[0].shape, lambda j: (0, 0))
     outs = pl.pallas_call(
-        stats_kernel,
+        functools.partial(stats_kernel, len(blocks), dim),
         grid=(width // tile,),
-        in_specs=[
-            pl.BlockSpec((count, dim), lambda j: (0, 0)),
-            pl.BlockSpec((tile, dim), lambda j: (j, 0)),
-            line,
-        ],
+        in_specs=[whole_block] * len(blocks) + [pl.BlockSpec((tile, dim), lambda j: (j, 0)), line],
         out_specs=[line, line, line, line],
         out_shape=[jax.ShapeDtypeStruct((1, count), jnp.float32)] * 4,
+        scratch_shapes=[pltpu.VMEM((count, dim), blocks[0].dtype)],
         cost_estimate=pl.CostEstimate(
             flops=2 * count * width * dim,
             transcendentals=count * width,
             bytes_accessed=2 * (count + width) * dim,
         ),
-    )(rows, vocab, spot.reshape(1, count))
+    )(*blocks, vocab, spot.reshape(1, count))
     return tuple(o.reshape(count) for o in outs)
 
 
@@ -123,7 +130,6 @@
         for step in range(1, reach + 1):
             cur = shift(cur, "y", ny, sign)
             blocks[(-sign * step) % ny] = cur
-    rows = jnp.concatenate([b[:, :dim] for b in blocks], axis=0)
     wanted = jnp.concatenate(
         [b[:, dim].astype(jnp.int32) * 128 + b[:, dim + 1].astype(jnp.int32) for b in blocks], axis=0
     )
@@ -135,7 +141,7 @@
     spot = ((far_z * nc + far_c) * nx + (far_x - x) % nx) * width + entry
     spot = jnp.where(shard == y, spot, -1)
 
-    stats = row_stats(rows, whole, spot)
+    stats = row_stats(blocks, dim, whole, spot)
 
     packed = jnp.roll(jnp.stack(stats).reshape(4, ny, mine), y, axis=1).reshape(4, ny * mine)
     got = lax.all_to_all(packed, "y", 1, 1, tiled=True).reshape(4, ny, mine)

time: 119 us -> 119 us (level)
  waiting for transfers between devices: 24.9 us -> 32.4 us
  local copies, waits for them, and re-layouts: 8.27 us -> 1.81 us
    all_gather x1, waiting for transfers between devices: 1.56 us -> 12.3 us  [on_device(): lax.all_gather(jnp.concatenate(near, axis=0), ('z', 'c'), axis=0, tiled=T...]
    unnamed x17 -> x26, local copies, waits for them, and re-layouts: 7 us -> 1.34 us
    ppermute x10, waiting for transfers between devices: 23.4 us -> 20.1 us  [shift(): lax.ppermute(value, axis, [(i, (i + step) % size) for i in range(size)])]
  transfers between devices with their start and end apart: 11 -> 11, of which waited for: 5 -> 7; matrix products, arithmetic and copies ran while one was open for 13% -> 7% of each run, Pallas kernels for 0% -> 0%
where the time goes in v15:
time: 119 us; the launch traced here: 118 us
  starting transfers between devices  33.3 us (28%)
  waiting for transfers between devices  32.4 us (27%)
  between operations  14.3 us (12%)
  Pallas kernels  13.6 us (11%)
  blocking collectives  12.9 us (11%)
  other arithmetic  9.74 us (8%)
  local copies, waits for them, and re-layouts  1.81 us (2%)
    ppermute x10, starting transfers between devices, shift(): lax.ppermute(value, axis, [(i, (i + step) % size) for i in range(size)])  33.3 us
    ppermute x10, waiting for transfers between devices, shift(): lax.ppermute(value, axis, [(i, (i + step) % size) for i in range(size)])  20.1 us
    pallas_call x1, Pallas kernels, row_stats(): pl.pallas_call(functools.partial(stats_kernel, len(blocks), dim), grid=(w...  13.6 us
    all_to_all x1, blocking collectives, on_device(): got = lax.all_to_all(packed, 'y', 1, 1, tiled=True).reshape(4, ny, mine)  12.9 us
    all_gather x1, waiting for transfers between devices, on_device(): lax.all_gather(jnp.concatenate(near, axis=0), ('z', 'c'), axis=0, tiled=T...  12.3 us
    another operation x3, other arithmetic  3.24 us
  transfers between devices with their start and end apart: 11, of which 7 were waited for; matrix products, arithmetic and copies ran while one was open for 7% of the time, Pallas kernels for 0%

profile of v15, /device:TPU:1, one launch (start us, length us, event | category | flops | bytes accessed | tf_op | source)
XLA Modules:
  0.0 118.1 jit_solution(463177952491491245)
XLA Ops:
  7.2 0.0 all-gather.2.cloned.1.call-start
  7.2 5.5 %collective-permute-start.1 = (bf16[32,1600]{1,0:T(8,128)(2,1)}, bf16[32,1600]{1,0:T(8,128)(2,1)S(1)}, u32[]{:S(2)}, u32[]{:S(2)}) collective-permute-start(bf16[32,1600]{1,0:T(8,128)(2,1)} %param.11), channel_id=1, source_target_pairs={{0,32},{16,48},{32,0},{48,16},{1,33},{17,49},{33,1},{49,17},{2,34}... | collective-permute-start | bytes 307208 | tf_op jit(solution)/shard_map/ppermute | solution.py:25
  12.7 2.8 %collective-permute-start = (bf16[32,1600]{1,0:T(8,128)(2,1)}, bf16[32,1600]{1,0:T(8,128)(2,1)S(1)}, u32[]{:S(2)}, u32[]{:S(2)}) collective-permute-start(bf16[32,1600]{1,0:T(8,128)(2,1)} %param.11), channel_id=1, source_target_pairs={{0,48},{16,0},{32,16},{48,32},{1,49},{17,1},{33,17},{49,33},{2,50}... | collective-permute-start | bytes 307208 | tf_op jit(solution)/shard_map/ppermute | solution.py:25
  15.5 2.5 %collective-permute-start.2 = (bf16[32,1600]{1,0:T(8,128)(2,1)}, bf16[32,1600]{1,0:T(8,128)(2,1)S(1)}, u32[]{:S(2)}, u32[]{:S(2)}) collective-permute-start(bf16[32,1600]{1,0:T(8,128)(2,1)} %param.11), channel_id=1, source_target_pairs={{0,16},{16,32},{32,48},{48,0},{1,17},{17,33},{33,49},{49,1},{2,18}... | collective-permute-start | bytes 307208 | tf_op jit(solution)/shard_map/ppermute | solution.py:25
  18.0 0.6 compare_reduce_fusion.1
  18.6 0.6 compare_reduce_fusion
  19.3 2.0 %fusion.11 = (bf16[128,1]{0,1:T(2,128)(2,1)S(1)}, bf16[128,1]{0,1:T(2,128)(2,1)S(1)}) fusion(pred[]{:T(512)} %compare_reduce_fusion, s32[128]{0:T(128)} %param.12, pred[]{:T(512)} %compare_reduce_fusion.1), kind=kLoop, calls=%fused_computation.71 | loop fusion | flops 2944 | bytes 1026 | tf_op jit(solution)/shard_map/reshape.452
  21.2 0.1 copy.15
  21.4 0.1 copy.14
  21.5 1.2 %copy.13 = bf16[128,1600]{1,0:T(8,128)(2,1)S(1)} copy(bf16[128,1600]{0,1:T(8,128)(2,1)} %param.9) | data formatting | bytes 819200 | tf_op args[0]
  22.8 0.2 fusion
  23.0 0.9 fusion.2
  23.8 0.2 scatter.9
  24.0 0.1 pad_maximum_fusion.refs_0_
  24.1 0.0 collective-permute-done.1
  24.1 0.0 collective-permute-done
  24.1 0.0 collective-permute-done.2
  24.2 1.8 %pad_maximum_fusion.1 = bf16[128,1600]{1,0:T(8,128)(2,1)} fusion(bf16[32,1600]{1,0:T(8,128)(2,1)S(1)} %collective-permute-done.2, bf16[32,1600]{1,0:T(8,128)(2,1)S(1)} %collective-permute-done.1, bf16[32,1600]{1,0:T(8,128)(2,1)S(1)} %collective-permute-done, bf16[32,1600]{1,0:T(8,128)(2,1)} %param.11), kind=kLoop, calls=%fused_computation.6 | loop fusion | flops 1638400 | bytes 819200 | tf_op jit(solution)/shard_map/concatenate | solution.py:137
  26.0 0.0 all-gather.2.cloned.1.call-update
  26.0 3.2 %collective-permute-start.6 = (bf16[128,1616]{1,0:T(8,128)(2,1)S(1)}, bf16[128,1616]{1,0:T(8,128)(2,1)S(1)}, u32[]{:S(2)}, u32[]{:S(2)}) collective-permute-start(bf16[128,1616]{1,0:T(8,128)(2,1)S(1)} %pad_maximum_fusion.refs_0_), channel_id=1, source_target_pairs={{0,1},{1,2},{2,3},{3,4},{4,5},{5,6},{6,7},{7,0},{8,9},{9,10},{10,1... | collective-permute-start | bytes 1241096 | tf_op jit(solution)/shard_map/ppermute | solution.py:25
  29.2 3.8 %collective-permute-start.3 = (bf16[128,1616]{1,0:T(8,128)(2,1)S(1)}, bf16[128,1616]{1,0:T(8,128)(2,1)S(1)}, u32[]{:S(2)}, u32[]{:S(2)}) collective-permute-start(bf16[128,1616]{1,0:T(8,128)(2,1)S(1)} %pad_maximum_fusion.refs_0_), channel_id=1, source_target_pairs={{0,7},{1,0},{2,1},{3,2},{4,3},{5,4},{6,5},{7,6},{8,15},{9,8},{10,9... | collective-permute-start | bytes 1241096 | tf_op jit(solution)/shard_map/ppermute | solution.py:25
  33.0 0.2 add_reduce_fusion.7
  33.2 4.3 %collective-permute-done.6.refs_7_ = bf16[128,1616]{1,0:T(8,128)(2,1)S(1)} collective-permute-done((bf16[128,1616]{1,0:T(8,128)(2,1)S(1)}, bf16[128,1616]{1,0:T(8,128)(2,1)S(1)}, u32[]{:S(2)}, u32[]{:S(2)}) %collective-permute-start.6) | collective-permute-done | bytes 413728 | tf_op jit(solution)/shard_map/ppermute | solution.py:25
  37.6 2.5 %collective-permute-start.7 = (bf16[128,1616]{1,0:T(8,128)(2,1)S(1)}, bf16[128,1616]{1,0:T(8,128)(2,1)S(1)}, u32[]{:S(2)}, u32[]{:S(2)}) collective-permute-start(bf16[128,1616]{1,0:T(8,128)(2,1)S(1)} %collective-permute-done.6.refs_7_), channel_id=1, source_target_pairs={{0,1},{1,2},{2,3},{3,4},{4,5},{5,6},{6,7},{7,0},{8,9},{9,10},{10,1... | collective-permute-start | bytes 1241096 | tf_op jit(solution)/shard_map/ppermute | solution.py:25
  40.1 0.0 collective-permute-done.3.refs_1_
  40.1 4.6 %collective-permute-start.4 = (bf16[128,1616]{1,0:T(8,128)(2,1)S(1)}, bf16[128,1616]{1,0:T(8,128)(2,1)S(1)}, u32[]{:S(2)}, u32[]{:S(2)}) collective-permute-start(bf16[128,1616]{1,0:T(8,128)(2,1)S(1)} %collective-permute-done.3.refs_1_), channel_id=1, source_target_pairs={{0,7},{1,0},{2,1},{3,2},{4,3},{5,4},{6,5},{7,6},{8,15},{9,8},{10,9... | collective-permute-start | bytes 1241096 | tf_op jit(solution)/shard_map/ppermute | solution.py:25
  44.7 0.2 add_reduce_fusion
  44.9 0.2 add_reduce_fusion.6
  45.1 3.8 %collective-permute-done.7.refs_6_ = bf16[128,1616]{1,0:T(8,128)(2,1)S(1)} collective-permute-done((bf16[128,1616]{1,0:T(8,128)(2,1)S(1)}, bf16[128,1616]{1,0:T(8,128)(2,1)S(1)}, u32[]{:S(2)}, u32[]{:S(2)}) %collective-permute-start.7) | collective-permute-done | bytes 413728 | tf_op jit(solution)/shard_map/ppermute | solution.py:25
  49.0 1.9 %collective-permute-start.8 = (bf16[128,1616]{1,0:T(8,128)(2,1)S(1)}, bf16[128,1616]{1,0:T(8,128)(2,1)S(1)}, u32[]{:S(2)}, u32[]{:S(2)}) collective-permute-start(bf16[128,1616]{1,0:T(8,128)(2,1)S(1)} %collective-permute-done.7.refs_6_), channel_id=1, source_target_pairs={{0,1},{1,2},{2,3},{3,4},{4,5},{5,6},{6,7},{7,0},{8,9},{9,10},{10,1... | collective-permute-start | bytes 1241096 | tf_op jit(solution)/shard_map/ppermute | solution.py:25
  50.9 0.1 collective-permute-done.4.refs_2_
  51.0 4.6 %collective-permute-start.5 = (bf16[128,1616]{1,0:T(8,128)(2,1)S(1)}, bf16[128,1616]{1,0:T(8,128)(2,1)S(1)}, u32[]{:S(2)}, u32[]{:S(2)}) collective-permute-start(bf16[128,1616]{1,0:T(8,128)(2,1)S(1)} %collective-permute-done.4.refs_2_), channel_id=1, source_target_pairs={{0,7},{1,0},{2,1},{3,2},{4,3},{5,4},{6,5},{7,6},{8,15},{9,8},{10,9... | collective-permute-start | bytes 1241096 | tf_op jit(solution)/shard_map/ppermute | solution.py:25
  55.6 0.2 add_reduce_fusion.1
  55.8 0.2 add_reduce_fusion.5
  56.0 3.6 %collective-permute-done.8.refs_5_ = bf16[128,1616]{1,0:T(8,128)(2,1)S(1)} collective-permute-done((bf16[128,1616]{1,0:T(8,128)(2,1)S(1)}, bf16[128,1616]{1,0:T(8,128)(2,1)S(1)}, u32[]{:S(2)}, u32[]{:S(2)}) %collective-permute-start.8) | collective-permute-done | bytes 413728 | tf_op jit(solution)/shard_map/ppermute | solution.py:25
  59.5 1.9 %collective-permute-start.9 = (bf16[128,1616]{1,0:T(8,128)(2,1)S(1)}, bf16[128,1616]{1,0:T(8,128)(2,1)S(1)}, u32[]{:S(2)}, u32[]{:S(2)}) collective-permute-start(bf16[128,1616]{1,0:T(8,128)(2,1)S(1)} %collective-permute-done.8.refs_5_), channel_id=1, source_target_pairs={{0,1},{1,2},{2,3},{3,4},{4,5},{5,6},{6,7},{7,0},{8,9},{9,10},{10,1... | collective-permute-start | bytes 1241096 | tf_op jit(solution)/shard_map/ppermute | solution.py:25
  61.5 0.2 add_reduce_fusion.2
  61.6 1.7 %collective-permute-done.5.refs_3_ = bf16[128,1616]{1,0:T(8,128)(2,1)S(1)} collective-permute-done((bf16[128,1616]{1,0:T(8,128)(2,1)S(1)}, bf16[128,1616]{1,0:T(8,128)(2,1)S(1)}, u32[]{:S(2)}, u32[]{:S(2)}) %collective-permute-start.5) | collective-permute-done | bytes 413728 | tf_op jit(solution)/shard_map/ppermute | solution.py:25
  63.4 0.2 add_reduce_fusion.4
  63.6 6.5 %collective-permute-done.9.refs_4_ = bf16[128,1616]{1,0:T(8,128)(2,1)S(1)} collective-permute-done((bf16[128,1616]{1,0:T(8,128)(2,1)S(1)}, bf16[128,1616]{1,0:T(8,128)(2,1)S(1)}, u32[]{:S(2)}, u32[]{:S(2)}) %collective-permute-start.9) | collective-permute-done | bytes 413728 | tf_op jit(solution)/shard_map/ppermute | solution.py:25
  70.0 0.2 add_reduce_fusion.3
  70.2 0.7 compare_select_fusion.4.refs_9_
  71.0 12.3 %all-gather.2.cloned.1.call-done.refs_8_ = bf16[2048,1600]{1,0:T(8,128)(2,1)} async-done(((bf16[128,1600]{1,0:T(8,128)(2,1)}), bf16[2048,1600]{1,0:T(8,128)(2,1)}) %all-gather.2.cloned.1.call-update) | async-done | bytes 6553616 | tf_op jit(solution)/shard_map/all_gather | solution.py:137
  83.3 0.0 copy-done.2
  83.4 13.6 %shard_map.68 = (f32[1,1024]{1,0:T(1,128)}, f32[1,1024]{1,0:T(1,128)}, f32[1,1024]{1,0:T(1,128)}, f32[1,1024]{1,0:T(1,128)}) custom-call(bf16[128,1616]{1,0:T(8,128)(2,1)} %copy-done, bf16[128,1616]{1,0:T(8,128)(2,1)} %copy-done.2, bf16[128,1616]{1,0:T(8,128)(2,1)} %copy-done.4, bf16[128,1616]{1,0:T(8,128)(2,1)} %copy-done.6, bf16[128,1616]{1,0:T(8,128)(2,1)} %copy-done.7, ...), custom_call_target="tpu_custom_call" | custom-call | flops 6710886400 | bytes 9830400 | tf_op jit(solution)/shard_map/pallas_call | solution.py:84
  97.0 0.7 maximum_bitcast_fusion
  97.7 12.9 %all_to_all.6 = f32[4,8,128]{2,0,1:T(4,128)S(1)} all-to-all(f32[4,8,128]{2,0,1:T(4,128)S(1)} %fusion.3), channel_id=1, replica_groups=mesh['z'=8,'x'=4,'c'=2,'y'=8] {'y'}, dimensions={1} | all-to-all | bytes 32768 | tf_op jit(solution)/shard_map/all_to_all | solution.py:147
  110.7 0.5 subtract_multiply_fusion
  (31 shorter events, 0.2 us)
Async XLA Ops:
  7.2 76.2 %all-gather.2.cloned.1.call-start = ((), (), s32[]{:S(2)}) async-start(), calls=%async_computation.1 | async-start | bytes 7241728 | tf_op jit(solution)/shard_map/all_gather | solution.py:137
  7.2 16.9 %collective-permute-start.1 = (bf16[32,1600]{1,0:T(8,128)(2,1)}, bf16[32,1600]{1,0:T(8,128)(2,1)S(1)}, u32[]{:S(2)}, u32[]{:S(2)}) collective-permute-start(bf16[32,1600]{1,0:T(8,128)(2,1)} %param.11), channel_id=1, source_target_pairs={{0,32},{16,48},{32,0},{48,16},{1,33},{17,49},{33,1},{49,17},{2,34}... | collective-permute-start | bytes 307208 | tf_op jit(solution)/shard_map/ppermute | solution.py:25
  12.7 11.4 %collective-permute-start = (bf16[32,1600]{1,0:T(8,128)(2,1)}, bf16[32,1600]{1,0:T(8,128)(2,1)S(1)}, u32[]{:S(2)}, u32[]{:S(2)}) collective-permute-start(bf16[32,1600]{1,0:T(8,128)(2,1)} %param.11), channel_id=1, source_target_pairs={{0,48},{16,0},{32,16},{48,32},{1,49},{17,1},{33,17},{49,33},{2,50}... | collective-permute-start | bytes 307208 | tf_op jit(solution)/shard_map/ppermute | solution.py:25
  15.5 8.7 %collective-permute-start.2 = (bf16[32,1600]{1,0:T(8,128)(2,1)}, bf16[32,1600]{1,0:T(8,128)(2,1)S(1)}, u32[]{:S(2)}, u32[]{:S(2)}) collective-permute-start(bf16[32,1600]{1,0:T(8,128)(2,1)} %param.11), channel_id=1, source_target_pairs={{0,16},{16,32},{32,48},{48,0},{1,17},{17,33},{33,49},{49,1},{2,18}... | collective-permute-start | bytes 307208 | tf_op jit(solution)/shard_map/ppermute | solution.py:25
  24.1 59.2 %copy-start = (bf16[128,1616]{1,0:T(8,128)(2,1)}, bf16[128,1616]{1,0:T(8,128)(2,1)S(1)}, u32[]{:S(2)}) copy-start(bf16[128,1616]{1,0:T(8,128)(2,1)S(1)} %pad_maximum_fusion.refs_0_) | copy-start | bytes 1241092
  26.0 11.6 %collective-permute-start.6 = (bf16[128,1616]{1,0:T(8,128)(2,1)S(1)}, bf16[128,1616]{1,0:T(8,128)(2,1)S(1)}, u32[]{:S(2)}, u32[]{:S(2)}) collective-permute-start(bf16[128,1616]{1,0:T(8,128)(2,1)S(1)} %pad_maximum_fusion.refs_0_), channel_id=1, source_target_pairs={{0,1},{1,2},{2,3},{3,4},{4,5},{5,6},{6,7},{7,0},{8,9},{9,10},{10,1... | collective-permute-start | bytes 1241096 | tf_op jit(solution)/shard_map/ppermute | solution.py:25
  29.2 10.9 %collective-permute-start.3 = (bf16[128,1616]{1,0:T(8,128)(2,1)S(1)}, bf16[128,1616]{1,0:T(8,128)(2,1)S(1)}, u32[]{:S(2)}, u32[]{:S(2)}) collective-permute-start(bf16[128,1616]{1,0:T(8,128)(2,1)S(1)} %pad_maximum_fusion.refs_0_), channel_id=1, source_target_pairs={{0,7},{1,0},{2,1},{3,2},{4,3},{5,4},{6,5},{7,6},{8,15},{9,8},{10,9... | collective-permute-start | bytes 1241096 | tf_op jit(solution)/shard_map/ppermute | solution.py:25
  37.6 45.8 %copy-start.1 = (bf16[128,1616]{1,0:T(8,128)(2,1)}, bf16[128,1616]{1,0:T(8,128)(2,1)S(1)}, u32[]{:S(2)}) copy-start(bf16[128,1616]{1,0:T(8,128)(2,1)S(1)} %collective-permute-done.6.refs_7_) | copy-start | bytes 1241092
  37.6 11.4 %collective-permute-start.7 = (bf16[128,1616]{1,0:T(8,128)(2,1)S(1)}, bf16[128,1616]{1,0:T(8,128)(2,1)S(1)}, u32[]{:S(2)}, u32[]{:S(2)}) collective-permute-start(bf16[128,1616]{1,0:T(8,128)(2,1)S(1)} %collective-permute-done.6.refs_7_), channel_id=1, source_target_pairs={{0,1},{1,2},{2,3},{3,4},{4,5},{5,6},{6,7},{7,0},{8,9},{9,10},{10,1... | collective-permute-start | bytes 1241096 | tf_op jit(solution)/shard_map/ppermute | solution.py:25
  40.1 43.2 %copy-start.2 = (bf16[128,1616]{1,0:T(8,128)(2,1)}, bf16[128,1616]{1,0:T(8,128)(2,1)S(1)}, u32[]{:S(2)}) copy-start(bf16[128,1616]{1,0:T(8,128)(2,1)S(1)} %collective-permute-done.3.refs_1_) | copy-start | bytes 1241092
  40.1 10.9 %collective-permute-start.4 = (bf16[128,1616]{1,0:T(8,128)(2,1)S(1)}, bf16[128,1616]{1,0:T(8,128)(2,1)S(1)}, u32[]{:S(2)}, u32[]{:S(2)}) collective-permute-start(bf16[128,1616]{1,0:T(8,128)(2,1)S(1)} %collective-permute-done.3.refs_1_), channel_id=1, source_target_pairs={{0,7},{1,0},{2,1},{3,2},{4,3},{5,4},{6,5},{7,6},{8,15},{9,8},{10,9... | collective-permute-start | bytes 1241096 | tf_op jit(solution)/shard_map/ppermute | solution.py:25
  49.0 34.4 %copy-start.3 = (bf16[128,1616]{1,0:T(8,128)(2,1)}, bf16[128,1616]{1,0:T(8,128)(2,1)S(1)}, u32[]{:S(2)}) copy-start(bf16[128,1616]{1,0:T(8,128)(2,1)S(1)} %collective-permute-done.7.refs_6_) | copy-start | bytes 1241092
  49.0 10.6 %collective-permute-start.8 = (bf16[128,1616]{1,0:T(8,128)(2,1)S(1)}, bf16[128,1616]{1,0:T(8,128)(2,1)S(1)}, u32[]{:S(2)}, u32[]{:S(2)}) collective-permute-start(bf16[128,1616]{1,0:T(8,128)(2,1)S(1)} %collective-permute-done.7.refs_6_), channel_id=1, source_target_pairs={{0,1},{1,2},{2,3},{3,4},{4,5},{5,6},{6,7},{7,0},{8,9},{9,10},{10,1... | collective-permute-start | bytes 1241096 | tf_op jit(solution)/shard_map/ppermute | solution.py:25
  51.0 32.3 %copy-start.4 = (bf16[128,1616]{1,0:T(8,128)(2,1)}, bf16[128,1616]{1,0:T(8,128)(2,1)S(1)}, u32[]{:S(2)}) copy-start(bf16[128,1616]{1,0:T(8,128)(2,1)S(1)} %collective-permute-done.4.refs_2_) | copy-start | bytes 1241092
  51.0 12.4 %collective-permute-start.5 = (bf16[128,1616]{1,0:T(8,128)(2,1)S(1)}, bf16[128,1616]{1,0:T(8,128)(2,1)S(1)}, u32[]{:S(2)}, u32[]{:S(2)}) collective-permute-start(bf16[128,1616]{1,0:T(8,128)(2,1)S(1)} %collective-permute-done.4.refs_2_), channel_id=1, source_target_pairs={{0,7},{1,0},{2,1},{3,2},{4,3},{5,4},{6,5},{7,6},{8,15},{9,8},{10,9... | collective-permute-start | bytes 1241096 | tf_op jit(solution)/shard_map/ppermute | solution.py:25
  59.5 23.8 %copy-start.5 = (bf16[128,1616]{1,0:T(8,128)(2,1)}, bf16[128,1616]{1,0:T(8,128)(2,1)S(1)}, u32[]{:S(2)}) copy-start(bf16[128,1616]{1,0:T(8,128)(2,1)S(1)} %collective-permute-done.8.refs_5_) | copy-start | bytes 1241092
  59.5 10.5 %collective-permute-start.9 = (bf16[128,1616]{1,0:T(8,128)(2,1)S(1)}, bf16[128,1616]{1,0:T(8,128)(2,1)S(1)}, u32[]{:S(2)}, u32[]{:S(2)}) collective-permute-start(bf16[128,1616]{1,0:T(8,128)(2,1)S(1)} %collective-permute-done.8.refs_5_), channel_id=1, source_target_pairs={{0,1},{1,2},{2,3},{3,4},{4,5},{5,6},{6,7},{7,0},{8,9},{9,10},{10,1... | collective-permute-start | bytes 1241096 | tf_op jit(solution)/shard_map/ppermute | solution.py:25
  63.4 20.0 %copy-start.6 = (bf16[128,1616]{1,0:T(8,128)(2,1)}, bf16[128,1616]{1,0:T(8,128)(2,1)S(1)}, u32[]{:S(2)}) copy-start(bf16[128,1616]{1,0:T(8,128)(2,1)S(1)} %collective-permute-done.5.refs_3_) | copy-start | bytes 1241092
  70.0 13.4 %copy-start.7 = (bf16[128,1616]{1,0:T(8,128)(2,1)}, bf16[128,1616]{1,0:T(8,128)(2,1)S(1)}, u32[]{:S(2)}) copy-start(bf16[128,1616]{1,0:T(8,128)(2,1)S(1)} %collective-permute-done.9.refs_4_) | copy-start | bytes 1241092
  71.0 39.7 %copy-start.8 = (s32[128]{0:T(128)S(1)}, s32[128]{0:T(128)}, u32[]{:S(2)}) copy-start(s32[128]{0:T(128)} %param.13) | copy-start | bytes 1540
Sparse Core Ops, SparseCore 0:
  26.1 57.1 all-gather.1

commit v16 on v15

--- a/solution.py
+++ b/solution.py
@@ -119,8 +119,8 @@
     nx = lax.axis_size("x")
     x = lax.axis_index("x")
     near = [unembed] + [shift(unembed, "x", nx, -d) for d in range(1, nx)]
-    block, *rest = lax.optimization_barrier((block, *near[1:]))
-    near[1:] = rest
+    table = jnp.concatenate(near, axis=0)
+    block, _ = lax.optimization_barrier((block, table))
 
     blocks = [None] * ny
     blocks[0] = block
@@ -134,7 +134,7 @@
         [b[:, dim].astype(jnp.int32) * 128 + b[:, dim + 1].astype(jnp.int32) for b in blocks], axis=0
     )
 
-    whole = lax.all_gather(jnp.concatenate(near, axis=0), ("z", "c"), axis=0, tiled=True)
+    whole = lax.all_gather(table, ("z", "c"), axis=0, tiled=True)
     owner, entry = wanted // width, wanted % width
     req, shard = owner // ny, owner % ny
     far_c, far_x, far_z = req % nc, (req // nc) % nx, req // (nc * nx)

time: 119 us -> 116 us (0.975)
  waiting for transfers between devices: 32.4 us -> 29.9 us
  other arithmetic: 9.74 us -> 7.93 us
  local copies, waits for them, and re-layouts: 1.81 us -> 3.52 us
    all_gather x1, waiting for transfers between devices: 12.3 us -> 6.34 us  [on_device(): whole = lax.all_gather(table, ('z', 'c'), axis=0, tiled=True)]
    ppermute x10, waiting for transfers between devices: 20.1 us -> 23.5 us  [shift(): lax.ppermute(value, axis, [(i, (i + step) % size) for i in range(size)])]
    concatenate x1 -> x0, other arithmetic: 1.82 us -> none  [on_device(): jnp.concatenate(near, axis=0)]
    unnamed x26 -> x31, local copies, waits for them, and re-layouts: 1.34 us -> 3.04 us
  transfers between devices with their start and end apart: 11 -> 11, of which waited for: 7 -> 6; matrix products, arithmetic and copies ran while one was open for 7% -> 8% of each run, Pallas kernels for 0% -> 0%
where the time goes in v16:
time: 116 us; the launch traced here: 114 us
  starting transfers between devices  32.2 us (28%)
  waiting for transfers between devices  29.9 us (26%)
  between operations  14.4 us (12%)
  Pallas kernels  13.6 us (12%)
  blocking collectives  12.9 us (11%)
  other arithmetic  7.93 us (7%)
  local copies, waits for them, and re-layouts  3.52 us (3%)
    ppermute x10, starting transfers between devices, shift(): lax.ppermute(value, axis, [(i, (i + step) % size) for i in range(size)])  32.1 us
    ppermute x10, waiting for transfers between devices, shift(): lax.ppermute(value, axis, [(i, (i + step) % size) for i in range(size)])  23.5 us
    pallas_call x1, Pallas kernels, row_stats(): pl.pallas_call(functools.partial(stats_kernel, len(blocks), dim), grid=(w...  13.6 us
    all_to_all x1, blocking collectives, on_device(): got = lax.all_to_all(packed, 'y', 1, 1, tiled=True).reshape(4, ny, mine)  12.9 us
    all_gather x1, waiting for transfers between devices, on_device(): whole = lax.all_gather(table, ('z', 'c'), axis=0, tiled=True)  6.34 us
    another operation x3, other arithmetic  3.24 us
    unnamed x31, local copies, waits for them, and re-layouts  3.04 us
  transfers between devices with their start and end apart: 11, of which 6 were waited for; matrix products, arithmetic and copies ran while one was open for 8% of the time, Pallas kernels for 0%

profile of v16, /device:TPU:1, one launch (start us, length us, event | category | flops | bytes accessed | tf_op | source)
XLA Modules:
  0.0 114.3 jit_solution(15088457996738424147)
XLA Ops:
  7.2 0.0 all-gather.2.cloned.1.call-start
  7.2 5.5 %collective-permute-start.1 = (bf16[32,1600]{1,0:T(8,128)(2,1)}, bf16[32,1600]{1,0:T(8,128)(2,1)S(1)}, u32[]{:S(2)}, u32[]{:S(2)}) collective-permute-start(bf16[32,1600]{1,0:T(8,128)(2,1)} %param.11), channel_id=1, source_target_pairs={{0,32},{16,48},{32,0},{48,16},{1,33},{17,49},{33,1},{49,17},{2,34}... | collective-permute-start | bytes 307208 | tf_op jit(solution)/shard_map/ppermute | solution.py:25
  12.7 2.8 %collective-permute-start = (bf16[32,1600]{1,0:T(8,128)(2,1)}, bf16[32,1600]{1,0:T(8,128)(2,1)S(1)}, u32[]{:S(2)}, u32[]{:S(2)}) collective-permute-start(bf16[32,1600]{1,0:T(8,128)(2,1)} %param.11), channel_id=1, source_target_pairs={{0,48},{16,0},{32,16},{48,32},{1,49},{17,1},{33,17},{49,33},{2,50}... | collective-permute-start | bytes 307208 | tf_op jit(solution)/shard_map/ppermute | solution.py:25
  15.5 2.5 %collective-permute-start.2 = (bf16[32,1600]{1,0:T(8,128)(2,1)}, bf16[32,1600]{1,0:T(8,128)(2,1)S(1)}, u32[]{:S(2)}, u32[]{:S(2)}) collective-permute-start(bf16[32,1600]{1,0:T(8,128)(2,1)} %param.11), channel_id=1, source_target_pairs={{0,16},{16,32},{32,48},{48,0},{1,17},{17,33},{33,49},{49,1},{2,18}... | collective-permute-start | bytes 307208 | tf_op jit(solution)/shard_map/ppermute | solution.py:25
  18.0 0.9 constant_dynamic-update-slice_fusion.3
  18.9 0.0 collective-permute-done
  18.9 0.0 collective-permute-done.1
  19.0 4.2 %collective-permute-done.2 = bf16[32,1600]{1,0:T(8,128)(2,1)S(1)} collective-permute-done((bf16[32,1600]{1,0:T(8,128)(2,1)}, bf16[32,1600]{1,0:T(8,128)(2,1)S(1)}, u32[]{:S(2)}, u32[]{:S(2)}) %collective-permute-start.2) | collective-permute-done | bytes 102432 | tf_op jit(solution)/shard_map/ppermute | solution.py:25
  23.2 0.7 copy-done
  23.9 0.0 all-gather.2.cloned.1.call-update
  23.9 0.6 compare_reduce_fusion.1
  24.6 0.6 compare_reduce_fusion
  25.2 2.0 %fusion.11 = (bf16[128,1]{0,1:T(2,128)(2,1)S(1)}, bf16[128,1]{0,1:T(2,128)(2,1)S(1)}) fusion(pred[]{:T(512)} %compare_reduce_fusion, s32[128]{0:T(128)} %param.12, pred[]{:T(512)} %compare_reduce_fusion.1), kind=kLoop, calls=%fused_computation.74 | loop fusion | flops 2944 | bytes 1026 | tf_op jit(solution)/shard_map/reshape.452
  27.2 0.1 copy.15
  27.3 0.1 copy.14
  27.5 1.2 %copy.13 = bf16[128,1600]{1,0:T(8,128)(2,1)S(1)} copy(bf16[128,1600]{0,1:T(8,128)(2,1)} %param.9) | data formatting | bytes 819200 | tf_op args[0]
  28.7 0.2 scatter.9
  28.9 0.2 fusion
  29.1 0.9 fusion.2
  30.0 0.1 pad_maximum_fusion.refs_0_
  30.1 2.4 %collective-permute-start.6 = (bf16[128,1616]{1,0:T(8,128)(2,1)S(1)}, bf16[128,1616]{1,0:T(8,128)(2,1)S(1)}, u32[]{:S(2)}, u32[]{:S(2)}) collective-permute-start(bf16[128,1616]{1,0:T(8,128)(2,1)S(1)} %pad_maximum_fusion.refs_0_), channel_id=1, source_target_pairs={{0,1},{1,2},{2,3},{3,4},{4,5},{5,6},{6,7},{7,0},{8,9},{9,10},{10,1... | collective-permute-start | bytes 1241096 | tf_op jit(solution)/shard_map/ppermute | solution.py:25
  32.5 4.1 %collective-permute-start.3 = (bf16[128,1616]{1,0:T(8,128)(2,1)S(1)}, bf16[128,1616]{1,0:T(8,128)(2,1)S(1)}, u32[]{:S(2)}, u32[]{:S(2)}) collective-permute-start(bf16[128,1616]{1,0:T(8,128)(2,1)S(1)} %pad_maximum_fusion.refs_0_), channel_id=1, source_target_pairs={{0,7},{1,0},{2,1},{3,2},{4,3},{5,4},{6,5},{7,6},{8,15},{9,8},{10,9... | collective-permute-start | bytes 1241096 | tf_op jit(solution)/shard_map/ppermute | solution.py:25
  36.6 0.2 add_reduce_fusion.7
  36.8 4.0 %collective-permute-done.6.refs_7_ = bf16[128,1616]{1,0:T(8,128)(2,1)S(1)} collective-permute-done((bf16[128,1616]{1,0:T(8,128)(2,1)S(1)}, bf16[128,1616]{1,0:T(8,128)(2,1)S(1)}, u32[]{:S(2)}, u32[]{:S(2)}) %collective-permute-start.6) | collective-permute-done | bytes 413728 | tf_op jit(solution)/shard_map/ppermute | solution.py:25
  40.8 1.9 %collective-permute-start.7 = (bf16[128,1616]{1,0:T(8,128)(2,1)S(1)}, bf16[128,1616]{1,0:T(8,128)(2,1)S(1)}, u32[]{:S(2)}, u32[]{:S(2)}) collective-permute-start(bf16[128,1616]{1,0:T(8,128)(2,1)S(1)} %collective-permute-done.6.refs_7_), channel_id=1, source_target_pairs={{0,1},{1,2},{2,3},{3,4},{4,5},{5,6},{6,7},{7,0},{8,9},{9,10},{10,1... | collective-permute-start | bytes 1241096 | tf_op jit(solution)/shard_map/ppermute | solution.py:25
  42.8 0.0 collective-permute-done.3.refs_1_
  42.8 4.5 %collective-permute-start.4 = (bf16[128,1616]{1,0:T(8,128)(2,1)S(1)}, bf16[128,1616]{1,0:T(8,128)(2,1)S(1)}, u32[]{:S(2)}, u32[]{:S(2)}) collective-permute-start(bf16[128,1616]{1,0:T(8,128)(2,1)S(1)} %collective-permute-done.3.refs_1_), channel_id=1, source_target_pairs={{0,7},{1,0},{2,1},{3,2},{4,3},{5,4},{6,5},{7,6},{8,15},{9,8},{10,9... | collective-permute-start | bytes 1241096 | tf_op jit(solution)/shard_map/ppermute | solution.py:25
  47.3 0.2 add_reduce_fusion
  47.5 0.2 add_reduce_fusion.6
  47.7 3.6 %collective-permute-done.7.refs_6_ = bf16[128,1616]{1,0:T(8,128)(2,1)S(1)} collective-permute-done((bf16[128,1616]{1,0:T(8,128)(2,1)S(1)}, bf16[128,1616]{1,0:T(8,128)(2,1)S(1)}, u32[]{:S(2)}, u32[]{:S(2)}) %collective-permute-start.7) | collective-permute-done | bytes 413728 | tf_op jit(solution)/shard_map/ppermute | solution.py:25
  51.3 1.9 %collective-permute-start.8 = (bf16[128,1616]{1,0:T(8,128)(2,1)S(1)}, bf16[128,1616]{1,0:T(8,128)(2,1)S(1)}, u32[]{:S(2)}, u32[]{:S(2)}) collective-permute-start(bf16[128,1616]{1,0:T(8,128)(2,1)S(1)} %collective-permute-done.7.refs_6_), channel_id=1, source_target_pairs={{0,1},{1,2},{2,3},{3,4},{4,5},{5,6},{6,7},{7,0},{8,9},{9,10},{10,1... | collective-permute-start | bytes 1241096 | tf_op jit(solution)/shard_map/ppermute | solution.py:25
  53.2 0.0 collective-permute-done.4.refs_2_
  53.2 4.6 %collective-permute-start.5 = (bf16[128,1616]{1,0:T(8,128)(2,1)S(1)}, bf16[128,1616]{1,0:T(8,128)(2,1)S(1)}, u32[]{:S(2)}, u32[]{:S(2)}) collective-permute-start(bf16[128,1616]{1,0:T(8,128)(2,1)S(1)} %collective-permute-done.4.refs_2_), channel_id=1, source_target_pairs={{0,7},{1,0},{2,1},{3,2},{4,3},{5,4},{6,5},{7,6},{8,15},{9,8},{10,9... | collective-permute-start | bytes 1241096 | tf_op jit(solution)/shard_map/ppermute | solution.py:25
  57.8 0.2 add_reduce_fusion.1
  58.0 0.2 add_reduce_fusion.5
  58.2 3.6 %collective-permute-done.8.refs_5_ = bf16[128,1616]{1,0:T(8,128)(2,1)S(1)} collective-permute-done((bf16[128,1616]{1,0:T(8,128)(2,1)S(1)}, bf16[128,1616]{1,0:T(8,128)(2,1)S(1)}, u32[]{:S(2)}, u32[]{:S(2)}) %collective-permute-start.8) | collective-permute-done | bytes 413728 | tf_op jit(solution)/shard_map/ppermute | solution.py:25
  61.8 1.9 %collective-permute-start.9 = (bf16[128,1616]{1,0:T(8,128)(2,1)S(1)}, bf16[128,1616]{1,0:T(8,128)(2,1)S(1)}, u32[]{:S(2)}, u32[]{:S(2)}) collective-permute-start(bf16[128,1616]{1,0:T(8,128)(2,1)S(1)} %collective-permute-done.8.refs_5_), channel_id=1, source_target_pairs={{0,1},{1,2},{2,3},{3,4},{4,5},{5,6},{6,7},{7,0},{8,9},{9,10},{10,1... | collective-permute-start | bytes 1241096 | tf_op jit(solution)/shard_map/ppermute | solution.py:25
  63.7 0.2 add_reduce_fusion.2
  63.9 0.0 collective-permute-done.5.refs_3_
  63.9 0.2 add_reduce_fusion.4
  64.1 8.2 %collective-permute-done.9.refs_4_ = bf16[128,1616]{1,0:T(8,128)(2,1)S(1)} collective-permute-done((bf16[128,1616]{1,0:T(8,128)(2,1)S(1)}, bf16[128,1616]{1,0:T(8,128)(2,1)S(1)}, u32[]{:S(2)}, u32[]{:S(2)}) %collective-permute-start.9) | collective-permute-done | bytes 413728 | tf_op jit(solution)/shard_map/ppermute | solution.py:25
  72.2 0.2 add_reduce_fusion.3
  72.5 0.7 compare_select_fusion.4.refs_9_
  73.2 6.3 %all-gather.2.cloned.1.call-done.refs_8_ = bf16[2048,1600]{1,0:T(8,128)(2,1)} async-done(((bf16[128,1600]{1,0:T(8,128)(2,1)}), bf16[2048,1600]{1,0:T(8,128)(2,1)}) %all-gather.2.cloned.1.call-update) | async-done | bytes 6553616 | tf_op jit(solution)/shard_map/all_gather | solution.py:137
  79.6 13.6 %shard_map.68 = (f32[1,1024]{1,0:T(1,128)}, f32[1,1024]{1,0:T(1,128)}, f32[1,1024]{1,0:T(1,128)}, f32[1,1024]{1,0:T(1,128)}) custom-call(bf16[128,1616]{1,0:T(8,128)(2,1)} %copy-done.1, bf16[128,1616]{1,0:T(8,128)(2,1)} %copy-done.3, bf16[128,1616]{1,0:T(8,128)(2,1)} %copy-done.5, bf16[128,1616]{1,0:T(8,128)(2,1)} %copy-done.7, bf16[128,1616]{1,0:T(8,128)(2,1)} %copy-done.8, ...), custom_call_target="tpu_custom_call" | custom-call | flops 6710886400 | bytes 9830400 | tf_op jit(solution)/shard_map/pallas_call | solution.py:84
  93.2 0.7 maximum_bitcast_fusion
  94.0 12.9 %all_to_all.6 = f32[4,8,128]{2,0,1:T(4,128)S(1)} all-to-all(f32[4,8,128]{2,0,1:T(4,128)S(1)} %fusion.3), channel_id=1, replica_groups=mesh['z'=8,'x'=4,'c'=2,'y'=8] {'y'}, dimensions={1} | all-to-all | bytes 32768 | tf_op jit(solution)/shard_map/all_to_all | solution.py:147
  106.9 0.5 subtract_multiply_fusion
  (36 shorter events, 0.3 us)
Async XLA Ops:
  7.2 72.4 %all-gather.2.cloned.1.call-start = ((), (), s32[]{:S(2)}) async-start(), calls=%async_computation.1 | async-start | bytes 7241728 | tf_op jit(solution)/shard_map/all_gather | solution.py:137
  7.2 11.7 %collective-permute-start.1 = (bf16[32,1600]{1,0:T(8,128)(2,1)}, bf16[32,1600]{1,0:T(8,128)(2,1)S(1)}, u32[]{:S(2)}, u32[]{:S(2)}) collective-permute-start(bf16[32,1600]{1,0:T(8,128)(2,1)} %param.11), channel_id=1, source_target_pairs={{0,32},{16,48},{32,0},{48,16},{1,33},{17,49},{33,1},{49,17},{2,34}... | collective-permute-start | bytes 307208 | tf_op jit(solution)/shard_map/ppermute | solution.py:25
  12.7 6.2 %collective-permute-start = (bf16[32,1600]{1,0:T(8,128)(2,1)}, bf16[32,1600]{1,0:T(8,128)(2,1)S(1)}, u32[]{:S(2)}, u32[]{:S(2)}) collective-permute-start(bf16[32,1600]{1,0:T(8,128)(2,1)} %param.11), channel_id=1, source_target_pairs={{0,48},{16,0},{32,16},{48,32},{1,49},{17,1},{33,17},{49,33},{2,50}... | collective-permute-start | bytes 307208 | tf_op jit(solution)/shard_map/ppermute | solution.py:25
  15.5 7.7 %collective-permute-start.2 = (bf16[32,1600]{1,0:T(8,128)(2,1)}, bf16[32,1600]{1,0:T(8,128)(2,1)S(1)}, u32[]{:S(2)}, u32[]{:S(2)}) collective-permute-start(bf16[32,1600]{1,0:T(8,128)(2,1)} %param.11), channel_id=1, source_target_pairs={{0,16},{16,32},{32,48},{48,0},{1,17},{17,33},{33,49},{49,1},{2,18}... | collective-permute-start | bytes 307208 | tf_op jit(solution)/shard_map/ppermute | solution.py:25
  23.2 0.8 copy-start
  30.1 49.5 %copy-start.1 = (bf16[128,1616]{1,0:T(8,128)(2,1)}, bf16[128,1616]{1,0:T(8,128)(2,1)S(1)}, u32[]{:S(2)}) copy-start(bf16[128,1616]{1,0:T(8,128)(2,1)S(1)} %pad_maximum_fusion.refs_0_) | copy-start | bytes 1241092
  30.1 10.8 %collective-permute-start.6 = (bf16[128,1616]{1,0:T(8,128)(2,1)S(1)}, bf16[128,1616]{1,0:T(8,128)(2,1)S(1)}, u32[]{:S(2)}, u32[]{:S(2)}) collective-permute-start(bf16[128,1616]{1,0:T(8,128)(2,1)S(1)} %pad_maximum_fusion.refs_0_), channel_id=1, source_target_pairs={{0,1},{1,2},{2,3},{3,4},{4,5},{5,6},{6,7},{7,0},{8,9},{9,10},{10,1... | collective-permute-start | bytes 1241096 | tf_op jit(solution)/shard_map/ppermute | solution.py:25
  32.5 10.3 %collective-permute-start.3 = (bf16[128,1616]{1,0:T(8,128)(2,1)S(1)}, bf16[128,1616]{1,0:T(8,128)(2,1)S(1)}, u32[]{:S(2)}, u32[]{:S(2)}) collective-permute-start(bf16[128,1616]{1,0:T(8,128)(2,1)S(1)} %pad_maximum_fusion.refs_0_), channel_id=1, source_target_pairs={{0,7},{1,0},{2,1},{3,2},{4,3},{5,4},{6,5},{7,6},{8,15},{9,8},{10,9... | collective-permute-start | bytes 1241096 | tf_op jit(solution)/shard_map/ppermute | solution.py:25
  40.8 38.7 %copy-start.2 = (bf16[128,1616]{1,0:T(8,128)(2,1)}, bf16[128,1616]{1,0:T(8,128)(2,1)S(1)}, u32[]{:S(2)}) copy-start(bf16[128,1616]{1,0:T(8,128)(2,1)S(1)} %collective-permute-done.6.refs_7_) | copy-start | bytes 1241092
  40.8 10.5 %collective-permute-start.7 = (bf16[128,1616]{1,0:T(8,128)(2,1)S(1)}, bf16[128,1616]{1,0:T(8,128)(2,1)S(1)}, u32[]{:S(2)}, u32[]{:S(2)}) collective-permute-start(bf16[128,1616]{1,0:T(8,128)(2,1)S(1)} %collective-permute-done.6.refs_7_), channel_id=1, source_target_pairs={{0,1},{1,2},{2,3},{3,4},{4,5},{5,6},{6,7},{7,0},{8,9},{9,10},{10,1... | collective-permute-start | bytes 1241096 | tf_op jit(solution)/shard_map/ppermute | solution.py:25
  42.8 36.8 %copy-start.3 = (bf16[128,1616]{1,0:T(8,128)(2,1)}, bf16[128,1616]{1,0:T(8,128)(2,1)S(1)}, u32[]{:S(2)}) copy-start(bf16[128,1616]{1,0:T(8,128)(2,1)S(1)} %collective-permute-done.3.refs_1_) | copy-start | bytes 1241092
  42.8 10.4 %collective-permute-start.4 = (bf16[128,1616]{1,0:T(8,128)(2,1)S(1)}, bf16[128,1616]{1,0:T(8,128)(2,1)S(1)}, u32[]{:S(2)}, u32[]{:S(2)}) collective-permute-start(bf16[128,1616]{1,0:T(8,128)(2,1)S(1)} %collective-permute-done.3.refs_1_), channel_id=1, source_target_pairs={{0,7},{1,0},{2,1},{3,2},{4,3},{5,4},{6,5},{7,6},{8,15},{9,8},{10,9... | collective-permute-start | bytes 1241096 | tf_op jit(solution)/shard_map/ppermute | solution.py:25
  51.3 28.3 %copy-start.4 = (bf16[128,1616]{1,0:T(8,128)(2,1)}, bf16[128,1616]{1,0:T(8,128)(2,1)S(1)}, u32[]{:S(2)}) copy-start(bf16[128,1616]{1,0:T(8,128)(2,1)S(1)} %collective-permute-done.7.refs_6_) | copy-start | bytes 1241092
  51.3 10.5 %collective-permute-start.8 = (bf16[128,1616]{1,0:T(8,128)(2,1)S(1)}, bf16[128,1616]{1,0:T(8,128)(2,1)S(1)}, u32[]{:S(2)}, u32[]{:S(2)}) collective-permute-start(bf16[128,1616]{1,0:T(8,128)(2,1)S(1)} %collective-permute-done.7.refs_6_), channel_id=1, source_target_pairs={{0,1},{1,2},{2,3},{3,4},{4,5},{5,6},{6,7},{7,0},{8,9},{9,10},{10,1... | collective-permute-start | bytes 1241096 | tf_op jit(solution)/shard_map/ppermute | solution.py:25
  53.2 26.4 %copy-start.5 = (bf16[128,1616]{1,0:T(8,128)(2,1)}, bf16[128,1616]{1,0:T(8,128)(2,1)S(1)}, u32[]{:S(2)}) copy-start(bf16[128,1616]{1,0:T(8,128)(2,1)S(1)} %collective-permute-done.4.refs_2_) | copy-start | bytes 1241092
  53.2 10.6 %collective-permute-start.5 = (bf16[128,1616]{1,0:T(8,128)(2,1)S(1)}, bf16[128,1616]{1,0:T(8,128)(2,1)S(1)}, u32[]{:S(2)}, u32[]{:S(2)}) collective-permute-start(bf16[128,1616]{1,0:T(8,128)(2,1)S(1)} %collective-permute-done.4.refs_2_), channel_id=1, source_target_pairs={{0,7},{1,0},{2,1},{3,2},{4,3},{5,4},{6,5},{7,6},{8,15},{9,8},{10,9... | collective-permute-start | bytes 1241096 | tf_op jit(solution)/shard_map/ppermute | solution.py:25
  61.8 17.8 %copy-start.6 = (bf16[128,1616]{1,0:T(8,128)(2,1)}, bf16[128,1616]{1,0:T(8,128)(2,1)S(1)}, u32[]{:S(2)}) copy-start(bf16[128,1616]{1,0:T(8,128)(2,1)S(1)} %collective-permute-done.8.refs_5_) | copy-start | bytes 1241092
  61.8 10.5 %collective-permute-start.9 = (bf16[128,1616]{1,0:T(8,128)(2,1)S(1)}, bf16[128,1616]{1,0:T(8,128)(2,1)S(1)}, u32[]{:S(2)}, u32[]{:S(2)}) collective-permute-start(bf16[128,1616]{1,0:T(8,128)(2,1)S(1)} %collective-permute-done.8.refs_5_), channel_id=1, source_target_pairs={{0,1},{1,2},{2,3},{3,4},{4,5},{5,6},{6,7},{7,0},{8,9},{9,10},{10,1... | collective-permute-start | bytes 1241096 | tf_op jit(solution)/shard_map/ppermute | solution.py:25
  63.9 15.7 %copy-start.7 = (bf16[128,1616]{1,0:T(8,128)(2,1)}, bf16[128,1616]{1,0:T(8,128)(2,1)S(1)}, u32[]{:S(2)}) copy-start(bf16[128,1616]{1,0:T(8,128)(2,1)S(1)} %collective-permute-done.5.refs_3_) | copy-start | bytes 1241092
  72.2 7.4 %copy-start.8 = (bf16[128,1616]{1,0:T(8,128)(2,1)}, bf16[128,1616]{1,0:T(8,128)(2,1)S(1)}, u32[]{:S(2)}) copy-start(bf16[128,1616]{1,0:T(8,128)(2,1)S(1)} %collective-permute-done.9.refs_4_) | copy-start | bytes 1241092
  73.2 33.7 %copy-start.9 = (s32[128]{0:T(128)S(1)}, s32[128]{0:T(128)}, u32[]{:S(2)}) copy-start(s32[128]{0:T(128)} %param.13) | copy-start | bytes 1540
Sparse Core Ops, SparseCore 0:
  24.1 55.4 all-gather.1

commit v17 on v16

--- a/solution.py
+++ b/solution.py
@@ -75,7 +75,7 @@
     top_ref[...] = top
 
 
-def row_stats(blocks, dim, vocab, spot, tile=512):
+def row_stats(blocks, dim, vocab, spot, tile=1024):
     size = blocks[0].shape[0]
     count = size * len(blocks)
     width = vocab.shape[0]

time: 116 us -> 116 us (level)
  no operation moved by 1% of the time
where the time goes in v17:
time: 116 us; the launch traced here: 114 us
  starting transfers between devices  32.2 us (28%)
  waiting for transfers between devices  29.9 us (26%)
  between operations  14.4 us (12%)
  Pallas kernels  13.6 us (12%)
  blocking collectives  12.9 us (11%)
  other arithmetic  7.93 us (7%)
  local copies, waits for them, and re-layouts  3.52 us (3%)
    ppermute x10, starting transfers between devices, shift(): lax.ppermute(value, axis, [(i, (i + step) % size) for i in range(size)])  32.1 us
    ppermute x10, waiting for transfers between devices, shift(): lax.ppermute(value, axis, [(i, (i + step) % size) for i in range(size)])  23.5 us
    pallas_call x1, Pallas kernels, row_stats(): pl.pallas_call(functools.partial(stats_kernel, len(blocks), dim), grid=(w...  13.6 us
    all_to_all x1, blocking collectives, on_device(): got = lax.all_to_all(packed, 'y', 1, 1, tiled=True).reshape(4, ny, mine)  12.9 us
    all_gather x1, waiting for transfers between devices, on_device(): whole = lax.all_gather(table, ('z', 'c'), axis=0, tiled=True)  6.34 us
    another operation x3, other arithmetic  3.24 us
    unnamed x31, local copies, waits for them, and re-layouts  3.04 us
  transfers between devices with their start and end apart: 11, of which 6 were waited for; matrix products, arithmetic and copies ran while one was open for 8% of the time, Pallas kernels for 0%

profile of v17, /device:TPU:1, one launch (start us, length us, event | category | flops | bytes accessed | tf_op | source)
XLA Modules:
  0.0 114.3 jit_solution(1232857281456118154)
XLA Ops:
  7.2 0.0 all-gather.2.cloned.1.call-start
  7.2 5.5 %collective-permute-start.1 = (bf16[32,1600]{1,0:T(8,128)(2,1)}, bf16[32,1600]{1,0:T(8,128)(2,1)S(1)}, u32[]{:S(2)}, u32[]{:S(2)}) collective-permute-start(bf16[32,1600]{1,0:T(8,128)(2,1)} %param.11), channel_id=1, source_target_pairs={{0,32},{16,48},{32,0},{48,16},{1,33},{17,49},{33,1},{49,17},{2,34}... | collective-permute-start | bytes 307208 | tf_op jit(solution)/shard_map/ppermute | solution.py:25
  12.7 2.8 %collective-permute-start = (bf16[32,1600]{1,0:T(8,128)(2,1)}, bf16[32,1600]{1,0:T(8,128)(2,1)S(1)}, u32[]{:S(2)}, u32[]{:S(2)}) collective-permute-start(bf16[32,1600]{1,0:T(8,128)(2,1)} %param.11), channel_id=1, source_target_pairs={{0,48},{16,0},{32,16},{48,32},{1,49},{17,1},{33,17},{49,33},{2,50}... | collective-permute-start | bytes 307208 | tf_op jit(solution)/shard_map/ppermute | solution.py:25
  15.5 2.5 %collective-permute-start.2 = (bf16[32,1600]{1,0:T(8,128)(2,1)}, bf16[32,1600]{1,0:T(8,128)(2,1)S(1)}, u32[]{:S(2)}, u32[]{:S(2)}) collective-permute-start(bf16[32,1600]{1,0:T(8,128)(2,1)} %param.11), channel_id=1, source_target_pairs={{0,16},{16,32},{32,48},{48,0},{1,17},{17,33},{33,49},{49,1},{2,18}... | collective-permute-start | bytes 307208 | tf_op jit(solution)/shard_map/ppermute | solution.py:25
  18.0 0.9 constant_dynamic-update-slice_fusion.3
  18.9 0.0 collective-permute-done
  18.9 0.0 collective-permute-done.1
  19.0 4.2 %collective-permute-done.2 = bf16[32,1600]{1,0:T(8,128)(2,1)S(1)} collective-permute-done((bf16[32,1600]{1,0:T(8,128)(2,1)}, bf16[32,1600]{1,0:T(8,128)(2,1)S(1)}, u32[]{:S(2)}, u32[]{:S(2)}) %collective-permute-start.2) | collective-permute-done | bytes 102432 | tf_op jit(solution)/shard_map/ppermute | solution.py:25
  23.2 0.7 copy-done
  23.9 0.0 all-gather.2.cloned.1.call-update
  23.9 0.6 compare_reduce_fusion.1
  24.6 0.6 compare_reduce_fusion
  25.2 2.0 %fusion.11 = (bf16[128,1]{0,1:T(2,128)(2,1)S(1)}, bf16[128,1]{0,1:T(2,128)(2,1)S(1)}) fusion(pred[]{:T(512)} %compare_reduce_fusion, s32[128]{0:T(128)} %param.12, pred[]{:T(512)} %compare_reduce_fusion.1), kind=kLoop, calls=%fused_computation.74 | loop fusion | flops 2944 | bytes 1026 | tf_op jit(solution)/shard_map/reshape.452
  27.2 0.1 copy.15
  27.3 0.1 copy.14
  27.5 1.2 %copy.13 = bf16[128,1600]{1,0:T(8,128)(2,1)S(1)} copy(bf16[128,1600]{0,1:T(8,128)(2,1)} %param.9) | data formatting | bytes 819200 | tf_op args[0]
  28.7 0.2 scatter.9
  28.9 0.2 fusion
  29.1 0.9 fusion.2
  30.0 0.1 pad_maximum_fusion.refs_0_
  30.1 2.4 %collective-permute-start.6 = (bf16[128,1616]{1,0:T(8,128)(2,1)S(1)}, bf16[128,1616]{1,0:T(8,128)(2,1)S(1)}, u32[]{:S(2)}, u32[]{:S(2)}) collective-permute-start(bf16[128,1616]{1,0:T(8,128)(2,1)S(1)} %pad_maximum_fusion.refs_0_), channel_id=1, source_target_pairs={{0,1},{1,2},{2,3},{3,4},{4,5},{5,6},{6,7},{7,0},{8,9},{9,10},{10,1... | collective-permute-start | bytes 1241096 | tf_op jit(solution)/shard_map/ppermute | solution.py:25
  32.5 4.1 %collective-permute-start.3 = (bf16[128,1616]{1,0:T(8,128)(2,1)S(1)}, bf16[128,1616]{1,0:T(8,128)(2,1)S(1)}, u32[]{:S(2)}, u32[]{:S(2)}) collective-permute-start(bf16[128,1616]{1,0:T(8,128)(2,1)S(1)} %pad_maximum_fusion.refs_0_), channel_id=1, source_target_pairs={{0,7},{1,0},{2,1},{3,2},{4,3},{5,4},{6,5},{7,6},{8,15},{9,8},{10,9... | collective-permute-start | bytes 1241096 | tf_op jit(solution)/shard_map/ppermute | solution.py:25
  36.6 0.2 add_reduce_fusion.7
  36.8 4.0 %collective-permute-done.6.refs_7_ = bf16[128,1616]{1,0:T(8,128)(2,1)S(1)} collective-permute-done((bf16[128,1616]{1,0:T(8,128)(2,1)S(1)}, bf16[128,1616]{1,0:T(8,128)(2,1)S(1)}, u32[]{:S(2)}, u32[]{:S(2)}) %collective-permute-start.6) | collective-permute-done | bytes 413728 | tf_op jit(solution)/shard_map/ppermute | solution.py:25
  40.8 1.9 %collective-permute-start.7 = (bf16[128,1616]{1,0:T(8,128)(2,1)S(1)}, bf16[128,1616]{1,0:T(8,128)(2,1)S(1)}, u32[]{:S(2)}, u32[]{:S(2)}) collective-permute-start(bf16[128,1616]{1,0:T(8,128)(2,1)S(1)} %collective-permute-done.6.refs_7_), channel_id=1, source_target_pairs={{0,1},{1,2},{2,3},{3,4},{4,5},{5,6},{6,7},{7,0},{8,9},{9,10},{10,1... | collective-permute-start | bytes 1241096 | tf_op jit(solution)/shard_map/ppermute | solution.py:25
  42.8 0.0 collective-permute-done.3.refs_1_
  42.8 4.5 %collective-permute-start.4 = (bf16[128,1616]{1,0:T(8,128)(2,1)S(1)}, bf16[128,1616]{1,0:T(8,128)(2,1)S(1)}, u32[]{:S(2)}, u32[]{:S(2)}) collective-permute-start(bf16[128,1616]{1,0:T(8,128)(2,1)S(1)} %collective-permute-done.3.refs_1_), channel_id=1, source_target_pairs={{0,7},{1,0},{2,1},{3,2},{4,3},{5,4},{6,5},{7,6},{8,15},{9,8},{10,9... | collective-permute-start | bytes 1241096 | tf_op jit(solution)/shard_map/ppermute | solution.py:25
  47.3 0.2 add_reduce_fusion
  47.5 0.2 add_reduce_fusion.6
  47.7 3.6 %collective-permute-done.7.refs_6_ = bf16[128,1616]{1,0:T(8,128)(2,1)S(1)} collective-permute-done((bf16[128,1616]{1,0:T(8,128)(2,1)S(1)}, bf16[128,1616]{1,0:T(8,128)(2,1)S(1)}, u32[]{:S(2)}, u32[]{:S(2)}) %collective-permute-start.7) | collective-permute-done | bytes 413728 | tf_op jit(solution)/shard_map/ppermute | solution.py:25
  51.3 1.9 %collective-permute-start.8 = (bf16[128,1616]{1,0:T(8,128)(2,1)S(1)}, bf16[128,1616]{1,0:T(8,128)(2,1)S(1)}, u32[]{:S(2)}, u32[]{:S(2)}) collective-permute-start(bf16[128,1616]{1,0:T(8,128)(2,1)S(1)} %collective-permute-done.7.refs_6_), channel_id=1, source_target_pairs={{0,1},{1,2},{2,3},{3,4},{4,5},{5,6},{6,7},{7,0},{8,9},{9,10},{10,1... | collective-permute-start | bytes 1241096 | tf_op jit(solution)/shard_map/ppermute | solution.py:25
  53.2 0.0 collective-permute-done.4.refs_2_
  53.2 4.6 %collective-permute-start.5 = (bf16[128,1616]{1,0:T(8,128)(2,1)S(1)}, bf16[128,1616]{1,0:T(8,128)(2,1)S(1)}, u32[]{:S(2)}, u32[]{:S(2)}) collective-permute-start(bf16[128,1616]{1,0:T(8,128)(2,1)S(1)} %collective-permute-done.4.refs_2_), channel_id=1, source_target_pairs={{0,7},{1,0},{2,1},{3,2},{4,3},{5,4},{6,5},{7,6},{8,15},{9,8},{10,9... | collective-permute-start | bytes 1241096 | tf_op jit(solution)/shard_map/ppermute | solution.py:25
  57.8 0.2 add_reduce_fusion.1
  58.0 0.2 add_reduce_fusion.5
  58.2 3.6 %collective-permute-done.8.refs_5_ = bf16[128,1616]{1,0:T(8,128)(2,1)S(1)} collective-permute-done((bf16[128,1616]{1,0:T(8,128)(2,1)S(1)}, bf16[128,1616]{1,0:T(8,128)(2,1)S(1)}, u32[]{:S(2)}, u32[]{:S(2)}) %collective-permute-start.8) | collective-permute-done | bytes 413728 | tf_op jit(solution)/shard_map/ppermute | solution.py:25
  61.8 1.9 %collective-permute-start.9 = (bf16[128,1616]{1,0:T(8,128)(2,1)S(1)}, bf16[128,1616]{1,0:T(8,128)(2,1)S(1)}, u32[]{:S(2)}, u32[]{:S(2)}) collective-permute-start(bf16[128,1616]{1,0:T(8,128)(2,1)S(1)} %collective-permute-done.8.refs_5_), channel_id=1, source_target_pairs={{0,1},{1,2},{2,3},{3,4},{4,5},{5,6},{6,7},{7,0},{8,9},{9,10},{10,1... | collective-permute-start | bytes 1241096 | tf_op jit(solution)/shard_map/ppermute | solution.py:25
  63.7 0.2 add_reduce_fusion.2
  63.9 0.0 collective-permute-done.5.refs_3_
  63.9 0.2 add_reduce_fusion.4
  64.1 8.2 %collective-permute-done.9.refs_4_ = bf16[128,1616]{1,0:T(8,128)(2,1)S(1)} collective-permute-done((bf16[128,1616]{1,0:T(8,128)(2,1)S(1)}, bf16[128,1616]{1,0:T(8,128)(2,1)S(1)}, u32[]{:S(2)}, u32[]{:S(2)}) %collective-permute-start.9) | collective-permute-done | bytes 413728 | tf_op jit(solution)/shard_map/ppermute | solution.py:25
  72.2 0.2 add_reduce_fusion.3
  72.5 0.7 compare_select_fusion.4.refs_9_
  73.2 6.3 %all-gather.2.cloned.1.call-done.refs_8_ = bf16[2048,1600]{1,0:T(8,128)(2,1)} async-done(((bf16[128,1600]{1,0:T(8,128)(2,1)}), bf16[2048,1600]{1,0:T(8,128)(2,1)}) %all-gather.2.cloned.1.call-update) | async-done | bytes 6553616 | tf_op jit(solution)/shard_map/all_gather | solution.py:137
  79.6 13.6 %shard_map.68 = (f32[1,1024]{1,0:T(1,128)}, f32[1,1024]{1,0:T(1,128)}, f32[1,1024]{1,0:T(1,128)}, f32[1,1024]{1,0:T(1,128)}) custom-call(bf16[128,1616]{1,0:T(8,128)(2,1)} %copy-done.1, bf16[128,1616]{1,0:T(8,128)(2,1)} %copy-done.3, bf16[128,1616]{1,0:T(8,128)(2,1)} %copy-done.5, bf16[128,1616]{1,0:T(8,128)(2,1)} %copy-done.7, bf16[128,1616]{1,0:T(8,128)(2,1)} %copy-done.8, ...), custom_call_target="tpu_custom_call" | custom-call | flops 6710886400 | bytes 9830400 | tf_op jit(solution)/shard_map/pallas_call | solution.py:84
  93.2 0.7 maximum_bitcast_fusion
  94.0 12.9 %all_to_all.6 = f32[4,8,128]{2,0,1:T(4,128)S(1)} all-to-all(f32[4,8,128]{2,0,1:T(4,128)S(1)} %fusion.3), channel_id=1, replica_groups=mesh['z'=8,'x'=4,'c'=2,'y'=8] {'y'}, dimensions={1} | all-to-all | bytes 32768 | tf_op jit(solution)/shard_map/all_to_all | solution.py:147
  106.9 0.5 subtract_multiply_fusion
  (36 shorter events, 0.3 us)
Async XLA Ops:
  7.2 72.4 %all-gather.2.cloned.1.call-start = ((), (), s32[]{:S(2)}) async-start(), calls=%async_computation.1 | async-start | bytes 7241728 | tf_op jit(solution)/shard_map/all_gather | solution.py:137
  7.2 11.7 %collective-permute-start.1 = (bf16[32,1600]{1,0:T(8,128)(2,1)}, bf16[32,1600]{1,0:T(8,128)(2,1)S(1)}, u32[]{:S(2)}, u32[]{:S(2)}) collective-permute-start(bf16[32,1600]{1,0:T(8,128)(2,1)} %param.11), channel_id=1, source_target_pairs={{0,32},{16,48},{32,0},{48,16},{1,33},{17,49},{33,1},{49,17},{2,34}... | collective-permute-start | bytes 307208 | tf_op jit(solution)/shard_map/ppermute | solution.py:25
  12.7 6.2 %collective-permute-start = (bf16[32,1600]{1,0:T(8,128)(2,1)}, bf16[32,1600]{1,0:T(8,128)(2,1)S(1)}, u32[]{:S(2)}, u32[]{:S(2)}) collective-permute-start(bf16[32,1600]{1,0:T(8,128)(2,1)} %param.11), channel_id=1, source_target_pairs={{0,48},{16,0},{32,16},{48,32},{1,49},{17,1},{33,17},{49,33},{2,50}... | collective-permute-start | bytes 307208 | tf_op jit(solution)/shard_map/ppermute | solution.py:25
  15.5 7.7 %collective-permute-start.2 = (bf16[32,1600]{1,0:T(8,128)(2,1)}, bf16[32,1600]{1,0:T(8,128)(2,1)S(1)}, u32[]{:S(2)}, u32[]{:S(2)}) collective-permute-start(bf16[32,1600]{1,0:T(8,128)(2,1)} %param.11), channel_id=1, source_target_pairs={{0,16},{16,32},{32,48},{48,0},{1,17},{17,33},{33,49},{49,1},{2,18}... | collective-permute-start | bytes 307208 | tf_op jit(solution)/shard_map/ppermute | solution.py:25
  23.2 0.8 copy-start
  30.1 49.5 %copy-start.1 = (bf16[128,1616]{1,0:T(8,128)(2,1)}, bf16[128,1616]{1,0:T(8,128)(2,1)S(1)}, u32[]{:S(2)}) copy-start(bf16[128,1616]{1,0:T(8,128)(2,1)S(1)} %pad_maximum_fusion.refs_0_) | copy-start | bytes 1241092
  30.1 10.8 %collective-permute-start.6 = (bf16[128,1616]{1,0:T(8,128)(2,1)S(1)}, bf16[128,1616]{1,0:T(8,128)(2,1)S(1)}, u32[]{:S(2)}, u32[]{:S(2)}) collective-permute-start(bf16[128,1616]{1,0:T(8,128)(2,1)S(1)} %pad_maximum_fusion.refs_0_), channel_id=1, source_target_pairs={{0,1},{1,2},{2,3},{3,4},{4,5},{5,6},{6,7},{7,0},{8,9},{9,10},{10,1... | collective-permute-start | bytes 1241096 | tf_op jit(solution)/shard_map/ppermute | solution.py:25
  32.5 10.3 %collective-permute-start.3 = (bf16[128,1616]{1,0:T(8,128)(2,1)S(1)}, bf16[128,1616]{1,0:T(8,128)(2,1)S(1)}, u32[]{:S(2)}, u32[]{:S(2)}) collective-permute-start(bf16[128,1616]{1,0:T(8,128)(2,1)S(1)} %pad_maximum_fusion.refs_0_), channel_id=1, source_target_pairs={{0,7},{1,0},{2,1},{3,2},{4,3},{5,4},{6,5},{7,6},{8,15},{9,8},{10,9... | collective-permute-start | bytes 1241096 | tf_op jit(solution)/shard_map/ppermute | solution.py:25
  40.8 38.7 %copy-start.2 = (bf16[128,1616]{1,0:T(8,128)(2,1)}, bf16[128,1616]{1,0:T(8,128)(2,1)S(1)}, u32[]{:S(2)}) copy-start(bf16[128,1616]{1,0:T(8,128)(2,1)S(1)} %collective-permute-done.6.refs_7_) | copy-start | bytes 1241092
  40.8 10.5 %collective-permute-start.7 = (bf16[128,1616]{1,0:T(8,128)(2,1)S(1)}, bf16[128,1616]{1,0:T(8,128)(2,1)S(1)}, u32[]{:S(2)}, u32[]{:S(2)}) collective-permute-start(bf16[128,1616]{1,0:T(8,128)(2,1)S(1)} %collective-permute-done.6.refs_7_), channel_id=1, source_target_pairs={{0,1},{1,2},{2,3},{3,4},{4,5},{5,6},{6,7},{7,0},{8,9},{9,10},{10,1... | collective-permute-start | bytes 1241096 | tf_op jit(solution)/shard_map/ppermute | solution.py:25
  42.8 36.8 %copy-start.3 = (bf16[128,1616]{1,0:T(8,128)(2,1)}, bf16[128,1616]{1,0:T(8,128)(2,1)S(1)}, u32[]{:S(2)}) copy-start(bf16[128,1616]{1,0:T(8,128)(2,1)S(1)} %collective-permute-done.3.refs_1_) | copy-start | bytes 1241092
  42.8 10.4 %collective-permute-start.4 = (bf16[128,1616]{1,0:T(8,128)(2,1)S(1)}, bf16[128,1616]{1,0:T(8,128)(2,1)S(1)}, u32[]{:S(2)}, u32[]{:S(2)}) collective-permute-start(bf16[128,1616]{1,0:T(8,128)(2,1)S(1)} %collective-permute-done.3.refs_1_), channel_id=1, source_target_pairs={{0,7},{1,0},{2,1},{3,2},{4,3},{5,4},{6,5},{7,6},{8,15},{9,8},{10,9... | collective-permute-start | bytes 1241096 | tf_op jit(solution)/shard_map/ppermute | solution.py:25
  51.3 28.3 %copy-start.4 = (bf16[128,1616]{1,0:T(8,128)(2,1)}, bf16[128,1616]{1,0:T(8,128)(2,1)S(1)}, u32[]{:S(2)}) copy-start(bf16[128,1616]{1,0:T(8,128)(2,1)S(1)} %collective-permute-done.7.refs_6_) | copy-start | bytes 1241092
  51.3 10.5 %collective-permute-start.8 = (bf16[128,1616]{1,0:T(8,128)(2,1)S(1)}, bf16[128,1616]{1,0:T(8,128)(2,1)S(1)}, u32[]{:S(2)}, u32[]{:S(2)}) collective-permute-start(bf16[128,1616]{1,0:T(8,128)(2,1)S(1)} %collective-permute-done.7.refs_6_), channel_id=1, source_target_pairs={{0,1},{1,2},{2,3},{3,4},{4,5},{5,6},{6,7},{7,0},{8,9},{9,10},{10,1... | collective-permute-start | bytes 1241096 | tf_op jit(solution)/shard_map/ppermute | solution.py:25
  53.2 26.4 %copy-start.5 = (bf16[128,1616]{1,0:T(8,128)(2,1)}, bf16[128,1616]{1,0:T(8,128)(2,1)S(1)}, u32[]{:S(2)}) copy-start(bf16[128,1616]{1,0:T(8,128)(2,1)S(1)} %collective-permute-done.4.refs_2_) | copy-start | bytes 1241092
  53.2 10.6 %collective-permute-start.5 = (bf16[128,1616]{1,0:T(8,128)(2,1)S(1)}, bf16[128,1616]{1,0:T(8,128)(2,1)S(1)}, u32[]{:S(2)}, u32[]{:S(2)}) collective-permute-start(bf16[128,1616]{1,0:T(8,128)(2,1)S(1)} %collective-permute-done.4.refs_2_), channel_id=1, source_target_pairs={{0,7},{1,0},{2,1},{3,2},{4,3},{5,4},{6,5},{7,6},{8,15},{9,8},{10,9... | collective-permute-start | bytes 1241096 | tf_op jit(solution)/shard_map/ppermute | solution.py:25
  61.8 17.8 %copy-start.6 = (bf16[128,1616]{1,0:T(8,128)(2,1)}, bf16[128,1616]{1,0:T(8,128)(2,1)S(1)}, u32[]{:S(2)}) copy-start(bf16[128,1616]{1,0:T(8,128)(2,1)S(1)} %collective-permute-done.8.refs_5_) | copy-start | bytes 1241092
  61.8 10.5 %collective-permute-start.9 = (bf16[128,1616]{1,0:T(8,128)(2,1)S(1)}, bf16[128,1616]{1,0:T(8,128)(2,1)S(1)}, u32[]{:S(2)}, u32[]{:S(2)}) collective-permute-start(bf16[128,1616]{1,0:T(8,128)(2,1)S(1)} %collective-permute-done.8.refs_5_), channel_id=1, source_target_pairs={{0,1},{1,2},{2,3},{3,4},{4,5},{5,6},{6,7},{7,0},{8,9},{9,10},{10,1... | collective-permute-start | bytes 1241096 | tf_op jit(solution)/shard_map/ppermute | solution.py:25
  63.9 15.7 %copy-start.7 = (bf16[128,1616]{1,0:T(8,128)(2,1)}, bf16[128,1616]{1,0:T(8,128)(2,1)S(1)}, u32[]{:S(2)}) copy-start(bf16[128,1616]{1,0:T(8,128)(2,1)S(1)} %collective-permute-done.5.refs_3_) | copy-start | bytes 1241092
  72.2 7.4 %copy-start.8 = (bf16[128,1616]{1,0:T(8,128)(2,1)}, bf16[128,1616]{1,0:T(8,128)(2,1)S(1)}, u32[]{:S(2)}) copy-start(bf16[128,1616]{1,0:T(8,128)(2,1)S(1)} %collective-permute-done.9.refs_4_) | copy-start | bytes 1241092
  73.2 33.7 %copy-start.9 = (s32[128]{0:T(128)S(1)}, s32[128]{0:T(128)}, u32[]{:S(2)}) copy-start(s32[128]{0:T(128)} %param.13) | copy-start | bytes 1540
Sparse Core Ops, SparseCore 0:
  24.1 55.4 all-gather.1

commit v18 on v17

--- a/solution.py
+++ b/solution.py
@@ -38,7 +38,7 @@
 
 def stats_kernel(parts, dim, *refs):
     block_refs = refs[:parts]
-    vocab_ref, spot_ref, top_ref, total_ref, spread_ref, chosen_ref, rows_ref = refs[parts:]
+    where_ref, vocab_ref, spot_ref, top_ref, total_ref, spread_ref, chosen_ref, rows_ref = refs[parts:]
     j = pl.program_id(0)
     tile = vocab_ref.shape[0]
     position = j * tile + lax.broadcasted_iota(jnp.int32, (tile, 1), 0)
@@ -47,7 +47,8 @@
     def _():
         size = block_refs[0].shape[0]
         for b, block_ref in enumerate(block_refs):
-            rows_ref[b * size : (b + 1) * size, :] = block_ref[:, :dim]
+            place = pl.multiple_of(((where_ref[0] + b) % parts) * size, size)
+            rows_ref[pl.ds(place, size), :] = block_ref[:, :dim]
         top_ref[...] = jnp.full(top_ref.shape, -1e30, jnp.float32)
         total_ref[...] = jnp.zeros(total_ref.shape, jnp.float32)
         spread_ref[...] = jnp.zeros(spread_ref.shape, jnp.float32)
@@ -75,7 +76,7 @@
     top_ref[...] = top
 
 
-def row_stats(blocks, dim, vocab, spot, tile=1024):
+def row_stats(blocks, dim, where, vocab, spot, tile=512):
     size = blocks[0].shape[0]
     count = size * len(blocks)
     width = vocab.shape[0]
@@ -84,7 +85,8 @@
     outs = pl.pallas_call(
         functools.partial(stats_kernel, len(blocks), dim),
         grid=(width // tile,),
-        in_specs=[whole_block] * len(blocks) + [pl.BlockSpec((tile, dim), lambda j: (j, 0)), line],
+        in_specs=[whole_block] * len(blocks)
+        + [pl.BlockSpec(memory_space=pltpu.SMEM), pl.BlockSpec((tile, dim), lambda j: (j, 0)), line],
         out_specs=[line, line, line, line],
         out_shape=[jax.ShapeDtypeStruct((1, count), jnp.float32)] * 4,
         scratch_shapes=[pltpu.VMEM((count, dim), blocks[0].dtype)],
@@ -93,7 +95,7 @@
             transcendentals=count * width,
             bytes_accessed=2 * (count + width) * dim,
         ),
-    )(*blocks, vocab, spot.reshape(1, count))
+    )(*blocks, where, vocab, spot.reshape(1, count))
     return tuple(o.reshape(count) for o in outs)
 
 
@@ -141,9 +143,10 @@
     spot = ((far_z * nc + far_c) * nx + (far_x - x) % nx) * width + entry
     spot = jnp.where(shard == y, spot, -1)
 
-    stats = row_stats(blocks, dim, whole, spot)
+    spot = jnp.roll(spot, y * mine)
+    stats = row_stats(blocks, dim, y.astype(jnp.int32).reshape(1), whole, spot)
 
-    packed = jnp.roll(jnp.stack(stats).reshape(4, ny, mine), y, axis=1).reshape(4, ny * mine)
+    packed = jnp.stack(stats)
     got = lax.all_to_all(packed, "y", 1, 1, tiled=True).reshape(4, ny, mine)
     tops, totals, spreads, chosen = got[0], got[1], got[2], got[3]
     top = jnp.max(tops, axis=0)

time: 116 us -> 116 us (level)
  transfers between devices with their start and end apart: 11 -> 11, of which waited for: 6 -> 7; matrix products, arithmetic and copies ran while one was open for 8% -> 8% of each run, Pallas kernels for 0% -> 0%
where the time goes in v18:
time: 116 us; the launch traced here: 114 us
  starting transfers between devices  32.2 us (28%)
  waiting for transfers between devices  29.9 us (26%)
  between operations  14.4 us (12%)
  Pallas kernels  13.6 us (12%)
  blocking collectives  12.9 us (11%)
  other arithmetic  7.88 us (7%)
  local copies, waits for them, and re-layouts  3.5 us (3%)
    ppermute x10, starting transfers between devices, shift(): lax.ppermute(value, axis, [(i, (i + step) % size) for i in range(size)])  32.1 us
    ppermute x10, waiting for transfers between devices, shift(): lax.ppermute(value, axis, [(i, (i + step) % size) for i in range(size)])  23.5 us
    pallas_call x1, Pallas kernels, row_stats(): pl.pallas_call(functools.partial(stats_kernel, len(blocks), dim), grid=(w...  13.6 us
    all_to_all x1, blocking collectives, on_device(): got = lax.all_to_all(packed, 'y', 1, 1, tiled=True).reshape(4, ny, mine)  12.9 us
    all_gather x1, waiting for transfers between devices, on_device(): whole = lax.all_gather(table, ('z', 'c'), axis=0, tiled=True)  6.36 us
    another operation x3, other arithmetic  3.24 us
    unnamed x31, local copies, waits for them, and re-layouts  3.02 us
  transfers between devices with their start and end apart: 11, of which 7 were waited for; matrix products, arithmetic and copies ran while one was open for 8% of the time, Pallas kernels for 0%

profile of v18, /device:TPU:1, one launch (start us, length us, event | category | flops | bytes accessed | tf_op | source)
XLA Modules:
  0.0 114.3 jit_solution(9779777492800810343)
XLA Ops:
  7.2 0.0 all-gather.2.cloned.1.call-start
  7.2 5.5 %collective-permute-start.1 = (bf16[32,1600]{1,0:T(8,128)(2,1)}, bf16[32,1600]{1,0:T(8,128)(2,1)S(1)}, u32[]{:S(2)}, u32[]{:S(2)}) collective-permute-start(bf16[32,1600]{1,0:T(8,128)(2,1)} %param.11), channel_id=1, source_target_pairs={{0,32},{16,48},{32,0},{48,16},{1,33},{17,49},{33,1},{49,17},{2,34}... | collective-permute-start | bytes 307208 | tf_op jit(solution)/shard_map/ppermute | solution.py:25
  12.7 2.8 %collective-permute-start = (bf16[32,1600]{1,0:T(8,128)(2,1)}, bf16[32,1600]{1,0:T(8,128)(2,1)S(1)}, u32[]{:S(2)}, u32[]{:S(2)}) collective-permute-start(bf16[32,1600]{1,0:T(8,128)(2,1)} %param.11), channel_id=1, source_target_pairs={{0,48},{16,0},{32,16},{48,32},{1,49},{17,1},{33,17},{49,33},{2,50}... | collective-permute-start | bytes 307208 | tf_op jit(solution)/shard_map/ppermute | solution.py:25
  15.5 2.5 %collective-permute-start.2 = (bf16[32,1600]{1,0:T(8,128)(2,1)}, bf16[32,1600]{1,0:T(8,128)(2,1)S(1)}, u32[]{:S(2)}, u32[]{:S(2)}) collective-permute-start(bf16[32,1600]{1,0:T(8,128)(2,1)} %param.11), channel_id=1, source_target_pairs={{0,16},{16,32},{32,48},{48,0},{1,17},{17,33},{33,49},{49,1},{2,18}... | collective-permute-start | bytes 307208 | tf_op jit(solution)/shard_map/ppermute | solution.py:25
  18.0 0.9 constant_dynamic-update-slice_fusion.3
  18.9 0.0 collective-permute-done.1
  19.0 4.2 %collective-permute-done.2 = bf16[32,1600]{1,0:T(8,128)(2,1)S(1)} collective-permute-done((bf16[32,1600]{1,0:T(8,128)(2,1)}, bf16[32,1600]{1,0:T(8,128)(2,1)S(1)}, u32[]{:S(2)}, u32[]{:S(2)}) %collective-permute-start.2) | collective-permute-done | bytes 102432 | tf_op jit(solution)/shard_map/ppermute | solution.py:25
  23.2 0.7 copy-done
  23.9 0.0 all-gather.2.cloned.1.call-update
  23.9 0.6 compare_reduce_fusion.1
  24.6 0.6 compare_reduce_fusion
  25.2 2.0 %fusion.22 = (bf16[128,1]{0,1:T(2,128)(2,1)S(1)}, bf16[128,1]{0,1:T(2,128)(2,1)S(1)}) fusion(pred[]{:T(512)} %compare_reduce_fusion, s32[128]{0:T(128)} %param.12, pred[]{:T(512)} %compare_reduce_fusion.1), kind=kLoop, calls=%fused_computation.87 | loop fusion | flops 2944 | bytes 1026 | tf_op jit(solution)/shard_map/reshape.83
  27.2 0.1 copy.15
  27.3 0.1 copy.14
  27.5 1.2 %copy.13 = bf16[128,1600]{1,0:T(8,128)(2,1)S(1)} copy(bf16[128,1600]{0,1:T(8,128)(2,1)} %param.9) | data formatting | bytes 819200 | tf_op args[0]
  28.7 0.2 scatter.9
  28.9 0.2 fusion
  29.1 0.9 fusion.2
  30.0 0.1 pad_maximum_fusion.refs_0_
  30.1 2.4 %collective-permute-start.6 = (bf16[128,1616]{1,0:T(8,128)(2,1)S(1)}, bf16[128,1616]{1,0:T(8,128)(2,1)S(1)}, u32[]{:S(2)}, u32[]{:S(2)}) collective-permute-start(bf16[128,1616]{1,0:T(8,128)(2,1)S(1)} %pad_maximum_fusion.refs_0_), channel_id=1, source_target_pairs={{0,1},{1,2},{2,3},{3,4},{4,5},{5,6},{6,7},{7,0},{8,9},{9,10},{10,1... | collective-permute-start | bytes 1241096 | tf_op jit(solution)/shard_map/ppermute | solution.py:25
  32.5 4.1 %collective-permute-start.3 = (bf16[128,1616]{1,0:T(8,128)(2,1)S(1)}, bf16[128,1616]{1,0:T(8,128)(2,1)S(1)}, u32[]{:S(2)}, u32[]{:S(2)}) collective-permute-start(bf16[128,1616]{1,0:T(8,128)(2,1)S(1)} %pad_maximum_fusion.refs_0_), channel_id=1, source_target_pairs={{0,7},{1,0},{2,1},{3,2},{4,3},{5,4},{6,5},{7,6},{8,15},{9,8},{10,9... | collective-permute-start | bytes 1241096 | tf_op jit(solution)/shard_map/ppermute | solution.py:25
  36.6 4.2 %collective-permute-done.6.refs_7_ = bf16[128,1616]{1,0:T(8,128)(2,1)S(1)} collective-permute-done((bf16[128,1616]{1,0:T(8,128)(2,1)S(1)}, bf16[128,1616]{1,0:T(8,128)(2,1)S(1)}, u32[]{:S(2)}, u32[]{:S(2)}) %collective-permute-start.6) | collective-permute-done | bytes 413728 | tf_op jit(solution)/shard_map/ppermute | solution.py:25
  40.8 1.9 %collective-permute-start.7 = (bf16[128,1616]{1,0:T(8,128)(2,1)S(1)}, bf16[128,1616]{1,0:T(8,128)(2,1)S(1)}, u32[]{:S(2)}, u32[]{:S(2)}) collective-permute-start(bf16[128,1616]{1,0:T(8,128)(2,1)S(1)} %collective-permute-done.6.refs_7_), channel_id=1, source_target_pairs={{0,1},{1,2},{2,3},{3,4},{4,5},{5,6},{6,7},{7,0},{8,9},{9,10},{10,1... | collective-permute-start | bytes 1241096 | tf_op jit(solution)/shard_map/ppermute | solution.py:25
  42.8 0.0 collective-permute-done.3.refs_1_
  42.8 4.5 %collective-permute-start.4 = (bf16[128,1616]{1,0:T(8,128)(2,1)S(1)}, bf16[128,1616]{1,0:T(8,128)(2,1)S(1)}, u32[]{:S(2)}, u32[]{:S(2)}) collective-permute-start(bf16[128,1616]{1,0:T(8,128)(2,1)S(1)} %collective-permute-done.3.refs_1_), channel_id=1, source_target_pairs={{0,7},{1,0},{2,1},{3,2},{4,3},{5,4},{6,5},{7,6},{8,15},{9,8},{10,9... | collective-permute-start | bytes 1241096 | tf_op jit(solution)/shard_map/ppermute | solution.py:25
  47.4 0.2 add_reduce_fusion.7
  47.6 0.2 add_reduce_fusion
  47.8 3.5 %collective-permute-done.7.refs_6_ = bf16[128,1616]{1,0:T(8,128)(2,1)S(1)} collective-permute-done((bf16[128,1616]{1,0:T(8,128)(2,1)S(1)}, bf16[128,1616]{1,0:T(8,128)(2,1)S(1)}, u32[]{:S(2)}, u32[]{:S(2)}) %collective-permute-start.7) | collective-permute-done | bytes 413728 | tf_op jit(solution)/shard_map/ppermute | solution.py:25
  51.3 1.9 %collective-permute-start.8 = (bf16[128,1616]{1,0:T(8,128)(2,1)S(1)}, bf16[128,1616]{1,0:T(8,128)(2,1)S(1)}, u32[]{:S(2)}, u32[]{:S(2)}) collective-permute-start(bf16[128,1616]{1,0:T(8,128)(2,1)S(1)} %collective-permute-done.7.refs_6_), channel_id=1, source_target_pairs={{0,1},{1,2},{2,3},{3,4},{4,5},{5,6},{6,7},{7,0},{8,9},{9,10},{10,1... | collective-permute-start | bytes 1241096 | tf_op jit(solution)/shard_map/ppermute | solution.py:25
  53.2 0.2 add_reduce_fusion.6
  53.4 0.0 collective-permute-done.4.refs_2_
  53.4 4.6 %collective-permute-start.5 = (bf16[128,1616]{1,0:T(8,128)(2,1)S(1)}, bf16[128,1616]{1,0:T(8,128)(2,1)S(1)}, u32[]{:S(2)}, u32[]{:S(2)}) collective-permute-start(bf16[128,1616]{1,0:T(8,128)(2,1)S(1)} %collective-permute-done.4.refs_2_), channel_id=1, source_target_pairs={{0,7},{1,0},{2,1},{3,2},{4,3},{5,4},{6,5},{7,6},{8,15},{9,8},{10,9... | collective-permute-start | bytes 1241096 | tf_op jit(solution)/shard_map/ppermute | solution.py:25
  58.0 0.2 add_reduce_fusion.1
  58.2 0.2 add_reduce_fusion.5
  58.4 3.4 %collective-permute-done.8.refs_5_ = bf16[128,1616]{1,0:T(8,128)(2,1)S(1)} collective-permute-done((bf16[128,1616]{1,0:T(8,128)(2,1)S(1)}, bf16[128,1616]{1,0:T(8,128)(2,1)S(1)}, u32[]{:S(2)}, u32[]{:S(2)}) %collective-permute-start.8) | collective-permute-done | bytes 413728 | tf_op jit(solution)/shard_map/ppermute | solution.py:25
  61.8 1.9 %collective-permute-start.9 = (bf16[128,1616]{1,0:T(8,128)(2,1)S(1)}, bf16[128,1616]{1,0:T(8,128)(2,1)S(1)}, u32[]{:S(2)}, u32[]{:S(2)}) collective-permute-start(bf16[128,1616]{1,0:T(8,128)(2,1)S(1)} %collective-permute-done.8.refs_5_), channel_id=1, source_target_pairs={{0,1},{1,2},{2,3},{3,4},{4,5},{5,6},{6,7},{7,0},{8,9},{9,10},{10,1... | collective-permute-start | bytes 1241096 | tf_op jit(solution)/shard_map/ppermute | solution.py:25
  63.7 0.1 collective-permute-done.5.refs_3_
  63.8 0.2 add_reduce_fusion.4
  64.0 0.2 add_reduce_fusion.2
  64.2 8.1 %collective-permute-done.9.refs_4_ = bf16[128,1616]{1,0:T(8,128)(2,1)S(1)} collective-permute-done((bf16[128,1616]{1,0:T(8,128)(2,1)S(1)}, bf16[128,1616]{1,0:T(8,128)(2,1)S(1)}, u32[]{:S(2)}, u32[]{:S(2)}) %collective-permute-start.9) | collective-permute-done | bytes 413728 | tf_op jit(solution)/shard_map/ppermute | solution.py:25
  72.2 0.2 add_reduce_fusion.3
  72.5 0.7 fusion.15
  73.2 6.4 %all-gather.2.cloned.1.call-done.refs_9_ = bf16[2048,1600]{1,0:T(8,128)(2,1)} async-done(((bf16[128,1600]{1,0:T(8,128)(2,1)}), bf16[2048,1600]{1,0:T(8,128)(2,1)}) %all-gather.2.cloned.1.call-update) | async-done | bytes 6553616 | tf_op jit(solution)/shard_map/all_gather | solution.py:139
  79.6 0.0 copy-start.9
  79.6 13.6 %shard_map.68 = (f32[1,1024]{1,0:T(1,128)}, f32[1,1024]{1,0:T(1,128)}, f32[1,1024]{1,0:T(1,128)}, f32[1,1024]{1,0:T(1,128)}) custom-call(bf16[128,1616]{1,0:T(8,128)(2,1)} %copy-done.1, bf16[128,1616]{1,0:T(8,128)(2,1)} %copy-done.3, bf16[128,1616]{1,0:T(8,128)(2,1)} %copy-done.5, bf16[128,1616]{1,0:T(8,128)(2,1)} %copy-done.7, bf16[128,1616]{1,0:T(8,128)(2,1)} %copy-done.8, ...), custom_call_target="tpu_custom_call" | custom-call | flops 6710886400 | bytes 9830400 | tf_op jit(solution)/shard_map/pallas_call | solution.py:85
  93.2 0.7 maximum_bitcast_fusion
  94.0 12.9 %all_to_all.9 = f32[4,8,128]{2,0,1:T(4,128)S(1)} all-to-all(f32[4,8,128]{2,0,1:T(4,128)S(1)} %maximum_bitcast_fusion), channel_id=1, replica_groups=mesh['z'=8,'x'=4,'c'=2,'y'=8] {'y'}, dimensions={1} | all-to-all | bytes 32768 | tf_op jit(solution)/shard_map/all_to_all | solution.py:150
  106.9 0.5 subtract_multiply_fusion
  (37 shorter events, 0.3 us)
Async XLA Ops:
  7.2 72.4 %all-gather.2.cloned.1.call-start = ((), (), s32[]{:S(2)}) async-start(), calls=%async_computation.1 | async-start | bytes 7241728 | tf_op jit(solution)/shard_map/all_gather | solution.py:139
  7.2 11.7 %collective-permute-start.1 = (bf16[32,1600]{1,0:T(8,128)(2,1)}, bf16[32,1600]{1,0:T(8,128)(2,1)S(1)}, u32[]{:S(2)}, u32[]{:S(2)}) collective-permute-start(bf16[32,1600]{1,0:T(8,128)(2,1)} %param.11), channel_id=1, source_target_pairs={{0,32},{16,48},{32,0},{48,16},{1,33},{17,49},{33,1},{49,17},{2,34}... | collective-permute-start | bytes 307208 | tf_op jit(solution)/shard_map/ppermute | solution.py:25
  12.7 6.2 %collective-permute-start = (bf16[32,1600]{1,0:T(8,128)(2,1)}, bf16[32,1600]{1,0:T(8,128)(2,1)S(1)}, u32[]{:S(2)}, u32[]{:S(2)}) collective-permute-start(bf16[32,1600]{1,0:T(8,128)(2,1)} %param.11), channel_id=1, source_target_pairs={{0,48},{16,0},{32,16},{48,32},{1,49},{17,1},{33,17},{49,33},{2,50}... | collective-permute-start | bytes 307208 | tf_op jit(solution)/shard_map/ppermute | solution.py:25
  15.5 7.7 %collective-permute-start.2 = (bf16[32,1600]{1,0:T(8,128)(2,1)}, bf16[32,1600]{1,0:T(8,128)(2,1)S(1)}, u32[]{:S(2)}, u32[]{:S(2)}) collective-permute-start(bf16[32,1600]{1,0:T(8,128)(2,1)} %param.11), channel_id=1, source_target_pairs={{0,16},{16,32},{32,48},{48,0},{1,17},{17,33},{33,49},{49,1},{2,18}... | collective-permute-start | bytes 307208 | tf_op jit(solution)/shard_map/ppermute | solution.py:25
  23.2 0.8 copy-start
  30.1 49.5 %copy-start.1 = (bf16[128,1616]{1,0:T(8,128)(2,1)}, bf16[128,1616]{1,0:T(8,128)(2,1)S(1)}, u32[]{:S(2)}) copy-start(bf16[128,1616]{1,0:T(8,128)(2,1)S(1)} %pad_maximum_fusion.refs_0_) | copy-start | bytes 1241092
  30.1 10.8 %collective-permute-start.6 = (bf16[128,1616]{1,0:T(8,128)(2,1)S(1)}, bf16[128,1616]{1,0:T(8,128)(2,1)S(1)}, u32[]{:S(2)}, u32[]{:S(2)}) collective-permute-start(bf16[128,1616]{1,0:T(8,128)(2,1)S(1)} %pad_maximum_fusion.refs_0_), channel_id=1, source_target_pairs={{0,1},{1,2},{2,3},{3,4},{4,5},{5,6},{6,7},{7,0},{8,9},{9,10},{10,1... | collective-permute-start | bytes 1241096 | tf_op jit(solution)/shard_map/ppermute | solution.py:25
  32.5 10.3 %collective-permute-start.3 = (bf16[128,1616]{1,0:T(8,128)(2,1)S(1)}, bf16[128,1616]{1,0:T(8,128)(2,1)S(1)}, u32[]{:S(2)}, u32[]{:S(2)}) collective-permute-start(bf16[128,1616]{1,0:T(8,128)(2,1)S(1)} %pad_maximum_fusion.refs_0_), channel_id=1, source_target_pairs={{0,7},{1,0},{2,1},{3,2},{4,3},{5,4},{6,5},{7,6},{8,15},{9,8},{10,9... | collective-permute-start | bytes 1241096 | tf_op jit(solution)/shard_map/ppermute | solution.py:25
  40.8 38.7 %copy-start.2 = (bf16[128,1616]{1,0:T(8,128)(2,1)}, bf16[128,1616]{1,0:T(8,128)(2,1)S(1)}, u32[]{:S(2)}) copy-start(bf16[128,1616]{1,0:T(8,128)(2,1)S(1)} %collective-permute-done.6.refs_7_) | copy-start | bytes 1241092
  40.8 10.5 %collective-permute-start.7 = (bf16[128,1616]{1,0:T(8,128)(2,1)S(1)}, bf16[128,1616]{1,0:T(8,128)(2,1)S(1)}, u32[]{:S(2)}, u32[]{:S(2)}) collective-permute-start(bf16[128,1616]{1,0:T(8,128)(2,1)S(1)} %collective-permute-done.6.refs_7_), channel_id=1, source_target_pairs={{0,1},{1,2},{2,3},{3,4},{4,5},{5,6},{6,7},{7,0},{8,9},{9,10},{10,1... | collective-permute-start | bytes 1241096 | tf_op jit(solution)/shard_map/ppermute | solution.py:25
  42.8 36.8 %copy-start.3 = (bf16[128,1616]{1,0:T(8,128)(2,1)}, bf16[128,1616]{1,0:T(8,128)(2,1)S(1)}, u32[]{:S(2)}) copy-start(bf16[128,1616]{1,0:T(8,128)(2,1)S(1)} %collective-permute-done.3.refs_1_) | copy-start | bytes 1241092
  42.8 10.6 %collective-permute-start.4 = (bf16[128,1616]{1,0:T(8,128)(2,1)S(1)}, bf16[128,1616]{1,0:T(8,128)(2,1)S(1)}, u32[]{:S(2)}, u32[]{:S(2)}) collective-permute-start(bf16[128,1616]{1,0:T(8,128)(2,1)S(1)} %collective-permute-done.3.refs_1_), channel_id=1, source_target_pairs={{0,7},{1,0},{2,1},{3,2},{4,3},{5,4},{6,5},{7,6},{8,15},{9,8},{10,9... | collective-permute-start | bytes 1241096 | tf_op jit(solution)/shard_map/ppermute | solution.py:25
  51.3 28.3 %copy-start.4 = (bf16[128,1616]{1,0:T(8,128)(2,1)}, bf16[128,1616]{1,0:T(8,128)(2,1)S(1)}, u32[]{:S(2)}) copy-start(bf16[128,1616]{1,0:T(8,128)(2,1)S(1)} %collective-permute-done.7.refs_6_) | copy-start | bytes 1241092
  51.3 10.5 %collective-permute-start.8 = (bf16[128,1616]{1,0:T(8,128)(2,1)S(1)}, bf16[128,1616]{1,0:T(8,128)(2,1)S(1)}, u32[]{:S(2)}, u32[]{:S(2)}) collective-permute-start(bf16[128,1616]{1,0:T(8,128)(2,1)S(1)} %collective-permute-done.7.refs_6_), channel_id=1, source_target_pairs={{0,1},{1,2},{2,3},{3,4},{4,5},{5,6},{6,7},{7,0},{8,9},{9,10},{10,1... | collective-permute-start | bytes 1241096 | tf_op jit(solution)/shard_map/ppermute | solution.py:25
  53.4 26.2 %copy-start.5 = (bf16[128,1616]{1,0:T(8,128)(2,1)}, bf16[128,1616]{1,0:T(8,128)(2,1)S(1)}, u32[]{:S(2)}) copy-start(bf16[128,1616]{1,0:T(8,128)(2,1)S(1)} %collective-permute-done.4.refs_2_) | copy-start | bytes 1241092
  53.4 10.4 %collective-permute-start.5 = (bf16[128,1616]{1,0:T(8,128)(2,1)S(1)}, bf16[128,1616]{1,0:T(8,128)(2,1)S(1)}, u32[]{:S(2)}, u32[]{:S(2)}) collective-permute-start(bf16[128,1616]{1,0:T(8,128)(2,1)S(1)} %collective-permute-done.4.refs_2_), channel_id=1, source_target_pairs={{0,7},{1,0},{2,1},{3,2},{4,3},{5,4},{6,5},{7,6},{8,15},{9,8},{10,9... | collective-permute-start | bytes 1241096 | tf_op jit(solution)/shard_map/ppermute | solution.py:25
  61.8 17.8 %copy-start.6 = (bf16[128,1616]{1,0:T(8,128)(2,1)}, bf16[128,1616]{1,0:T(8,128)(2,1)S(1)}, u32[]{:S(2)}) copy-start(bf16[128,1616]{1,0:T(8,128)(2,1)S(1)} %collective-permute-done.8.refs_5_) | copy-start | bytes 1241092
  61.8 10.5 %collective-permute-start.9 = (bf16[128,1616]{1,0:T(8,128)(2,1)S(1)}, bf16[128,1616]{1,0:T(8,128)(2,1)S(1)}, u32[]{:S(2)}, u32[]{:S(2)}) collective-permute-start(bf16[128,1616]{1,0:T(8,128)(2,1)S(1)} %collective-permute-done.8.refs_5_), channel_id=1, source_target_pairs={{0,1},{1,2},{2,3},{3,4},{4,5},{5,6},{6,7},{7,0},{8,9},{9,10},{10,1... | collective-permute-start | bytes 1241096 | tf_op jit(solution)/shard_map/ppermute | solution.py:25
  63.8 15.8 %copy-start.7 = (bf16[128,1616]{1,0:T(8,128)(2,1)}, bf16[128,1616]{1,0:T(8,128)(2,1)S(1)}, u32[]{:S(2)}) copy-start(bf16[128,1616]{1,0:T(8,128)(2,1)S(1)} %collective-permute-done.5.refs_3_) | copy-start | bytes 1241092
  72.2 7.4 %copy-start.8 = (bf16[128,1616]{1,0:T(8,128)(2,1)}, bf16[128,1616]{1,0:T(8,128)(2,1)S(1)}, u32[]{:S(2)}) copy-start(bf16[128,1616]{1,0:T(8,128)(2,1)S(1)} %collective-permute-done.9.refs_4_) | copy-start | bytes 1241092
  79.6 27.3 %copy-start.9 = (s32[128]{0:T(128)S(1)}, s32[128]{0:T(128)}, u32[]{:S(2)}) copy-start(s32[128]{0:T(128)} %param.13) | copy-start | bytes 1540
Sparse Core Ops, SparseCore 0:
  24.1 55.4 all-gather.1
